TPU v7x, 32 devices: a whole 2x2x4 slice. The times are simulated.
32 devices in a mesh: dp: 8 (over z, x), head: 4 (over y, core).
Axes of the slice: x: 2, y: 2, z: 4, core: 2. Of those that a mesh axis runs over, the one named last changes fastest.
Arguments:
- tokens: bfloat16 [4096, 3072], P(('dp', 'head')), may hold values from -6 to 6
- norm_gain: bfloat16 [3072], replicated, may hold values from 0.099609375 to 1.8984375
- w_query: bfloat16 [3072, 1536], P(None, 'head'), may hold values from -0.109375 to 0.109375
- key_value_weight: bfloat16 [3072, 512], P(None, 'head'), may hold values from -0.21875 to 0.21875
- w_out: bfloat16 [1536, 3072], P('head'), may hold values from -0.15625 to 0.15625
- kv_pool: bfloat16 [384, 2, 2, 128, 128], P('dp'), may hold values from -400 to 400
- cache_lengths: int32 [8], replicated, may hold values from 3969 to 8192, as said below
- page_table: int32 [8, 64], replicated, may hold values from -1 to 383, as said below
- token_mask: int32 [4096], replicated, may hold values 0 or 1
Outputs:
- attn_out: bfloat16 [4096, 3072], P(('dp', 'head'))
Inputs may be any that keep to these rules, and one draw needn't show every extreme that they name: Request r caches cache_lengths[r] tokens in its first ceil(cache_lengths[r] / 128) logical pages; exactly one request caches 64 * 128 tokens. page_table[r, j] is the pool page of logical page j of request r while j is below that request's page count, else -1; no pool page is named twice; pool page p sits on dp index p // 48; at most 8 pages of one request sit on one dp index, and one request has exactly 8 on every dp index.
All inputs are finite; a program needn't handle non-finite values.
Results may differ from a plain program's by a relative error of at most 0.0049.
The roundings to bfloat16 on the way count: a program that leaves them out, or rounds other values in their place, can miss the bound.
Values may be sent and summed in bfloat16 or wider, within the bound.
No kernel may reach another device: no remote copies, remote signals or barrier semaphores. Data moves between devices by JAX's collectives and lax.ppermute only.
A program may use at most 192 MiB of HBM per device.

v0:
```python
import math

import jax
import jax.numpy as jnp
from jax import lax
from jax.sharding import PartitionSpec as P

KEY_VALUE_HEADS = 2
HEAD_SIZE = 128
NEWTOK = 512
REQ_DEV = 1


rope_base = 100000000000.0


def from_partner(value, axis, stride):
    mask = 2**stride
    pairs = [(source, source ^ mask) for source in range(lax.axis_size(axis))]
    return lax.ppermute(value, axis, pairs)


def rotate(values, positions):
    half_dim = values.shape[-1] // 2
    freqs = jnp.exp(
        jnp.arange(half_dim, dtype=jnp.float32) * (-2.0 * math.log(rope_base) / values.shape[-1])
    )
    angles = positions.astype(jnp.float32)[:, None] * freqs[None, :]
    cosine = jnp.cos(angles)[:, None, :]
    sine = jnp.sin(angles)[:, None, :]
    first = values[..., :half_dim]
    second = values[..., half_dim:]
    return jnp.concatenate([first * cosine - second * sine, second * cosine + first * sine], -1)


def body(
    tokens,
    norm_gain,
    w_query,
    key_value_weight,
    w_out,
    kv_pool,
    cache_lengths,
    page_table,
    token_mask,
):
    n_dp = lax.axis_size("dp")
    head_number = lax.axis_size("head")
    me_dp = lax.axis_index("dp")
    current_head = lax.axis_index("head")
    local_rows = tokens.shape[0]
    block_rows = local_rows * head_number
    head_dim = HEAD_SIZE
    group_heads = w_query.shape[1] // head_dim
    page_len = kv_pool.shape[3]
    pool_rows = kv_pool.shape[0]
    max_pages = page_table.shape[1]
    slots = max_pages // n_dp
    key_value_head = current_head // (head_number // KEY_VALUE_HEADS)
    owner_of = jnp.where(page_table >= 0, page_table // pool_rows, -1)
    mine = (owner_of == me_dp).astype(jnp.int32)
    rank = jnp.cumsum(mine, 1) - 1
    slot_ids = jnp.arange(slots, dtype=jnp.int32)
    select = (mine[:, None, :] == 1) & (rank[:, None, :] == slot_ids[None, :, None])
    local_page = jnp.sum(jnp.where(select, (page_table % pool_rows)[:, None, :], 0), -1)
    present = jnp.any(select, -1).reshape(-1)
    outgoing = kv_pool[local_page.reshape(-1), key_value_head]
    outgoing = jnp.where(present[:, None, None, None], outgoing, jnp.zeros_like(outgoing))
    received = lax.all_to_all(outgoing, "dp", split_axis=0, concat_axis=0, tiled=True)
    within = jnp.arange(page_len, dtype=jnp.int32)
    owners_mine = lax.dynamic_slice_in_dim(owner_of, me_dp * REQ_DEV, REQ_DEV, 0)
    hits = (owners_mine[None, :, :] == jnp.arange(n_dp, dtype=jnp.int32)[:, None, None]).astype(
        jnp.int32
    )
    hit_rank = jnp.cumsum(hits, -1) - 1
    chosen = (hits[:, :, None, :] == 1) & (hit_rank[:, :, None, :] == slot_ids[None, None, :, None])
    logical = jnp.sum(
        jnp.where(chosen, jnp.arange(max_pages, dtype=jnp.int32)[None, None, None, :], 0), -1
    )
    has_page = jnp.any(chosen, -1)
    key_pos = logical[..., None] * page_len + within[None, None, None, :]
    received = received.reshape(n_dp, REQ_DEV, slots, 2, page_len, head_dim)
    wide = tokens.astype(jnp.float32)
    meansq = jnp.mean(wide * wide, -1, keepdims=True)
    normalized_input = (wide * lax.rsqrt(meansq + 1e-05) * norm_gain.astype(jnp.float32)).astype(
        jnp.bfloat16
    )
    piece = lax.all_gather(normalized_input, "head", axis=0, tiled=True)
    q_part = jnp.dot(piece, w_query, preferred_element_type=jnp.float32)
    kv_part = jnp.dot(piece, key_value_weight, preferred_element_type=jnp.float32)
    projected = jnp.concatenate([q_part, kv_part], 1)
    q_width = group_heads * head_dim
    row_ids = jnp.arange(block_rows, dtype=jnp.int32)
    my_lengths = lax.dynamic_slice_in_dim(cache_lengths, me_dp * REQ_DEV, REQ_DEV, 0)
    positions = my_lengths[row_ids // NEWTOK] + row_ids % NEWTOK
    queries = rotate(
        projected[:, :q_width].reshape(block_rows, group_heads, head_dim), positions
    ).astype(jnp.bfloat16)
    own_part = projected[:, q_width:]
    holds_keys = current_head % 2 == 0
    turned = rotate(own_part[:, None, :], positions)[:, 0]
    own_ready = jnp.where(holds_keys, turned, own_part).astype(jnp.bfloat16)
    partner_ready = from_partner(own_ready, "head", 0)
    new_keys = jnp.where(holds_keys, own_ready, partner_ready)
    new_values = jnp.where(holds_keys, partner_ready, own_ready)
    mask_rows = lax.dynamic_slice_in_dim(token_mask, me_dp * block_rows, block_rows, 0)
    scale = 1.0 / math.sqrt(head_dim)
    local_idx = jnp.arange(NEWTOK, dtype=jnp.int32)
    cache_keys = received[:, 0, :, 0].reshape(-1, head_dim)
    cache_vals = received[:, 0, :, 1].reshape(-1, head_dim)
    cache_ok = (has_page[:, 0, :, None] & (key_pos[:, 0] < my_lengths[0])).reshape(-1)
    new_ok = (mask_rows[None, :] == 1) & (local_idx[None, :] <= local_idx[:, None])
    valid = jnp.concatenate(
        [jnp.broadcast_to(cache_ok[None, :], (NEWTOK, cache_ok.shape[0])), new_ok], 1
    )
    keys = jnp.concatenate([cache_keys, new_keys], 0)
    vals = jnp.concatenate([cache_vals, new_values], 0)
    head_outs = []
    for head in range(group_heads):
        scores = (
            lax.dot_general(
                queries[0:NEWTOK, head],
                keys,
                (((1,), (1,)), ((), ())),
                preferred_element_type=jnp.float32,
            )
            * scale
        )
        masked = jnp.where(valid, scores, -jnp.inf)
        top = jnp.max(masked, -1, keepdims=True)
        expo = jnp.exp(masked - top)
        probs = expo / jnp.sum(expo, -1, keepdims=True)
        weights = probs.astype(jnp.bfloat16)
        head_outs.append(
            jnp.dot(weights, vals, preferred_element_type=jnp.float32).astype(jnp.bfloat16)
        )
    pieces = jnp.concatenate(head_outs, -1)
    summed = lax.psum_scatter(
        jnp.dot(pieces, w_out, preferred_element_type=jnp.float32),
        "head",
        scatter_dimension=0,
        tiled=True,
    )
    return summed.astype(jnp.bfloat16)


def solution(mesh):
    in_specs = (
        P(("dp", "head"), None),
        P(),
        P(None, "head"),
        P(None, "head"),
        P("head", None),
        P("dp", None, None, None, None),
        P(),
        P(),
        P(),
    )
    out_specs = P(("dp", "head"), None)
    return jax.shard_map(body, mesh=mesh, in_specs=in_specs, out_specs=out_specs, check_vma=False)
```

profile of v0, /device:TPU:0, one launch (start us, length us, event | category | flops | bytes accessed | tf_op | source)
XLA Modules:
  0.0 279.4 jit_solution(7255772518021541009)
XLA Ops:
  6.5 0.0 copy-start
  6.5 0.8 add_select_fusion
  7.4 0.7 broadcast_compare_fusion
  8.1 0.2 reduce_window_sum.23
  8.3 0.2 fusion.41
  8.5 0.2 select_reduce_fusion
  8.8 0.1 reshape.296
  8.8 0.1 broadcast_in_dim.50
  8.9 5.8 %gather_fusion = bf16[64,2,128,128]{3,2,1,0:T(8,128)(2,1)} fusion(bf16[48,2,2,128,128]{4,3,2,1,0:T(8,128)(2,1)} %param.14, s32[64]{0:T(128)S(1)} %fusion.53), kind=kCustom, calls=%fused_computation | custom fusion | bytes 8389120 | tf_op jit(solution)/shard_map/gather | solution.py:67
  14.8 4.5 %broadcast_select_fusion = bf16[64,2,128,128]{3,2,1,0:T(8,128)(2,1)} fusion(bf16[64,2,128,128]{3,2,1,0:T(8,128)(2,1)} %gather_fusion, pred[64]{0:T(512)(128)(4,1)S(1)} %broadcast_in_dim.50), kind=kLoop, calls=%fused_computation.17 | loop fusion | flops 2097152 | bytes 8388672 | tf_op jit(solution)/shard_map/jit(_where)/select_n | solution.py:68
  19.3 7.4 %all-to-all-start = ((bf16[64,2,128,128]{3,2,1,0:T(8,128)(2,1)}), bf16[64,2,128,128]{3,2,1,0:T(8,128)(2,1)}, u32[]{:S(2)}, u32[]{:S(2)}) async-start(bf16[64,2,128,128]{3,2,1,0:T(8,128)(2,1)} %broadcast_select_fusion), calls=%async_computation | async-start | bytes 8388608 | tf_op jit(solution)/shard_map/all_to_all | solution.py:69
  26.7 0.0 all-gather.2.cloned.1.call-start
  26.7 0.0 copy-done.1
  26.7 0.2 fusion.6
  27.0 0.0 copy-done.7
  27.0 1.1 fusion.8
  28.1 0.0 all-gather.2.cloned.1.call-update
  28.2 0.0 reduce-scatter.2.cloned.1.call-start
  28.2 0.0 copy-done.8
  28.2 0.6 dynamic_slice.10
  28.9 0.2 reduce_window_sum.22
  29.1 0.2 fusion.37
  29.3 0.2 select_reduce_fusion.1
  29.6 0.7 fusion.39
  30.3 0.8 dynamic-slice_compare_fusion
  31.0 0.6 fusion.46
  31.7 0.1 fusion.12
  31.7 0.5 multiply_cosine_fusion.1
  32.3 26.8 %all-gather.2.cloned.1.call-done = bf16[512,3072]{1,0:T(8,128)(2,1)} async-done(((bf16[128,3072]{1,0:T(8,128)(2,1)}), bf16[512,3072]{1,0:T(8,128)(2,1)}) %all-gather.2.cloned.1.call-update) | async-done | bytes 3145744 | tf_op jit(solution)/shard_map/all_gather | solution.py:88
  59.1 3.4 %fusion.67 = f32[512,128]{0,1:T(8,128)S(1)} fusion(bf16[512,3072]{1,0:T(8,128)(2,1)} %all-gather.2.cloned.1.call-done, bf16[3072,128]{1,0:T(8,128)(2,1)} %param.12), kind=kOutput, calls=%fused_computation.117 | convolution fusion | flops 402653184 | bytes 4194304 | tf_op jit(solution)/shard_map/dot_general | solution.py:90
  62.5 0.6 fusion.25
  63.1 0.3 collective-permute-start
  63.4 0.0 copy-done.2
  63.4 3.1 %fusion.66 = f32[512,384]{0,1:T(8,128)S(1)} fusion(bf16[512,3072]{1,0:T(8,128)(2,1)S(1)} %copy-done.2, bf16[3072,384]{1,0:T(8,128)(2,1)} %param.11), kind=kOutput, calls=%fused_computation.116 | convolution fusion | flops 1207959552 | bytes 6291456 | tf_op jit(solution)/shard_map/dot_general | solution.py:89
  66.5 0.1 subtract_convert_fusion
  66.6 0.0 collective-permute-done
  66.7 0.8 copy.13
  67.4 0.1 copy.12
  67.5 52.4 %all-to-all-done = bf16[64,2,128,128]{3,2,1,0:T(8,128)(2,1)} async-done(((bf16[64,2,128,128]{3,2,1,0:T(8,128)(2,1)}), bf16[64,2,128,128]{3,2,1,0:T(8,128)(2,1)}, u32[]{:S(2)}, u32[]{:S(2)}) %all-to-all-start) | async-done | bytes 4194336 | tf_op jit(solution)/shard_map/all_to_all | solution.py:69
  120.0 4.2 %fusion.62 = (bf16[8,1,8,1,128,128]{5,4,3,2,0,1:T(8,128)(2,1)}, bf16[8,1,8,1,128,128]{5,4,3,2,0,1:T(8,128)(2,1)S(1)}) fusion(bf16[8,1,8,2,128,128]{5,4,3,2,0,1:T(8,128)(2,1)} %bitcast.6), kind=kLoop, calls=%fused_computation.112 | loop fusion | bytes 8388608 | tf_op jit(solution)/shard_map/slice | solution.py:110
  124.1 10.6 %fusion.64 = (f32[512]{0:T(512)S(1)}, f32[512,8704]{1,0:T(8,128)}) fusion(bf16[512,128]{1,0:T(8,128)(2,1)S(1)} %copy.12, bf16[8192,128]{1,0:T(8,128)(2,1)S(1)} %bitcast.44, bf16[512,3,64]{0,2,1:T(8,128)(2,1)S(1)} %get-tuple-element.10, bf16[512,3,64]{0,2,1:T(8,128)(2,1)S(1)} %get-tuple-element.11, pred[512,512]{1,0:T(32,128)(4,1)S(1)} %fusion.12, ...), kind=kOutput, calls=%fused_computation.114 | convolution fusion | flops 1163394560 | bytes 20720128 | tf_op jit(solution)/shard_map/dot_general | solution.py:121
  134.8 10.6 %fusion.63 = (f32[512]{0:T(512)S(1)}, f32[512,8704]{1,0:T(8,128)}) fusion(bf16[512,128]{1,0:T(8,128)(2,1)S(1)} %copy.12, bf16[8192,128]{1,0:T(8,128)(2,1)S(1)} %bitcast.45, bf16[512,3,64]{0,2,1:T(8,128)(2,1)S(1)} %get-tuple-element.11, bf16[512,3,64]{0,2,1:T(8,128)(2,1)S(1)} %get-tuple-element.10, pred[512,512]{1,0:T(32,128)(4,1)S(1)} %fusion.12, ...), kind=kOutput, calls=%fused_computation.113 | convolution fusion | flops 1163394560 | bytes 20720128 | tf_op jit(solution)/shard_map/dot_general | solution.py:121
  145.4 10.7 %fusion.65 = (f32[512]{0:T(512)S(1)}, f32[512,8704]{1,0:T(8,128)}) fusion(bf16[512,128]{1,0:T(8,128)(2,1)S(1)} %copy.12, bf16[8192,128]{1,0:T(8,128)(2,1)S(1)} %bitcast.46, bf16[512,3,64]{0,2,1:T(8,128)(2,1)S(1)} %get-tuple-element.10, bf16[512,3,64]{0,2,1:T(8,128)(2,1)S(1)} %get-tuple-element.11, pred[512,512]{1,0:T(32,128)(4,1)S(1)} %fusion.12, ...), kind=kOutput, calls=%fused_computation.115 | convolution fusion | flops 1163394560 | bytes 20720128 | tf_op jit(solution)/shard_map/dot_general | solution.py:121
  156.1 9.1 %fusion.1 = f32[512]{0:T(512)} fusion(f32[512,8704]{1,0:T(8,128)} %get-tuple-element.23, f32[512]{0:T(512)S(1)} %get-tuple-element.22), kind=kLoop, calls=%fused_computation.12 | loop fusion | flops 8912384 | bytes 17829888 | tf_op jit(solution)/shard_map/reduce_sum | solution.py:132
  165.2 8.6 %fusion.2 = f32[512]{0:T(512)S(1)} fusion(f32[512,8704]{1,0:T(8,128)} %get-tuple-element.21, f32[512]{0:T(512)S(1)} %get-tuple-element.20), kind=kLoop, calls=%fused_computation.13 | loop fusion | flops 8912384 | bytes 17829888 | tf_op jit(solution)/shard_map/reduce_sum | solution.py:132
  173.9 0.0 slice-start.2
  173.9 0.0 slice-start.3
  173.9 0.0 slice-start.4
  173.9 0.0 copy-start.3
  173.9 0.0 copy-start.5
  173.9 9.7 %fusion.10 = bf16[512,128]{1,0:T(8,128)(2,1)S(1)} fusion(f32[512,8704]{1,0:T(8,128)} %get-tuple-element.23, f32[512]{0:T(512)} %fusion.1, f32[512]{0:T(512)S(1)} %get-tuple-element.22, bf16[512,128]{1,0:T(8,128)(2,1)} %copy.13, bf16[8192,128]{1,0:T(8,128)(2,1)} %bitcast.41), kind=kOutput, calls=%fused_computation.26 | convolution fusion | flops 1158742016 | bytes 20189184 | tf_op jit(solution)/shard_map/dot_general | solution.py:135
  183.6 0.0 slice-done
  183.6 0.1 slice-done.2
  183.7 1.2 slice-done.3
  184.9 1.2 slice-done.4
  186.1 0.0 copy-done.5
  186.1 3.5 %fusion.9 = bf16[512,128]{1,0:T(8,128)(2,1)} fusion(f32[512,8704]{1,0:T(8,128)S(1)} %bitcast.39, f32[512]{0:T(512)S(1)} %fusion.2, f32[512]{0:T(512)S(1)} %get-tuple-element.20, bf16[512,128]{1,0:T(8,128)(2,1)S(1)} %copy-done.5, bf16[8192,128]{1,0:T(8,128)(2,1)S(1)} %bitcast.43), kind=kOutput, calls=%fused_computation.25 | convolution fusion | flops 1158742016 | bytes 20189184 | tf_op jit(solution)/shard_map/dot_general | solution.py:135
  189.6 8.8 %fusion = f32[512]{0:T(512)S(1)} fusion(f32[512,8704]{1,0:T(8,128)} %get-tuple-element.25, f32[512]{0:T(512)S(1)} %get-tuple-element.24), kind=kLoop, calls=%fused_computation.11 | loop fusion | flops 8912384 | bytes 17829888 | tf_op jit(solution)/shard_map/reduce_sum | solution.py:132
  198.5 0.0 copy-done.6
  198.5 9.5 %fusion.11 = bf16[512,128]{1,0:T(8,128)(2,1)S(1)} fusion(f32[512,8704]{1,0:T(8,128)} %get-tuple-element.25, f32[512]{0:T(512)S(1)} %fusion, f32[512]{0:T(512)S(1)} %get-tuple-element.24, bf16[512,128]{1,0:T(8,128)(2,1)S(1)} %copy-done.6, bf16[8192,128]{1,0:T(8,128)(2,1)} %bitcast.42), kind=kOutput, calls=%fused_computation.27 | convolution fusion | flops 1158742016 | bytes 20189184 | tf_op jit(solution)/shard_map/dot_general | solution.py:135
  208.0 4.5 %fusion.13 = f32[512,3072]{1,0:T(8,128)} fusion(bf16[384,3072]{1,0:T(8,128)(2,1)S(1)} %copy-done, bf16[512,128]{1,0:T(8,128)(2,1)S(1)} %copy-done.4, bf16[512,128]{1,0:T(8,128)(2,1)S(1)} %fusion.10, bf16[512,128]{1,0:T(8,128)(2,1)S(1)} %fusion.11), kind=kOutput, calls=%fused_computation.34 | convolution fusion | flops 1209139200 | bytes 9043968 | tf_op jit(solution)/shard_map/dot_general | solution.py:139
  212.5 0.0 reduce-scatter.2.cloned.1.call-update
  212.5 57.6 %reduce-scatter.2.cloned.1.call-done = f32[128,3072]{1,0:T(8,128)} async-done(((f32[512,3072]{1,0:T(8,128)}), f32[128,3072]{1,0:T(8,128)}) %reduce-scatter.2.cloned.1.call-update) | async-done | bytes 1572880 | tf_op jit(solution)/shard_map/reduce_scatter | solution.py:138
  270.1 2.4 convert_element_type.74
  (25 shorter events, 0.1 us)
Async XLA Ops:
  6.5 201.5 %copy-start = (bf16[384,3072]{1,0:T(8,128)(2,1)S(1)}, bf16[384,3072]{1,0:T(8,128)(2,1)}, u32[]{:S(2)}) copy-start(bf16[384,3072]{1,0:T(8,128)(2,1)} %param.13) | copy-start | bytes 7077892
  19.3 7.4 %copy-start.1 = (bf16[128,3072]{1,0:T(8,128)(2,1)S(1)}, bf16[128,3072]{1,0:T(8,128)(2,1)}, u32[]{:S(2)}) copy-start(bf16[128,3072]{1,0:T(8,128)(2,1)} %param.9) | copy-start | bytes 2359300
  19.3 7.7 %copy-start.7 = (bf16[3072]{0:T(1024)(128)(2,1)S(1)}, bf16[3072]{0:T(1024)(128)(2,1)}, u32[]{:S(2)}) copy-start(bf16[3072]{0:T(1024)(128)(2,1)} %param.10) | copy-start | bytes 18436
  19.3 8.9 %copy-start.8 = (s32[8]{0:T(128)S(1)}, s32[8]{0:T(128)}, u32[]{:S(2)}) copy-start(s32[8]{0:T(128)} %param.15) | copy-start | bytes 100
  19.3 100.7 %all-to-all-start = ((bf16[64,2,128,128]{3,2,1,0:T(8,128)(2,1)}), bf16[64,2,128,128]{3,2,1,0:T(8,128)(2,1)}, u32[]{:S(2)}, u32[]{:S(2)}) async-start(bf16[64,2,128,128]{3,2,1,0:T(8,128)(2,1)} %broadcast_select_fusion), calls=%async_computation | async-start | bytes 8388608 | tf_op jit(solution)/shard_map/all_to_all | solution.py:69
  26.7 32.4 %all-gather.2.cloned.1.call-start = ((), (), s32[]{:S(2)}) async-start(), calls=%async_computation.2 | async-start | bytes 3932160 | tf_op jit(solution)/shard_map/all_gather | solution.py:88
  28.2 242.0 %reduce-scatter.2.cloned.1.call-start = ((), (), s32[]{:S(2)}) async-start(), calls=%async_computation.3 | async-start | bytes 7864320 | tf_op jit(solution)/shard_map/reduce_scatter | solution.py:138
  59.1 4.3 %copy-start.2 = (bf16[512,3072]{1,0:T(8,128)(2,1)S(1)}, bf16[512,3072]{1,0:T(8,128)(2,1)}, u32[]{:S(2)}) copy-start(bf16[512,3072]{1,0:T(8,128)(2,1)} %all-gather.2.cloned.1.call-done) | copy-start | bytes 9437188
  63.1 3.5 %collective-permute-start = (bf16[512,128]{0,1:T(8,128)(2,1)S(1)}, bf16[512,128]{0,1:T(8,128)(2,1)S(1)}, u32[]{:S(2)}, u32[]{:S(2)}) collective-permute-start(bf16[512,128]{0,1:T(8,128)(2,1)S(1)} %fusion.20), channel_id=1, source_target_pairs={{0,1},{1,0},{2,3},{3,2},{4,5},{5,4},{6,7},{7,6},{8,9},{9,8},{10,11... | collective-permute-start | bytes 393224 | tf_op jit(solution)/shard_map/ppermute | solution.py:20
  165.2 18.4 %slice-start = ((s8[17825792]{0:T(1024)(128)(4,1)}), s8[1048576]{0:T(1024)(128)(4,1)S(1)}, s32[]{:S(2)}) async-start(s8[17825792]{0:T(1024)(128)(4,1)} %bitcast.38), calls=%async_computation.4 | async-start | bytes 2097152
  173.9 9.7 %slice-start.1 = ((s8[17825792]{0:T(1024)(128)(4,1)}), s8[4194304]{0:T(1024)(128)(4,1)S(1)}, s32[]{:S(2)}) async-start(s8[17825792]{0:T(1024)(128)(4,1)} %bitcast.38), calls=%async_computation.5 | async-start | bytes 8388608
  173.9 9.8 %slice-start.2 = ((s8[17825792]{0:T(1024)(128)(4,1)}), s8[4194304]{0:T(1024)(128)(4,1)S(1)}, s32[]{:S(2)}) async-start(s8[17825792]{0:T(1024)(128)(4,1)} %bitcast.38), calls=%async_computation.6 | async-start | bytes 8388608
  173.9 11.0 %slice-start.3 = ((s8[17825792]{0:T(1024)(128)(4,1)}), s8[4194304]{0:T(1024)(128)(4,1)S(1)}, s32[]{:S(2)}) async-start(s8[17825792]{0:T(1024)(128)(4,1)} %bitcast.38), calls=%async_computation.7 | async-start | bytes 8388608
  173.9 12.2 %slice-start.4 = ((s8[17825792]{0:T(1024)(128)(4,1)}), s8[4194304]{0:T(1024)(128)(4,1)S(1)}, s32[]{:S(2)}) async-start(s8[17825792]{0:T(1024)(128)(4,1)} %bitcast.38), calls=%async_computation.8 | async-start | bytes 8388608
  173.9 12.2 %copy-start.3 = (bf16[8,1,8,1,128,128]{5,4,3,2,0,1:T(8,128)(2,1)S(1)}, bf16[8,1,8,1,128,128]{5,4,3,2,0,1:T(8,128)(2,1)}, u32[]{:S(2)}) copy-start(bf16[8,1,8,1,128,128]{5,4,3,2,0,1:T(8,128)(2,1)} %get-tuple-element.8) | copy-start | bytes 6291460
  173.9 12.2 %copy-start.5 = (bf16[512,128]{1,0:T(8,128)(2,1)S(1)}, bf16[512,128]{1,0:T(8,128)(2,1)}, u32[]{:S(2)}) copy-start(bf16[512,128]{1,0:T(8,128)(2,1)} %copy.13) | copy-start | bytes 393220
  189.6 8.8 %copy-start.6 = (bf16[512,128]{1,0:T(8,128)(2,1)S(1)}, bf16[512,128]{1,0:T(8,128)(2,1)}, u32[]{:S(2)}) copy-start(bf16[512,128]{1,0:T(8,128)(2,1)} %copy.13) | copy-start | bytes 393220
  198.5 9.5 %copy-start.4 = (bf16[512,128]{1,0:T(8,128)(2,1)S(1)}, bf16[512,128]{1,0:T(8,128)(2,1)}, u32[]{:S(2)}) copy-start(bf16[512,128]{1,0:T(8,128)(2,1)} %fusion.9) | copy-start | bytes 393220
Sparse Core Ops, SparseCore 0:
  29.1 29.9 all-gather.1
  212.6 57.4 reduce-scatter.1
where the time goes:
time: 280 us; the launch traced here: 279 us
  waiting for transfers between devices  137 us (49%)
  matrix products  65.6 us (23%)
  other arithmetic  41.2 us (15%)
  local copies, waits for them, and re-layouts  14.2 us (5%)
  between operations  13.7 us (5%)
  starting transfers between devices  7.77 us (3%)
    reduce_scatter x1, waiting for transfers between devices, body(): lax.psum_scatter(jnp.dot(pieces, w_out, preferred_element_type=jnp.float3...  57.6 us
    all_to_all x1, waiting for transfers between devices, body(): lax.all_to_all(outgoing, 'dp', split_axis=0, concat_axis=0, tiled=True)  52.4 us
    dot_general x3, matrix products, body(): lax.dot_general(queries[0:NEWTOK, head], keys, (((1,), (1,)), ((), ())),...  31.9 us
    all_gather x1, waiting for transfers between devices, body(): piece = lax.all_gather(normalized_input, 'head', axis=0, tiled=True)  26.8 us
    reduce_sum x3, other arithmetic, body(): probs = expo / jnp.sum(expo, -1, keepdims=True)  26.6 us
    dot_general x3, matrix products, body(): jnp.dot(weights, vals, preferred_element_type=jnp.float32)  22.7 us
    all_to_all x1, starting transfers between devices, body(): lax.all_to_all(outgoing, 'dp', split_axis=0, concat_axis=0, tiled=True)  7.38 us
    gather x1, local copies, waits for them, and re-layouts, body(): outgoing = kv_pool[local_page.reshape(-1), key_value_head]  5.84 us
  transfers between devices with their start and end apart: 4, of which 3 were waited for; matrix products, arithmetic and copies ran while one was open for 5% of the time, Pallas kernels for 0%

commit v1 on v0

--- a/solution.py
+++ b/solution.py
@@ -16,6 +16,11 @@
 
 def from_partner(value, axis, stride):
     mask = 2**stride
+    pairs = [(source, source ^ mask) for source in range(lax.axis_size(axis))]
+    return lax.ppermute(value, axis, pairs)
+
+
+def exchange(value, axis, mask):
     pairs = [(source, source ^ mask) for source in range(lax.axis_size(axis))]
     return lax.ppermute(value, axis, pairs)
 
@@ -57,6 +62,13 @@
     max_pages = page_table.shape[1]
     slots = max_pages // n_dp
     key_value_head = current_head // (head_number // KEY_VALUE_HEADS)
+    held_w = w_out
+    held_ids = current_head[None]
+    stride = head_number // 2
+    while stride >= 1:
+        held_w = jnp.concatenate([held_w, exchange(held_w, "head", stride)], 0)
+        held_ids = jnp.concatenate([held_ids, held_ids ^ stride], 0)
+        stride //= 2
     owner_of = jnp.where(page_table >= 0, page_table // pool_rows, -1)
     mine = (owner_of == me_dp).astype(jnp.int32)
     rank = jnp.cumsum(mine, 1) - 1
@@ -135,13 +147,11 @@
             jnp.dot(weights, vals, preferred_element_type=jnp.float32).astype(jnp.bfloat16)
         )
     pieces = jnp.concatenate(head_outs, -1)
-    summed = lax.psum_scatter(
-        jnp.dot(pieces, w_out, preferred_element_type=jnp.float32),
-        "head",
-        scatter_dimension=0,
-        tiled=True,
-    )
-    return summed.astype(jnp.bfloat16)
+    gathered = lax.all_to_all(pieces, "head", split_axis=0, concat_axis=1, tiled=True)
+    gathered = gathered.reshape(local_rows, head_number, group_heads * head_dim)
+    ordered = jnp.take(gathered, held_ids, axis=1).reshape(local_rows, -1)
+    out = jnp.dot(ordered, held_w, preferred_element_type=jnp.float32)
+    return out.astype(jnp.bfloat16)
 
 
 def solution(mesh):

time: 280 us -> 231 us (0.82)
  waiting for transfers between devices: 137 us -> 81.2 us
  starting transfers between devices: 7.77 us -> 13 us
  other arithmetic: 41.2 us -> 45.3 us
    ppermute x0 -> x2, waiting for transfers between devices: none -> 63.3 us  [exchange(): return lax.ppermute(value, axis, pairs)]
    reduce_scatter x1 -> x0, waiting for transfers between devices: 57.6 us -> none  [body(): lax.psum_scatter(jnp.dot(pieces, w_out, preferred_element_type=jnp.float3...]
    all_to_all x1, waiting for transfers between devices: 52.4 us -> 8.61 us  [body(): lax.all_to_all(outgoing, 'dp', split_axis=0, concat_axis=0, tiled=True)]
    all_gather x1, waiting for transfers between devices: 26.8 us -> 0.01 us  [body(): piece = lax.all_gather(normalized_input, 'head', axis=0, tiled=True)]
    all_to_all x0 -> x1, waiting for transfers between devices: none -> 7.24 us  [body(): lax.all_to_all(pieces, 'head', split_axis=0, concat_axis=1, tiled=True)]
    concatenate x0 -> x3, other arithmetic: none -> 4.95 us  [the longest x1 4.84 us: body(): held_w = jnp.concatenate([held_w, exchange(held_w, 'head', stride)], 0)]
    all_to_all x0 -> x1, starting transfers between devices: none -> 3.46 us  [body(): lax.all_to_all(pieces, 'head', split_axis=0, concat_axis=1, tiled=True)]
  transfers between devices with their start and end apart: 4 -> 6, of which waited for: 3 -> 4; matrix products, arithmetic and copies ran while one was open for 5% -> 45% of each run, Pallas kernels for 0% -> 0%
where the time goes in v1:
time: 231 us
  waiting for transfers between devices  81.2 us (35%)
  matrix products  64.6 us (28%)
  other arithmetic  45.3 us (20%)
  between operations  13.8 us (6%)
  starting transfers between devices  13 us (6%)
  local copies, waits for them, and re-layouts  12.9 us (6%)
    ppermute x2, waiting for transfers between devices, exchange(): return lax.ppermute(value, axis, pairs)  63.3 us
    dot_general x3, matrix products, body(): lax.dot_general(queries[0:NEWTOK, head], keys, (((1,), (1,)), ((), ())),...  31.6 us
    reduce_sum x3, other arithmetic, body(): probs = expo / jnp.sum(expo, -1, keepdims=True)  26.9 us
    dot_general x3, matrix products, body(): jnp.dot(weights, vals, preferred_element_type=jnp.float32)  23 us
    all_to_all x1, waiting for transfers between devices, body(): lax.all_to_all(outgoing, 'dp', split_axis=0, concat_axis=0, tiled=True)  8.61 us
    all_to_all x1, starting transfers between devices, body(): lax.all_to_all(outgoing, 'dp', split_axis=0, concat_axis=0, tiled=True)  7.38 us
    all_to_all x1, waiting for transfers between devices, body(): lax.all_to_all(pieces, 'head', split_axis=0, concat_axis=1, tiled=True)  7.24 us
    gather x1, local copies, waits for them, and re-layouts, body(): outgoing = kv_pool[local_page.reshape(-1), key_value_head]  5.84 us
  transfers between devices with their start and end apart: 6, of which 4 were waited for; matrix products, arithmetic and copies ran while one was open for 45% of the time, Pallas kernels for 0%

profile of v1, /device:TPU:0, one launch (start us, length us, event | category | flops | bytes accessed | tf_op | source)
XLA Modules:
  0.0 230.9 jit_solution(2578698756887149463)
XLA Ops:
  6.5 0.8 add_select_fusion
  7.4 0.7 broadcast_compare_fusion
  8.1 0.2 reduce_window_sum.23
  8.3 0.2 fusion.44
  8.5 0.2 select_reduce_fusion
  8.8 0.1 reshape.466
  8.8 0.1 broadcast_in_dim.65
  8.9 5.8 %gather_fusion = bf16[64,2,128,128]{3,2,1,0:T(8,128)(2,1)} fusion(bf16[48,2,2,128,128]{4,3,2,1,0:T(8,128)(2,1)} %param.14, s32[64]{0:T(128)S(1)} %fusion.56), kind=kCustom, calls=%fused_computation | custom fusion | bytes 8389120 | tf_op jit(solution)/shard_map/gather | solution.py:79
  14.8 4.5 %broadcast_select_fusion = bf16[64,2,128,128]{3,2,1,0:T(8,128)(2,1)} fusion(bf16[64,2,128,128]{3,2,1,0:T(8,128)(2,1)} %gather_fusion, pred[64]{0:T(512)(128)(4,1)S(1)} %broadcast_in_dim.65), kind=kLoop, calls=%fused_computation.25 | loop fusion | flops 2097152 | bytes 8388672 | tf_op jit(solution)/shard_map/jit(_where)/select_n | solution.py:80
  19.3 7.4 %all-to-all-start = ((bf16[64,2,128,128]{3,2,1,0:T(8,128)(2,1)}), bf16[64,2,128,128]{3,2,1,0:T(8,128)(2,1)}, u32[]{:S(2)}, u32[]{:S(2)}) async-start(bf16[64,2,128,128]{3,2,1,0:T(8,128)(2,1)} %broadcast_select_fusion), calls=%async_computation | async-start | bytes 8388608 | tf_op jit(solution)/shard_map/all_to_all | solution.py:81
  26.7 0.0 all-gather.2.cloned.1.call-start
  26.7 0.2 fusion.15
  27.0 1.2 fusion.17
  28.1 0.0 all-gather.2.cloned.1.call-update
  28.2 1.6 collective-permute-start.1
  29.8 0.6 dynamic_slice.10
  30.4 0.2 reduce_window_sum.22
  30.6 0.1 add_xor_fusion
  30.7 0.1 compare_and_fusion
  30.8 0.1 broadcast_in_dim.58
  30.9 0.2 fusion.40
  31.1 0.2 select_reduce_fusion.1
  31.4 0.7 fusion.42
  32.1 0.8 dynamic-slice_compare_fusion
  32.9 0.6 fusion.49
  33.5 0.8 fusion.21
  34.3 0.5 multiply_cosine_fusion.1
  34.8 0.0 copy-start.5
  34.8 63.3 %collective-permute-done.1 = bf16[384,3072]{1,0:T(8,128)(2,1)} collective-permute-done((bf16[384,3072]{1,0:T(8,128)(2,1)}, bf16[384,3072]{1,0:T(8,128)(2,1)}, u32[]{:S(2)}, u32[]{:S(2)}) %collective-permute-start.1) | collective-permute-done | bytes 2359328 | tf_op jit(solution)/shard_map/ppermute | solution.py:25
  98.1 4.8 %pad_maximum_fusion = bf16[768,3072]{1,0:T(8,128)(2,1)} fusion(bf16[384,3072]{1,0:T(8,128)(2,1)} %collective-permute-done.1, bf16[384,3072]{1,0:T(8,128)(2,1)} %param.13), kind=kLoop, calls=%fused_computation.24 | loop fusion | flops 9437184 | bytes 9437184 | tf_op jit(solution)/shard_map/concatenate | solution.py:69
  103.0 3.2 %fusion.71 = f32[512,128]{0,1:T(8,128)S(1)} fusion(bf16[512,3072]{1,0:T(8,128)(2,1)} %all-gather.2.cloned.1.call-done, bf16[3072,128]{1,0:T(8,128)(2,1)S(1)} %copy-done.5), kind=kOutput, calls=%fused_computation.128 | convolution fusion | flops 402653184 | bytes 4194304 | tf_op jit(solution)/shard_map/dot_general | solution.py:102
  106.2 0.6 fusion.28
  106.8 0.6 collective-permute-start
  107.4 1.4 fusion.70
  108.8 0.1 subtract_convert_fusion
  108.9 0.0 copy-start.9
  109.0 2.1 collective-permute-done
  111.1 0.1 copy.16
  111.2 0.1 copy.17
  111.3 8.6 %all-to-all-done = bf16[64,2,128,128]{3,2,1,0:T(8,128)(2,1)} async-done(((bf16[64,2,128,128]{3,2,1,0:T(8,128)(2,1)}), bf16[64,2,128,128]{3,2,1,0:T(8,128)(2,1)}, u32[]{:S(2)}, u32[]{:S(2)}) %all-to-all-start) | async-done | bytes 4194336 | tf_op jit(solution)/shard_map/all_to_all | solution.py:81
  120.0 2.8 %fusion.66 = (bf16[8,1,8,1,128,128]{5,4,3,2,0,1:T(8,128)(2,1)S(1)}, bf16[8,1,8,1,128,128]{5,4,3,2,0,1:T(8,128)(2,1)S(1)}) fusion(bf16[8,1,8,2,128,128]{5,4,3,2,0,1:T(8,128)(2,1)} %bitcast.7), kind=kLoop, calls=%fused_computation.123 | loop fusion | bytes 8388608 | tf_op jit(solution)/shard_map/slice | solution.py:122
  122.8 10.8 %fusion.69 = (f32[512]{0:T(512)S(1)}, f32[512,8704]{1,0:T(8,128)}) fusion(bf16[512,128]{1,0:T(8,128)(2,1)S(1)} %copy.16, bf16[8192,128]{1,0:T(8,128)(2,1)S(1)} %bitcast.56, bf16[512,3,64]{0,2,1:T(8,128)(2,1)S(1)} %get-tuple-element.10, bf16[512,3,64]{0,2,1:T(8,128)(2,1)S(1)} %get-tuple-element.11, pred[512,512]{1,0:T(32,128)(4,1)S(1)} %copy-done.6, ...), kind=kOutput, calls=%fused_computation.126 | convolution fusion | flops 1163394560 | bytes 20720128 | tf_op jit(solution)/shard_map/dot_general | solution.py:133
  133.6 11.2 %fusion.68 = (f32[512]{0:T(512)}, f32[512,8704]{1,0:T(8,128)}) fusion(bf16[512,128]{1,0:T(8,128)(2,1)S(1)} %copy.16, bf16[8192,128]{1,0:T(8,128)(2,1)S(1)} %bitcast.57, bf16[512,3,64]{0,2,1:T(8,128)(2,1)S(1)} %get-tuple-element.10, bf16[512,3,64]{0,2,1:T(8,128)(2,1)S(1)} %get-tuple-element.11, pred[512,512]{1,0:T(32,128)(4,1)S(1)} %copy-done.6, ...), kind=kOutput, calls=%fused_computation.125 | convolution fusion | flops 1163394560 | bytes 20720128 | tf_op jit(solution)/shard_map/dot_general | solution.py:133
  144.9 9.1 %fusion = f32[512]{0:T(512)} fusion(f32[512,8704]{1,0:T(8,128)} %get-tuple-element.25, f32[512]{0:T(512)S(1)} %get-tuple-element.24), kind=kLoop, calls=%fused_computation.12 | loop fusion | flops 8912384 | bytes 17829888 | tf_op jit(solution)/shard_map/reduce_sum | solution.py:144
  154.0 9.2 %fusion.1 = f32[512]{0:T(512)} fusion(f32[512,8704]{1,0:T(8,128)} %get-tuple-element.23, f32[512]{0:T(512)} %get-tuple-element.22), kind=kLoop, calls=%fused_computation.13 | loop fusion | flops 8912384 | bytes 17829888 | tf_op jit(solution)/shard_map/reduce_sum | solution.py:144
  163.3 9.7 %fusion.20 = bf16[512,128]{0,1:T(8,128)(2,1)} fusion(f32[512,8704]{1,0:T(8,128)} %get-tuple-element.25, f32[512]{0:T(512)} %fusion, f32[512]{0:T(512)} %copy-done.17, bf16[512,128]{1,0:T(8,128)(2,1)S(1)} %copy.17, bf16[8192,128]{1,0:T(8,128)(2,1)S(1)} %bitcast.53), kind=kOutput, calls=%fused_computation.36 | convolution fusion | flops 1158742016 | bytes 20189184 | tf_op jit(solution)/shard_map/dot_general | solution.py:147
  172.9 0.0 slice-done.3
  173.0 1.2 slice-done.4
  174.2 0.0 copy-start.10
  174.2 4.4 %fusion.19 = bf16[512,128]{0,1:T(8,128)(2,1)} fusion(f32[512,8704]{1,0:T(8,128)S(1)} %bitcast.51, f32[512]{0:T(512)S(1)} %copy-done.18, f32[512]{0:T(512)S(1)} %copy-done.16, bf16[512,128]{1,0:T(8,128)(2,1)S(1)} %copy.17, bf16[8192,128]{1,0:T(8,128)(2,1)S(1)} %bitcast.54), kind=kOutput, calls=%fused_computation.35 | convolution fusion | flops 1158742016 | bytes 20189184 | tf_op jit(solution)/shard_map/dot_general | solution.py:147
  178.6 9.5 %fusion.67 = (f32[512]{0:T(512)S(1)}, f32[512,8704]{1,0:T(8,128)}) fusion(bf16[512,128]{1,0:T(8,128)(2,1)S(1)} %copy-done.12, bf16[8192,128]{1,0:T(8,128)(2,1)} %bitcast.58, bf16[512,3,64]{0,2,1:T(8,128)(2,1)S(1)} %copy-done.10, bf16[512,3,64]{0,2,1:T(8,128)(2,1)S(1)} %copy-done.8, pred[512,512]{1,0:T(32,128)(4,1)S(1)} %copy-done.6, ...), kind=kOutput, calls=%fused_computation.124 | convolution fusion | flops 1163394560 | bytes 20720128 | tf_op jit(solution)/shard_map/dot_general | solution.py:133
  188.1 8.5 %fusion.2 = f32[512]{0:T(512)S(1)} fusion(f32[512,8704]{1,0:T(8,128)} %get-tuple-element.21, f32[512]{0:T(512)S(1)} %get-tuple-element.20), kind=kLoop, calls=%fused_computation.14 | loop fusion | flops 8912384 | bytes 17829888 | tf_op jit(solution)/shard_map/reduce_sum | solution.py:144
  196.7 8.9 %fusion.18 = bf16[512,128]{0,1:T(8,128)(2,1)S(1)} fusion(f32[512,8704]{1,0:T(8,128)} %get-tuple-element.21, f32[512]{0:T(512)S(1)} %fusion.2, f32[512]{0:T(512)S(1)} %get-tuple-element.20, bf16[512,128]{1,0:T(8,128)(2,1)S(1)} %copy.17, bf16[8192,128]{1,0:T(8,128)(2,1)S(1)} %bitcast.55), kind=kOutput, calls=%fused_computation.34 | convolution fusion | flops 1158742016 | bytes 20189184 | tf_op jit(solution)/shard_map/dot_general | solution.py:147
  205.7 0.9 copy.20
  206.6 3.5 %all-to-all-start.1 = ((bf16[4,128,384]{2,1,0:T(8,128)(2,1)}), bf16[4,128,384]{2,1,0:T(8,128)(2,1)S(1)}, u32[]{:S(2)}, u32[]{:S(2)}) async-start(bf16[4,128,384]{2,1,0:T(8,128)(2,1)} %bitcast.14), calls=%async_computation.1 | async-start | bytes 786432 | tf_op jit(solution)/shard_map/all_to_all | solution.py:150
  210.1 0.1 fusion.77
  210.2 0.1 fusion.57
  210.3 7.2 %all-to-all-done.1 = bf16[4,128,384]{2,1,0:T(8,128)(2,1)S(1)} async-done(((bf16[4,128,384]{2,1,0:T(8,128)(2,1)}), bf16[4,128,384]{2,1,0:T(8,128)(2,1)S(1)}, u32[]{:S(2)}, u32[]{:S(2)}) %all-to-all-start.1) | async-done | bytes 393248 | tf_op jit(solution)/shard_map/all_to_all | solution.py:150
  217.5 0.6 gather_fusion.1
  218.1 0.2 copy.19
  218.4 0.3 bitcast_select_fusion
  218.6 0.0 collective-permute-done.2
  218.7 0.0 copy-start.1
  218.7 5.4 %fusion.12 = bf16[128,3072]{1,0:T(8,128)(2,1)} fusion(bf16[128,1536]{0,1:T(8,128)(2,1)S(1)} %bitcast_select_fusion, bf16[768,3072]{1,0:T(8,128)(2,1)} %collective-permute-done.2, bf16[384,3072]{1,0:T(8,128)(2,1)} %collective-permute-done.1, bf16[384,3072]{1,0:T(8,128)(2,1)} %param.13), kind=kOutput, calls=%fused_computation.26 | convolution fusion | flops 1236664320 | bytes 10616832 | tf_op jit(solution)/shard_map/dot_general | solution.py:153
  (62 shorter events, 0.3 us)
Async XLA Ops:
  6.5 100.8 %copy-start = (bf16[3072,384]{1,0:T(8,128)(2,1)S(1)}, bf16[3072,384]{1,0:T(8,128)(2,1)}, u32[]{:S(2)}) copy-start(bf16[3072,384]{1,0:T(8,128)(2,1)} %param.11) | copy-start | bytes 7077892
  19.3 7.4 %copy-start.15 = (bf16[3072]{0:T(1024)(128)(2,1)S(1)}, bf16[3072]{0:T(1024)(128)(2,1)}, u32[]{:S(2)}) copy-start(bf16[3072]{0:T(1024)(128)(2,1)} %param.10) | copy-start | bytes 18436
  19.3 7.5 %copy-start.2 = (bf16[128,3072]{1,0:T(8,128)(2,1)S(1)}, bf16[128,3072]{1,0:T(8,128)(2,1)}, u32[]{:S(2)}) copy-start(bf16[128,3072]{1,0:T(8,128)(2,1)} %param.9) | copy-start | bytes 2359300
  19.3 10.5 %copy-start.19 = (s32[8]{0:T(128)S(1)}, s32[8]{0:T(128)}, u32[]{:S(2)}) copy-start(s32[8]{0:T(128)} %param.15) | copy-start | bytes 100
  19.3 100.7 %all-to-all-start = ((bf16[64,2,128,128]{3,2,1,0:T(8,128)(2,1)}), bf16[64,2,128,128]{3,2,1,0:T(8,128)(2,1)}, u32[]{:S(2)}, u32[]{:S(2)}) async-start(bf16[64,2,128,128]{3,2,1,0:T(8,128)(2,1)} %broadcast_select_fusion), calls=%async_computation | async-start | bytes 8388608 | tf_op jit(solution)/shard_map/all_to_all | solution.py:81
  26.7 76.3 %all-gather.2.cloned.1.call-start = ((), (), s32[]{:S(2)}) async-start(), calls=%async_computation.2 | async-start | bytes 3932160 | tf_op jit(solution)/shard_map/all_gather | solution.py:100
  28.2 69.9 %collective-permute-start.1 = (bf16[384,3072]{1,0:T(8,128)(2,1)}, bf16[384,3072]{1,0:T(8,128)(2,1)}, u32[]{:S(2)}, u32[]{:S(2)}) collective-permute-start(bf16[384,3072]{1,0:T(8,128)(2,1)} %param.13), channel_id=1, source_target_pairs={{0,2},{1,3},{2,0},{3,1},{4,6},{5,7},{6,4},{7,5},{8,10},{9,11},{10,... | collective-permute-start | bytes 7077896 | tf_op jit(solution)/shard_map/ppermute | solution.py:25
  34.8 68.1 %copy-start.5 = (bf16[3072,128]{1,0:T(8,128)(2,1)S(1)}, bf16[3072,128]{1,0:T(8,128)(2,1)}, u32[]{:S(2)}) copy-start(bf16[3072,128]{1,0:T(8,128)(2,1)} %param.12) | copy-start | bytes 2359300
  103.0 115.7 %collective-permute-start.2 = (bf16[768,3072]{1,0:T(8,128)(2,1)}, bf16[768,3072]{1,0:T(8,128)(2,1)}, u32[]{:S(2)}, u32[]{:S(2)}) collective-permute-start(bf16[768,3072]{1,0:T(8,128)(2,1)} %pad_maximum_fusion), channel_id=1, source_target_pairs={{0,1},{1,0},{2,3},{3,2},{4,5},{5,4},{6,7},{7,6},{8,9},{9,8},{10,11... | collective-permute-start | bytes 14155784 | tf_op jit(solution)/shard_map/ppermute | solution.py:25
  103.0 4.4 %copy-start.3 = (bf16[512,3072]{1,0:T(8,128)(2,1)S(1)}, bf16[512,3072]{1,0:T(8,128)(2,1)}, u32[]{:S(2)}) copy-start(bf16[512,3072]{1,0:T(8,128)(2,1)} %all-gather.2.cloned.1.call-done) | copy-start | bytes 9437188
  106.8 4.3 %collective-permute-start = (bf16[512,128]{0,1:T(8,128)(2,1)S(1)}, bf16[512,128]{0,1:T(8,128)(2,1)S(1)}, u32[]{:S(2)}, u32[]{:S(2)}) collective-permute-start(bf16[512,128]{0,1:T(8,128)(2,1)S(1)} %fusion.23), channel_id=1, source_target_pairs={{0,1},{1,0},{2,3},{3,2},{4,5},{5,4},{6,7},{7,6},{8,9},{9,8},{10,11... | collective-permute-start | bytes 393224 | tf_op jit(solution)/shard_map/ppermute | solution.py:20
  108.9 24.7 %copy-start.7 = (bf16[512,3,64]{0,2,1:T(8,128)(2,1)}, bf16[512,3,64]{0,2,1:T(8,128)(2,1)S(1)}, u32[]{:S(2)}) copy-start(bf16[512,3,64]{0,2,1:T(8,128)(2,1)S(1)} %get-tuple-element.10) | copy-start | bytes 589828
  108.9 24.7 %copy-start.9 = (bf16[512,3,64]{0,2,1:T(8,128)(2,1)}, bf16[512,3,64]{0,2,1:T(8,128)(2,1)S(1)}, u32[]{:S(2)}) copy-start(bf16[512,3,64]{0,2,1:T(8,128)(2,1)S(1)} %get-tuple-element.11) | copy-start | bytes 589828
  111.1 11.7 %copy-start.6 = (pred[512,512]{1,0:T(32,128)(4,1)S(1)}, pred[512,512]{1,0:T(32,128)(4,1)}, u32[]{:S(2)}) copy-start(pred[512,512]{1,0:T(32,128)(4,1)} %fusion.21) | copy-start | bytes 786436
  111.2 22.4 %copy-start.11 = (bf16[512,128]{1,0:T(8,128)(2,1)}, bf16[512,128]{1,0:T(8,128)(2,1)S(1)}, u32[]{:S(2)}) copy-start(bf16[512,128]{1,0:T(8,128)(2,1)S(1)} %copy.16) | copy-start | bytes 393220
  122.8 10.8 %copy-start.4 = (bf16[8,1,8,1,128,128]{5,4,3,2,0,1:T(8,128)(2,1)}, bf16[8,1,8,1,128,128]{5,4,3,2,0,1:T(8,128)(2,1)S(1)}, u32[]{:S(2)}) copy-start(bf16[8,1,8,1,128,128]{5,4,3,2,0,1:T(8,128)(2,1)S(1)} %get-tuple-element.9) | copy-start | bytes 6291460
  133.6 11.3 %copy-start.17 = (f32[512]{0:T(512)}, f32[512]{0:T(512)S(1)}, u32[]{:S(2)}) copy-start(f32[512]{0:T(512)S(1)} %get-tuple-element.24) | copy-start | bytes 6148
  154.0 18.9 %slice-start = ((s8[17825792]{0:T(1024)(128)(4,1)}), s8[1048576]{0:T(1024)(128)(4,1)S(1)}, s32[]{:S(2)}) async-start(s8[17825792]{0:T(1024)(128)(4,1)} %bitcast.50), calls=%async_computation.3 | async-start | bytes 2097152
  163.2 9.7 %slice-start.1 = ((s8[17825792]{0:T(1024)(128)(4,1)}), s8[4194304]{0:T(1024)(128)(4,1)S(1)}, s32[]{:S(2)}) async-start(s8[17825792]{0:T(1024)(128)(4,1)} %bitcast.50), calls=%async_computation.4 | async-start | bytes 8388608
  163.2 9.7 %slice-start.2 = ((s8[17825792]{0:T(1024)(128)(4,1)}), s8[4194304]{0:T(1024)(128)(4,1)S(1)}, s32[]{:S(2)}) async-start(s8[17825792]{0:T(1024)(128)(4,1)} %bitcast.50), calls=%async_computation.5 | async-start | bytes 8388608
  163.2 9.7 %slice-start.3 = ((s8[17825792]{0:T(1024)(128)(4,1)}), s8[4194304]{0:T(1024)(128)(4,1)S(1)}, s32[]{:S(2)}) async-start(s8[17825792]{0:T(1024)(128)(4,1)} %bitcast.50), calls=%async_computation.6 | async-start | bytes 8388608
  163.2 11.0 %slice-start.4 = ((s8[17825792]{0:T(1024)(128)(4,1)}), s8[4194304]{0:T(1024)(128)(4,1)S(1)}, s32[]{:S(2)}) async-start(s8[17825792]{0:T(1024)(128)(4,1)} %bitcast.50), calls=%async_computation.7 | async-start | bytes 8388608
  163.2 11.0 %copy-start.16 = (f32[512]{0:T(512)S(1)}, f32[512]{0:T(512)}, u32[]{:S(2)}) copy-start(f32[512]{0:T(512)} %get-tuple-element.22) | copy-start | bytes 6148
  163.2 11.0 %copy-start.18 = (f32[512]{0:T(512)S(1)}, f32[512]{0:T(512)}, u32[]{:S(2)}) copy-start(f32[512]{0:T(512)} %fusion.1) | copy-start | bytes 6148
  174.2 4.4 %copy-start.8 = (bf16[512,3,64]{0,2,1:T(8,128)(2,1)S(1)}, bf16[512,3,64]{0,2,1:T(8,128)(2,1)}, u32[]{:S(2)}) copy-start(bf16[512,3,64]{0,2,1:T(8,128)(2,1)} %copy-done.7) | copy-start | bytes 589828
  174.2 4.4 %copy-start.10 = (bf16[512,3,64]{0,2,1:T(8,128)(2,1)S(1)}, bf16[512,3,64]{0,2,1:T(8,128)(2,1)}, u32[]{:S(2)}) copy-start(bf16[512,3,64]{0,2,1:T(8,128)(2,1)} %copy-done.9) | copy-start | bytes 589828
  174.2 4.4 %copy-start.12 = (bf16[512,128]{1,0:T(8,128)(2,1)S(1)}, bf16[512,128]{1,0:T(8,128)(2,1)}, u32[]{:S(2)}) copy-start(bf16[512,128]{1,0:T(8,128)(2,1)} %copy-done.11) | copy-start | bytes 393220
  196.7 9.0 %copy-start.13 = (bf16[512,128]{0,1:T(8,128)(2,1)S(1)}, bf16[512,128]{0,1:T(8,128)(2,1)}, u32[]{:S(2)}) copy-start(bf16[512,128]{0,1:T(8,128)(2,1)} %fusion.20) | copy-start | bytes 393220
  196.7 9.0 %copy-start.14 = (bf16[512,128]{0,1:T(8,128)(2,1)S(1)}, bf16[512,128]{0,1:T(8,128)(2,1)}, u32[]{:S(2)}) copy-start(bf16[512,128]{0,1:T(8,128)(2,1)} %fusion.19) | copy-start | bytes 393220
  206.6 10.9 %all-to-all-start.1 = ((bf16[4,128,384]{2,1,0:T(8,128)(2,1)}), bf16[4,128,384]{2,1,0:T(8,128)(2,1)S(1)}, u32[]{:S(2)}, u32[]{:S(2)}) async-start(bf16[4,128,384]{2,1,0:T(8,128)(2,1)} %bitcast.14), calls=%async_computation.1 | async-start | bytes 786432 | tf_op jit(solution)/shard_map/all_to_all | solution.py:150
  218.7 5.4 %copy-start.1 = (bf16[3072,384]{1,0:T(8,128)(2,1)S(1)}, bf16[3072,384]{1,0:T(8,128)(2,1)}, u32[]{:S(2)}) copy-start(bf16[3072,384]{1,0:T(8,128)(2,1)} %param.11) | copy-start | bytes 7077892
Sparse Core Ops, SparseCore 0:
  29.1 46.9 all-gather.1

commit v2 on v1

--- a/solution.py
+++ b/solution.py
@@ -62,13 +62,6 @@
     max_pages = page_table.shape[1]
     slots = max_pages // n_dp
     key_value_head = current_head // (head_number // KEY_VALUE_HEADS)
-    held_w = w_out
-    held_ids = current_head[None]
-    stride = head_number // 2
-    while stride >= 1:
-        held_w = jnp.concatenate([held_w, exchange(held_w, "head", stride)], 0)
-        held_ids = jnp.concatenate([held_ids, held_ids ^ stride], 0)
-        stride //= 2
     owner_of = jnp.where(page_table >= 0, page_table // pool_rows, -1)
     mine = (owner_of == me_dp).astype(jnp.int32)
     rank = jnp.cumsum(mine, 1) - 1
@@ -76,9 +69,12 @@
     select = (mine[:, None, :] == 1) & (rank[:, None, :] == slot_ids[None, :, None])
     local_page = jnp.sum(jnp.where(select, (page_table % pool_rows)[:, None, :], 0), -1)
     present = jnp.any(select, -1).reshape(-1)
-    outgoing = kv_pool[local_page.reshape(-1), key_value_head]
-    outgoing = jnp.where(present[:, None, None, None], outgoing, jnp.zeros_like(outgoing))
+    part = current_head % 2
+    outgoing = kv_pool[local_page.reshape(-1), key_value_head, part]
     received = lax.all_to_all(outgoing, "dp", split_axis=0, concat_axis=0, tiled=True)
+    other_half = exchange(received, "head", 1)
+    cache_keys = jnp.where(part == 0, received, other_half).reshape(-1, HEAD_SIZE)
+    cache_vals = jnp.where(part == 0, other_half, received).reshape(-1, HEAD_SIZE)
     within = jnp.arange(page_len, dtype=jnp.int32)
     owners_mine = lax.dynamic_slice_in_dim(owner_of, me_dp * REQ_DEV, REQ_DEV, 0)
     hits = (owners_mine[None, :, :] == jnp.arange(n_dp, dtype=jnp.int32)[:, None, None]).astype(
@@ -91,7 +87,6 @@
     )
     has_page = jnp.any(chosen, -1)
     key_pos = logical[..., None] * page_len + within[None, None, None, :]
-    received = received.reshape(n_dp, REQ_DEV, slots, 2, page_len, head_dim)
     wide = tokens.astype(jnp.float32)
     meansq = jnp.mean(wide * wide, -1, keepdims=True)
     normalized_input = (wide * lax.rsqrt(meansq + 1e-05) * norm_gain.astype(jnp.float32)).astype(
@@ -108,6 +103,18 @@
     queries = rotate(
         projected[:, :q_width].reshape(block_rows, group_heads, head_dim), positions
     ).astype(jnp.bfloat16)
+    held_w = [w_out]
+    held_ids = [current_head]
+    stride = head_number // 2
+    while stride >= 1:
+        if stride != head_number // 2:
+            late, queries = lax.optimization_barrier((held_w[1:], queries))
+            held_w = held_w[:1] + list(late)
+        held_w = held_w + [exchange(piece, "head", stride) for piece in held_w]
+        held_ids = held_ids + [ident ^ stride for ident in held_ids]
+        stride //= 2
+    held_w = jnp.concatenate(held_w, 0)
+    held_ids = jnp.stack(held_ids)
     own_part = projected[:, q_width:]
     holds_keys = current_head % 2 == 0
     turned = rotate(own_part[:, None, :], positions)[:, 0]
@@ -118,8 +125,6 @@
     mask_rows = lax.dynamic_slice_in_dim(token_mask, me_dp * block_rows, block_rows, 0)
     scale = 1.0 / math.sqrt(head_dim)
     local_idx = jnp.arange(NEWTOK, dtype=jnp.int32)
-    cache_keys = received[:, 0, :, 0].reshape(-1, head_dim)
-    cache_vals = received[:, 0, :, 1].reshape(-1, head_dim)
     cache_ok = (has_page[:, 0, :, None] & (key_pos[:, 0] < my_lengths[0])).reshape(-1)
     new_ok = (mask_rows[None, :] == 1) & (local_idx[None, :] <= local_idx[:, None])
     valid = jnp.concatenate(

time: 231 us -> 202 us (0.87)
  waiting for transfers between devices: 81.2 us -> 61.1 us
  other arithmetic: 45.3 us -> 39.8 us
  local copies, waits for them, and re-layouts: 12.9 us -> 9.55 us
    ppermute x2 -> x4, waiting for transfers between devices: 63.3 us -> 11 us  [exchange(): return lax.ppermute(value, axis, pairs)]
    all_to_all x1, waiting for transfers between devices: 8.61 us -> 42.9 us  [body(): lax.all_to_all(outgoing, 'dp', split_axis=0, concat_axis=0, tiled=True)]
    concatenate x3 -> x2, other arithmetic: 4.93 us -> 0.04 us  [the longest x1 0.03 us: rotate(): jnp.concatenate([first * cosine - second * sine, second * cosine + first...]
    slice x1 -> x0, local copies, waits for them, and re-layouts: 2.81 us -> none  [body(): cache_vals = received[:, 0, :, 1].reshape(-1, head_dim)]
  transfers between devices with their start and end apart: 6 -> 8, of which waited for: 4 -> 3; matrix products, arithmetic and copies ran while one was open for 45% -> 51% of each run, Pallas kernels for 0% -> 0%
where the time goes in v2:
time: 202 us
  matrix products  64.5 us (32%)
  waiting for transfers between devices  61.1 us (30%)
  other arithmetic  39.8 us (20%)
  between operations  13.8 us (7%)
  starting transfers between devices  12.8 us (6%)
  local copies, waits for them, and re-layouts  9.55 us (5%)
    all_to_all x1, waiting for transfers between devices, body(): lax.all_to_all(outgoing, 'dp', split_axis=0, concat_axis=0, tiled=True)  42.9 us
    dot_general x3, matrix products, body(): lax.dot_general(queries[0:NEWTOK, head], keys, (((1,), (1,)), ((), ())),...  32.5 us
    reduce_sum x3, other arithmetic, body(): probs = expo / jnp.sum(expo, -1, keepdims=True)  25.7 us
    dot_general x3, matrix products, body(): jnp.dot(weights, vals, preferred_element_type=jnp.float32)  21.9 us
    ppermute x4, waiting for transfers between devices, exchange(): return lax.ppermute(value, axis, pairs)  11 us
    all_to_all x1, starting transfers between devices, body(): lax.all_to_all(outgoing, 'dp', split_axis=0, concat_axis=0, tiled=True)  7.25 us
    all_to_all x1, waiting for transfers between devices, body(): lax.all_to_all(pieces, 'head', split_axis=0, concat_axis=1, tiled=True)  7.13 us
    dot_general x1, matrix products, body(): out = jnp.dot(ordered, held_w, preferred_element_type=jnp.float32)  5.44 us
  transfers between devices with their start and end apart: 8, of which 3 were waited for; matrix products, arithmetic and copies ran while one was open for 51% of the time, Pallas kernels for 0%

profile of v2, /device:TPU:0, one launch (start us, length us, event | category | flops | bytes accessed | tf_op | source)
XLA Modules:
  0.0 201.5 jit_solution(16508272018247816408)
XLA Ops:
  6.5 0.8 convert_element_type.63
  7.4 1.4 fusion.17
  8.8 2.3 %fusion.19 = bf16[128,3072]{1,0:T(8,128)(2,1)} fusion(bf16[128,3072]{1,0:T(8,128)(2,1)} %param.9, f32[3072]{0:T(1024)S(1)} %convert_element_type.63, f32[128]{0:T(128)S(1)} %add_rsqrt_fusion), kind=kLoop, calls=%fused_computation.35 | loop fusion | flops 1572864 | bytes 1585664 | tf_op jit(solution)/shard_map/convert_element_type | solution.py:92
  11.0 0.0 all-gather.2.cloned.1.call-update
  11.1 0.0 copy-start.8
  11.1 0.7 broadcast_compare_fusion
  11.8 0.2 reduce_window_sum.23
  12.0 0.7 add_select_fusion
  12.7 0.2 select_reduce_fusion
  13.0 0.1 reshape.487
  13.1 0.0 copy-start.3
  13.1 5.1 %gather_fusion = bf16[64,128,128]{2,1,0:T(8,128)(2,1)} fusion(bf16[48,2,2,128,128]{4,3,2,1,0:T(8,128)(2,1)} %param.14, s32[64]{0:T(128)S(1)} %fusion.55), kind=kCustom, calls=%fused_computation | custom fusion | bytes 4195072 | tf_op jit(solution)/shard_map/gather | solution.py:73
  18.2 7.3 %all-to-all-start = ((bf16[64,128,128]{2,1,0:T(8,128)(2,1)}), bf16[64,128,128]{2,1,0:T(8,128)(2,1)}, u32[]{:S(2)}, u32[]{:S(2)}) async-start(bf16[64,128,128]{2,1,0:T(8,128)(2,1)} %gather_fusion), calls=%async_computation | async-start | bytes 4194304 | tf_op jit(solution)/shard_map/all_to_all | solution.py:74
  25.4 1.5 collective-permute-start
  26.9 0.0 collective-permute-start.3
  27.0 0.6 dynamic_slice.10
  27.6 0.2 reduce_window_sum.22
  27.8 0.2 fusion.39
  28.0 0.2 select_reduce_fusion.1
  28.2 0.7 fusion.41
  28.9 0.8 dynamic-slice_compare_fusion
  29.7 0.6 fusion.47
  30.3 0.5 multiply_cosine_fusion.1
  30.8 42.9 %all-to-all-done = bf16[64,128,128]{2,1,0:T(8,128)(2,1)} async-done(((bf16[64,128,128]{2,1,0:T(8,128)(2,1)}), bf16[64,128,128]{2,1,0:T(8,128)(2,1)}, u32[]{:S(2)}, u32[]{:S(2)}) %all-to-all-start) | async-done | bytes 2097184 | tf_op jit(solution)/shard_map/all_to_all | solution.py:74
  73.8 0.0 collective-permute-start.1
  73.8 0.8 fusion.23
  74.6 3.2 %fusion.69 = f32[512,128]{0,1:T(8,128)S(1)} fusion(bf16[512,3072]{1,0:T(8,128)(2,1)} %all-gather.2.cloned.1.call-done, bf16[3072,128]{1,0:T(8,128)(2,1)S(1)} %copy-done.3), kind=kOutput, calls=%fused_computation.124 | convolution fusion | flops 402653184 | bytes 4194304 | tf_op jit(solution)/shard_map/dot_general | solution.py:97
  77.8 0.6 fusion.30
  78.4 0.6 collective-permute-start.2
  79.0 1.4 fusion.68
  80.4 0.1 subtract_convert_fusion
  80.6 11.0 %collective-permute-done = bf16[384,3072]{1,0:T(8,128)(2,1)} collective-permute-done((bf16[384,3072]{1,0:T(8,128)(2,1)}, bf16[384,3072]{1,0:T(8,128)(2,1)}, u32[]{:S(2)}, u32[]{:S(2)}) %collective-permute-start) | collective-permute-done | bytes 2359328 | tf_op jit(solution)/shard_map/ppermute | solution.py:25
  91.6 0.0 collective-permute-start.4
  91.6 0.0 collective-permute-done.2
  91.6 0.1 copy.16
  91.7 0.1 copy.17
  91.9 0.0 collective-permute-done.1
  91.9 2.5 %broadcast_select_fusion = (bf16[64,128,128]{2,1,0:T(8,128)(2,1)S(1)}, bf16[64,128,128]{2,1,0:T(8,128)(2,1)S(1)}) fusion(bf16[64,128,128]{2,1,0:T(8,128)(2,1)} %collective-permute-done.1, bf16[64,128,128]{2,1,0:T(8,128)(2,1)} %all-to-all-done, pred[]{:T(512)S(6)} %eq.114), kind=kLoop, calls=%fused_computation.29 | loop fusion | flops 2097152 | bytes 8388609 | tf_op jit(solution)/shard_map/jit(_where)/select_n | solution.py:77
  94.4 10.6 %fusion.67 = (f32[512]{0:T(512)S(1)}, f32[512,8704]{1,0:T(8,128)}) fusion(bf16[512,128]{1,0:T(8,128)(2,1)S(1)} %copy.16, bf16[8192,128]{1,0:T(8,128)(2,1)S(1)} %bitcast.58, bf16[512,3,128]{0,2,1:T(8,128)(2,1)S(1)} %pad_maximum_fusion.8, pred[512,512]{1,0:T(32,128)(4,1)S(1)} %copy-done.4, pred[8704]{0:T(1024)(128)(4,1)S(1)} %pad.19.clone), kind=kOutput, calls=%fused_computation.122 | convolution fusion | flops 1163132416 | bytes 20458496 | tf_op jit(solution)/shard_map/dot_general | solution.py:138
  105.0 11.2 %fusion.66 = (f32[512]{0:T(512)}, f32[512,8704]{1,0:T(8,128)}) fusion(bf16[512,128]{1,0:T(8,128)(2,1)S(1)} %copy.16, bf16[8192,128]{1,0:T(8,128)(2,1)S(1)} %bitcast.59, bf16[512,3,128]{0,2,1:T(8,128)(2,1)S(1)} %pad_maximum_fusion.8, pred[512,512]{1,0:T(32,128)(4,1)S(1)} %copy-done.4, pred[8704]{0:T(1024)(128)(4,1)S(1)} %pad.19.clone), kind=kOutput, calls=%fused_computation.121 | convolution fusion | flops 1163132416 | bytes 20458496 | tf_op jit(solution)/shard_map/dot_general | solution.py:138
  116.2 10.6 %fusion.65 = (f32[512]{0:T(512)S(1)}, f32[512,8704]{1,0:T(8,128)}) fusion(bf16[512,128]{1,0:T(8,128)(2,1)S(1)} %copy.16, bf16[8192,128]{1,0:T(8,128)(2,1)S(1)} %bitcast.60, bf16[512,3,128]{0,2,1:T(8,128)(2,1)S(1)} %pad_maximum_fusion.8, pred[512,512]{1,0:T(32,128)(4,1)S(1)} %copy-done.4, pred[8704]{0:T(1024)(128)(4,1)S(1)} %pad.19.clone), kind=kOutput, calls=%fused_computation.120 | convolution fusion | flops 1163132416 | bytes 20458496 | tf_op jit(solution)/shard_map/dot_general | solution.py:138
  126.9 8.6 %fusion = f32[512]{0:T(512)S(1)} fusion(f32[512,8704]{1,0:T(8,128)} %get-tuple-element.29, f32[512]{0:T(512)S(1)} %get-tuple-element.28), kind=kLoop, calls=%fused_computation.12 | loop fusion | flops 8912384 | bytes 17829888 | tf_op jit(solution)/shard_map/reduce_sum | solution.py:149
  135.4 0.0 slice-start
  135.4 8.6 %fusion.1 = f32[512]{0:T(512)S(1)} fusion(f32[512,8704]{1,0:T(8,128)} %get-tuple-element.27, f32[512]{0:T(512)S(1)} %copy-done.5), kind=kLoop, calls=%fused_computation.13 | loop fusion | flops 8912384 | bytes 17829888 | tf_op jit(solution)/shard_map/reduce_sum | solution.py:149
  144.1 0.0 slice-start.2
  144.1 0.0 slice-start.3
  144.1 9.3 %fusion.22 = bf16[512,128]{0,1:T(8,128)(2,1)S(1)} fusion(f32[512,8704]{1,0:T(8,128)} %get-tuple-element.29, f32[512]{0:T(512)S(1)} %fusion, f32[512]{0:T(512)S(1)} %copy-done.7, bf16[512,128]{1,0:T(8,128)(2,1)S(1)} %copy.17, bf16[8192,128]{1,0:T(8,128)(2,1)S(1)} %bitcast.55), kind=kOutput, calls=%fused_computation.38 | convolution fusion | flops 1158742016 | bytes 20189184 | tf_op jit(solution)/shard_map/dot_general | solution.py:152
  153.4 0.4 slice-done.3
  153.8 1.2 slice-done.4
  155.0 3.7 %fusion.21 = bf16[512,128]{0,1:T(8,128)(2,1)S(1)} fusion(f32[512,8704]{1,0:T(8,128)S(1)} %bitcast.53, f32[512]{0:T(512)S(1)} %fusion.1, f32[512]{0:T(512)S(1)} %copy-done.5, bf16[512,128]{1,0:T(8,128)(2,1)S(1)} %copy.17, bf16[8192,128]{1,0:T(8,128)(2,1)S(1)} %bitcast.56), kind=kOutput, calls=%fused_computation.37 | convolution fusion | flops 1158742016 | bytes 20189184 | tf_op jit(solution)/shard_map/dot_general | solution.py:152
  158.8 8.5 %fusion.2 = f32[512]{0:T(512)S(1)} fusion(f32[512,8704]{1,0:T(8,128)} %get-tuple-element.25, f32[512]{0:T(512)S(1)} %get-tuple-element.24), kind=kLoop, calls=%fused_computation.14 | loop fusion | flops 8912384 | bytes 17829888 | tf_op jit(solution)/shard_map/reduce_sum | solution.py:149
  167.3 8.9 %fusion.20 = bf16[512,128]{0,1:T(8,128)(2,1)S(1)} fusion(f32[512,8704]{1,0:T(8,128)} %get-tuple-element.25, f32[512]{0:T(512)S(1)} %fusion.2, f32[512]{0:T(512)S(1)} %get-tuple-element.24, bf16[512,128]{1,0:T(8,128)(2,1)S(1)} %copy.17, bf16[8192,128]{1,0:T(8,128)(2,1)S(1)} %bitcast.57), kind=kOutput, calls=%fused_computation.36 | convolution fusion | flops 1158742016 | bytes 20189184 | tf_op jit(solution)/shard_map/dot_general | solution.py:152
  176.2 0.9 copy.20
  177.2 3.5 %all-to-all-start.1 = ((bf16[4,128,384]{2,1,0:T(8,128)(2,1)}), bf16[4,128,384]{2,1,0:T(8,128)(2,1)S(1)}, u32[]{:S(2)}, u32[]{:S(2)}) async-start(bf16[4,128,384]{2,1,0:T(8,128)(2,1)} %bitcast.16), calls=%async_computation.1 | async-start | bytes 786432 | tf_op jit(solution)/shard_map/all_to_all | solution.py:155
  180.6 0.1 compare_and_fusion
  180.7 0.1 broadcast_in_dim.50
  180.8 0.1 fusion.56
  180.9 7.1 %all-to-all-done.1 = bf16[4,128,384]{2,1,0:T(8,128)(2,1)S(1)} async-done(((bf16[4,128,384]{2,1,0:T(8,128)(2,1)}), bf16[4,128,384]{2,1,0:T(8,128)(2,1)S(1)}, u32[]{:S(2)}, u32[]{:S(2)}) %all-to-all-start.1) | async-done | bytes 393248 | tf_op jit(solution)/shard_map/all_to_all | solution.py:155
  188.0 0.6 gather_fusion.1
  188.7 0.2 copy.19
  188.9 0.3 bitcast_select_fusion
  189.2 0.0 collective-permute-done.3
  189.2 0.0 copy-start.1
  189.2 5.4 %fusion.14 = bf16[128,3072]{1,0:T(8,128)(2,1)} fusion(bf16[128,1536]{0,1:T(8,128)(2,1)S(1)} %bitcast_select_fusion, bf16[384,3072]{1,0:T(8,128)(2,1)} %collective-permute-done.4, bf16[384,3072]{1,0:T(8,128)(2,1)} %collective-permute-done.3, bf16[384,3072]{1,0:T(8,128)(2,1)} %collective-permute-done, bf16[384,3072]{1,0:T(8,128)(2,1)} %param.13), kind=kOutput, calls=%fused_computation.26 | convolution fusion | flops 1246101504 | bytes 10616832 | tf_op jit(solution)/shard_map/dot_general | solution.py:158
  (39 shorter events, 0.3 us)
Async XLA Ops:
  6.5 72.4 %copy-start = (bf16[3072,384]{1,0:T(8,128)(2,1)S(1)}, bf16[3072,384]{1,0:T(8,128)(2,1)}, u32[]{:S(2)}) copy-start(bf16[3072,384]{1,0:T(8,128)(2,1)} %param.11) | copy-start | bytes 7077892
  6.5 68.0 %all-gather.2.cloned.1.call-start = ((), (), s32[]{:S(2)}) async-start(), calls=%async_computation.2 | async-start | bytes 3932160 | tf_op jit(solution)/shard_map/all_gather | solution.py:95
  11.1 15.9 %copy-start.8 = (s32[8]{0:T(128)S(1)}, s32[8]{0:T(128)}, u32[]{:S(2)}) copy-start(s32[8]{0:T(128)} %param.15) | copy-start | bytes 100
  13.1 61.5 %copy-start.3 = (bf16[3072,128]{1,0:T(8,128)(2,1)S(1)}, bf16[3072,128]{1,0:T(8,128)(2,1)}, u32[]{:S(2)}) copy-start(bf16[3072,128]{1,0:T(8,128)(2,1)} %param.12) | copy-start | bytes 2359300
  18.2 55.6 %all-to-all-start = ((bf16[64,128,128]{2,1,0:T(8,128)(2,1)}), bf16[64,128,128]{2,1,0:T(8,128)(2,1)}, u32[]{:S(2)}, u32[]{:S(2)}) async-start(bf16[64,128,128]{2,1,0:T(8,128)(2,1)} %gather_fusion), calls=%async_computation | async-start | bytes 4194304 | tf_op jit(solution)/shard_map/all_to_all | solution.py:74
  25.4 66.1 %collective-permute-start = (bf16[384,3072]{1,0:T(8,128)(2,1)}, bf16[384,3072]{1,0:T(8,128)(2,1)}, u32[]{:S(2)}, u32[]{:S(2)}) collective-permute-start(bf16[384,3072]{1,0:T(8,128)(2,1)} %param.13), channel_id=1, source_target_pairs={{0,2},{1,3},{2,0},{3,1},{4,6},{5,7},{6,4},{7,5},{8,10},{9,11},{10,... | collective-permute-start | bytes 7077896 | tf_op jit(solution)/shard_map/ppermute | solution.py:25
  26.9 162.2 %collective-permute-start.3 = (bf16[384,3072]{1,0:T(8,128)(2,1)}, bf16[384,3072]{1,0:T(8,128)(2,1)}, u32[]{:S(2)}, u32[]{:S(2)}) collective-permute-start(bf16[384,3072]{1,0:T(8,128)(2,1)} %param.13), channel_id=1, source_target_pairs={{0,1},{1,0},{2,3},{3,2},{4,5},{5,4},{6,7},{7,6},{8,9},{9,8},{10,11... | collective-permute-start | bytes 7077896 | tf_op jit(solution)/shard_map/ppermute | solution.py:25
  73.8 18.1 %collective-permute-start.1 = (bf16[64,128,128]{2,1,0:T(8,128)(2,1)}, bf16[64,128,128]{2,1,0:T(8,128)(2,1)}, u32[]{:S(2)}, u32[]{:S(2)}) collective-permute-start(bf16[64,128,128]{2,1,0:T(8,128)(2,1)} %all-to-all-done), channel_id=1, source_target_pairs={{0,1},{1,0},{2,3},{3,2},{4,5},{5,4},{6,7},{7,6},{8,9},{9,8},{10,11... | collective-permute-start | bytes 6291464 | tf_op jit(solution)/shard_map/ppermute | solution.py:25
  74.6 4.4 %copy-start.2 = (bf16[512,3072]{1,0:T(8,128)(2,1)S(1)}, bf16[512,3072]{1,0:T(8,128)(2,1)}, u32[]{:S(2)}) copy-start(bf16[512,3072]{1,0:T(8,128)(2,1)} %all-gather.2.cloned.1.call-done) | copy-start | bytes 9437188
  78.4 13.2 %collective-permute-start.2 = (bf16[512,128]{0,1:T(8,128)(2,1)S(1)}, bf16[512,128]{0,1:T(8,128)(2,1)S(1)}, u32[]{:S(2)}, u32[]{:S(2)}) collective-permute-start(bf16[512,128]{0,1:T(8,128)(2,1)S(1)} %fusion.25), channel_id=1, source_target_pairs={{0,1},{1,0},{2,3},{3,2},{4,5},{5,4},{6,7},{7,6},{8,9},{9,8},{10,11... | collective-permute-start | bytes 393224 | tf_op jit(solution)/shard_map/ppermute | solution.py:20
  91.6 97.6 %collective-permute-start.4 = (bf16[384,3072]{1,0:T(8,128)(2,1)}, bf16[384,3072]{1,0:T(8,128)(2,1)}, u32[]{:S(2)}, u32[]{:S(2)}) collective-permute-start(bf16[384,3072]{1,0:T(8,128)(2,1)} %collective-permute-done), channel_id=1, source_target_pairs={{0,1},{1,0},{2,3},{3,2},{4,5},{5,4},{6,7},{7,6},{8,9},{9,8},{10,11... | collective-permute-start | bytes 7077896 | tf_op jit(solution)/shard_map/ppermute | solution.py:25
  91.6 2.8 %copy-start.4 = (pred[512,512]{1,0:T(32,128)(4,1)S(1)}, pred[512,512]{1,0:T(32,128)(4,1)}, u32[]{:S(2)}) copy-start(pred[512,512]{1,0:T(32,128)(4,1)} %fusion.23) | copy-start | bytes 786436
  105.0 21.8 %copy-start.6 = (f32[512]{0:T(512)}, f32[512]{0:T(512)S(1)}, u32[]{:S(2)}) copy-start(f32[512]{0:T(512)S(1)} %get-tuple-element.28) | copy-start | bytes 6148
  126.9 8.6 %copy-start.5 = (f32[512]{0:T(512)S(1)}, f32[512]{0:T(512)}, u32[]{:S(2)}) copy-start(f32[512]{0:T(512)} %get-tuple-element.26) | copy-start | bytes 6148
  135.4 8.7 %copy-start.7 = (f32[512]{0:T(512)S(1)}, f32[512]{0:T(512)}, u32[]{:S(2)}) copy-start(f32[512]{0:T(512)} %copy-done.6) | copy-start | bytes 6148
  135.4 18.0 %slice-start = ((s8[17825792]{0:T(1024)(128)(4,1)}), s8[1048576]{0:T(1024)(128)(4,1)S(1)}, s32[]{:S(2)}) async-start(s8[17825792]{0:T(1024)(128)(4,1)} %bitcast.52), calls=%async_computation.3 | async-start | bytes 2097152
  144.1 9.3 %slice-start.1 = ((s8[17825792]{0:T(1024)(128)(4,1)}), s8[4194304]{0:T(1024)(128)(4,1)S(1)}, s32[]{:S(2)}) async-start(s8[17825792]{0:T(1024)(128)(4,1)} %bitcast.52), calls=%async_computation.4 | async-start | bytes 8388608
  144.1 9.3 %slice-start.2 = ((s8[17825792]{0:T(1024)(128)(4,1)}), s8[4194304]{0:T(1024)(128)(4,1)S(1)}, s32[]{:S(2)}) async-start(s8[17825792]{0:T(1024)(128)(4,1)} %bitcast.52), calls=%async_computation.5 | async-start | bytes 8388608
  144.1 9.7 %slice-start.3 = ((s8[17825792]{0:T(1024)(128)(4,1)}), s8[4194304]{0:T(1024)(128)(4,1)S(1)}, s32[]{:S(2)}) async-start(s8[17825792]{0:T(1024)(128)(4,1)} %bitcast.52), calls=%async_computation.6 | async-start | bytes 8388608
  144.1 10.9 %slice-start.4 = ((s8[17825792]{0:T(1024)(128)(4,1)}), s8[4194304]{0:T(1024)(128)(4,1)S(1)}, s32[]{:S(2)}) async-start(s8[17825792]{0:T(1024)(128)(4,1)} %bitcast.52), calls=%async_computation.7 | async-start | bytes 8388608
  177.2 10.9 %all-to-all-start.1 = ((bf16[4,128,384]{2,1,0:T(8,128)(2,1)}), bf16[4,128,384]{2,1,0:T(8,128)(2,1)S(1)}, u32[]{:S(2)}, u32[]{:S(2)}) async-start(bf16[4,128,384]{2,1,0:T(8,128)(2,1)} %bitcast.16), calls=%async_computation.1 | async-start | bytes 786432 | tf_op jit(solution)/shard_map/all_to_all | solution.py:155
  189.2 5.5 %copy-start.1 = (bf16[3072,384]{1,0:T(8,128)(2,1)S(1)}, bf16[3072,384]{1,0:T(8,128)(2,1)}, u32[]{:S(2)}) copy-start(bf16[3072,384]{1,0:T(8,128)(2,1)} %param.11) | copy-start | bytes 7077892
Sparse Core Ops, SparseCore 0:
  11.2 44.0 all-gather.1

commit v3 on v2

--- a/solution.py
+++ b/solution.py
@@ -4,6 +4,8 @@
 import jax.numpy as jnp
 from jax import lax
 from jax.sharding import PartitionSpec as P
+from jax.experimental import pallas as pl
+from jax.experimental.pallas import tpu as pltpu
 
 KEY_VALUE_HEADS = 2
 HEAD_SIZE = 128
@@ -18,6 +20,74 @@
     mask = 2**stride
     pairs = [(source, source ^ mask) for source in range(lax.axis_size(axis))]
     return lax.ppermute(value, axis, pairs)
+
+
+def attend_kernel(n_cache, tk, scale, q_ref, k_ref, v_ref, ok_ref, o_ref, s_scr):
+    bq = q_ref.shape[0]
+    total = k_ref.shape[0]
+    chunks = total // tk
+    q = q_ref[...]
+    row = pl.program_id(1) * bq + lax.broadcasted_iota(jnp.int32, (bq, tk), 0)
+    lane = lax.broadcasted_iota(jnp.int32, (bq, tk), 1)
+
+    def scores(c, top):
+        start = pl.multiple_of(c * tk, tk)
+        keys = k_ref[pl.ds(start, tk), :]
+        s = lax.dot_general(q, keys, (((1,), (1,)), ((), ())), preferred_element_type=jnp.float32)
+        s = s * scale
+        col = start + lane
+        ok = (ok_ref[:, pl.ds(start, tk)] != 0) & ((col < n_cache) | (col - n_cache <= row))
+        s = jnp.where(ok, s, -jnp.inf)
+        s_scr[:, pl.ds(start, tk)] = s
+        return jnp.maximum(top, jnp.max(s, -1, keepdims=True))
+
+    top = lax.fori_loop(0, chunks, scores, jnp.full((bq, 1), -jnp.inf, jnp.float32))
+
+    def expo(c, total_sum):
+        start = pl.multiple_of(c * tk, tk)
+        e = jnp.exp(s_scr[:, pl.ds(start, tk)] - top)
+        s_scr[:, pl.ds(start, tk)] = e
+        return total_sum + jnp.sum(e, -1, keepdims=True)
+
+    denom = lax.fori_loop(0, chunks, expo, jnp.zeros((bq, 1), jnp.float32))
+
+    def weigh(c, acc):
+        start = pl.multiple_of(c * tk, tk)
+        w = (s_scr[:, pl.ds(start, tk)] / denom).astype(jnp.bfloat16)
+        return acc + jnp.dot(w, v_ref[pl.ds(start, tk), :], preferred_element_type=jnp.float32)
+
+    acc = lax.fori_loop(0, chunks, weigh, jnp.zeros((bq, q.shape[1]), jnp.float32))
+    o_ref[...] = acc.astype(o_ref.dtype)
+
+
+def attend(queries, keys, vals, key_ok, n_cache):
+    rows, width = queries.shape
+    total, head_dim = keys.shape
+    heads = width // head_dim
+    bq = 256 if rows % 256 == 0 else rows
+    tk = next(t for t in (512, 256, 128) if total % t == 0 and n_cache % t == 0)
+    scale = 1.0 / math.sqrt(head_dim)
+    cost = pl.CostEstimate(
+        flops=4 * rows * total * head_dim * heads,
+        transcendentals=rows * total * heads,
+        bytes_accessed=2 * (2 * total * head_dim + 2 * rows * width) + 4 * total,
+    )
+    return pl.pallas_call(
+        lambda *refs: attend_kernel(n_cache, tk, scale, *refs),
+        out_shape=jax.ShapeDtypeStruct((rows, width), jnp.bfloat16),
+        grid=(heads, rows // bq),
+        in_specs=[
+            pl.BlockSpec((bq, head_dim), lambda h, b: (b, h)),
+            pl.BlockSpec((total, head_dim), lambda h, b: (0, 0)),
+            pl.BlockSpec((total, head_dim), lambda h, b: (0, 0)),
+            pl.BlockSpec((1, total), lambda h, b: (0, 0)),
+        ],
+        out_specs=pl.BlockSpec((bq, head_dim), lambda h, b: (b, h)),
+        scratch_shapes=[pltpu.VMEM((bq, total), jnp.float32)],
+        compiler_params=pltpu.CompilerParams(dimension_semantics=("arbitrary", "arbitrary")),
+        cost_estimate=cost,
+        name="paged_prefill_attention",
+    )(queries, keys, vals, key_ok)
 
 
 def exchange(value, axis, mask):
@@ -123,35 +193,17 @@
     new_keys = jnp.where(holds_keys, own_ready, partner_ready)
     new_values = jnp.where(holds_keys, partner_ready, own_ready)
     mask_rows = lax.dynamic_slice_in_dim(token_mask, me_dp * block_rows, block_rows, 0)
-    scale = 1.0 / math.sqrt(head_dim)
-    local_idx = jnp.arange(NEWTOK, dtype=jnp.int32)
     cache_ok = (has_page[:, 0, :, None] & (key_pos[:, 0] < my_lengths[0])).reshape(-1)
-    new_ok = (mask_rows[None, :] == 1) & (local_idx[None, :] <= local_idx[:, None])
-    valid = jnp.concatenate(
-        [jnp.broadcast_to(cache_ok[None, :], (NEWTOK, cache_ok.shape[0])), new_ok], 1
-    )
+    key_ok = jnp.concatenate([cache_ok.astype(jnp.int32), (mask_rows == 1).astype(jnp.int32)])
     keys = jnp.concatenate([cache_keys, new_keys], 0)
     vals = jnp.concatenate([cache_vals, new_values], 0)
-    head_outs = []
-    for head in range(group_heads):
-        scores = (
-            lax.dot_general(
-                queries[0:NEWTOK, head],
-                keys,
-                (((1,), (1,)), ((), ())),
-                preferred_element_type=jnp.float32,
-            )
-            * scale
-        )
-        masked = jnp.where(valid, scores, -jnp.inf)
-        top = jnp.max(masked, -1, keepdims=True)
-        expo = jnp.exp(masked - top)
-        probs = expo / jnp.sum(expo, -1, keepdims=True)
-        weights = probs.astype(jnp.bfloat16)
-        head_outs.append(
-            jnp.dot(weights, vals, preferred_element_type=jnp.float32).astype(jnp.bfloat16)
-        )
-    pieces = jnp.concatenate(head_outs, -1)
+    pieces = attend(
+        queries[0:NEWTOK].reshape(NEWTOK, group_heads * head_dim),
+        keys,
+        vals,
+        key_ok.reshape(1, -1),
+        cache_ok.shape[0],
+    )
     gathered = lax.all_to_all(pieces, "head", split_axis=0, concat_axis=1, tiled=True)
     gathered = gathered.reshape(local_rows, head_number, group_heads * head_dim)
     ordered = jnp.take(gathered, held_ids, axis=1).reshape(local_rows, -1)

time: 202 us -> 205 us (1.015)
  Pallas kernels: 0 us -> 79.8 us
  matrix products: 64.5 us -> 9.74 us
  other arithmetic: 39.8 us -> 18.6 us
    pallas_call x0 -> x1, Pallas kernels: none -> 79.8 us  [attend(): pl.pallas_call(lambda *refs: attend_kernel(n_cache, tk, scale, *refs), ou...]
    dot_general x6 -> x0, matrix products: 54.4 us -> none  [the longest x3 32.5 us: body(): lax.dot_general(queries[0:NEWTOK, head], keys, (((1,), (1,)), ((), ())),...]
    reduce_sum x3 -> x0, other arithmetic: 25.7 us -> none  [body(): probs = expo / jnp.sum(expo, -1, keepdims=True)]
    concatenate x1, other arithmetic: 0.03 us -> 5.86 us  [body(): keys = jnp.concatenate([cache_keys, new_keys], 0)]
  transfers between devices with their start and end apart: 8 -> 8, of which waited for: 3 -> 3; matrix products, arithmetic and copies ran while one was open for 51% -> 13% of each run, Pallas kernels for 0% -> 39%
where the time goes in v3:
time: 205 us
  Pallas kernels  79.8 us (39%)
  waiting for transfers between devices  61.9 us (30%)
  other arithmetic  18.6 us (9%)
  between operations  13.6 us (7%)
  starting transfers between devices  12.9 us (6%)
  matrix products  9.74 us (5%)
  local copies, waits for them, and re-layouts  8.21 us (4%)
    pallas_call x1, Pallas kernels, attend(): pl.pallas_call(lambda *refs: attend_kernel(n_cache, tk, scale, *refs), ou...  79.8 us
    all_to_all x1, waiting for transfers between devices, body(): lax.all_to_all(outgoing, 'dp', split_axis=0, concat_axis=0, tiled=True)  42.7 us
    ppermute x4, waiting for transfers between devices, exchange(): return lax.ppermute(value, axis, pairs)  12 us
    all_to_all x1, starting transfers between devices, body(): lax.all_to_all(outgoing, 'dp', split_axis=0, concat_axis=0, tiled=True)  7.38 us
    all_to_all x1, waiting for transfers between devices, body(): lax.all_to_all(pieces, 'head', split_axis=0, concat_axis=1, tiled=True)  7.13 us
    concatenate x1, other arithmetic, body(): keys = jnp.concatenate([cache_keys, new_keys], 0)  5.86 us
    dot_general x1, matrix products, body(): out = jnp.dot(ordered, held_w, preferred_element_type=jnp.float32)  5.31 us
    gather x1, local copies, waits for them, and re-layouts, body(): outgoing = kv_pool[local_page.reshape(-1), key_value_head, part]  4.98 us
  transfers between devices with their start and end apart: 8, of which 3 were waited for; matrix products, arithmetic and copies ran while one was open for 13% of the time, Pallas kernels for 39%

profile of v3, /device:TPU:0, one launch (start us, length us, event | category | flops | bytes accessed | tf_op | source)
XLA Modules:
  0.0 204.9 jit_solution(14829766473859603615)
XLA Ops:
  6.5 0.0 copy-start
  6.5 0.0 copy-start.3
  6.5 0.0 all-gather.2.cloned.1.call-start
  6.5 1.5 fusion.11
  8.1 0.7 convert_element_type.49
  8.8 2.3 %fusion.13 = bf16[128,3072]{1,0:T(8,128)(2,1)} fusion(bf16[128,3072]{1,0:T(8,128)(2,1)} %param.9, f32[3072]{0:T(1024)S(1)} %convert_element_type.49, f32[128]{0:T(128)S(1)} %add_rsqrt_fusion), kind=kLoop, calls=%fused_computation.19 | loop fusion | flops 1572864 | bytes 1585664 | tf_op jit(solution)/shard_map/convert_element_type | solution.py:162
  11.1 0.0 all-gather.2.cloned.1.call-update
  11.1 0.0 copy-done.3
  11.2 0.2 reduce_window_sum.22
  11.4 0.2 select_reduce_fusion.1
  11.6 0.1 reshape.473
  11.7 5.0 %gather_fusion = bf16[64,128,128]{2,1,0:T(8,128)(2,1)} fusion(bf16[48,2,2,128,128]{4,3,2,1,0:T(8,128)(2,1)} %param.14, s32[64]{0:T(128)S(1)} %fusion.39), kind=kCustom, calls=%fused_computation | custom fusion | bytes 4195072 | tf_op jit(solution)/shard_map/gather | solution.py:143
  16.7 0.0 copy-start.4
  16.7 0.0 copy-start.2
  16.7 7.4 %all-to-all-start = ((bf16[64,128,128]{2,1,0:T(8,128)(2,1)}), bf16[64,128,128]{2,1,0:T(8,128)(2,1)}, u32[]{:S(2)}, u32[]{:S(2)}) async-start(bf16[64,128,128]{2,1,0:T(8,128)(2,1)} %gather_fusion), calls=%async_computation | async-start | bytes 4194304 | tf_op jit(solution)/shard_map/all_to_all | solution.py:144
  24.1 1.5 collective-permute-start
  25.6 0.0 collective-permute-start.3
  25.6 0.0 copy-done.4
  25.6 0.6 dynamic_slice.11
  26.2 0.2 reduce_window_sum.23
  26.5 0.2 fusion.24
  26.7 0.2 select_reduce_fusion
  26.9 0.7 fusion.26
  27.6 0.8 dynamic-slice_compare_fusion
  28.4 0.6 reshape.479.refs_3_
  29.0 0.6 fusion.31
  29.7 42.7 %all-to-all-done = bf16[64,128,128]{2,1,0:T(8,128)(2,1)} async-done(((bf16[64,128,128]{2,1,0:T(8,128)(2,1)}), bf16[64,128,128]{2,1,0:T(8,128)(2,1)}, u32[]{:S(2)}, u32[]{:S(2)}) %all-to-all-start) | async-done | bytes 2097184 | tf_op jit(solution)/shard_map/all_to_all | solution.py:144
  72.4 0.0 collective-permute-start.1
  72.4 0.5 multiply_cosine_fusion.1
  73.0 0.0 all-gather.2.cloned.1.call-done
  73.0 0.0 copy-done.2
  73.0 0.0 copy-start.1
  73.0 3.0 %fusion.44 = f32[512,128]{1,0:T(8,128)S(1)} fusion(bf16[512,3072]{1,0:T(8,128)(2,1)} %all-gather.2.cloned.1.call-done, bf16[3072,128]{1,0:T(8,128)(2,1)S(1)} %copy-done.2), kind=kOutput, calls=%fused_computation.88 | convolution fusion | flops 402653184 | bytes 4194304 | tf_op jit(solution)/shard_map/dot_general | solution.py:167
  76.0 1.2 fusion.18
  77.3 0.1 fusion.21
  77.4 0.6 collective-permute-start.2
  77.9 0.0 copy-done
  77.9 0.0 copy-done.1
  77.9 1.4 fusion.43
  79.4 0.1 subtract_convert_fusion
  79.6 12.0 %collective-permute-done = bf16[384,3072]{1,0:T(8,128)(2,1)} collective-permute-done((bf16[384,3072]{1,0:T(8,128)(2,1)}, bf16[384,3072]{1,0:T(8,128)(2,1)}, u32[]{:S(2)}, u32[]{:S(2)}) %collective-permute-start) | collective-permute-done | bytes 2359328 | tf_op jit(solution)/shard_map/ppermute | solution.py:95
  91.6 0.9 copy.23.refs_0_
  92.5 0.0 collective-permute-start.4
  92.5 0.0 collective-permute-done.2
  92.5 0.0 collective-permute-done.1
  92.5 2.5 %broadcast_select_fusion = (bf16[64,128,128]{2,1,0:T(8,128)(2,1)S(1)}, bf16[64,128,128]{2,1,0:T(8,128)(2,1)S(1)}) fusion(bf16[64,128,128]{2,1,0:T(8,128)(2,1)} %collective-permute-done.1, bf16[64,128,128]{2,1,0:T(8,128)(2,1)} %all-to-all-done, pred[]{:T(512)S(6)} %eq.100), kind=kLoop, calls=%fused_computation.13 | loop fusion | flops 2097152 | bytes 8388609 | tf_op jit(solution)/shard_map/jit(_where)/select_n | solution.py:147
  95.0 5.9 %pad_maximum_fusion = (bf16[8704,128]{1,0:T(8,128)(2,1)}, bf16[8704,128]{1,0:T(8,128)(2,1)}) fusion(bf16[512,128]{1,0:T(8,128)(2,1)S(1)} %get-tuple-element.19, bf16[8192,128]{1,0:T(8,128)(2,1)S(1)} %bitcast.39, bf16[512,128]{1,0:T(8,128)(2,1)S(1)} %get-tuple-element.18, bf16[8192,128]{1,0:T(8,128)(2,1)S(1)} %bitcast.38), kind=kLoop, calls=%fused_computation.11 | loop fusion | flops 8912896 | bytes 8912896 | tf_op jit(solution)/shard_map/concatenate | solution.py:198
  100.9 79.8 %paged_prefill_attention.1 = bf16[512,384]{1,0:T(8,128)(2,1)} custom-call(bf16[512,384]{1,0:T(8,128)(2,1)} %copy.23.refs_0_, bf16[8704,128]{1,0:T(8,128)(2,1)} %get-tuple-element.24.refs_1_, bf16[8704,128]{1,0:T(8,128)(2,1)} %get-tuple-element.25.refs_2_, s32[1,8704]{1,0:T(1,128)} %reshape.479.refs_3_), custom_call_target="tpu_custom_call" | custom-call | flops 6845104128 | bytes 5277696 | tf_op jit(solution)/shard_map/paged_prefill_attention/pallas_call | solution.py:75
  180.7 3.5 %all-to-all-start.1 = ((bf16[4,128,384]{2,1,0:T(8,128)(2,1)}), bf16[4,128,384]{2,1,0:T(8,128)(2,1)S(1)}, u32[]{:S(2)}, u32[]{:S(2)}) async-start(bf16[4,128,384]{2,1,0:T(8,128)(2,1)} %bitcast.45), calls=%async_computation.1 | async-start | bytes 786432 | tf_op jit(solution)/shard_map/all_to_all | solution.py:207
  184.2 0.1 compare_and_fusion
  184.3 0.1 broadcast_in_dim.43
  184.4 0.1 fusion.40
  184.5 7.1 %all-to-all-done.1 = bf16[4,128,384]{2,1,0:T(8,128)(2,1)S(1)} async-done(((bf16[4,128,384]{2,1,0:T(8,128)(2,1)}), bf16[4,128,384]{2,1,0:T(8,128)(2,1)S(1)}, u32[]{:S(2)}, u32[]{:S(2)}) %all-to-all-start.1) | async-done | bytes 393248 | tf_op jit(solution)/shard_map/all_to_all | solution.py:207
  191.6 0.6 gather_fusion.1
  192.2 0.2 copy.24
  192.5 0.3 bitcast_select_fusion
  192.7 0.0 collective-permute-done.3
  192.7 0.0 collective-permute-done.4
  192.8 5.3 %fusion.8 = bf16[128,3072]{1,0:T(8,128)(2,1)} fusion(bf16[128,1536]{0,1:T(8,128)(2,1)S(1)} %bitcast_select_fusion, bf16[384,3072]{1,0:T(8,128)(2,1)} %collective-permute-done.4, bf16[384,3072]{1,0:T(8,128)(2,1)} %collective-permute-done.3, bf16[384,3072]{1,0:T(8,128)(2,1)} %collective-permute-done, bf16[384,3072]{1,0:T(8,128)(2,1)} %param.13), kind=kOutput, calls=%fused_computation.10 | convolution fusion | flops 1246101504 | bytes 10616832 | tf_op jit(solution)/shard_map/dot_general | solution.py:210
  (15 shorter events, 0.2 us)
Async XLA Ops:
  6.5 71.4 %copy-start = (bf16[3072,384]{1,0:T(8,128)(2,1)S(1)}, bf16[3072,384]{1,0:T(8,128)(2,1)}, u32[]{:S(2)}) copy-start(bf16[3072,384]{1,0:T(8,128)(2,1)} %param.11) | copy-start | bytes 7077892
  6.5 4.6 %copy-start.3 = (s32[8,64]{1,0:T(8,128)S(1)}, s32[8,64]{1,0:T(8,128)}, u32[]{:S(2)}) copy-start(s32[8,64]{1,0:T(8,128)} %param.16) | copy-start | bytes 6148
  6.5 66.4 %all-gather.2.cloned.1.call-start = ((), (), s32[]{:S(2)}) async-start(), calls=%async_computation.2 | async-start | bytes 3932160 | tf_op jit(solution)/shard_map/all_gather | solution.py:165
  16.7 8.9 %copy-start.4 = (s32[8]{0:T(128)S(1)}, s32[8]{0:T(128)}, u32[]{:S(2)}) copy-start(s32[8]{0:T(128)} %param.15) | copy-start | bytes 100
  16.7 56.3 %copy-start.2 = (bf16[3072,128]{1,0:T(8,128)(2,1)S(1)}, bf16[3072,128]{1,0:T(8,128)(2,1)}, u32[]{:S(2)}) copy-start(bf16[3072,128]{1,0:T(8,128)(2,1)} %param.12) | copy-start | bytes 2359300
  16.7 55.7 %all-to-all-start = ((bf16[64,128,128]{2,1,0:T(8,128)(2,1)}), bf16[64,128,128]{2,1,0:T(8,128)(2,1)}, u32[]{:S(2)}, u32[]{:S(2)}) async-start(bf16[64,128,128]{2,1,0:T(8,128)(2,1)} %gather_fusion), calls=%async_computation | async-start | bytes 4194304 | tf_op jit(solution)/shard_map/all_to_all | solution.py:144
  24.1 67.5 %collective-permute-start = (bf16[384,3072]{1,0:T(8,128)(2,1)}, bf16[384,3072]{1,0:T(8,128)(2,1)}, u32[]{:S(2)}, u32[]{:S(2)}) collective-permute-start(bf16[384,3072]{1,0:T(8,128)(2,1)} %param.13), channel_id=1, source_target_pairs={{0,2},{1,3},{2,0},{3,1},{4,6},{5,7},{6,4},{7,5},{8,10},{9,11},{10,... | collective-permute-start | bytes 7077896 | tf_op jit(solution)/shard_map/ppermute | solution.py:95
  25.6 167.1 %collective-permute-start.3 = (bf16[384,3072]{1,0:T(8,128)(2,1)}, bf16[384,3072]{1,0:T(8,128)(2,1)}, u32[]{:S(2)}, u32[]{:S(2)}) collective-permute-start(bf16[384,3072]{1,0:T(8,128)(2,1)} %param.13), channel_id=1, source_target_pairs={{0,1},{1,0},{2,3},{3,2},{4,5},{5,4},{6,7},{7,6},{8,9},{9,8},{10,11... | collective-permute-start | bytes 7077896 | tf_op jit(solution)/shard_map/ppermute | solution.py:95
  72.4 20.1 %collective-permute-start.1 = (bf16[64,128,128]{2,1,0:T(8,128)(2,1)}, bf16[64,128,128]{2,1,0:T(8,128)(2,1)}, u32[]{:S(2)}, u32[]{:S(2)}) collective-permute-start(bf16[64,128,128]{2,1,0:T(8,128)(2,1)} %all-to-all-done), channel_id=1, source_target_pairs={{0,1},{1,0},{2,3},{3,2},{4,5},{5,4},{6,7},{7,6},{8,9},{9,8},{10,11... | collective-permute-start | bytes 6291464 | tf_op jit(solution)/shard_map/ppermute | solution.py:95
  73.0 5.0 %copy-start.1 = (bf16[512,3072]{1,0:T(8,128)(2,1)S(1)}, bf16[512,3072]{1,0:T(8,128)(2,1)}, u32[]{:S(2)}) copy-start(bf16[512,3072]{1,0:T(8,128)(2,1)} %all-gather.2.cloned.1.call-done) | copy-start | bytes 9437188
  77.4 15.1 %collective-permute-start.2 = (bf16[512,128]{1,0:T(8,128)(2,1)S(1)}, bf16[512,128]{1,0:T(8,128)(2,1)S(1)}, u32[]{:S(2)}, u32[]{:S(2)}) collective-permute-start(bf16[512,128]{1,0:T(8,128)(2,1)S(1)} %fusion.21), channel_id=1, source_target_pairs={{0,1},{1,0},{2,3},{3,2},{4,5},{5,4},{6,7},{7,6},{8,9},{9,8},{10,11... | collective-permute-start | bytes 393224 | tf_op jit(solution)/shard_map/ppermute | solution.py:22
  92.5 100.3 %collective-permute-start.4 = (bf16[384,3072]{1,0:T(8,128)(2,1)}, bf16[384,3072]{1,0:T(8,128)(2,1)}, u32[]{:S(2)}, u32[]{:S(2)}) collective-permute-start(bf16[384,3072]{1,0:T(8,128)(2,1)} %collective-permute-done), channel_id=1, source_target_pairs={{0,1},{1,0},{2,3},{3,2},{4,5},{5,4},{6,7},{7,6},{8,9},{9,8},{10,11... | collective-permute-start | bytes 7077896 | tf_op jit(solution)/shard_map/ppermute | solution.py:95
  180.7 10.9 %all-to-all-start.1 = ((bf16[4,128,384]{2,1,0:T(8,128)(2,1)}), bf16[4,128,384]{2,1,0:T(8,128)(2,1)S(1)}, u32[]{:S(2)}, u32[]{:S(2)}) async-start(bf16[4,128,384]{2,1,0:T(8,128)(2,1)} %bitcast.45), calls=%async_computation.1 | async-start | bytes 786432 | tf_op jit(solution)/shard_map/all_to_all | solution.py:207
Sparse Core Ops, SparseCore 0:
  11.2 45.4 all-gather.1

commit v4 on v3

--- a/solution.py
+++ b/solution.py
@@ -22,50 +22,57 @@
     return lax.ppermute(value, axis, pairs)
 
 
-def attend_kernel(n_cache, tk, scale, q_ref, k_ref, v_ref, ok_ref, o_ref, s_scr):
-    bq = q_ref.shape[0]
+def attend_kernel(n_cache, tk, scale, q_ref, k_ref, v_ref, bias_ref, o_ref, s_scr):
+    bq, head_dim = q_ref.shape
     total = k_ref.shape[0]
-    chunks = total // tk
+    groups = tk // 128
     q = q_ref[...]
     row = pl.program_id(1) * bq + lax.broadcasted_iota(jnp.int32, (bq, tk), 0)
     lane = lax.broadcasted_iota(jnp.int32, (bq, tk), 1)
 
-    def scores(c, top):
+    def scores(c, top, causal):
         start = pl.multiple_of(c * tk, tk)
         keys = k_ref[pl.ds(start, tk), :]
         s = lax.dot_general(q, keys, (((1,), (1,)), ((), ())), preferred_element_type=jnp.float32)
-        s = s * scale
-        col = start + lane
-        ok = (ok_ref[:, pl.ds(start, tk)] != 0) & ((col < n_cache) | (col - n_cache <= row))
-        s = jnp.where(ok, s, -jnp.inf)
+        s = s * scale + bias_ref[:, pl.ds(start, tk)]
+        if causal:
+            s = jnp.where(start - n_cache + lane <= row, s, -jnp.inf)
         s_scr[:, pl.ds(start, tk)] = s
-        return jnp.maximum(top, jnp.max(s, -1, keepdims=True))
-
-    top = lax.fori_loop(0, chunks, scores, jnp.full((bq, 1), -jnp.inf, jnp.float32))
-
-    def expo(c, total_sum):
+        for g in range(groups):
+            top = jnp.maximum(top, s[:, g * 128:(g + 1) * 128])
+        return top
+
+    top = jnp.full((bq, 128), -jnp.inf, jnp.float32)
+    top = lax.fori_loop(0, n_cache // tk, lambda c, t: scores(c, t, False), top, unroll=2)
+    top = lax.fori_loop(n_cache // tk, total // tk, lambda c, t: scores(c, t, True), top)
+    top = jnp.max(top, -1, keepdims=True)
+
+    def expo(c, part):
         start = pl.multiple_of(c * tk, tk)
         e = jnp.exp(s_scr[:, pl.ds(start, tk)] - top)
         s_scr[:, pl.ds(start, tk)] = e
-        return total_sum + jnp.sum(e, -1, keepdims=True)
-
-    denom = lax.fori_loop(0, chunks, expo, jnp.zeros((bq, 1), jnp.float32))
+        for g in range(groups):
+            part = part + e[:, g * 128:(g + 1) * 128]
+        return part
+
+    part = lax.fori_loop(0, total // tk, expo, jnp.zeros((bq, 128), jnp.float32), unroll=2)
+    inverse = 1.0 / jnp.sum(part, -1, keepdims=True)
 
     def weigh(c, acc):
         start = pl.multiple_of(c * tk, tk)
-        w = (s_scr[:, pl.ds(start, tk)] / denom).astype(jnp.bfloat16)
+        w = (s_scr[:, pl.ds(start, tk)] * inverse).astype(jnp.bfloat16)
         return acc + jnp.dot(w, v_ref[pl.ds(start, tk), :], preferred_element_type=jnp.float32)
 
-    acc = lax.fori_loop(0, chunks, weigh, jnp.zeros((bq, q.shape[1]), jnp.float32))
+    acc = lax.fori_loop(0, total // tk, weigh, jnp.zeros((bq, head_dim), jnp.float32), unroll=2)
     o_ref[...] = acc.astype(o_ref.dtype)
 
 
-def attend(queries, keys, vals, key_ok, n_cache):
+def attend(queries, keys, vals, bias, n_cache):
     rows, width = queries.shape
     total, head_dim = keys.shape
     heads = width // head_dim
-    bq = 256 if rows % 256 == 0 else rows
-    tk = next(t for t in (512, 256, 128) if total % t == 0 and n_cache % t == 0)
+    bq = rows
+    tk = next(t for t in (256, 128) if total % t == 0 and n_cache % t == 0)
     scale = 1.0 / math.sqrt(head_dim)
     cost = pl.CostEstimate(
         flops=4 * rows * total * head_dim * heads,
@@ -87,7 +94,7 @@
         compiler_params=pltpu.CompilerParams(dimension_semantics=("arbitrary", "arbitrary")),
         cost_estimate=cost,
         name="paged_prefill_attention",
-    )(queries, keys, vals, key_ok)
+    )(queries, keys, vals, bias)
 
 
 def exchange(value, axis, mask):
@@ -194,14 +201,15 @@
     new_values = jnp.where(holds_keys, partner_ready, own_ready)
     mask_rows = lax.dynamic_slice_in_dim(token_mask, me_dp * block_rows, block_rows, 0)
     cache_ok = (has_page[:, 0, :, None] & (key_pos[:, 0] < my_lengths[0])).reshape(-1)
-    key_ok = jnp.concatenate([cache_ok.astype(jnp.int32), (mask_rows == 1).astype(jnp.int32)])
+    key_ok = jnp.concatenate([cache_ok, mask_rows == 1])
+    bias = jnp.where(key_ok, 0.0, -jnp.inf).astype(jnp.float32)
     keys = jnp.concatenate([cache_keys, new_keys], 0)
     vals = jnp.concatenate([cache_vals, new_values], 0)
     pieces = attend(
         queries[0:NEWTOK].reshape(NEWTOK, group_heads * head_dim),
         keys,
         vals,
-        key_ok.reshape(1, -1),
+        bias.reshape(1, -1),
         cache_ok.shape[0],
     )
     gathered = lax.all_to_all(pieces, "head", split_axis=0, concat_axis=1, tiled=True)

time: 205 us -> 175 us (0.85)
  Pallas kernels: 79.8 us -> 49.6 us
    pallas_call x1, Pallas kernels: 79.8 us -> 49.6 us  [attend(): pl.pallas_call(lambda *refs: attend_kernel(n_cache, tk, scale, *refs), ou...]
  transfers between devices with their start and end apart: 8 -> 8, of which waited for: 3 -> 3; matrix products, arithmetic and copies ran while one was open for 13% -> 15% of each run, Pallas kernels for 39% -> 28%
where the time goes in v4:
time: 175 us
  waiting for transfers between devices  61.9 us (35%)
  Pallas kernels  49.6 us (28%)
  other arithmetic  19.3 us (11%)
  between operations  13.6 us (8%)
  starting transfers between devices  12.9 us (7%)
  matrix products  9.74 us (6%)
  local copies, waits for them, and re-layouts  7.58 us (4%)
    pallas_call x1, Pallas kernels, attend(): pl.pallas_call(lambda *refs: attend_kernel(n_cache, tk, scale, *refs), ou...  49.6 us
    all_to_all x1, waiting for transfers between devices, body(): lax.all_to_all(outgoing, 'dp', split_axis=0, concat_axis=0, tiled=True)  42.7 us
    ppermute x4, waiting for transfers between devices, exchange(): return lax.ppermute(value, axis, pairs)  12 us
    all_to_all x1, starting transfers between devices, body(): lax.all_to_all(outgoing, 'dp', split_axis=0, concat_axis=0, tiled=True)  7.38 us
    all_to_all x1, waiting for transfers between devices, body(): lax.all_to_all(pieces, 'head', split_axis=0, concat_axis=1, tiled=True)  7.13 us
    concatenate x1, other arithmetic, body(): keys = jnp.concatenate([cache_keys, new_keys], 0)  5.85 us
    dot_general x1, matrix products, body(): out = jnp.dot(ordered, held_w, preferred_element_type=jnp.float32)  5.31 us
    gather x1, local copies, waits for them, and re-layouts, body(): outgoing = kv_pool[local_page.reshape(-1), key_value_head, part]  4.98 us
  transfers between devices with their start and end apart: 8, of which 3 were waited for; matrix products, arithmetic and copies ran while one was open for 15% of the time, Pallas kernels for 28%

profile of v4, /device:TPU:0, one launch (start us, length us, event | category | flops | bytes accessed | tf_op | source)
XLA Modules:
  0.0 174.7 jit_solution(8728766429966426750)
XLA Ops:
  6.5 0.0 copy-start
  6.5 0.0 copy-start.3
  6.5 0.0 all-gather.2.cloned.1.call-start
  6.5 1.5 fusion.11
  8.1 0.7 convert_element_type.44
  8.8 2.3 %fusion.13 = bf16[128,3072]{1,0:T(8,128)(2,1)} fusion(bf16[128,3072]{1,0:T(8,128)(2,1)} %param.9, f32[3072]{0:T(1024)S(1)} %convert_element_type.44, f32[128]{0:T(128)S(1)} %add_rsqrt_fusion), kind=kLoop, calls=%fused_computation.19 | loop fusion | flops 1572864 | bytes 1585664 | tf_op jit(solution)/shard_map/convert_element_type | solution.py:169
  11.1 0.0 all-gather.2.cloned.1.call-update
  11.1 0.0 copy-done.3
  11.2 0.2 reduce_window_sum.22
  11.4 0.2 select_reduce_fusion.1
  11.6 0.1 reshape.509
  11.7 5.0 %gather_fusion = bf16[64,128,128]{2,1,0:T(8,128)(2,1)} fusion(bf16[48,2,2,128,128]{4,3,2,1,0:T(8,128)(2,1)} %param.14, s32[64]{0:T(128)S(1)} %fusion.38), kind=kCustom, calls=%fused_computation | custom fusion | bytes 4195072 | tf_op jit(solution)/shard_map/gather | solution.py:150
  16.7 0.0 copy-start.4
  16.7 0.0 copy-start.2
  16.7 7.4 %all-to-all-start = ((bf16[64,128,128]{2,1,0:T(8,128)(2,1)}), bf16[64,128,128]{2,1,0:T(8,128)(2,1)}, u32[]{:S(2)}, u32[]{:S(2)}) async-start(bf16[64,128,128]{2,1,0:T(8,128)(2,1)} %gather_fusion), calls=%async_computation | async-start | bytes 4194304 | tf_op jit(solution)/shard_map/all_to_all | solution.py:151
  24.1 1.5 collective-permute-start
  25.6 0.0 collective-permute-start.3
  25.6 0.8 dynamic-slice_compare_fusion
  26.4 0.0 copy-done.4
  26.4 0.6 dynamic_slice.11
  27.0 0.2 reduce_window_sum.23
  27.2 0.2 fusion.24
  27.4 0.2 select_reduce_fusion
  27.7 0.7 fusion.25
  28.4 0.7 add_select_fusion.refs_3_
  29.1 0.6 fusion.30
  29.7 42.7 %all-to-all-done = bf16[64,128,128]{2,1,0:T(8,128)(2,1)} async-done(((bf16[64,128,128]{2,1,0:T(8,128)(2,1)}), bf16[64,128,128]{2,1,0:T(8,128)(2,1)}, u32[]{:S(2)}, u32[]{:S(2)}) %all-to-all-start) | async-done | bytes 2097184 | tf_op jit(solution)/shard_map/all_to_all | solution.py:151
  72.4 0.0 collective-permute-start.1
  72.4 0.5 multiply_cosine_fusion.1
  72.9 0.0 all-gather.2.cloned.1.call-done
  73.0 0.0 copy-done.2
  73.0 0.0 copy-start.1
  73.0 3.0 %fusion.43 = f32[512,128]{1,0:T(8,128)S(1)} fusion(bf16[512,3072]{1,0:T(8,128)(2,1)} %all-gather.2.cloned.1.call-done, bf16[3072,128]{1,0:T(8,128)(2,1)S(1)} %copy-done.2), kind=kOutput, calls=%fused_computation.87 | convolution fusion | flops 402653184 | bytes 4194304 | tf_op jit(solution)/shard_map/dot_general | solution.py:174
  76.0 1.2 fusion.18
  77.2 0.1 fusion.21
  77.4 0.6 collective-permute-start.2
  77.9 0.0 copy-done
  77.9 0.0 copy-done.1
  77.9 1.4 fusion.42
  79.4 0.1 subtract_convert_fusion
  79.5 12.0 %collective-permute-done = bf16[384,3072]{1,0:T(8,128)(2,1)} collective-permute-done((bf16[384,3072]{1,0:T(8,128)(2,1)}, bf16[384,3072]{1,0:T(8,128)(2,1)}, u32[]{:S(2)}, u32[]{:S(2)}) %collective-permute-start) | collective-permute-done | bytes 2359328 | tf_op jit(solution)/shard_map/ppermute | solution.py:102
  91.6 0.9 copy.23.refs_0_
  92.5 0.0 collective-permute-start.4
  92.5 0.0 collective-permute-done.2
  92.5 0.0 collective-permute-done.1
  92.5 2.5 %broadcast_select_fusion = (bf16[64,128,128]{2,1,0:T(8,128)(2,1)S(1)}, bf16[64,128,128]{2,1,0:T(8,128)(2,1)S(1)}) fusion(bf16[64,128,128]{2,1,0:T(8,128)(2,1)} %collective-permute-done.1, bf16[64,128,128]{2,1,0:T(8,128)(2,1)} %all-to-all-done, pred[]{:T(512)S(6)} %eq.100), kind=kLoop, calls=%fused_computation.13 | loop fusion | flops 2097152 | bytes 8388609 | tf_op jit(solution)/shard_map/jit(_where)/select_n | solution.py:154
  95.0 5.9 %pad_maximum_fusion = (bf16[8704,128]{1,0:T(8,128)(2,1)}, bf16[8704,128]{1,0:T(8,128)(2,1)}) fusion(bf16[512,128]{1,0:T(8,128)(2,1)S(1)} %get-tuple-element.19, bf16[8192,128]{1,0:T(8,128)(2,1)S(1)} %bitcast.37, bf16[512,128]{1,0:T(8,128)(2,1)S(1)} %get-tuple-element.18, bf16[8192,128]{1,0:T(8,128)(2,1)S(1)} %bitcast.36), kind=kLoop, calls=%fused_computation.11 | loop fusion | flops 8912896 | bytes 8912896 | tf_op jit(solution)/shard_map/concatenate | solution.py:206
  100.9 49.6 %paged_prefill_attention.1 = bf16[512,384]{1,0:T(8,128)(2,1)} custom-call(bf16[512,384]{1,0:T(8,128)(2,1)} %copy.23.refs_0_, bf16[8704,128]{1,0:T(8,128)(2,1)} %get-tuple-element.24.refs_1_, bf16[8704,128]{1,0:T(8,128)(2,1)} %get-tuple-element.25.refs_2_, f32[1,8704]{1,0:T(1,128)} %add_select_fusion.refs_3_), custom_call_target="tpu_custom_call" | custom-call | flops 6845104128 | bytes 5277696 | tf_op jit(solution)/shard_map/paged_prefill_attention/pallas_call | solution.py:82
  150.5 3.5 %all-to-all-start.1 = ((bf16[4,128,384]{2,1,0:T(8,128)(2,1)}), bf16[4,128,384]{2,1,0:T(8,128)(2,1)S(1)}, u32[]{:S(2)}, u32[]{:S(2)}) async-start(bf16[4,128,384]{2,1,0:T(8,128)(2,1)} %bitcast.43), calls=%async_computation.1 | async-start | bytes 786432 | tf_op jit(solution)/shard_map/all_to_all | solution.py:215
  154.0 0.1 compare_and_fusion
  154.1 0.1 broadcast_in_dim.51
  154.2 0.1 fusion.39
  154.3 7.1 %all-to-all-done.1 = bf16[4,128,384]{2,1,0:T(8,128)(2,1)S(1)} async-done(((bf16[4,128,384]{2,1,0:T(8,128)(2,1)}), bf16[4,128,384]{2,1,0:T(8,128)(2,1)S(1)}, u32[]{:S(2)}, u32[]{:S(2)}) %all-to-all-start.1) | async-done | bytes 393248 | tf_op jit(solution)/shard_map/all_to_all | solution.py:215
  161.4 0.6 gather_fusion.1
  162.0 0.2 copy.24
  162.3 0.3 bitcast_select_fusion
  162.5 0.0 collective-permute-done.3
  162.5 0.0 collective-permute-done.4
  162.6 5.3 %fusion.8 = bf16[128,3072]{1,0:T(8,128)(2,1)} fusion(bf16[128,1536]{0,1:T(8,128)(2,1)S(1)} %bitcast_select_fusion, bf16[384,3072]{1,0:T(8,128)(2,1)} %collective-permute-done.4, bf16[384,3072]{1,0:T(8,128)(2,1)} %collective-permute-done.3, bf16[384,3072]{1,0:T(8,128)(2,1)} %collective-permute-done, bf16[384,3072]{1,0:T(8,128)(2,1)} %param.13), kind=kOutput, calls=%fused_computation.10 | convolution fusion | flops 1246101504 | bytes 10616832 | tf_op jit(solution)/shard_map/dot_general | solution.py:218
  (16 shorter events, 0.2 us)
Async XLA Ops:
  6.5 71.4 %copy-start = (bf16[3072,384]{1,0:T(8,128)(2,1)S(1)}, bf16[3072,384]{1,0:T(8,128)(2,1)}, u32[]{:S(2)}) copy-start(bf16[3072,384]{1,0:T(8,128)(2,1)} %param.11) | copy-start | bytes 7077892
  6.5 4.6 %copy-start.3 = (s32[8,64]{1,0:T(8,128)S(1)}, s32[8,64]{1,0:T(8,128)}, u32[]{:S(2)}) copy-start(s32[8,64]{1,0:T(8,128)} %param.16) | copy-start | bytes 6148
  6.5 66.4 %all-gather.2.cloned.1.call-start = ((), (), s32[]{:S(2)}) async-start(), calls=%async_computation.2 | async-start | bytes 3932160 | tf_op jit(solution)/shard_map/all_gather | solution.py:172
  16.7 9.7 %copy-start.4 = (s32[8]{0:T(128)S(1)}, s32[8]{0:T(128)}, u32[]{:S(2)}) copy-start(s32[8]{0:T(128)} %param.15) | copy-start | bytes 100
  16.7 56.3 %copy-start.2 = (bf16[3072,128]{1,0:T(8,128)(2,1)S(1)}, bf16[3072,128]{1,0:T(8,128)(2,1)}, u32[]{:S(2)}) copy-start(bf16[3072,128]{1,0:T(8,128)(2,1)} %param.12) | copy-start | bytes 2359300
  16.7 55.7 %all-to-all-start = ((bf16[64,128,128]{2,1,0:T(8,128)(2,1)}), bf16[64,128,128]{2,1,0:T(8,128)(2,1)}, u32[]{:S(2)}, u32[]{:S(2)}) async-start(bf16[64,128,128]{2,1,0:T(8,128)(2,1)} %gather_fusion), calls=%async_computation | async-start | bytes 4194304 | tf_op jit(solution)/shard_map/all_to_all | solution.py:151
  24.1 67.5 %collective-permute-start = (bf16[384,3072]{1,0:T(8,128)(2,1)}, bf16[384,3072]{1,0:T(8,128)(2,1)}, u32[]{:S(2)}, u32[]{:S(2)}) collective-permute-start(bf16[384,3072]{1,0:T(8,128)(2,1)} %param.13), channel_id=1, source_target_pairs={{0,2},{1,3},{2,0},{3,1},{4,6},{5,7},{6,4},{7,5},{8,10},{9,11},{10,... | collective-permute-start | bytes 7077896 | tf_op jit(solution)/shard_map/ppermute | solution.py:102
  25.6 137.0 %collective-permute-start.3 = (bf16[384,3072]{1,0:T(8,128)(2,1)}, bf16[384,3072]{1,0:T(8,128)(2,1)}, u32[]{:S(2)}, u32[]{:S(2)}) collective-permute-start(bf16[384,3072]{1,0:T(8,128)(2,1)} %param.13), channel_id=1, source_target_pairs={{0,1},{1,0},{2,3},{3,2},{4,5},{5,4},{6,7},{7,6},{8,9},{9,8},{10,11... | collective-permute-start | bytes 7077896 | tf_op jit(solution)/shard_map/ppermute | solution.py:102
  72.4 20.1 %collective-permute-start.1 = (bf16[64,128,128]{2,1,0:T(8,128)(2,1)}, bf16[64,128,128]{2,1,0:T(8,128)(2,1)}, u32[]{:S(2)}, u32[]{:S(2)}) collective-permute-start(bf16[64,128,128]{2,1,0:T(8,128)(2,1)} %all-to-all-done), channel_id=1, source_target_pairs={{0,1},{1,0},{2,3},{3,2},{4,5},{5,4},{6,7},{7,6},{8,9},{9,8},{10,11... | collective-permute-start | bytes 6291464 | tf_op jit(solution)/shard_map/ppermute | solution.py:102
  73.0 5.0 %copy-start.1 = (bf16[512,3072]{1,0:T(8,128)(2,1)S(1)}, bf16[512,3072]{1,0:T(8,128)(2,1)}, u32[]{:S(2)}) copy-start(bf16[512,3072]{1,0:T(8,128)(2,1)} %all-gather.2.cloned.1.call-done) | copy-start | bytes 9437188
  77.4 15.1 %collective-permute-start.2 = (bf16[512,128]{1,0:T(8,128)(2,1)S(1)}, bf16[512,128]{1,0:T(8,128)(2,1)S(1)}, u32[]{:S(2)}, u32[]{:S(2)}) collective-permute-start(bf16[512,128]{1,0:T(8,128)(2,1)S(1)} %fusion.21), channel_id=1, source_target_pairs={{0,1},{1,0},{2,3},{3,2},{4,5},{5,4},{6,7},{7,6},{8,9},{9,8},{10,11... | collective-permute-start | bytes 393224 | tf_op jit(solution)/shard_map/ppermute | solution.py:22
  92.5 70.1 %collective-permute-start.4 = (bf16[384,3072]{1,0:T(8,128)(2,1)}, bf16[384,3072]{1,0:T(8,128)(2,1)}, u32[]{:S(2)}, u32[]{:S(2)}) collective-permute-start(bf16[384,3072]{1,0:T(8,128)(2,1)} %collective-permute-done), channel_id=1, source_target_pairs={{0,1},{1,0},{2,3},{3,2},{4,5},{5,4},{6,7},{7,6},{8,9},{9,8},{10,11... | collective-permute-start | bytes 7077896 | tf_op jit(solution)/shard_map/ppermute | solution.py:102
  150.5 10.9 %all-to-all-start.1 = ((bf16[4,128,384]{2,1,0:T(8,128)(2,1)}), bf16[4,128,384]{2,1,0:T(8,128)(2,1)S(1)}, u32[]{:S(2)}, u32[]{:S(2)}) async-start(bf16[4,128,384]{2,1,0:T(8,128)(2,1)} %bitcast.43), calls=%async_computation.1 | async-start | bytes 786432 | tf_op jit(solution)/shard_map/all_to_all | solution.py:215
Sparse Core Ops, SparseCore 0:
  11.2 45.4 all-gather.1

commit v5 on v4

--- a/solution.py
+++ b/solution.py
@@ -22,17 +22,43 @@
     return lax.ppermute(value, axis, pairs)
 
 
-def attend_kernel(n_cache, tk, scale, q_ref, k_ref, v_ref, bias_ref, o_ref, s_scr):
+def attend_kernel(
+    n_cache, tk, scale, part_ref, q_ref, mine_hbm, other_hbm, nk_hbm, nv_hbm, bias_ref,
+    o_ref, k_scr, v_scr, s_scr, sems,
+):
     bq, head_dim = q_ref.shape
-    total = k_ref.shape[0]
+    total = k_scr.shape[0]
     groups = tk // 128
+
+    @pl.when(pl.program_id(0) == 0)
+    def _():
+        def load(src_k, src_v):
+            copies = [
+                pltpu.make_async_copy(src_k, k_scr.at[pl.ds(0, n_cache)], sems.at[0]),
+                pltpu.make_async_copy(src_v, v_scr.at[pl.ds(0, n_cache)], sems.at[1]),
+                pltpu.make_async_copy(nk_hbm, k_scr.at[pl.ds(n_cache, total - n_cache)], sems.at[2]),
+                pltpu.make_async_copy(nv_hbm, v_scr.at[pl.ds(n_cache, total - n_cache)], sems.at[3]),
+            ]
+            for copy in copies:
+                copy.start()
+            for copy in copies:
+                copy.wait()
+
+        @pl.when(part_ref[0] == 0)
+        def _():
+            load(mine_hbm, other_hbm)
+
+        @pl.when(part_ref[0] != 0)
+        def _():
+            load(other_hbm, mine_hbm)
+
     q = q_ref[...]
-    row = pl.program_id(1) * bq + lax.broadcasted_iota(jnp.int32, (bq, tk), 0)
+    row = lax.broadcasted_iota(jnp.int32, (bq, tk), 0)
     lane = lax.broadcasted_iota(jnp.int32, (bq, tk), 1)
 
     def scores(c, top, causal):
         start = pl.multiple_of(c * tk, tk)
-        keys = k_ref[pl.ds(start, tk), :]
+        keys = k_scr[pl.ds(start, tk), :]
         s = lax.dot_general(q, keys, (((1,), (1,)), ((), ())), preferred_element_type=jnp.float32)
         s = s * scale + bias_ref[:, pl.ds(start, tk)]
         if causal:
@@ -61,17 +87,17 @@
     def weigh(c, acc):
         start = pl.multiple_of(c * tk, tk)
         w = (s_scr[:, pl.ds(start, tk)] * inverse).astype(jnp.bfloat16)
-        return acc + jnp.dot(w, v_ref[pl.ds(start, tk), :], preferred_element_type=jnp.float32)
+        return acc + jnp.dot(w, v_scr[pl.ds(start, tk), :], preferred_element_type=jnp.float32)
 
     acc = lax.fori_loop(0, total // tk, weigh, jnp.zeros((bq, head_dim), jnp.float32), unroll=2)
     o_ref[...] = acc.astype(o_ref.dtype)
 
 
-def attend(queries, keys, vals, bias, n_cache):
+def attend(queries, mine, other, new_keys, new_values, part, bias):
     rows, width = queries.shape
-    total, head_dim = keys.shape
+    n_cache, head_dim = mine.shape
+    total = n_cache + new_keys.shape[0]
     heads = width // head_dim
-    bq = rows
     tk = next(t for t in (256, 128) if total % t == 0 and n_cache % t == 0)
     scale = 1.0 / math.sqrt(head_dim)
     cost = pl.CostEstimate(
@@ -79,22 +105,34 @@
         transcendentals=rows * total * heads,
         bytes_accessed=2 * (2 * total * head_dim + 2 * rows * width) + 4 * total,
     )
+    any_spec = pl.BlockSpec(memory_space=pl.ANY)
+    grid_spec = pltpu.PrefetchScalarGridSpec(
+        num_scalar_prefetch=1,
+        grid=(heads,),
+        in_specs=[
+            pl.BlockSpec((rows, head_dim), lambda h, p: (0, h)),
+            any_spec,
+            any_spec,
+            any_spec,
+            any_spec,
+            pl.BlockSpec((1, total), lambda h, p: (0, 0)),
+        ],
+        out_specs=pl.BlockSpec((rows, head_dim), lambda h, p: (0, h)),
+        scratch_shapes=[
+            pltpu.VMEM((total, head_dim), jnp.bfloat16),
+            pltpu.VMEM((total, head_dim), jnp.bfloat16),
+            pltpu.VMEM((rows, total), jnp.float32),
+            pltpu.SemaphoreType.DMA((4,)),
+        ],
+    )
     return pl.pallas_call(
         lambda *refs: attend_kernel(n_cache, tk, scale, *refs),
         out_shape=jax.ShapeDtypeStruct((rows, width), jnp.bfloat16),
-        grid=(heads, rows // bq),
-        in_specs=[
-            pl.BlockSpec((bq, head_dim), lambda h, b: (b, h)),
-            pl.BlockSpec((total, head_dim), lambda h, b: (0, 0)),
-            pl.BlockSpec((total, head_dim), lambda h, b: (0, 0)),
-            pl.BlockSpec((1, total), lambda h, b: (0, 0)),
-        ],
-        out_specs=pl.BlockSpec((bq, head_dim), lambda h, b: (b, h)),
-        scratch_shapes=[pltpu.VMEM((bq, total), jnp.float32)],
-        compiler_params=pltpu.CompilerParams(dimension_semantics=("arbitrary", "arbitrary")),
+        grid_spec=grid_spec,
+        compiler_params=pltpu.CompilerParams(dimension_semantics=("arbitrary",)),
         cost_estimate=cost,
         name="paged_prefill_attention",
-    )(queries, keys, vals, bias)
+    )(part.reshape(1).astype(jnp.int32), queries, mine, other, new_keys, new_values, bias)
 
 
 def exchange(value, axis, mask):
@@ -149,9 +187,6 @@
     part = current_head % 2
     outgoing = kv_pool[local_page.reshape(-1), key_value_head, part]
     received = lax.all_to_all(outgoing, "dp", split_axis=0, concat_axis=0, tiled=True)
-    other_half = exchange(received, "head", 1)
-    cache_keys = jnp.where(part == 0, received, other_half).reshape(-1, HEAD_SIZE)
-    cache_vals = jnp.where(part == 0, other_half, received).reshape(-1, HEAD_SIZE)
     within = jnp.arange(page_len, dtype=jnp.int32)
     owners_mine = lax.dynamic_slice_in_dim(owner_of, me_dp * REQ_DEV, REQ_DEV, 0)
     hits = (owners_mine[None, :, :] == jnp.arange(n_dp, dtype=jnp.int32)[:, None, None]).astype(
@@ -183,15 +218,10 @@
     held_w = [w_out]
     held_ids = [current_head]
     stride = head_number // 2
-    while stride >= 1:
-        if stride != head_number // 2:
-            late, queries = lax.optimization_barrier((held_w[1:], queries))
-            held_w = held_w[:1] + list(late)
+    while stride > 1:
         held_w = held_w + [exchange(piece, "head", stride) for piece in held_w]
         held_ids = held_ids + [ident ^ stride for ident in held_ids]
         stride //= 2
-    held_w = jnp.concatenate(held_w, 0)
-    held_ids = jnp.stack(held_ids)
     own_part = projected[:, q_width:]
     holds_keys = current_head % 2 == 0
     turned = rotate(own_part[:, None, :], positions)[:, 0]
@@ -203,15 +233,26 @@
     cache_ok = (has_page[:, 0, :, None] & (key_pos[:, 0] < my_lengths[0])).reshape(-1)
     key_ok = jnp.concatenate([cache_ok, mask_rows == 1])
     bias = jnp.where(key_ok, 0.0, -jnp.inf).astype(jnp.float32)
-    keys = jnp.concatenate([cache_keys, new_keys], 0)
-    vals = jnp.concatenate([cache_vals, new_values], 0)
+    queries = queries[0:NEWTOK].reshape(NEWTOK, group_heads * head_dim)
+    received, queries, new_keys, new_values = lax.optimization_barrier(
+        (received, queries, new_keys, new_values)
+    )
+    other_half = exchange(received, "head", 1)
     pieces = attend(
-        queries[0:NEWTOK].reshape(NEWTOK, group_heads * head_dim),
-        keys,
-        vals,
+        queries,
+        received.reshape(-1, head_dim),
+        other_half.reshape(-1, head_dim),
+        new_keys,
+        new_values,
+        part,
         bias.reshape(1, -1),
-        cache_ok.shape[0],
-    )
+    )
+    late_w, pieces = lax.optimization_barrier((held_w[1:], pieces))
+    held_w = held_w[:1] + list(late_w)
+    held_w = held_w + [exchange(piece, "head", 1) for piece in held_w]
+    held_ids = held_ids + [ident ^ 1 for ident in held_ids]
+    held_w = jnp.concatenate(held_w, 0)
+    held_ids = jnp.stack(held_ids)
     gathered = lax.all_to_all(pieces, "head", split_axis=0, concat_axis=1, tiled=True)
     gathered = gathered.reshape(local_rows, head_number, group_heads * head_dim)
     ordered = jnp.take(gathered, held_ids, axis=1).reshape(local_rows, -1)

time: 175 us -> 152 us (0.87)
  waiting for transfers between devices: 61.9 us -> 45.9 us
  other arithmetic: 19.3 us -> 11.6 us
    all_to_all x1, waiting for transfers between devices: 42.7 us -> 8.66 us  [body(): lax.all_to_all(outgoing, 'dp', split_axis=0, concat_axis=0, tiled=True)]
    all_gather x1, waiting for transfers between devices: 0.02 us -> 29.3 us  [body(): piece = lax.all_gather(normalized_input, 'head', axis=0, tiled=True)]
    ppermute x4, waiting for transfers between devices: 12 us -> 0.74 us  [exchange(): return lax.ppermute(value, axis, pairs)]
    concatenate x1 -> x0, other arithmetic: 5.85 us -> none  [body(): keys = jnp.concatenate([cache_keys, new_keys], 0)]
    select_n x1 -> x0, other arithmetic: 2.5 us -> none  [body(): jnp.where(part == 0, other_half, received).reshape(-1, HEAD_SIZE)]
  transfers between devices with their start and end apart: 8 -> 8, of which waited for: 3 -> 4; matrix products, arithmetic and copies ran while one was open for 15% -> 13% of each run, Pallas kernels for 28% -> 33%
where the time goes in v5:
time: 152 us
  Pallas kernels  50.3 us (33%)
  waiting for transfers between devices  45.9 us (30%)
  between operations  13.6 us (9%)
  starting transfers between devices  12.9 us (8%)
  other arithmetic  11.6 us (8%)
  matrix products  9.74 us (6%)
  local copies, waits for them, and re-layouts  7.58 us (5%)
    pallas_call x1, Pallas kernels, attend(): pl.pallas_call(lambda *refs: attend_kernel(n_cache, tk, scale, *refs), ou...  50.3 us
    all_gather x1, waiting for transfers between devices, body(): piece = lax.all_gather(normalized_input, 'head', axis=0, tiled=True)  29.3 us
    all_to_all x1, waiting for transfers between devices, body(): lax.all_to_all(outgoing, 'dp', split_axis=0, concat_axis=0, tiled=True)  8.66 us
    all_to_all x1, starting transfers between devices, body(): lax.all_to_all(outgoing, 'dp', split_axis=0, concat_axis=0, tiled=True)  7.38 us
    all_to_all x1, waiting for transfers between devices, body(): lax.all_to_all(pieces, 'head', split_axis=0, concat_axis=1, tiled=True)  7.13 us
    dot_general x1, matrix products, body(): out = jnp.dot(ordered, held_w, preferred_element_type=jnp.float32)  5.31 us
    gather x1, local copies, waits for them, and re-layouts, body(): outgoing = kv_pool[local_page.reshape(-1), key_value_head, part]  4.99 us
    all_to_all x1, starting transfers between devices, body(): lax.all_to_all(pieces, 'head', split_axis=0, concat_axis=1, tiled=True)  3.46 us
  transfers between devices with their start and end apart: 8, of which 4 were waited for; matrix products, arithmetic and copies ran while one was open for 13% of the time, Pallas kernels for 33%

profile of v5, /device:TPU:0, one launch (start us, length us, event | category | flops | bytes accessed | tf_op | source)
XLA Modules:
  0.0 151.6 jit_solution(13334452479961722384)
XLA Ops:
  6.5 0.0 copy-start
  6.5 0.0 copy-start.3
  6.5 0.0 all-gather.2.cloned.1.call-start
  6.5 1.5 %fusion.11 = f32[128]{0:T(128)S(1)} fusion(bf16[128,3072]{1,0:T(8,128)(2,1)} %param.9), kind=kLoop, calls=%fused_computation.13 | loop fusion | flops 1179520 | bytes 786944 | tf_op jit(solution)/shard_map/reduce_sum | solution.py:203
  8.1 0.7 convert_element_type.49
  8.8 2.3 %fusion.13 = bf16[128,3072]{1,0:T(8,128)(2,1)} fusion(bf16[128,3072]{1,0:T(8,128)(2,1)} %param.9, f32[3072]{0:T(1024)S(1)} %convert_element_type.49, f32[128]{0:T(128)S(1)} %add_rsqrt_fusion), kind=kLoop, calls=%fused_computation.15 | loop fusion | flops 1572864 | bytes 1585664 | tf_op jit(solution)/shard_map/convert_element_type | solution.py:204
  11.1 0.0 all-gather.2.cloned.1.call-update
  11.1 0.0 copy-done.3
  11.2 0.2 reduce_window_sum.22
  11.4 0.2 select_reduce_fusion.1
  11.6 0.1 reshape.511
  11.7 5.0 %gather_fusion = bf16[64,128,128]{2,1,0:T(8,128)(2,1)} fusion(bf16[48,2,2,128,128]{4,3,2,1,0:T(8,128)(2,1)} %param.14, s32[64]{0:T(128)S(1)} %fusion.38), kind=kCustom, calls=%fused_computation | custom fusion | bytes 4195072 | tf_op jit(solution)/shard_map/gather | solution.py:188
  16.7 0.0 copy-start.4
  16.7 0.0 copy-start.2
  16.7 7.4 %all-to-all-start = ((bf16[64,128,128]{2,1,0:T(8,128)(2,1)}), bf16[64,128,128]{2,1,0:T(8,128)(2,1)}, u32[]{:S(2)}, u32[]{:S(2)}) async-start(bf16[64,128,128]{2,1,0:T(8,128)(2,1)} %gather_fusion), calls=%async_computation | async-start | bytes 4194304 | tf_op jit(solution)/shard_map/all_to_all | solution.py:189
  24.1 1.5 %collective-permute-start = (bf16[384,3072]{1,0:T(8,128)(2,1)}, bf16[384,3072]{1,0:T(8,128)(2,1)}, u32[]{:S(2)}, u32[]{:S(2)}) collective-permute-start(bf16[384,3072]{1,0:T(8,128)(2,1)} %param.13), channel_id=1, source_target_pairs={{0,2},{1,3},{2,0},{3,1},{4,6},{5,7},{6,4},{7,5},{8,10},{9,11},{10,... | collective-permute-start | bytes 7077896 | tf_op jit(solution)/shard_map/ppermute | solution.py:140
  25.6 0.0 collective-permute-start.3
  25.6 0.0 copy-done.4
  25.6 0.6 dynamic_slice.11
  26.2 0.6 fusion.30
  26.8 0.5 multiply_cosine_fusion.1
  27.4 29.3 %all-gather.2.cloned.1.call-done = bf16[512,3072]{1,0:T(8,128)(2,1)} async-done(((bf16[128,3072]{1,0:T(8,128)(2,1)}), bf16[512,3072]{1,0:T(8,128)(2,1)}) %all-gather.2.cloned.1.call-update) | async-done | bytes 3145744 | tf_op jit(solution)/shard_map/all_gather | solution.py:207
  56.7 0.0 copy-done.2
  56.7 0.0 copy-start.1
  56.7 3.0 %fusion.43 = f32[512,128]{1,0:T(8,128)S(1)} fusion(bf16[512,3072]{1,0:T(8,128)(2,1)} %all-gather.2.cloned.1.call-done, bf16[3072,128]{1,0:T(8,128)(2,1)S(1)} %copy-done.2), kind=kOutput, calls=%fused_computation.83 | convolution fusion | flops 402653184 | bytes 4194304 | tf_op jit(solution)/shard_map/dot_general | solution.py:209
  59.7 1.2 fusion.18
  61.0 0.1 fusion.21
  61.1 0.3 collective-permute-start.1
  61.4 0.0 copy-done
  61.4 0.0 copy-done.1
  61.4 1.4 fusion.42
  62.8 0.1 subtract_convert_fusion
  63.0 0.0 collective-permute-done.1
  63.0 0.7 broadcast_select_fusion
  63.8 8.7 %all-to-all-done = bf16[64,128,128]{2,1,0:T(8,128)(2,1)} async-done(((bf16[64,128,128]{2,1,0:T(8,128)(2,1)}), bf16[64,128,128]{2,1,0:T(8,128)(2,1)}, u32[]{:S(2)}, u32[]{:S(2)}) %all-to-all-start) | async-done | bytes 2097184 | tf_op jit(solution)/shard_map/all_to_all | solution.py:189
  72.4 0.0 collective-permute-start.2
  72.4 0.2 reduce_window_sum.23
  72.7 0.8 dynamic-slice_compare_fusion
  73.4 0.2 fusion.24
  73.6 0.2 select_reduce_fusion
  73.9 0.7 fusion.25
  74.6 0.7 add_select_fusion.refs_6_
  75.3 0.9 copy.23.refs_1_
  76.2 0.7 collective-permute-done.2
  76.9 50.3 %paged_prefill_attention.1 = bf16[512,384]{1,0:T(8,128)(2,1)} custom-call(s32[1]{0:T(128)} %bitcast.4.refs_0_, bf16[512,384]{1,0:T(8,128)(2,1)} %copy.23.refs_1_, bf16[8192,128]{1,0:T(8,128)(2,1)} %bitcast.11.refs_2_, bf16[8192,128]{1,0:T(8,128)(2,1)} %bitcast.12.refs_3_, bf16[512,128]{1,0:T(8,128)(2,1)} %get-tuple-element.13.refs_4_, ...), custom_call_target="tpu_custom_call" | custom-call | flops 6845104128 | bytes 5277696 | tf_op jit(solution)/shard_map/paged_prefill_attention/pallas_call | solution.py:128
  127.2 0.0 collective-permute-done
  127.2 0.2 collective-permute-start.4
  127.4 3.5 %all-to-all-start.1 = ((bf16[4,128,384]{2,1,0:T(8,128)(2,1)}), bf16[4,128,384]{2,1,0:T(8,128)(2,1)S(1)}, u32[]{:S(2)}, u32[]{:S(2)}) async-start(bf16[4,128,384]{2,1,0:T(8,128)(2,1)} %bitcast.42), calls=%async_computation.1 | async-start | bytes 786432 | tf_op jit(solution)/shard_map/all_to_all | solution.py:256
  130.9 0.1 compare_and_fusion
  131.0 0.1 broadcast_in_dim.51
  131.1 0.1 fusion.39
  131.2 7.1 %all-to-all-done.1 = bf16[4,128,384]{2,1,0:T(8,128)(2,1)S(1)} async-done(((bf16[4,128,384]{2,1,0:T(8,128)(2,1)}), bf16[4,128,384]{2,1,0:T(8,128)(2,1)S(1)}, u32[]{:S(2)}, u32[]{:S(2)}) %all-to-all-start.1) | async-done | bytes 393248 | tf_op jit(solution)/shard_map/all_to_all | solution.py:256
  138.3 0.6 gather_fusion.1
  138.9 0.2 copy.24
  139.2 0.3 bitcast_select_fusion
  139.5 0.0 collective-permute-done.3
  139.5 0.0 collective-permute-done.4
  139.5 5.3 %fusion.8 = bf16[128,3072]{1,0:T(8,128)(2,1)} fusion(bf16[128,1536]{0,1:T(8,128)(2,1)S(1)} %bitcast_select_fusion, bf16[384,3072]{1,0:T(8,128)(2,1)} %collective-permute-done.4, bf16[384,3072]{1,0:T(8,128)(2,1)} %collective-permute-done.3, bf16[384,3072]{1,0:T(8,128)(2,1)} %collective-permute-done, bf16[384,3072]{1,0:T(8,128)(2,1)} %param.13), kind=kOutput, calls=%fused_computation.10 | convolution fusion | flops 1246101504 | bytes 10616832 | tf_op jit(solution)/shard_map/dot_general | solution.py:259
  (15 shorter events, 0.2 us)
Async XLA Ops:
  6.5 54.9 %copy-start = (bf16[3072,384]{1,0:T(8,128)(2,1)S(1)}, bf16[3072,384]{1,0:T(8,128)(2,1)}, u32[]{:S(2)}) copy-start(bf16[3072,384]{1,0:T(8,128)(2,1)} %param.11) | copy-start | bytes 7077892
  6.5 4.6 %copy-start.3 = (s32[8,64]{1,0:T(8,128)S(1)}, s32[8,64]{1,0:T(8,128)}, u32[]{:S(2)}) copy-start(s32[8,64]{1,0:T(8,128)} %param.16) | copy-start | bytes 6148
  6.5 50.2 %all-gather.2.cloned.1.call-start = ((), (), s32[]{:S(2)}) async-start(), calls=%async_computation.2 | async-start | bytes 3932160 | tf_op jit(solution)/shard_map/all_gather | solution.py:207
  16.7 8.9 %copy-start.4 = (s32[8]{0:T(128)S(1)}, s32[8]{0:T(128)}, u32[]{:S(2)}) copy-start(s32[8]{0:T(128)} %param.15) | copy-start | bytes 100
  16.7 40.0 %copy-start.2 = (bf16[3072,128]{1,0:T(8,128)(2,1)S(1)}, bf16[3072,128]{1,0:T(8,128)(2,1)}, u32[]{:S(2)}) copy-start(bf16[3072,128]{1,0:T(8,128)(2,1)} %param.12) | copy-start | bytes 2359300
  16.7 55.7 %all-to-all-start = ((bf16[64,128,128]{2,1,0:T(8,128)(2,1)}), bf16[64,128,128]{2,1,0:T(8,128)(2,1)}, u32[]{:S(2)}, u32[]{:S(2)}) async-start(bf16[64,128,128]{2,1,0:T(8,128)(2,1)} %gather_fusion), calls=%async_computation | async-start | bytes 4194304 | tf_op jit(solution)/shard_map/all_to_all | solution.py:189
  24.1 103.2 %collective-permute-start = (bf16[384,3072]{1,0:T(8,128)(2,1)}, bf16[384,3072]{1,0:T(8,128)(2,1)}, u32[]{:S(2)}, u32[]{:S(2)}) collective-permute-start(bf16[384,3072]{1,0:T(8,128)(2,1)} %param.13), channel_id=1, source_target_pairs={{0,2},{1,3},{2,0},{3,1},{4,6},{5,7},{6,4},{7,5},{8,10},{9,11},{10,... | collective-permute-start | bytes 7077896 | tf_op jit(solution)/shard_map/ppermute | solution.py:140
  25.6 113.9 %collective-permute-start.3 = (bf16[384,3072]{1,0:T(8,128)(2,1)}, bf16[384,3072]{1,0:T(8,128)(2,1)}, u32[]{:S(2)}, u32[]{:S(2)}) collective-permute-start(bf16[384,3072]{1,0:T(8,128)(2,1)} %param.13), channel_id=1, source_target_pairs={{0,1},{1,0},{2,3},{3,2},{4,5},{5,4},{6,7},{7,6},{8,9},{9,8},{10,11... | collective-permute-start | bytes 7077896 | tf_op jit(solution)/shard_map/ppermute | solution.py:140
  56.7 4.7 %copy-start.1 = (bf16[512,3072]{1,0:T(8,128)(2,1)S(1)}, bf16[512,3072]{1,0:T(8,128)(2,1)}, u32[]{:S(2)}) copy-start(bf16[512,3072]{1,0:T(8,128)(2,1)} %all-gather.2.cloned.1.call-done) | copy-start | bytes 9437188
  61.1 1.9 %collective-permute-start.1 = (bf16[512,128]{1,0:T(8,128)(2,1)S(1)}, bf16[512,128]{1,0:T(8,128)(2,1)S(1)}, u32[]{:S(2)}, u32[]{:S(2)}) collective-permute-start(bf16[512,128]{1,0:T(8,128)(2,1)S(1)} %fusion.21), channel_id=1, source_target_pairs={{0,1},{1,0},{2,3},{3,2},{4,5},{5,4},{6,7},{7,6},{8,9},{9,8},{10,11... | collective-permute-start | bytes 393224 | tf_op jit(solution)/shard_map/ppermute | solution.py:22
  72.4 4.5 %collective-permute-start.2 = (bf16[64,128,128]{2,1,0:T(8,128)(2,1)}, bf16[64,128,128]{2,1,0:T(8,128)(2,1)}, u32[]{:S(2)}, u32[]{:S(2)}) collective-permute-start(bf16[64,128,128]{2,1,0:T(8,128)(2,1)} %all-to-all-done), channel_id=1, source_target_pairs={{0,1},{1,0},{2,3},{3,2},{4,5},{5,4},{6,7},{7,6},{8,9},{9,8},{10,11... | collective-permute-start | bytes 6291464 | tf_op jit(solution)/shard_map/ppermute | solution.py:140
  127.2 12.2 %collective-permute-start.4 = (bf16[384,3072]{1,0:T(8,128)(2,1)}, bf16[384,3072]{1,0:T(8,128)(2,1)}, u32[]{:S(2)}, u32[]{:S(2)}) collective-permute-start(bf16[384,3072]{1,0:T(8,128)(2,1)} %collective-permute-done), channel_id=1, source_target_pairs={{0,1},{1,0},{2,3},{3,2},{4,5},{5,4},{6,7},{7,6},{8,9},{9,8},{10,11... | collective-permute-start | bytes 7077896 | tf_op jit(solution)/shard_map/ppermute | solution.py:140
  127.4 10.9 %all-to-all-start.1 = ((bf16[4,128,384]{2,1,0:T(8,128)(2,1)}), bf16[4,128,384]{2,1,0:T(8,128)(2,1)S(1)}, u32[]{:S(2)}, u32[]{:S(2)}) async-start(bf16[4,128,384]{2,1,0:T(8,128)(2,1)} %bitcast.42), calls=%async_computation.1 | async-start | bytes 786432 | tf_op jit(solution)/shard_map/all_to_all | solution.py:256
Sparse Core Ops, SparseCore 0:
  11.2 45.4 all-gather.1

commit v6 on v5

--- a/solution.py
+++ b/solution.py
@@ -69,7 +69,7 @@
         return top
 
     top = jnp.full((bq, 128), -jnp.inf, jnp.float32)
-    top = lax.fori_loop(0, n_cache // tk, lambda c, t: scores(c, t, False), top, unroll=2)
+    top = lax.fori_loop(0, n_cache // tk, lambda c, t: scores(c, t, False), top, unroll=8)
     top = lax.fori_loop(n_cache // tk, total // tk, lambda c, t: scores(c, t, True), top)
     top = jnp.max(top, -1, keepdims=True)
 
@@ -81,7 +81,7 @@
             part = part + e[:, g * 128:(g + 1) * 128]
         return part
 
-    part = lax.fori_loop(0, total // tk, expo, jnp.zeros((bq, 128), jnp.float32), unroll=2)
+    part = lax.fori_loop(0, total // tk, expo, jnp.zeros((bq, 128), jnp.float32), unroll=8)
     inverse = 1.0 / jnp.sum(part, -1, keepdims=True)
 
     def weigh(c, acc):
@@ -89,7 +89,7 @@
         w = (s_scr[:, pl.ds(start, tk)] * inverse).astype(jnp.bfloat16)
         return acc + jnp.dot(w, v_scr[pl.ds(start, tk), :], preferred_element_type=jnp.float32)
 
-    acc = lax.fori_loop(0, total // tk, weigh, jnp.zeros((bq, head_dim), jnp.float32), unroll=2)
+    acc = lax.fori_loop(0, total // tk, weigh, jnp.zeros((bq, head_dim), jnp.float32), unroll=8)
     o_ref[...] = acc.astype(o_ref.dtype)
 
 
@@ -98,7 +98,7 @@
     n_cache, head_dim = mine.shape
     total = n_cache + new_keys.shape[0]
     heads = width // head_dim
-    tk = next(t for t in (256, 128) if total % t == 0 and n_cache % t == 0)
+    tk = next(t for t in (512, 256, 128) if total % t == 0 and n_cache % t == 0)
     scale = 1.0 / math.sqrt(head_dim)
     cost = pl.CostEstimate(
         flops=4 * rows * total * head_dim * heads,

time: 152 us -> 132 us (0.87)
  Pallas kernels: 50.3 us -> 30.7 us
    pallas_call x1, Pallas kernels: 50.3 us -> 30.7 us  [attend(): pl.pallas_call(lambda *refs: attend_kernel(n_cache, tk, scale, *refs), ou...]
  transfers between devices with their start and end apart: 8 -> 8, of which waited for: 4 -> 4; matrix products, arithmetic and copies ran while one was open for 13% -> 14% of each run, Pallas kernels for 33% -> 23%
where the time goes in v6:
time: 132 us
  waiting for transfers between devices  45.9 us (35%)
  Pallas kernels  30.7 us (23%)
  between operations  13.6 us (10%)
  starting transfers between devices  12.9 us (10%)
  other arithmetic  11.6 us (9%)
  matrix products  9.74 us (7%)
  local copies, waits for them, and re-layouts  7.58 us (6%)
    pallas_call x1, Pallas kernels, attend(): pl.pallas_call(lambda *refs: attend_kernel(n_cache, tk, scale, *refs), ou...  30.7 us
    all_gather x1, waiting for transfers between devices, body(): piece = lax.all_gather(normalized_input, 'head', axis=0, tiled=True)  29.3 us
    all_to_all x1, waiting for transfers between devices, body(): lax.all_to_all(outgoing, 'dp', split_axis=0, concat_axis=0, tiled=True)  8.66 us
    all_to_all x1, starting transfers between devices, body(): lax.all_to_all(outgoing, 'dp', split_axis=0, concat_axis=0, tiled=True)  7.38 us
    all_to_all x1, waiting for transfers between devices, body(): lax.all_to_all(pieces, 'head', split_axis=0, concat_axis=1, tiled=True)  7.13 us
    dot_general x1, matrix products, body(): out = jnp.dot(ordered, held_w, preferred_element_type=jnp.float32)  5.31 us
    gather x1, local copies, waits for them, and re-layouts, body(): outgoing = kv_pool[local_page.reshape(-1), key_value_head, part]  4.99 us
    all_to_all x1, starting transfers between devices, body(): lax.all_to_all(pieces, 'head', split_axis=0, concat_axis=1, tiled=True)  3.46 us
  transfers between devices with their start and end apart: 8, of which 4 were waited for; matrix products, arithmetic and copies ran while one was open for 14% of the time, Pallas kernels for 23%

profile of v6, /device:TPU:0, one launch (start us, length us, event | category | flops | bytes accessed | tf_op | source)
XLA Modules:
  0.0 132.1 jit_solution(1485422890706920430)
XLA Ops:
  6.5 0.0 copy-start
  6.5 0.0 copy-start.3
  6.5 0.0 all-gather.2.cloned.1.call-start
  6.5 1.5 %fusion.11 = f32[128]{0:T(128)S(1)} fusion(bf16[128,3072]{1,0:T(8,128)(2,1)} %param.9), kind=kLoop, calls=%fused_computation.13 | loop fusion | flops 1179520 | bytes 786944 | tf_op jit(solution)/shard_map/reduce_sum | solution.py:203
  8.1 0.7 convert_element_type.49
  8.8 2.3 %fusion.13 = bf16[128,3072]{1,0:T(8,128)(2,1)} fusion(bf16[128,3072]{1,0:T(8,128)(2,1)} %param.9, f32[3072]{0:T(1024)S(1)} %convert_element_type.49, f32[128]{0:T(128)S(1)} %add_rsqrt_fusion), kind=kLoop, calls=%fused_computation.15 | loop fusion | flops 1572864 | bytes 1585664 | tf_op jit(solution)/shard_map/convert_element_type | solution.py:204
  11.1 0.0 all-gather.2.cloned.1.call-update
  11.1 0.0 copy-done.3
  11.2 0.2 reduce_window_sum.22
  11.4 0.2 select_reduce_fusion.1
  11.6 0.1 reshape.511
  11.7 5.0 %gather_fusion = bf16[64,128,128]{2,1,0:T(8,128)(2,1)} fusion(bf16[48,2,2,128,128]{4,3,2,1,0:T(8,128)(2,1)} %param.14, s32[64]{0:T(128)S(1)} %fusion.38), kind=kCustom, calls=%fused_computation | custom fusion | bytes 4195072 | tf_op jit(solution)/shard_map/gather | solution.py:188
  16.7 0.0 copy-start.4
  16.7 0.0 copy-start.2
  16.7 7.4 %all-to-all-start = ((bf16[64,128,128]{2,1,0:T(8,128)(2,1)}), bf16[64,128,128]{2,1,0:T(8,128)(2,1)}, u32[]{:S(2)}, u32[]{:S(2)}) async-start(bf16[64,128,128]{2,1,0:T(8,128)(2,1)} %gather_fusion), calls=%async_computation | async-start | bytes 4194304 | tf_op jit(solution)/shard_map/all_to_all | solution.py:189
  24.1 1.5 %collective-permute-start = (bf16[384,3072]{1,0:T(8,128)(2,1)}, bf16[384,3072]{1,0:T(8,128)(2,1)}, u32[]{:S(2)}, u32[]{:S(2)}) collective-permute-start(bf16[384,3072]{1,0:T(8,128)(2,1)} %param.13), channel_id=1, source_target_pairs={{0,2},{1,3},{2,0},{3,1},{4,6},{5,7},{6,4},{7,5},{8,10},{9,11},{10,... | collective-permute-start | bytes 7077896 | tf_op jit(solution)/shard_map/ppermute | solution.py:140
  25.6 0.0 collective-permute-start.3
  25.6 0.0 copy-done.4
  25.6 0.6 dynamic_slice.11
  26.2 0.6 fusion.30
  26.8 0.5 multiply_cosine_fusion.1
  27.4 29.3 %all-gather.2.cloned.1.call-done = bf16[512,3072]{1,0:T(8,128)(2,1)} async-done(((bf16[128,3072]{1,0:T(8,128)(2,1)}), bf16[512,3072]{1,0:T(8,128)(2,1)}) %all-gather.2.cloned.1.call-update) | async-done | bytes 3145744 | tf_op jit(solution)/shard_map/all_gather | solution.py:207
  56.7 0.0 copy-done.2
  56.7 0.0 copy-start.1
  56.7 3.0 %fusion.43 = f32[512,128]{1,0:T(8,128)S(1)} fusion(bf16[512,3072]{1,0:T(8,128)(2,1)} %all-gather.2.cloned.1.call-done, bf16[3072,128]{1,0:T(8,128)(2,1)S(1)} %copy-done.2), kind=kOutput, calls=%fused_computation.83 | convolution fusion | flops 402653184 | bytes 4194304 | tf_op jit(solution)/shard_map/dot_general | solution.py:209
  59.7 1.2 fusion.18
  61.0 0.1 fusion.21
  61.1 0.3 collective-permute-start.1
  61.4 0.0 copy-done
  61.4 0.0 copy-done.1
  61.4 1.4 %fusion.42 = f32[512,384]{0,1:T(8,128)S(1)} fusion(bf16[512,3072]{1,0:T(8,128)(2,1)S(1)} %copy-done.1, bf16[3072,384]{1,0:T(8,128)(2,1)S(1)} %copy-done), kind=kOutput, calls=%fused_computation.82 | convolution fusion | flops 1207959552 | bytes 6291456 | tf_op jit(solution)/shard_map/dot_general | solution.py:208
  62.8 0.1 subtract_convert_fusion
  63.0 0.0 collective-permute-done.1
  63.0 0.7 broadcast_select_fusion
  63.8 8.7 %all-to-all-done = bf16[64,128,128]{2,1,0:T(8,128)(2,1)} async-done(((bf16[64,128,128]{2,1,0:T(8,128)(2,1)}), bf16[64,128,128]{2,1,0:T(8,128)(2,1)}, u32[]{:S(2)}, u32[]{:S(2)}) %all-to-all-start) | async-done | bytes 2097184 | tf_op jit(solution)/shard_map/all_to_all | solution.py:189
  72.4 0.0 collective-permute-start.2
  72.4 0.2 reduce_window_sum.23
  72.7 0.8 dynamic-slice_compare_fusion
  73.4 0.2 fusion.24
  73.6 0.2 select_reduce_fusion
  73.9 0.7 fusion.25
  74.6 0.7 add_select_fusion.refs_6_
  75.3 0.9 copy.23.refs_1_
  76.2 0.7 collective-permute-done.2
  76.9 30.7 %paged_prefill_attention.1 = bf16[512,384]{1,0:T(8,128)(2,1)} custom-call(s32[1]{0:T(128)} %bitcast.4.refs_0_, bf16[512,384]{1,0:T(8,128)(2,1)} %copy.23.refs_1_, bf16[8192,128]{1,0:T(8,128)(2,1)} %bitcast.11.refs_2_, bf16[8192,128]{1,0:T(8,128)(2,1)} %bitcast.12.refs_3_, bf16[512,128]{1,0:T(8,128)(2,1)} %get-tuple-element.13.refs_4_, ...), custom_call_target="tpu_custom_call" | custom-call | flops 6845104128 | bytes 5277696 | tf_op jit(solution)/shard_map/paged_prefill_attention/pallas_call | solution.py:128
  107.6 0.0 collective-permute-done
  107.7 0.2 collective-permute-start.4
  107.9 3.5 %all-to-all-start.1 = ((bf16[4,128,384]{2,1,0:T(8,128)(2,1)}), bf16[4,128,384]{2,1,0:T(8,128)(2,1)S(1)}, u32[]{:S(2)}, u32[]{:S(2)}) async-start(bf16[4,128,384]{2,1,0:T(8,128)(2,1)} %bitcast.42), calls=%async_computation.1 | async-start | bytes 786432 | tf_op jit(solution)/shard_map/all_to_all | solution.py:256
  111.3 0.1 compare_and_fusion
  111.4 0.1 broadcast_in_dim.51
  111.5 0.1 fusion.39
  111.6 7.1 %all-to-all-done.1 = bf16[4,128,384]{2,1,0:T(8,128)(2,1)S(1)} async-done(((bf16[4,128,384]{2,1,0:T(8,128)(2,1)}), bf16[4,128,384]{2,1,0:T(8,128)(2,1)S(1)}, u32[]{:S(2)}, u32[]{:S(2)}) %all-to-all-start.1) | async-done | bytes 393248 | tf_op jit(solution)/shard_map/all_to_all | solution.py:256
  118.7 0.6 gather_fusion.1
  119.4 0.2 copy.24
  119.6 0.3 bitcast_select_fusion
  119.9 0.0 collective-permute-done.3
  119.9 0.0 collective-permute-done.4
  119.9 5.3 %fusion.8 = bf16[128,3072]{1,0:T(8,128)(2,1)} fusion(bf16[128,1536]{0,1:T(8,128)(2,1)S(1)} %bitcast_select_fusion, bf16[384,3072]{1,0:T(8,128)(2,1)} %collective-permute-done.4, bf16[384,3072]{1,0:T(8,128)(2,1)} %collective-permute-done.3, bf16[384,3072]{1,0:T(8,128)(2,1)} %collective-permute-done, bf16[384,3072]{1,0:T(8,128)(2,1)} %param.13), kind=kOutput, calls=%fused_computation.10 | convolution fusion | flops 1246101504 | bytes 10616832 | tf_op jit(solution)/shard_map/dot_general | solution.py:259
  (15 shorter events, 0.2 us)
Async XLA Ops:
  6.5 54.9 %copy-start = (bf16[3072,384]{1,0:T(8,128)(2,1)S(1)}, bf16[3072,384]{1,0:T(8,128)(2,1)}, u32[]{:S(2)}) copy-start(bf16[3072,384]{1,0:T(8,128)(2,1)} %param.11) | copy-start | bytes 7077892
  6.5 4.6 %copy-start.3 = (s32[8,64]{1,0:T(8,128)S(1)}, s32[8,64]{1,0:T(8,128)}, u32[]{:S(2)}) copy-start(s32[8,64]{1,0:T(8,128)} %param.16) | copy-start | bytes 6148
  6.5 50.2 %all-gather.2.cloned.1.call-start = ((), (), s32[]{:S(2)}) async-start(), calls=%async_computation.2 | async-start | bytes 3932160 | tf_op jit(solution)/shard_map/all_gather | solution.py:207
  16.7 8.9 %copy-start.4 = (s32[8]{0:T(128)S(1)}, s32[8]{0:T(128)}, u32[]{:S(2)}) copy-start(s32[8]{0:T(128)} %param.15) | copy-start | bytes 100
  16.7 40.0 %copy-start.2 = (bf16[3072,128]{1,0:T(8,128)(2,1)S(1)}, bf16[3072,128]{1,0:T(8,128)(2,1)}, u32[]{:S(2)}) copy-start(bf16[3072,128]{1,0:T(8,128)(2,1)} %param.12) | copy-start | bytes 2359300
  16.7 55.7 %all-to-all-start = ((bf16[64,128,128]{2,1,0:T(8,128)(2,1)}), bf16[64,128,128]{2,1,0:T(8,128)(2,1)}, u32[]{:S(2)}, u32[]{:S(2)}) async-start(bf16[64,128,128]{2,1,0:T(8,128)(2,1)} %gather_fusion), calls=%async_computation | async-start | bytes 4194304 | tf_op jit(solution)/shard_map/all_to_all | solution.py:189
  24.1 83.6 %collective-permute-start = (bf16[384,3072]{1,0:T(8,128)(2,1)}, bf16[384,3072]{1,0:T(8,128)(2,1)}, u32[]{:S(2)}, u32[]{:S(2)}) collective-permute-start(bf16[384,3072]{1,0:T(8,128)(2,1)} %param.13), channel_id=1, source_target_pairs={{0,2},{1,3},{2,0},{3,1},{4,6},{5,7},{6,4},{7,5},{8,10},{9,11},{10,... | collective-permute-start | bytes 7077896 | tf_op jit(solution)/shard_map/ppermute | solution.py:140
  25.6 94.3 %collective-permute-start.3 = (bf16[384,3072]{1,0:T(8,128)(2,1)}, bf16[384,3072]{1,0:T(8,128)(2,1)}, u32[]{:S(2)}, u32[]{:S(2)}) collective-permute-start(bf16[384,3072]{1,0:T(8,128)(2,1)} %param.13), channel_id=1, source_target_pairs={{0,1},{1,0},{2,3},{3,2},{4,5},{5,4},{6,7},{7,6},{8,9},{9,8},{10,11... | collective-permute-start | bytes 7077896 | tf_op jit(solution)/shard_map/ppermute | solution.py:140
  56.7 4.7 %copy-start.1 = (bf16[512,3072]{1,0:T(8,128)(2,1)S(1)}, bf16[512,3072]{1,0:T(8,128)(2,1)}, u32[]{:S(2)}) copy-start(bf16[512,3072]{1,0:T(8,128)(2,1)} %all-gather.2.cloned.1.call-done) | copy-start | bytes 9437188
  61.1 1.9 %collective-permute-start.1 = (bf16[512,128]{1,0:T(8,128)(2,1)S(1)}, bf16[512,128]{1,0:T(8,128)(2,1)S(1)}, u32[]{:S(2)}, u32[]{:S(2)}) collective-permute-start(bf16[512,128]{1,0:T(8,128)(2,1)S(1)} %fusion.21), channel_id=1, source_target_pairs={{0,1},{1,0},{2,3},{3,2},{4,5},{5,4},{6,7},{7,6},{8,9},{9,8},{10,11... | collective-permute-start | bytes 393224 | tf_op jit(solution)/shard_map/ppermute | solution.py:22
  72.4 4.5 %collective-permute-start.2 = (bf16[64,128,128]{2,1,0:T(8,128)(2,1)}, bf16[64,128,128]{2,1,0:T(8,128)(2,1)}, u32[]{:S(2)}, u32[]{:S(2)}) collective-permute-start(bf16[64,128,128]{2,1,0:T(8,128)(2,1)} %all-to-all-done), channel_id=1, source_target_pairs={{0,1},{1,0},{2,3},{3,2},{4,5},{5,4},{6,7},{7,6},{8,9},{9,8},{10,11... | collective-permute-start | bytes 6291464 | tf_op jit(solution)/shard_map/ppermute | solution.py:140
  107.7 12.2 %collective-permute-start.4 = (bf16[384,3072]{1,0:T(8,128)(2,1)}, bf16[384,3072]{1,0:T(8,128)(2,1)}, u32[]{:S(2)}, u32[]{:S(2)}) collective-permute-start(bf16[384,3072]{1,0:T(8,128)(2,1)} %collective-permute-done), channel_id=1, source_target_pairs={{0,1},{1,0},{2,3},{3,2},{4,5},{5,4},{6,7},{7,6},{8,9},{9,8},{10,11... | collective-permute-start | bytes 7077896 | tf_op jit(solution)/shard_map/ppermute | solution.py:140
  107.9 10.9 %all-to-all-start.1 = ((bf16[4,128,384]{2,1,0:T(8,128)(2,1)}), bf16[4,128,384]{2,1,0:T(8,128)(2,1)S(1)}, u32[]{:S(2)}, u32[]{:S(2)}) async-start(bf16[4,128,384]{2,1,0:T(8,128)(2,1)} %bitcast.42), calls=%async_computation.1 | async-start | bytes 786432 | tf_op jit(solution)/shard_map/all_to_all | solution.py:256
Sparse Core Ops, SparseCore 0:
  11.2 45.4 all-gather.1

commit v7 on v6

--- a/solution.py
+++ b/solution.py
@@ -186,6 +186,7 @@
     present = jnp.any(select, -1).reshape(-1)
     part = current_head % 2
     outgoing = kv_pool[local_page.reshape(-1), key_value_head, part]
+    outgoing, tokens = lax.optimization_barrier((outgoing, tokens))
     received = lax.all_to_all(outgoing, "dp", split_axis=0, concat_axis=0, tiled=True)
     within = jnp.arange(page_len, dtype=jnp.int32)
     owners_mine = lax.dynamic_slice_in_dim(owner_of, me_dp * REQ_DEV, REQ_DEV, 0)
@@ -205,6 +206,14 @@
         jnp.bfloat16
     )
     piece = lax.all_gather(normalized_input, "head", axis=0, tiled=True)
+    w_late, piece = lax.optimization_barrier((w_out, piece))
+    held_w = [w_out]
+    masks = [0]
+    stride = head_number // 2
+    while stride > 1:
+        held_w = held_w + [exchange(w_late if i == 0 else p, "head", stride) for i, p in enumerate(held_w)]
+        masks = masks + [m ^ stride for m in masks]
+        stride //= 2
     q_part = jnp.dot(piece, w_query, preferred_element_type=jnp.float32)
     kv_part = jnp.dot(piece, key_value_weight, preferred_element_type=jnp.float32)
     projected = jnp.concatenate([q_part, kv_part], 1)
@@ -215,13 +224,6 @@
     queries = rotate(
         projected[:, :q_width].reshape(block_rows, group_heads, head_dim), positions
     ).astype(jnp.bfloat16)
-    held_w = [w_out]
-    held_ids = [current_head]
-    stride = head_number // 2
-    while stride > 1:
-        held_w = held_w + [exchange(piece, "head", stride) for piece in held_w]
-        held_ids = held_ids + [ident ^ stride for ident in held_ids]
-        stride //= 2
     own_part = projected[:, q_width:]
     holds_keys = current_head % 2 == 0
     turned = rotate(own_part[:, None, :], positions)[:, 0]
@@ -250,12 +252,13 @@
     late_w, pieces = lax.optimization_barrier((held_w[1:], pieces))
     held_w = held_w[:1] + list(late_w)
     held_w = held_w + [exchange(piece, "head", 1) for piece in held_w]
-    held_ids = held_ids + [ident ^ 1 for ident in held_ids]
+    masks = masks + [m ^ 1 for m in masks]
     held_w = jnp.concatenate(held_w, 0)
-    held_ids = jnp.stack(held_ids)
-    gathered = lax.all_to_all(pieces, "head", split_axis=0, concat_axis=1, tiled=True)
-    gathered = gathered.reshape(local_rows, head_number, group_heads * head_dim)
-    ordered = jnp.take(gathered, held_ids, axis=1).reshape(local_rows, -1)
+    columns = []
+    for m in masks:
+        block = lax.dynamic_slice_in_dim(pieces, (current_head ^ m) * local_rows, local_rows, 0)
+        columns.append(block if m == 0 else exchange(block, "head", m))
+    ordered = jnp.concatenate(columns, 1)
     out = jnp.dot(ordered, held_w, preferred_element_type=jnp.float32)
     return out.astype(jnp.bfloat16)
 

time: 132 us -> 147 us (1.11)
  waiting for transfers between devices: 45.9 us -> 62.7 us
    ppermute x4 -> x7, waiting for transfers between devices: 0.74 us -> 23.2 us  [exchange(): return lax.ppermute(value, axis, pairs)]
    all_to_all x1, waiting for transfers between devices: 8.66 us -> 17.3 us  [body(): lax.all_to_all(outgoing, 'dp', split_axis=0, concat_axis=0, tiled=True)]
    all_gather x1, waiting for transfers between devices: 29.3 us -> 22.1 us  [body(): piece = lax.all_gather(normalized_input, 'head', axis=0, tiled=True)]
    all_to_all x1 -> x0, waiting for transfers between devices: 7.13 us -> none  [body(): lax.all_to_all(pieces, 'head', split_axis=0, concat_axis=1, tiled=True)]
    all_to_all x1 -> x0, starting transfers between devices: 3.46 us -> none  [body(): lax.all_to_all(pieces, 'head', split_axis=0, concat_axis=1, tiled=True)]
    ppermute x4 -> x7, starting transfers between devices: 1.73 us -> 3.74 us  [exchange(): return lax.ppermute(value, axis, pairs)]
  transfers between devices with their start and end apart: 8 -> 10, of which waited for: 4 -> 5; matrix products, arithmetic and copies ran while one was open for 14% -> 9% of each run, Pallas kernels for 23% -> 21%
where the time goes in v7:
time: 147 us; the launch traced here: 146 us
  waiting for transfers between devices  62.7 us (43%)
  Pallas kernels  30.7 us (21%)
  between operations  13.5 us (9%)
  starting transfers between devices  11.5 us (8%)
  other arithmetic  10.3 us (7%)
  matrix products  9.71 us (7%)
  local copies, waits for them, and re-layouts  7.81 us (5%)
    pallas_call x1, Pallas kernels, attend(): pl.pallas_call(lambda *refs: attend_kernel(n_cache, tk, scale, *refs), ou...  30.7 us
    ppermute x7, waiting for transfers between devices, exchange(): return lax.ppermute(value, axis, pairs)  23.2 us
    all_gather x1, waiting for transfers between devices, body(): piece = lax.all_gather(normalized_input, 'head', axis=0, tiled=True)  22.1 us
    all_to_all x1, waiting for transfers between devices, body(): lax.all_to_all(outgoing, 'dp', split_axis=0, concat_axis=0, tiled=True)  17.3 us
    all_to_all x1, starting transfers between devices, body(): lax.all_to_all(outgoing, 'dp', split_axis=0, concat_axis=0, tiled=True)  7.4 us
    dot_general x1, matrix products, body(): out = jnp.dot(ordered, held_w, preferred_element_type=jnp.float32)  5.27 us
    gather x1, local copies, waits for them, and re-layouts, body(): outgoing = kv_pool[local_page.reshape(-1), key_value_head, part]  5.05 us
    ppermute x7, starting transfers between devices, exchange(): return lax.ppermute(value, axis, pairs)  3.74 us
  transfers between devices with their start and end apart: 10, of which 5 were waited for; matrix products, arithmetic and copies ran while one was open for 9% of the time, Pallas kernels for 21%

profile of v7, /device:TPU:0, one launch (start us, length us, event | category | flops | bytes accessed | tf_op | source)
XLA Modules:
  0.0 146.2 jit_solution(8781679490249165915)
XLA Ops:
  6.5 0.0 copy-start
  6.5 0.0 copy-start.1
  6.5 0.0 all-gather.2.cloned.1.call-start
  6.5 0.9 broadcast_compare_fusion.1
  7.4 0.2 reduce_window_sum.22
  7.6 0.7 add_select_fusion.1
  8.3 0.2 select_reduce_fusion.1
  8.5 0.1 reshape.321
  8.6 0.7 convert_element_type.49
  9.3 5.1 %gather_fusion = bf16[64,128,128]{2,1,0:T(8,128)(2,1)} fusion(bf16[48,2,2,128,128]{4,3,2,1,0:T(8,128)(2,1)} %param.14, s32[64]{0:T(128)S(1)} %fusion.46), kind=kCustom, calls=%fused_computation | custom fusion | bytes 4195072 | tf_op jit(solution)/shard_map/gather | solution.py:188
  14.4 0.0 copy-done.1
  14.4 0.2 fusion.11
  14.6 1.2 fusion.13
  15.8 0.0 copy-start.4
  15.8 0.0 all-gather.2.cloned.1.call-update
  15.8 0.0 copy-start.3
  15.8 7.4 %all-to-all-start = ((bf16[64,128,128]{2,1,0:T(8,128)(2,1)}), bf16[64,128,128]{2,1,0:T(8,128)(2,1)}, u32[]{:S(2)}, u32[]{:S(2)}) async-start(bf16[64,128,128]{2,1,0:T(8,128)(2,1)} %gather_fusion), calls=%async_computation | async-start | bytes 4194304 | tf_op jit(solution)/shard_map/all_to_all | solution.py:190
  23.2 0.0 collective-permute-start.6
  23.2 0.0 copy-done.4
  23.2 0.6 dynamic_slice.23
  23.9 0.6 fusion.37
  24.5 0.5 multiply_cosine_fusion.1
  25.1 22.1 %all-gather.2.cloned.1.call-done = bf16[512,3072]{1,0:T(8,128)(2,1)} async-done(((bf16[128,3072]{1,0:T(8,128)(2,1)}), bf16[512,3072]{1,0:T(8,128)(2,1)}) %all-gather.2.cloned.1.call-update) | async-done | bytes 3145744 | tf_op jit(solution)/shard_map/all_gather | solution.py:208
  47.2 0.0 copy-done.3
  47.2 0.0 copy-start.2
  47.2 3.0 %fusion.50 = f32[512,128]{1,0:T(8,128)S(1)} fusion(bf16[512,3072]{1,0:T(8,128)(2,1)} %all-gather.2.cloned.1.call-done, bf16[3072,128]{1,0:T(8,128)(2,1)S(1)} %copy-done.3), kind=kOutput, calls=%fused_computation.88 | convolution fusion | flops 402653184 | bytes 4194304 | tf_op jit(solution)/shard_map/dot_general | solution.py:218
  50.2 1.2 fusion.25
  51.4 0.1 fusion.28
  51.6 0.3 collective-permute-start.1
  51.9 0.0 copy-done
  51.9 0.0 copy-done.2
  51.9 1.4 fusion.49
  53.3 0.1 subtract_convert_fusion
  53.5 0.0 collective-permute-done.1
  53.5 0.8 broadcast_select_fusion
  54.2 17.3 %all-to-all-done = bf16[64,128,128]{2,1,0:T(8,128)(2,1)} async-done(((bf16[64,128,128]{2,1,0:T(8,128)(2,1)}), bf16[64,128,128]{2,1,0:T(8,128)(2,1)}, u32[]{:S(2)}, u32[]{:S(2)}) %all-to-all-start) | async-done | bytes 2097184 | tf_op jit(solution)/shard_map/all_to_all | solution.py:190
  71.6 0.0 collective-permute-start.2
  71.6 0.2 reduce_window_sum.23
  71.8 1.5 %collective-permute-start = (bf16[384,3072]{1,0:T(8,128)(2,1)}, bf16[384,3072]{1,0:T(8,128)(2,1)}, u32[]{:S(2)}, u32[]{:S(2)}) collective-permute-start(bf16[384,3072]{1,0:T(8,128)(2,1)} %param.13), channel_id=1, source_target_pairs={{0,2},{1,3},{2,0},{3,1},{4,6},{5,7},{6,4},{7,5},{8,10},{9,11},{10,... | collective-permute-start | bytes 7077896 | tf_op jit(solution)/shard_map/ppermute | solution.py:140
  73.3 0.8 dynamic-slice_compare_fusion
  74.1 0.2 fusion.31
  74.3 0.2 select_reduce_fusion
  74.5 0.7 fusion.32
  75.3 0.7 add_select_fusion.refs_6_
  76.0 0.9 copy.19.refs_1_
  76.9 0.0 collective-permute-done.2
  76.9 30.7 %paged_prefill_attention.1 = bf16[512,384]{1,0:T(8,128)(2,1)} custom-call(s32[1]{0:T(128)} %bitcast.1.refs_0_, bf16[512,384]{1,0:T(8,128)(2,1)} %copy.19.refs_1_, bf16[8192,128]{1,0:T(8,128)(2,1)} %bitcast.7.refs_2_, bf16[8192,128]{1,0:T(8,128)(2,1)} %bitcast.8.refs_3_, bf16[512,128]{1,0:T(8,128)(2,1)} %get-tuple-element.21.refs_4_, ...), custom_call_target="tpu_custom_call" | custom-call | flops 6845104128 | bytes 5277696 | tf_op jit(solution)/shard_map/paged_prefill_attention/pallas_call | solution.py:128
  107.6 18.2 %collective-permute-done = bf16[384,3072]{1,0:T(8,128)(2,1)} collective-permute-done((bf16[384,3072]{1,0:T(8,128)(2,1)}, bf16[384,3072]{1,0:T(8,128)(2,1)}, u32[]{:S(2)}, u32[]{:S(2)}) %collective-permute-start) | collective-permute-done | bytes 2359328 | tf_op jit(solution)/shard_map/ppermute | solution.py:140
  125.8 0.0 collective-permute-start.7
  125.8 1.1 constant_dynamic-slice_fusion.3
  126.9 1.7 %collective-permute-start.5 = (bf16[128,384]{1,0:T(8,128)(2,1)S(1)}, bf16[128,384]{1,0:T(8,128)(2,1)S(1)}, u32[]{:S(2)}, u32[]{:S(2)}) collective-permute-start(bf16[128,384]{1,0:T(8,128)(2,1)S(1)} %get-tuple-element.31), channel_id=1, source_target_pairs={{0,3},{1,2},{2,1},{3,0},{4,7},{5,6},{6,5},{7,4},{8,11},{9,10},{10,... | collective-permute-start | bytes 294920 | tf_op jit(solution)/shard_map/ppermute | solution.py:140
  128.6 0.0 collective-permute-start.4
  128.6 0.5 collective-permute-start.3
  129.1 0.0 collective-permute-done.6
  129.1 2.6 %collective-permute-done.5 = bf16[128,384]{1,0:T(8,128)(2,1)S(1)} collective-permute-done((bf16[128,384]{1,0:T(8,128)(2,1)S(1)}, bf16[128,384]{1,0:T(8,128)(2,1)S(1)}, u32[]{:S(2)}, u32[]{:S(2)}) %collective-permute-start.5) | collective-permute-done | bytes 98336 | tf_op jit(solution)/shard_map/ppermute | solution.py:140
  131.7 0.0 collective-permute-done.4
  131.7 2.4 %collective-permute-done.3 = bf16[128,384]{1,0:T(8,128)(2,1)S(1)} collective-permute-done((bf16[128,384]{1,0:T(8,128)(2,1)S(1)}, bf16[128,384]{1,0:T(8,128)(2,1)S(1)}, u32[]{:S(2)}, u32[]{:S(2)}) %collective-permute-start.3) | collective-permute-done | bytes 98336 | tf_op jit(solution)/shard_map/ppermute | solution.py:140
  134.1 0.0 collective-permute-done.7
  134.1 5.3 %fusion.8 = bf16[128,3072]{1,0:T(8,128)(2,1)} fusion(bf16[384,3072]{1,0:T(8,128)(2,1)} %collective-permute-done.7, bf16[384,3072]{1,0:T(8,128)(2,1)} %collective-permute-done.6, bf16[384,3072]{1,0:T(8,128)(2,1)} %collective-permute-done, bf16[384,3072]{1,0:T(8,128)(2,1)} %param.13, bf16[128,384]{1,0:T(8,128)(2,1)S(1)} %collective-permute-done.5, ...), kind=kOutput, calls=%fused_computation.9 | convolution fusion | flops 1247674368 | bytes 10616832 | tf_op jit(solution)/shard_map/dot_general | solution.py:262
  (10 shorter events, 0.1 us)
Async XLA Ops:
  6.5 45.3 %copy-start = (bf16[3072,384]{1,0:T(8,128)(2,1)S(1)}, bf16[3072,384]{1,0:T(8,128)(2,1)}, u32[]{:S(2)}) copy-start(bf16[3072,384]{1,0:T(8,128)(2,1)} %param.11) | copy-start | bytes 7077892
  6.5 7.8 %copy-start.1 = (bf16[128,3072]{1,0:T(8,128)(2,1)S(1)}, bf16[128,3072]{1,0:T(8,128)(2,1)}, u32[]{:S(2)}) copy-start(bf16[128,3072]{1,0:T(8,128)(2,1)} %param.9) | copy-start | bytes 2359300
  6.5 40.7 %all-gather.2.cloned.1.call-start = ((), (), s32[]{:S(2)}) async-start(), calls=%async_computation.1 | async-start | bytes 3932160 | tf_op jit(solution)/shard_map/all_gather | solution.py:208
  15.8 7.5 %copy-start.4 = (s32[8]{0:T(128)S(1)}, s32[8]{0:T(128)}, u32[]{:S(2)}) copy-start(s32[8]{0:T(128)} %param.15) | copy-start | bytes 100
  15.8 31.4 %copy-start.3 = (bf16[3072,128]{1,0:T(8,128)(2,1)S(1)}, bf16[3072,128]{1,0:T(8,128)(2,1)}, u32[]{:S(2)}) copy-start(bf16[3072,128]{1,0:T(8,128)(2,1)} %param.12) | copy-start | bytes 2359300
  15.8 55.7 %all-to-all-start = ((bf16[64,128,128]{2,1,0:T(8,128)(2,1)}), bf16[64,128,128]{2,1,0:T(8,128)(2,1)}, u32[]{:S(2)}, u32[]{:S(2)}) async-start(bf16[64,128,128]{2,1,0:T(8,128)(2,1)} %gather_fusion), calls=%async_computation | async-start | bytes 4194304 | tf_op jit(solution)/shard_map/all_to_all | solution.py:190
  23.2 105.9 %collective-permute-start.6 = (bf16[384,3072]{1,0:T(8,128)(2,1)}, bf16[384,3072]{1,0:T(8,128)(2,1)}, u32[]{:S(2)}, u32[]{:S(2)}) collective-permute-start(bf16[384,3072]{1,0:T(8,128)(2,1)} %param.13), channel_id=1, source_target_pairs={{0,1},{1,0},{2,3},{3,2},{4,5},{5,4},{6,7},{7,6},{8,9},{9,8},{10,11... | collective-permute-start | bytes 7077896 | tf_op jit(solution)/shard_map/ppermute | solution.py:140
  47.2 4.7 %copy-start.2 = (bf16[512,3072]{1,0:T(8,128)(2,1)S(1)}, bf16[512,3072]{1,0:T(8,128)(2,1)}, u32[]{:S(2)}) copy-start(bf16[512,3072]{1,0:T(8,128)(2,1)} %all-gather.2.cloned.1.call-done) | copy-start | bytes 9437188
  51.6 1.9 %collective-permute-start.1 = (bf16[512,128]{1,0:T(8,128)(2,1)S(1)}, bf16[512,128]{1,0:T(8,128)(2,1)S(1)}, u32[]{:S(2)}, u32[]{:S(2)}) collective-permute-start(bf16[512,128]{1,0:T(8,128)(2,1)S(1)} %fusion.28), channel_id=1, source_target_pairs={{0,1},{1,0},{2,3},{3,2},{4,5},{5,4},{6,7},{7,6},{8,9},{9,8},{10,11... | collective-permute-start | bytes 393224 | tf_op jit(solution)/shard_map/ppermute | solution.py:22
  71.6 5.3 %collective-permute-start.2 = (bf16[64,128,128]{2,1,0:T(8,128)(2,1)}, bf16[64,128,128]{2,1,0:T(8,128)(2,1)}, u32[]{:S(2)}, u32[]{:S(2)}) collective-permute-start(bf16[64,128,128]{2,1,0:T(8,128)(2,1)} %all-to-all-done), channel_id=1, source_target_pairs={{0,1},{1,0},{2,3},{3,2},{4,5},{5,4},{6,7},{7,6},{8,9},{9,8},{10,11... | collective-permute-start | bytes 6291464 | tf_op jit(solution)/shard_map/ppermute | solution.py:140
  71.8 54.0 %collective-permute-start = (bf16[384,3072]{1,0:T(8,128)(2,1)}, bf16[384,3072]{1,0:T(8,128)(2,1)}, u32[]{:S(2)}, u32[]{:S(2)}) collective-permute-start(bf16[384,3072]{1,0:T(8,128)(2,1)} %param.13), channel_id=1, source_target_pairs={{0,2},{1,3},{2,0},{3,1},{4,6},{5,7},{6,4},{7,5},{8,10},{9,11},{10,... | collective-permute-start | bytes 7077896 | tf_op jit(solution)/shard_map/ppermute | solution.py:140
  125.8 8.4 %collective-permute-start.7 = (bf16[384,3072]{1,0:T(8,128)(2,1)}, bf16[384,3072]{1,0:T(8,128)(2,1)}, u32[]{:S(2)}, u32[]{:S(2)}) collective-permute-start(bf16[384,3072]{1,0:T(8,128)(2,1)} %collective-permute-done), channel_id=1, source_target_pairs={{0,1},{1,0},{2,3},{3,2},{4,5},{5,4},{6,7},{7,6},{8,9},{9,8},{10,11... | collective-permute-start | bytes 7077896 | tf_op jit(solution)/shard_map/ppermute | solution.py:140
  126.9 4.8 %collective-permute-start.5 = (bf16[128,384]{1,0:T(8,128)(2,1)S(1)}, bf16[128,384]{1,0:T(8,128)(2,1)S(1)}, u32[]{:S(2)}, u32[]{:S(2)}) collective-permute-start(bf16[128,384]{1,0:T(8,128)(2,1)S(1)} %get-tuple-element.31), channel_id=1, source_target_pairs={{0,3},{1,2},{2,1},{3,0},{4,7},{5,6},{6,5},{7,4},{8,11},{9,10},{10,... | collective-permute-start | bytes 294920 | tf_op jit(solution)/shard_map/ppermute | solution.py:140
  128.6 3.1 %collective-permute-start.4 = (bf16[128,384]{1,0:T(8,128)(2,1)S(1)}, bf16[128,384]{1,0:T(8,128)(2,1)S(1)}, u32[]{:S(2)}, u32[]{:S(2)}) collective-permute-start(bf16[128,384]{1,0:T(8,128)(2,1)S(1)} %get-tuple-element.32), channel_id=1, source_target_pairs={{0,1},{1,0},{2,3},{3,2},{4,5},{5,4},{6,7},{7,6},{8,9},{9,8},{10,11... | collective-permute-start | bytes 294920 | tf_op jit(solution)/shard_map/ppermute | solution.py:140
  128.6 5.6 %collective-permute-start.3 = (bf16[128,384]{1,0:T(8,128)(2,1)S(1)}, bf16[128,384]{1,0:T(8,128)(2,1)S(1)}, u32[]{:S(2)}, u32[]{:S(2)}) collective-permute-start(bf16[128,384]{1,0:T(8,128)(2,1)S(1)} %get-tuple-element.33), channel_id=1, source_target_pairs={{0,2},{1,3},{2,0},{3,1},{4,6},{5,7},{6,4},{7,5},{8,10},{9,11},{10,... | collective-permute-start | bytes 294920 | tf_op jit(solution)/shard_map/ppermute | solution.py:140
Sparse Core Ops, SparseCore 0:
  15.9 31.2 all-gather.1

commit v8 on v7

--- a/solution.py
+++ b/solution.py
@@ -206,12 +206,11 @@
         jnp.bfloat16
     )
     piece = lax.all_gather(normalized_input, "head", axis=0, tiled=True)
-    w_late, piece = lax.optimization_barrier((w_out, piece))
     held_w = [w_out]
     masks = [0]
     stride = head_number // 2
     while stride > 1:
-        held_w = held_w + [exchange(w_late if i == 0 else p, "head", stride) for i, p in enumerate(held_w)]
+        held_w = held_w + [exchange(p, "head", stride) for p in held_w]
         masks = masks + [m ^ stride for m in masks]
         stride //= 2
     q_part = jnp.dot(piece, w_query, preferred_element_type=jnp.float32)

time: 147 us -> 128 us (0.87)
  waiting for transfers between devices: 62.7 us -> 43.7 us
    ppermute x7, waiting for transfers between devices: 23.2 us -> 5.78 us  [exchange(): return lax.ppermute(value, axis, pairs)]
    all_to_all x1, waiting for transfers between devices: 17.3 us -> 0.36 us  [body(): lax.all_to_all(outgoing, 'dp', split_axis=0, concat_axis=0, tiled=True)]
    all_gather x1, waiting for transfers between devices: 22.1 us -> 37.6 us  [body(): piece = lax.all_gather(normalized_input, 'head', axis=0, tiled=True)]
  transfers between devices with their start and end apart: 10 -> 10, of which waited for: 5 -> 5; matrix products, arithmetic and copies ran while one was open for 9% -> 10% of each run, Pallas kernels for 21% -> 24%
where the time goes in v8:
time: 128 us; the launch traced here: 127 us
  waiting for transfers between devices  43.7 us (34%)
  Pallas kernels  30.7 us (24%)
  between operations  13.5 us (11%)
  starting transfers between devices  11.7 us (9%)
  other arithmetic  10.3 us (8%)
  matrix products  9.7 us (8%)
  local copies, waits for them, and re-layouts  7.76 us (6%)
    all_gather x1, waiting for transfers between devices, body(): piece = lax.all_gather(normalized_input, 'head', axis=0, tiled=True)  37.6 us
    pallas_call x1, Pallas kernels, attend(): pl.pallas_call(lambda *refs: attend_kernel(n_cache, tk, scale, *refs), ou...  30.7 us
    all_to_all x1, starting transfers between devices, body(): lax.all_to_all(outgoing, 'dp', split_axis=0, concat_axis=0, tiled=True)  7.4 us
    ppermute x7, waiting for transfers between devices, exchange(): return lax.ppermute(value, axis, pairs)  5.78 us
    dot_general x1, matrix products, body(): out = jnp.dot(ordered, held_w, preferred_element_type=jnp.float32)  5.27 us
    gather x1, local copies, waits for them, and re-layouts, body(): outgoing = kv_pool[local_page.reshape(-1), key_value_head, part]  4.98 us
    ppermute x7, starting transfers between devices, exchange(): return lax.ppermute(value, axis, pairs)  3.95 us
    dot_general x1, matrix products, body(): jnp.dot(piece, key_value_weight, preferred_element_type=jnp.float32)  3.01 us
  transfers between devices with their start and end apart: 10, of which 5 were waited for; matrix products, arithmetic and copies ran while one was open for 10% of the time, Pallas kernels for 24%

profile of v8, /device:TPU:0, one launch (start us, length us, event | category | flops | bytes accessed | tf_op | source)
XLA Modules:
  0.0 127.4 jit_solution(2680443584755142808)
XLA Ops:
  6.5 0.0 copy-start
  6.5 0.0 copy-start.1
  6.5 0.0 all-gather.2.cloned.1.call-start
  6.5 0.9 broadcast_compare_fusion.1
  7.4 0.2 reduce_window_sum.22
  7.6 0.7 add_select_fusion.1
  8.3 0.2 select_reduce_fusion.1
  8.5 0.1 reshape.322
  8.6 0.7 convert_element_type.49
  9.3 5.0 %gather_fusion = bf16[64,128,128]{2,1,0:T(8,128)(2,1)} fusion(bf16[48,2,2,128,128]{4,3,2,1,0:T(8,128)(2,1)} %param.14, s32[64]{0:T(128)S(1)} %fusion.46), kind=kCustom, calls=%fused_computation | custom fusion | bytes 4195072 | tf_op jit(solution)/shard_map/gather | solution.py:188
  14.3 0.0 copy-done.1
  14.3 0.2 fusion.11
  14.6 1.2 fusion.13
  15.7 0.0 copy-start.4
  15.7 0.0 all-gather.2.cloned.1.call-update
  15.7 0.0 copy-start.3
  15.7 7.4 %all-to-all-start = ((bf16[64,128,128]{2,1,0:T(8,128)(2,1)}), bf16[64,128,128]{2,1,0:T(8,128)(2,1)}, u32[]{:S(2)}, u32[]{:S(2)}) async-start(bf16[64,128,128]{2,1,0:T(8,128)(2,1)} %gather_fusion), calls=%async_computation | async-start | bytes 4194304 | tf_op jit(solution)/shard_map/all_to_all | solution.py:190
  23.1 1.5 %collective-permute-start = (bf16[384,3072]{1,0:T(8,128)(2,1)}, bf16[384,3072]{1,0:T(8,128)(2,1)}, u32[]{:S(2)}, u32[]{:S(2)}) collective-permute-start(bf16[384,3072]{1,0:T(8,128)(2,1)} %param.13), channel_id=1, source_target_pairs={{0,2},{1,3},{2,0},{3,1},{4,6},{5,7},{6,4},{7,5},{8,10},{9,11},{10,... | collective-permute-start | bytes 7077896 | tf_op jit(solution)/shard_map/ppermute | solution.py:140
  24.7 0.0 collective-permute-start.6
  24.7 0.0 copy-done.4
  24.7 0.6 dynamic_slice.23
  25.3 0.6 fusion.37
  26.0 0.5 multiply_cosine_fusion.1
  26.5 37.6 %all-gather.2.cloned.1.call-done = bf16[512,3072]{1,0:T(8,128)(2,1)} async-done(((bf16[128,3072]{1,0:T(8,128)(2,1)}), bf16[512,3072]{1,0:T(8,128)(2,1)}) %all-gather.2.cloned.1.call-update) | async-done | bytes 3145744 | tf_op jit(solution)/shard_map/all_gather | solution.py:208
  64.1 0.0 copy-done.3
  64.1 0.0 copy-start.2
  64.1 3.0 %fusion.50 = f32[512,128]{1,0:T(8,128)S(1)} fusion(bf16[512,3072]{1,0:T(8,128)(2,1)} %all-gather.2.cloned.1.call-done, bf16[3072,128]{1,0:T(8,128)(2,1)S(1)} %copy-done.3), kind=kOutput, calls=%fused_computation.88 | convolution fusion | flops 402653184 | bytes 4194304 | tf_op jit(solution)/shard_map/dot_general | solution.py:217
  67.1 1.2 fusion.25
  68.4 0.1 fusion.28
  68.5 0.3 collective-permute-start.1
  68.8 0.0 copy-done
  68.8 0.0 copy-done.2
  68.8 1.4 %fusion.49 = f32[512,384]{0,1:T(8,128)S(1)} fusion(bf16[512,3072]{1,0:T(8,128)(2,1)S(1)} %copy-done.2, bf16[3072,384]{1,0:T(8,128)(2,1)S(1)} %copy-done), kind=kOutput, calls=%fused_computation.87 | convolution fusion | flops 1207959552 | bytes 6291456 | tf_op jit(solution)/shard_map/dot_general | solution.py:216
  70.2 0.1 subtract_convert_fusion
  70.4 0.0 collective-permute-done.1
  70.4 0.7 broadcast_select_fusion
  71.1 0.4 all-to-all-done
  71.5 0.0 collective-permute-start.2
  71.5 0.2 reduce_window_sum.23
  71.7 0.8 dynamic-slice_compare_fusion
  72.5 0.2 fusion.31
  72.7 0.2 select_reduce_fusion
  72.9 0.7 fusion.32
  73.7 0.7 add_select_fusion.refs_6_
  74.4 0.9 copy.19.refs_1_
  75.3 0.7 collective-permute-done.2
  76.0 30.7 %paged_prefill_attention.1 = bf16[512,384]{1,0:T(8,128)(2,1)} custom-call(s32[1]{0:T(128)} %bitcast.refs_0_, bf16[512,384]{1,0:T(8,128)(2,1)} %copy.19.refs_1_, bf16[8192,128]{1,0:T(8,128)(2,1)} %bitcast.7.refs_2_, bf16[8192,128]{1,0:T(8,128)(2,1)} %bitcast.8.refs_3_, bf16[512,128]{1,0:T(8,128)(2,1)} %get-tuple-element.17.refs_4_, ...), custom_call_target="tpu_custom_call" | custom-call | flops 6845104128 | bytes 5277696 | tf_op jit(solution)/shard_map/paged_prefill_attention/pallas_call | solution.py:128
  106.7 0.0 collective-permute-done
  106.7 0.2 collective-permute-start.7
  106.9 1.1 constant_dynamic-slice_fusion.3
  108.0 1.6 %collective-permute-start.5 = (bf16[128,384]{1,0:T(8,128)(2,1)S(1)}, bf16[128,384]{1,0:T(8,128)(2,1)S(1)}, u32[]{:S(2)}, u32[]{:S(2)}) collective-permute-start(bf16[128,384]{1,0:T(8,128)(2,1)S(1)} %get-tuple-element.27), channel_id=1, source_target_pairs={{0,3},{1,2},{2,1},{3,0},{4,7},{5,6},{6,5},{7,4},{8,11},{9,10},{10,... | collective-permute-start | bytes 294920 | tf_op jit(solution)/shard_map/ppermute | solution.py:140
  109.6 0.2 collective-permute-start.4
  109.7 0.5 collective-permute-start.3
  110.2 0.0 collective-permute-done.6
  110.2 2.5 %collective-permute-done.5 = bf16[128,384]{1,0:T(8,128)(2,1)S(1)} collective-permute-done((bf16[128,384]{1,0:T(8,128)(2,1)S(1)}, bf16[128,384]{1,0:T(8,128)(2,1)S(1)}, u32[]{:S(2)}, u32[]{:S(2)}) %collective-permute-start.5) | collective-permute-done | bytes 98336 | tf_op jit(solution)/shard_map/ppermute | solution.py:140
  112.7 0.0 collective-permute-done.4
  112.7 2.6 %collective-permute-done.3 = bf16[128,384]{1,0:T(8,128)(2,1)S(1)} collective-permute-done((bf16[128,384]{1,0:T(8,128)(2,1)S(1)}, bf16[128,384]{1,0:T(8,128)(2,1)S(1)}, u32[]{:S(2)}, u32[]{:S(2)}) %collective-permute-start.3) | collective-permute-done | bytes 98336 | tf_op jit(solution)/shard_map/ppermute | solution.py:140
  115.3 0.0 collective-permute-done.7
  115.3 5.3 %fusion.8 = bf16[128,3072]{1,0:T(8,128)(2,1)} fusion(bf16[384,3072]{1,0:T(8,128)(2,1)} %collective-permute-done.7, bf16[384,3072]{1,0:T(8,128)(2,1)} %collective-permute-done.6, bf16[384,3072]{1,0:T(8,128)(2,1)} %collective-permute-done, bf16[384,3072]{1,0:T(8,128)(2,1)} %param.13, bf16[128,384]{1,0:T(8,128)(2,1)S(1)} %collective-permute-done.5, ...), kind=kOutput, calls=%fused_computation.9 | convolution fusion | flops 1247674368 | bytes 10616832 | tf_op jit(solution)/shard_map/dot_general | solution.py:261
  (10 shorter events, 0.1 us)
Async XLA Ops:
  6.5 62.2 %copy-start = (bf16[3072,384]{1,0:T(8,128)(2,1)S(1)}, bf16[3072,384]{1,0:T(8,128)(2,1)}, u32[]{:S(2)}) copy-start(bf16[3072,384]{1,0:T(8,128)(2,1)} %param.11) | copy-start | bytes 7077892
  6.5 7.8 %copy-start.1 = (bf16[128,3072]{1,0:T(8,128)(2,1)S(1)}, bf16[128,3072]{1,0:T(8,128)(2,1)}, u32[]{:S(2)}) copy-start(bf16[128,3072]{1,0:T(8,128)(2,1)} %param.9) | copy-start | bytes 2359300
  6.5 57.6 %all-gather.2.cloned.1.call-start = ((), (), s32[]{:S(2)}) async-start(), calls=%async_computation.1 | async-start | bytes 3932160 | tf_op jit(solution)/shard_map/all_gather | solution.py:208
  15.7 9.0 %copy-start.4 = (s32[8]{0:T(128)S(1)}, s32[8]{0:T(128)}, u32[]{:S(2)}) copy-start(s32[8]{0:T(128)} %param.15) | copy-start | bytes 100
  15.7 48.4 %copy-start.3 = (bf16[3072,128]{1,0:T(8,128)(2,1)S(1)}, bf16[3072,128]{1,0:T(8,128)(2,1)}, u32[]{:S(2)}) copy-start(bf16[3072,128]{1,0:T(8,128)(2,1)} %param.12) | copy-start | bytes 2359300
  15.7 55.7 %all-to-all-start = ((bf16[64,128,128]{2,1,0:T(8,128)(2,1)}), bf16[64,128,128]{2,1,0:T(8,128)(2,1)}, u32[]{:S(2)}, u32[]{:S(2)}) async-start(bf16[64,128,128]{2,1,0:T(8,128)(2,1)} %gather_fusion), calls=%async_computation | async-start | bytes 4194304 | tf_op jit(solution)/shard_map/all_to_all | solution.py:190
  23.1 83.6 %collective-permute-start = (bf16[384,3072]{1,0:T(8,128)(2,1)}, bf16[384,3072]{1,0:T(8,128)(2,1)}, u32[]{:S(2)}, u32[]{:S(2)}) collective-permute-start(bf16[384,3072]{1,0:T(8,128)(2,1)} %param.13), channel_id=1, source_target_pairs={{0,2},{1,3},{2,0},{3,1},{4,6},{5,7},{6,4},{7,5},{8,10},{9,11},{10,... | collective-permute-start | bytes 7077896 | tf_op jit(solution)/shard_map/ppermute | solution.py:140
  24.7 85.6 %collective-permute-start.6 = (bf16[384,3072]{1,0:T(8,128)(2,1)}, bf16[384,3072]{1,0:T(8,128)(2,1)}, u32[]{:S(2)}, u32[]{:S(2)}) collective-permute-start(bf16[384,3072]{1,0:T(8,128)(2,1)} %param.13), channel_id=1, source_target_pairs={{0,1},{1,0},{2,3},{3,2},{4,5},{5,4},{6,7},{7,6},{8,9},{9,8},{10,11... | collective-permute-start | bytes 7077896 | tf_op jit(solution)/shard_map/ppermute | solution.py:140
  64.1 4.7 %copy-start.2 = (bf16[512,3072]{1,0:T(8,128)(2,1)S(1)}, bf16[512,3072]{1,0:T(8,128)(2,1)}, u32[]{:S(2)}) copy-start(bf16[512,3072]{1,0:T(8,128)(2,1)} %all-gather.2.cloned.1.call-done) | copy-start | bytes 9437188
  68.5 1.9 %collective-permute-start.1 = (bf16[512,128]{1,0:T(8,128)(2,1)S(1)}, bf16[512,128]{1,0:T(8,128)(2,1)S(1)}, u32[]{:S(2)}, u32[]{:S(2)}) collective-permute-start(bf16[512,128]{1,0:T(8,128)(2,1)S(1)} %fusion.28), channel_id=1, source_target_pairs={{0,1},{1,0},{2,3},{3,2},{4,5},{5,4},{6,7},{7,6},{8,9},{9,8},{10,11... | collective-permute-start | bytes 393224 | tf_op jit(solution)/shard_map/ppermute | solution.py:22
  71.5 4.5 %collective-permute-start.2 = (bf16[64,128,128]{2,1,0:T(8,128)(2,1)}, bf16[64,128,128]{2,1,0:T(8,128)(2,1)}, u32[]{:S(2)}, u32[]{:S(2)}) collective-permute-start(bf16[64,128,128]{2,1,0:T(8,128)(2,1)} %all-to-all-done), channel_id=1, source_target_pairs={{0,1},{1,0},{2,3},{3,2},{4,5},{5,4},{6,7},{7,6},{8,9},{9,8},{10,11... | collective-permute-start | bytes 6291464 | tf_op jit(solution)/shard_map/ppermute | solution.py:140
  106.7 8.6 %collective-permute-start.7 = (bf16[384,3072]{1,0:T(8,128)(2,1)}, bf16[384,3072]{1,0:T(8,128)(2,1)}, u32[]{:S(2)}, u32[]{:S(2)}) collective-permute-start(bf16[384,3072]{1,0:T(8,128)(2,1)} %collective-permute-done), channel_id=1, source_target_pairs={{0,1},{1,0},{2,3},{3,2},{4,5},{5,4},{6,7},{7,6},{8,9},{9,8},{10,11... | collective-permute-start | bytes 7077896 | tf_op jit(solution)/shard_map/ppermute | solution.py:140
  108.0 4.7 %collective-permute-start.5 = (bf16[128,384]{1,0:T(8,128)(2,1)S(1)}, bf16[128,384]{1,0:T(8,128)(2,1)S(1)}, u32[]{:S(2)}, u32[]{:S(2)}) collective-permute-start(bf16[128,384]{1,0:T(8,128)(2,1)S(1)} %get-tuple-element.27), channel_id=1, source_target_pairs={{0,3},{1,2},{2,1},{3,0},{4,7},{5,6},{6,5},{7,4},{8,11},{9,10},{10,... | collective-permute-start | bytes 294920 | tf_op jit(solution)/shard_map/ppermute | solution.py:140
  109.6 3.1 %collective-permute-start.4 = (bf16[128,384]{1,0:T(8,128)(2,1)S(1)}, bf16[128,384]{1,0:T(8,128)(2,1)S(1)}, u32[]{:S(2)}, u32[]{:S(2)}) collective-permute-start(bf16[128,384]{1,0:T(8,128)(2,1)S(1)} %get-tuple-element.28), channel_id=1, source_target_pairs={{0,1},{1,0},{2,3},{3,2},{4,5},{5,4},{6,7},{7,6},{8,9},{9,8},{10,11... | collective-permute-start | bytes 294920 | tf_op jit(solution)/shard_map/ppermute | solution.py:140
  109.7 5.6 %collective-permute-start.3 = (bf16[128,384]{1,0:T(8,128)(2,1)S(1)}, bf16[128,384]{1,0:T(8,128)(2,1)S(1)}, u32[]{:S(2)}, u32[]{:S(2)}) collective-permute-start(bf16[128,384]{1,0:T(8,128)(2,1)S(1)} %get-tuple-element.29), channel_id=1, source_target_pairs={{0,2},{1,3},{2,0},{3,1},{4,6},{5,7},{6,4},{7,5},{8,10},{9,11},{10,... | collective-permute-start | bytes 294920 | tf_op jit(solution)/shard_map/ppermute | solution.py:140
Sparse Core Ops, SparseCore 0:
  15.9 48.1 all-gather.1

commit v9 on v8

--- a/solution.py
+++ b/solution.py
@@ -205,7 +205,16 @@
     normalized_input = (wide * lax.rsqrt(meansq + 1e-05) * norm_gain.astype(jnp.float32)).astype(
         jnp.bfloat16
     )
-    piece = lax.all_gather(normalized_input, "head", axis=0, tiled=True)
+    rows_in = [normalized_input]
+    masks = [0]
+    stride = head_number // 2
+    while stride >= 1:
+        rows_in = rows_in + [exchange(p, "head", stride) for p in rows_in]
+        masks = masks + [m ^ stride for m in masks]
+        stride //= 2
+    piece = jnp.zeros((block_rows, normalized_input.shape[1]), normalized_input.dtype)
+    for p, m in zip(rows_in, masks):
+        piece = lax.dynamic_update_slice_in_dim(piece, p, (current_head ^ m) * local_rows, 0)
     held_w = [w_out]
     masks = [0]
     stride = head_number // 2

time: 128 us -> 116 us (0.906)
  between operations: 13.5 us -> 0.17 us
  waiting for transfers between devices: 43.7 us -> 36.5 us
  local copies, waits for them, and re-layouts: 7.76 us -> 14.8 us
    all_gather x1 -> x0, waiting for transfers between devices: 37.6 us -> none  [body(): piece = lax.all_gather(normalized_input, 'head', axis=0, tiled=True)]
    all_to_all x1, waiting for transfers between devices: 0.36 us -> 21.1 us  [body(): lax.all_to_all(outgoing, 'dp', split_axis=0, concat_axis=0, tiled=True)]
    ppermute x7 -> x10, waiting for transfers between devices: 5.78 us -> 15.5 us  [exchange(): return lax.ppermute(value, axis, pairs)]
    dynamic_update_slice x0 -> x3, local copies, waits for them, and re-layouts: none -> 5.09 us  [body(): lax.dynamic_update_slice_in_dim(piece, p, (current_head ^ m) * local_rows...]
    ppermute x7 -> x10, starting transfers between devices: 3.95 us -> 6.26 us  [exchange(): return lax.ppermute(value, axis, pairs)]
    broadcast_in_dim x0 -> x1, local copies, waits for them, and re-layouts: none -> 2.02 us  [body(): jnp.zeros((block_rows, normalized_input.shape[1]), normalized_input.dtype)]
    dot_general x1, matrix products: 1.43 us -> 3.31 us  [body(): q_part = jnp.dot(piece, w_query, preferred_element_type=jnp.float32)]
    all_to_all x1, starting transfers between devices: 7.4 us -> 5.81 us  [body(): lax.all_to_all(outgoing, 'dp', split_axis=0, concat_axis=0, tiled=True)]
  transfers between devices with their start and end apart: 10 -> 12, of which waited for: 5 -> 5; matrix products, arithmetic and copies ran while one was open for 10% -> 17% of each run, Pallas kernels for 24% -> 27%
where the time goes in v9:
time: 116 us
  waiting for transfers between devices  36.5 us (31%)
  Pallas kernels  30.7 us (26%)
  local copies, waits for them, and re-layouts  14.8 us (13%)
  starting transfers between devices  12.6 us (11%)
  matrix products  10.8 us (9%)
  other arithmetic  9.87 us (9%)
    pallas_call x1, Pallas kernels, attend(): pl.pallas_call(lambda *refs: attend_kernel(n_cache, tk, scale, *refs), ou...  30.7 us
    all_to_all x1, waiting for transfers between devices, body(): lax.all_to_all(outgoing, 'dp', split_axis=0, concat_axis=0, tiled=True)  21.1 us
    ppermute x10, waiting for transfers between devices, exchange(): return lax.ppermute(value, axis, pairs)  15.5 us
    ppermute x10, starting transfers between devices, exchange(): return lax.ppermute(value, axis, pairs)  6.26 us
    all_to_all x1, starting transfers between devices, body(): lax.all_to_all(outgoing, 'dp', split_axis=0, concat_axis=0, tiled=True)  5.81 us
    dynamic_update_slice x3, local copies, waits for them, and re-layouts, body(): lax.dynamic_update_slice_in_dim(piece, p, (current_head ^ m) * local_rows...  5.09 us
    gather x1, local copies, waits for them, and re-layouts, body(): outgoing = kv_pool[local_page.reshape(-1), key_value_head, part]  4.98 us
    dot_general x1, matrix products, body(): out = jnp.dot(ordered, held_w, preferred_element_type=jnp.float32)  4.6 us
  transfers between devices with their start and end apart: 12, of which 5 were waited for; matrix products, arithmetic and copies ran while one was open for 17% of the time, Pallas kernels for 27%

profile of v9, /device:TPU:0, one launch (start us, length us, event | category | flops | bytes accessed | tf_op | source)
XLA Modules:
  0.0 115.5 jit_solution(17249268641135797947)
XLA Ops:
  0.0 0.0 copy-start
  0.0 0.0 copy-start.1
  0.0 0.0 copy-start.3
  0.0 0.9 broadcast_compare_fusion.1
  0.9 0.2 reduce_window_sum.22
  1.1 0.7 add_select_fusion.1
  1.8 0.2 select_reduce_fusion.1
  2.0 0.1 reshape.322
  2.1 5.0 %gather_fusion = bf16[64,128,128]{2,1,0:T(8,128)(2,1)} fusion(bf16[48,2,2,128,128]{4,3,2,1,0:T(8,128)(2,1)} %param.14, s32[64]{0:T(128)S(1)} %fusion.46), kind=kCustom, calls=%fused_computation | custom fusion | bytes 4195072 | tf_op jit(solution)/shard_map/gather | solution.py:188
  7.1 0.0 copy-done.1
  7.1 0.2 fusion.11
  7.3 0.0 copy-done.3
  7.3 2.0 %broadcast_in_dim.44 = bf16[512,3072]{1,0:T(8,128)(2,1)} broadcast(bf16[]{:T(256)} %constant.105.clone.1), dimensions={} | broadcast | bytes 3145730 | tf_op jit(solution)/shard_map/broadcast_in_dim | solution.py:215
  9.4 0.0 copy-start.4
  9.4 1.5 %constant_dynamic-update-slice_fusion.3 = (bf16[512,3072]{1,0:T(8,128)(2,1)}, bf16[128,3072]{1,0:T(8,128)(2,1)}) fusion(bf16[512,3072]{1,0:T(8,128)(2,1)} %broadcast_in_dim.44, s32[]{:T(128)S(6)} %select_n.135, f32[3072]{0:T(1024)S(1)} %convert_element_type.49, f32[128]{0:T(128)S(1)} %add_rsqrt_fusion, bf16[128,3072]{1,0:T(8,128)(2,1)S(1)} %copy-done.1), kind=kLoop, calls=%fused_computation.69 | loop fusion | flops 1572864 | bytes 2372100 | tf_op jit(solution)/shard_map/dynamic_update_slice | solution.py:217
  10.8 3.0 %collective-permute-start.1 = (bf16[128,3072]{1,0:T(8,128)(2,1)}, bf16[128,3072]{1,0:T(8,128)(2,1)}, u32[]{:S(2)}, u32[]{:S(2)}) collective-permute-start(bf16[128,3072]{1,0:T(8,128)(2,1)} %get-tuple-element.22), channel_id=1, source_target_pairs={{0,2},{1,3},{2,0},{3,1},{4,6},{5,7},{6,4},{7,5},{8,10},{9,11},{10,... | collective-permute-start | bytes 2359304 | tf_op jit(solution)/shard_map/ppermute | solution.py:140
  13.8 5.8 %all-to-all-start = ((bf16[64,128,128]{2,1,0:T(8,128)(2,1)}), bf16[64,128,128]{2,1,0:T(8,128)(2,1)}, u32[]{:S(2)}, u32[]{:S(2)}) async-start(bf16[64,128,128]{2,1,0:T(8,128)(2,1)} %gather_fusion), calls=%async_computation | async-start | bytes 4194304 | tf_op jit(solution)/shard_map/all_to_all | solution.py:190
  19.6 0.1 collective-permute-start.2
  19.7 0.6 collective-permute-start
  20.3 0.2 collective-permute-start.9
  20.5 0.0 copy-done.4
  20.5 0.6 dynamic_slice.23
  21.1 0.6 fusion.37
  21.7 0.5 multiply_cosine_fusion.1
  22.2 10.3 %collective-permute-done.1 = bf16[128,3072]{1,0:T(8,128)(2,1)} collective-permute-done((bf16[128,3072]{1,0:T(8,128)(2,1)}, bf16[128,3072]{1,0:T(8,128)(2,1)}, u32[]{:S(2)}, u32[]{:S(2)}) %collective-permute-start.1) | collective-permute-done | bytes 786464 | tf_op jit(solution)/shard_map/ppermute | solution.py:140
  32.5 0.0 collective-permute-start.3
  32.5 2.1 %constant_dynamic-update-slice_fusion.2 = bf16[512,3072]{1,0:T(8,128)(2,1)} fusion(bf16[512,3072]{1,0:T(8,128)(2,1)} %get-tuple-element.21, bf16[128,3072]{1,0:T(8,128)(2,1)} %collective-permute-done.1, s32[]{:T(128)S(6)} %select_n.136), kind=kLoop, calls=%fused_computation.68 | loop fusion | bytes 1572868 | tf_op jit(solution)/shard_map/dynamic_update_slice | solution.py:217
  34.6 0.0 collective-permute-done.2
  34.6 2.1 %constant_dynamic-update-slice_fusion.1 = bf16[512,3072]{1,0:T(8,128)(2,1)} fusion(bf16[512,3072]{1,0:T(8,128)(2,1)} %constant_dynamic-update-slice_fusion.2, bf16[128,3072]{1,0:T(8,128)(2,1)} %collective-permute-done.2, s32[]{:T(128)S(6)} %select_n.137), kind=kLoop, calls=%fused_computation.67 | loop fusion | bytes 1572868 | tf_op jit(solution)/shard_map/dynamic_update_slice | solution.py:217
  36.7 0.0 collective-permute-done.3
  36.7 0.9 constant_dynamic-update-slice_fusion
  37.6 0.0 copy-done.2
  37.6 2.9 %fusion.51 = f32[512,128]{1,0:T(8,128)S(1)} fusion(bf16[512,3072]{1,0:T(8,128)(2,1)} %constant_dynamic-update-slice_fusion, bf16[3072,128]{1,0:T(8,128)(2,1)S(1)} %copy-done.2), kind=kOutput, calls=%fused_computation.92 | convolution fusion | flops 402653184 | bytes 4194304 | tf_op jit(solution)/shard_map/dot_general | solution.py:226
  40.5 1.2 %fusion.25 = (bf16[512,1,64]{2,0,1:T(8,128)(2,1)S(1)}, bf16[512,1,64]{2,0,1:T(8,128)(2,1)S(1)}) fusion(f32[512,1,128]{2,0,1:T(8,128)S(1)} %bitcast.21, f32[64]{0:T(128)S(1)} %multiply_exponential_fusion, f32[512]{0:T(512)S(1)} %fusion.37), kind=kLoop, calls=%fused_computation.31 | loop fusion | flops 294912 | bytes 395520 | tf_op jit(solution)/shard_map/sub | solution.py:153
  41.7 0.1 fusion.28
  41.8 0.5 collective-permute-start.4
  42.4 0.0 copy-done
  42.4 3.3 %fusion.50 = f32[512,384]{0,1:T(8,128)S(1)} fusion(bf16[512,3072]{1,0:T(8,128)(2,1)} %constant_dynamic-update-slice_fusion, bf16[3072,384]{1,0:T(8,128)(2,1)S(1)} %copy-done), kind=kOutput, calls=%fused_computation.91 | convolution fusion | flops 1207959552 | bytes 6291456 | tf_op jit(solution)/shard_map/dot_general | solution.py:225
  45.7 0.1 subtract_convert_fusion
  45.9 0.0 collective-permute-done.4
  45.9 0.7 broadcast_select_fusion
  46.6 21.1 %all-to-all-done = bf16[64,128,128]{2,1,0:T(8,128)(2,1)} async-done(((bf16[64,128,128]{2,1,0:T(8,128)(2,1)}), bf16[64,128,128]{2,1,0:T(8,128)(2,1)}, u32[]{:S(2)}, u32[]{:S(2)}) %all-to-all-start) | async-done | bytes 2097184 | tf_op jit(solution)/shard_map/all_to_all | solution.py:190
  67.7 0.0 collective-permute-start.5
  67.7 0.2 reduce_window_sum.23
  67.9 0.2 fusion.31
  68.2 0.2 select_reduce_fusion
  68.4 0.7 fusion.32
  69.1 0.8 dynamic-slice_compare_fusion
  69.9 0.7 add_select_fusion.refs_6_
  70.5 0.9 copy.19.refs_1_
  71.5 0.7 collective-permute-done.5
  72.2 30.7 %paged_prefill_attention.1 = bf16[512,384]{1,0:T(8,128)(2,1)} custom-call(s32[1]{0:T(128)} %bitcast.refs_0_, bf16[512,384]{1,0:T(8,128)(2,1)} %copy.19.refs_1_, bf16[8192,128]{1,0:T(8,128)(2,1)} %bitcast.7.refs_2_, bf16[8192,128]{1,0:T(8,128)(2,1)} %bitcast.8.refs_3_, bf16[512,128]{1,0:T(8,128)(2,1)} %get-tuple-element.17.refs_4_, ...), custom_call_target="tpu_custom_call" | custom-call | flops 6845104128 | bytes 5277696 | tf_op jit(solution)/shard_map/paged_prefill_attention/pallas_call | solution.py:128
  102.9 0.0 collective-permute-done
  102.9 0.2 collective-permute-start.10
  103.1 1.1 constant_dynamic-slice_fusion.3
  104.2 0.6 collective-permute-start.6
  104.8 0.1 collective-permute-start.7
  104.9 1.5 %collective-permute-start.8 = (bf16[128,384]{1,0:T(8,128)(2,1)S(1)}, bf16[128,384]{1,0:T(8,128)(2,1)S(1)}, u32[]{:S(2)}, u32[]{:S(2)}) collective-permute-start(bf16[128,384]{1,0:T(8,128)(2,1)S(1)} %get-tuple-element.29), channel_id=1, source_target_pairs={{0,3},{1,2},{2,1},{3,0},{4,7},{5,6},{6,5},{7,4},{8,11},{9,10},{10,... | collective-permute-start | bytes 294920 | tf_op jit(solution)/shard_map/ppermute | solution.py:140
  106.4 0.0 collective-permute-done.9
  106.4 3.5 %collective-permute-done.6 = bf16[128,384]{1,0:T(8,128)(2,1)S(1)} collective-permute-done((bf16[128,384]{1,0:T(8,128)(2,1)S(1)}, bf16[128,384]{1,0:T(8,128)(2,1)S(1)}, u32[]{:S(2)}, u32[]{:S(2)}) %collective-permute-start.6) | collective-permute-done | bytes 98336 | tf_op jit(solution)/shard_map/ppermute | solution.py:140
  109.9 0.0 collective-permute-done.7
  109.9 1.0 collective-permute-done.8
  110.9 0.0 collective-permute-done.10
  110.9 4.6 %fusion.8 = bf16[128,3072]{1,0:T(8,128)(2,1)} fusion(bf16[384,3072]{1,0:T(8,128)(2,1)S(1)} %collective-permute-done.10, bf16[384,3072]{1,0:T(8,128)(2,1)} %collective-permute-done.9, bf16[384,3072]{1,0:T(8,128)(2,1)} %collective-permute-done, bf16[384,3072]{1,0:T(8,128)(2,1)} %param.13, bf16[128,384]{1,0:T(8,128)(2,1)S(1)} %collective-permute-done.8, ...), kind=kOutput, calls=%fused_computation.9 | convolution fusion | flops 1247674368 | bytes 10616832 | tf_op jit(solution)/shard_map/dot_general | solution.py:270
  (12 shorter events, 0.1 us)
Async XLA Ops:
  0.0 42.4 %copy-start = (bf16[3072,384]{1,0:T(8,128)(2,1)S(1)}, bf16[3072,384]{1,0:T(8,128)(2,1)}, u32[]{:S(2)}) copy-start(bf16[3072,384]{1,0:T(8,128)(2,1)} %param.11) | copy-start | bytes 7077892
  0.0 7.1 %copy-start.1 = (bf16[128,3072]{1,0:T(8,128)(2,1)S(1)}, bf16[128,3072]{1,0:T(8,128)(2,1)}, u32[]{:S(2)}) copy-start(bf16[128,3072]{1,0:T(8,128)(2,1)} %param.9) | copy-start | bytes 2359300
  0.0 7.3 %copy-start.3 = (bf16[3072]{0:T(1024)(128)(2,1)S(1)}, bf16[3072]{0:T(1024)(128)(2,1)}, u32[]{:S(2)}) copy-start(bf16[3072]{0:T(1024)(128)(2,1)} %param.10) | copy-start | bytes 18436
  9.4 11.1 %copy-start.4 = (s32[8]{0:T(128)S(1)}, s32[8]{0:T(128)}, u32[]{:S(2)}) copy-start(s32[8]{0:T(128)} %param.15) | copy-start | bytes 100
  10.8 21.7 %collective-permute-start.1 = (bf16[128,3072]{1,0:T(8,128)(2,1)}, bf16[128,3072]{1,0:T(8,128)(2,1)}, u32[]{:S(2)}, u32[]{:S(2)}) collective-permute-start(bf16[128,3072]{1,0:T(8,128)(2,1)} %get-tuple-element.22), channel_id=1, source_target_pairs={{0,2},{1,3},{2,0},{3,1},{4,6},{5,7},{6,4},{7,5},{8,10},{9,11},{10,... | collective-permute-start | bytes 2359304 | tf_op jit(solution)/shard_map/ppermute | solution.py:140
  13.8 53.9 %all-to-all-start = ((bf16[64,128,128]{2,1,0:T(8,128)(2,1)}), bf16[64,128,128]{2,1,0:T(8,128)(2,1)}, u32[]{:S(2)}, u32[]{:S(2)}) async-start(bf16[64,128,128]{2,1,0:T(8,128)(2,1)} %gather_fusion), calls=%async_computation | async-start | bytes 4194304 | tf_op jit(solution)/shard_map/all_to_all | solution.py:190
  19.6 18.0 %copy-start.2 = (bf16[3072,128]{1,0:T(8,128)(2,1)S(1)}, bf16[3072,128]{1,0:T(8,128)(2,1)}, u32[]{:S(2)}) copy-start(bf16[3072,128]{1,0:T(8,128)(2,1)} %param.12) | copy-start | bytes 2359300
  19.6 15.0 %collective-permute-start.2 = (bf16[128,3072]{1,0:T(8,128)(2,1)}, bf16[128,3072]{1,0:T(8,128)(2,1)}, u32[]{:S(2)}, u32[]{:S(2)}) collective-permute-start(bf16[128,3072]{1,0:T(8,128)(2,1)} %get-tuple-element.22), channel_id=1, source_target_pairs={{0,1},{1,0},{2,3},{3,2},{4,5},{5,4},{6,7},{7,6},{8,9},{9,8},{10,11... | collective-permute-start | bytes 2359304 | tf_op jit(solution)/shard_map/ppermute | solution.py:140
  19.7 83.2 %collective-permute-start = (bf16[384,3072]{1,0:T(8,128)(2,1)}, bf16[384,3072]{1,0:T(8,128)(2,1)}, u32[]{:S(2)}, u32[]{:S(2)}) collective-permute-start(bf16[384,3072]{1,0:T(8,128)(2,1)} %param.13), channel_id=1, source_target_pairs={{0,2},{1,3},{2,0},{3,1},{4,6},{5,7},{6,4},{7,5},{8,10},{9,11},{10,... | collective-permute-start | bytes 7077896 | tf_op jit(solution)/shard_map/ppermute | solution.py:140
  20.3 86.2 %collective-permute-start.9 = (bf16[384,3072]{1,0:T(8,128)(2,1)}, bf16[384,3072]{1,0:T(8,128)(2,1)}, u32[]{:S(2)}, u32[]{:S(2)}) collective-permute-start(bf16[384,3072]{1,0:T(8,128)(2,1)} %param.13), channel_id=1, source_target_pairs={{0,1},{1,0},{2,3},{3,2},{4,5},{5,4},{6,7},{7,6},{8,9},{9,8},{10,11... | collective-permute-start | bytes 7077896 | tf_op jit(solution)/shard_map/ppermute | solution.py:140
  32.5 4.2 %collective-permute-start.3 = (bf16[128,3072]{1,0:T(8,128)(2,1)}, bf16[128,3072]{1,0:T(8,128)(2,1)S(1)}, u32[]{:S(2)}, u32[]{:S(2)}) collective-permute-start(bf16[128,3072]{1,0:T(8,128)(2,1)} %collective-permute-done.1), channel_id=1, source_target_pairs={{0,1},{1,0},{2,3},{3,2},{4,5},{5,4},{6,7},{7,6},{8,9},{9,8},{10,11... | collective-permute-start | bytes 2359304 | tf_op jit(solution)/shard_map/ppermute | solution.py:140
  41.8 4.0 %collective-permute-start.4 = (bf16[512,128]{1,0:T(8,128)(2,1)S(1)}, bf16[512,128]{1,0:T(8,128)(2,1)S(1)}, u32[]{:S(2)}, u32[]{:S(2)}) collective-permute-start(bf16[512,128]{1,0:T(8,128)(2,1)S(1)} %fusion.28), channel_id=1, source_target_pairs={{0,1},{1,0},{2,3},{3,2},{4,5},{5,4},{6,7},{7,6},{8,9},{9,8},{10,11... | collective-permute-start | bytes 393224 | tf_op jit(solution)/shard_map/ppermute | solution.py:22
  67.7 4.5 %collective-permute-start.5 = (bf16[64,128,128]{2,1,0:T(8,128)(2,1)}, bf16[64,128,128]{2,1,0:T(8,128)(2,1)}, u32[]{:S(2)}, u32[]{:S(2)}) collective-permute-start(bf16[64,128,128]{2,1,0:T(8,128)(2,1)} %all-to-all-done), channel_id=1, source_target_pairs={{0,1},{1,0},{2,3},{3,2},{4,5},{5,4},{6,7},{7,6},{8,9},{9,8},{10,11... | collective-permute-start | bytes 6291464 | tf_op jit(solution)/shard_map/ppermute | solution.py:140
  102.9 8.0 %collective-permute-start.10 = (bf16[384,3072]{1,0:T(8,128)(2,1)}, bf16[384,3072]{1,0:T(8,128)(2,1)S(1)}, u32[]{:S(2)}, u32[]{:S(2)}) collective-permute-start(bf16[384,3072]{1,0:T(8,128)(2,1)} %collective-permute-done), channel_id=1, source_target_pairs={{0,1},{1,0},{2,3},{3,2},{4,5},{5,4},{6,7},{7,6},{8,9},{9,8},{10,11... | collective-permute-start | bytes 7077896 | tf_op jit(solution)/shard_map/ppermute | solution.py:140
  104.2 5.7 %collective-permute-start.6 = (bf16[128,384]{1,0:T(8,128)(2,1)S(1)}, bf16[128,384]{1,0:T(8,128)(2,1)S(1)}, u32[]{:S(2)}, u32[]{:S(2)}) collective-permute-start(bf16[128,384]{1,0:T(8,128)(2,1)S(1)} %get-tuple-element.31), channel_id=1, source_target_pairs={{0,2},{1,3},{2,0},{3,1},{4,6},{5,7},{6,4},{7,5},{8,10},{9,11},{10,... | collective-permute-start | bytes 294920 | tf_op jit(solution)/shard_map/ppermute | solution.py:140
  104.8 5.1 %collective-permute-start.7 = (bf16[128,384]{1,0:T(8,128)(2,1)S(1)}, bf16[128,384]{1,0:T(8,128)(2,1)S(1)}, u32[]{:S(2)}, u32[]{:S(2)}) collective-permute-start(bf16[128,384]{1,0:T(8,128)(2,1)S(1)} %get-tuple-element.30), channel_id=1, source_target_pairs={{0,1},{1,0},{2,3},{3,2},{4,5},{5,4},{6,7},{7,6},{8,9},{9,8},{10,11... | collective-permute-start | bytes 294920 | tf_op jit(solution)/shard_map/ppermute | solution.py:140
  104.9 6.0 %collective-permute-start.8 = (bf16[128,384]{1,0:T(8,128)(2,1)S(1)}, bf16[128,384]{1,0:T(8,128)(2,1)S(1)}, u32[]{:S(2)}, u32[]{:S(2)}) collective-permute-start(bf16[128,384]{1,0:T(8,128)(2,1)S(1)} %get-tuple-element.29), channel_id=1, source_target_pairs={{0,3},{1,2},{2,1},{3,0},{4,7},{5,6},{6,5},{7,4},{8,11},{9,10},{10,... | collective-permute-start | bytes 294920 | tf_op jit(solution)/shard_map/ppermute | solution.py:140

commit v10 on v9

--- a/solution.py
+++ b/solution.py
@@ -24,7 +24,7 @@
 
 def attend_kernel(
     n_cache, tk, scale, part_ref, q_ref, mine_hbm, other_hbm, nk_hbm, nv_hbm, bias_ref,
-    o_ref, k_scr, v_scr, s_scr, sems,
+    row_ref, key_ref, o_ref, k_scr, v_scr, s_scr, sems,
 ):
     bq, head_dim = q_ref.shape
     total = k_scr.shape[0]
@@ -53,8 +53,6 @@
             load(other_hbm, mine_hbm)
 
     q = q_ref[...]
-    row = lax.broadcasted_iota(jnp.int32, (bq, tk), 0)
-    lane = lax.broadcasted_iota(jnp.int32, (bq, tk), 1)
 
     def scores(c, top, causal):
         start = pl.multiple_of(c * tk, tk)
@@ -62,7 +60,7 @@
         s = lax.dot_general(q, keys, (((1,), (1,)), ((), ())), preferred_element_type=jnp.float32)
         s = s * scale + bias_ref[:, pl.ds(start, tk)]
         if causal:
-            s = jnp.where(start - n_cache + lane <= row, s, -jnp.inf)
+            s = jnp.where(key_ref[:, pl.ds(start - n_cache, tk)] <= row_ref[...], s, -jnp.inf)
         s_scr[:, pl.ds(start, tk)] = s
         for g in range(groups):
             top = jnp.maximum(top, s[:, g * 128:(g + 1) * 128])
@@ -93,7 +91,7 @@
     o_ref[...] = acc.astype(o_ref.dtype)
 
 
-def attend(queries, mine, other, new_keys, new_values, part, bias):
+def attend(queries, mine, other, new_keys, new_values, part, bias, true_row):
     rows, width = queries.shape
     n_cache, head_dim = mine.shape
     total = n_cache + new_keys.shape[0]
@@ -116,6 +114,8 @@
             any_spec,
             any_spec,
             pl.BlockSpec((1, total), lambda h, p: (0, 0)),
+            pl.BlockSpec((rows, 1), lambda h, p: (0, 0)),
+            pl.BlockSpec((1, rows), lambda h, p: (0, 0)),
         ],
         out_specs=pl.BlockSpec((rows, head_dim), lambda h, p: (0, h)),
         scratch_shapes=[
@@ -132,7 +132,10 @@
         compiler_params=pltpu.CompilerParams(dimension_semantics=("arbitrary",)),
         cost_estimate=cost,
         name="paged_prefill_attention",
-    )(part.reshape(1).astype(jnp.int32), queries, mine, other, new_keys, new_values, bias)
+    )(
+        part.reshape(1).astype(jnp.int32), queries, mine, other, new_keys, new_values, bias,
+        true_row.reshape(rows, 1), true_row.reshape(1, rows),
+    )
 
 
 def exchange(value, axis, mask):
@@ -206,15 +209,15 @@
         jnp.bfloat16
     )
     rows_in = [normalized_input]
-    masks = [0]
+    row_masks = [0]
     stride = head_number // 2
     while stride >= 1:
         rows_in = rows_in + [exchange(p, "head", stride) for p in rows_in]
-        masks = masks + [m ^ stride for m in masks]
+        row_masks = row_masks + [m ^ stride for m in row_masks]
         stride //= 2
-    piece = jnp.zeros((block_rows, normalized_input.shape[1]), normalized_input.dtype)
-    for p, m in zip(rows_in, masks):
-        piece = lax.dynamic_update_slice_in_dim(piece, p, (current_head ^ m) * local_rows, 0)
+    piece = jnp.concatenate(rows_in, 0)
+    within_rows = jnp.arange(local_rows, dtype=jnp.int32)
+    true_row = jnp.concatenate([(current_head ^ m) * local_rows + within_rows for m in row_masks])
     held_w = [w_out]
     masks = [0]
     stride = head_number // 2
@@ -226,9 +229,8 @@
     kv_part = jnp.dot(piece, key_value_weight, preferred_element_type=jnp.float32)
     projected = jnp.concatenate([q_part, kv_part], 1)
     q_width = group_heads * head_dim
-    row_ids = jnp.arange(block_rows, dtype=jnp.int32)
     my_lengths = lax.dynamic_slice_in_dim(cache_lengths, me_dp * REQ_DEV, REQ_DEV, 0)
-    positions = my_lengths[row_ids // NEWTOK] + row_ids % NEWTOK
+    positions = my_lengths[true_row // NEWTOK] + true_row % NEWTOK
     queries = rotate(
         projected[:, :q_width].reshape(block_rows, group_heads, head_dim), positions
     ).astype(jnp.bfloat16)
@@ -237,11 +239,15 @@
     turned = rotate(own_part[:, None, :], positions)[:, 0]
     own_ready = jnp.where(holds_keys, turned, own_part).astype(jnp.bfloat16)
     partner_ready = from_partner(own_ready, "head", 0)
+    partner_blocks = [row_masks.index(m ^ 1) for m in row_masks]
+    partner_ready = jnp.concatenate(
+        [partner_ready[j * local_rows:(j + 1) * local_rows] for j in partner_blocks], 0
+    )
     new_keys = jnp.where(holds_keys, own_ready, partner_ready)
     new_values = jnp.where(holds_keys, partner_ready, own_ready)
     mask_rows = lax.dynamic_slice_in_dim(token_mask, me_dp * block_rows, block_rows, 0)
     cache_ok = (has_page[:, 0, :, None] & (key_pos[:, 0] < my_lengths[0])).reshape(-1)
-    key_ok = jnp.concatenate([cache_ok, mask_rows == 1])
+    key_ok = jnp.concatenate([cache_ok, jnp.take(mask_rows, true_row) == 1])
     bias = jnp.where(key_ok, 0.0, -jnp.inf).astype(jnp.float32)
     queries = queries[0:NEWTOK].reshape(NEWTOK, group_heads * head_dim)
     received, queries, new_keys, new_values = lax.optimization_barrier(
@@ -256,6 +262,7 @@
         new_values,
         part,
         bias.reshape(1, -1),
+        true_row,
     )
     late_w, pieces = lax.optimization_barrier((held_w[1:], pieces))
     held_w = held_w[:1] + list(late_w)
@@ -264,7 +271,8 @@
     held_w = jnp.concatenate(held_w, 0)
     columns = []
     for m in masks:
-        block = lax.dynamic_slice_in_dim(pieces, (current_head ^ m) * local_rows, local_rows, 0)
+        k = row_masks.index(m)
+        block = pieces[k * local_rows:(k + 1) * local_rows]
         columns.append(block if m == 0 else exchange(block, "head", m))
     ordered = jnp.concatenate(columns, 1)
     out = jnp.dot(ordered, held_w, preferred_element_type=jnp.float32)

time: 116 us -> 116 us (level)
  waiting for transfers between devices: 36.5 us -> 39.6 us
  local copies, waits for them, and re-layouts: 14.8 us -> 12.9 us
    dynamic_update_slice x3 -> x0, local copies, waits for them, and re-layouts: 5.09 us -> none  [body(): lax.dynamic_update_slice_in_dim(piece, p, (current_head ^ m) * local_rows...]
    gather x0 -> x1, local copies, waits for them, and re-layouts: none -> 3.49 us  [body(): key_ok = jnp.concatenate([cache_ok, jnp.take(mask_rows, true_row) == 1])]
    all_to_all x1, waiting for transfers between devices: 21.1 us -> 23.2 us  [body(): lax.all_to_all(outgoing, 'dp', split_axis=0, concat_axis=0, tiled=True)]
    broadcast_in_dim x1 -> x0, local copies, waits for them, and re-layouts: 2.02 us -> none  [body(): jnp.zeros((block_rows, normalized_input.shape[1]), normalized_input.dtype)]
    dynamic_update_slice x1 -> x0, other arithmetic: 1.46 us -> none  [body(): lax.dynamic_update_slice_in_dim(piece, p, (current_head ^ m) * local_rows...]
  transfers between devices with their start and end apart: 12 -> 12, of which waited for: 5 -> 5; matrix products, arithmetic and copies ran while one was open for 17% -> 16% of each run, Pallas kernels for 27% -> 27%
where the time goes in v10:
time: 116 us
  waiting for transfers between devices  39.6 us (34%)
  Pallas kernels  30.8 us (27%)
  local copies, waits for them, and re-layouts  12.9 us (11%)
  starting transfers between devices  12.5 us (11%)
  matrix products  10.4 us (9%)
  other arithmetic  9.61 us (8%)
    pallas_call x1, Pallas kernels, attend(): pl.pallas_call(lambda *refs: attend_kernel(n_cache, tk, scale, *refs), ou...  30.8 us
    all_to_all x1, waiting for transfers between devices, body(): lax.all_to_all(outgoing, 'dp', split_axis=0, concat_axis=0, tiled=True)  23.2 us
    ppermute x10, waiting for transfers between devices, exchange(): return lax.ppermute(value, axis, pairs)  16.4 us
    all_to_all x1, starting transfers between devices, body(): lax.all_to_all(outgoing, 'dp', split_axis=0, concat_axis=0, tiled=True)  6.03 us
    ppermute x10, starting transfers between devices, exchange(): return lax.ppermute(value, axis, pairs)  5.91 us
    gather x1, local copies, waits for them, and re-layouts, body(): outgoing = kv_pool[local_page.reshape(-1), key_value_head, part]  5.06 us
    dot_general x1, matrix products, body(): out = jnp.dot(ordered, held_w, preferred_element_type=jnp.float32)  4.6 us
    gather x1, local copies, waits for them, and re-layouts, body(): key_ok = jnp.concatenate([cache_ok, jnp.take(mask_rows, true_row) == 1])  3.49 us
  transfers between devices with their start and end apart: 12, of which 5 were waited for; matrix products, arithmetic and copies ran while one was open for 16% of the time, Pallas kernels for 27%

profile of v10, /device:TPU:0, one launch (start us, length us, event | category | flops | bytes accessed | tf_op | source)
XLA Modules:
  0.0 116.0 jit_solution(5928134407608293342)
XLA Ops:
  0.0 0.0 copy-start
  0.0 0.0 copy-start.1
  0.0 0.9 broadcast_compare_fusion.1
  0.9 0.2 reduce_window_sum.22
  1.1 0.7 add_select_fusion.1
  1.8 0.2 select_reduce_fusion.1
  2.0 0.1 reshape.528
  2.1 0.7 convert_element_type.49
  2.8 5.1 %gather_fusion = bf16[64,128,128]{2,1,0:T(8,128)(2,1)} fusion(bf16[48,2,2,128,128]{4,3,2,1,0:T(8,128)(2,1)} %param.14, s32[64]{0:T(128)S(1)} %fusion.45), kind=kCustom, calls=%fused_computation | custom fusion | bytes 4195072 | tf_op jit(solution)/shard_map/gather | solution.py:191
  7.8 0.0 copy-done.1
  7.8 0.0 copy-start.3
  7.8 0.2 fusion.11
  8.1 1.2 fusion.13
  9.3 3.0 %collective-permute-start.1 = (bf16[128,3072]{1,0:T(8,128)(2,1)}, bf16[128,3072]{1,0:T(8,128)(2,1)}, u32[]{:S(2)}, u32[]{:S(2)}) collective-permute-start(bf16[128,3072]{1,0:T(8,128)(2,1)} %fusion.13), channel_id=1, source_target_pairs={{0,2},{1,3},{2,0},{3,1},{4,6},{5,7},{6,4},{7,5},{8,10},{9,11},{10,... | collective-permute-start | bytes 2359304 | tf_op jit(solution)/shard_map/ppermute | solution.py:143
  12.2 0.0 collective-permute-start.2
  12.2 0.0 collective-permute-start
  12.3 0.5 collective-permute-start.9
  12.7 6.0 %all-to-all-start = ((bf16[64,128,128]{2,1,0:T(8,128)(2,1)}), bf16[64,128,128]{2,1,0:T(8,128)(2,1)}, u32[]{:S(2)}, u32[]{:S(2)}) async-start(bf16[64,128,128]{2,1,0:T(8,128)(2,1)} %gather_fusion), calls=%async_computation | async-start | bytes 4194304 | tf_op jit(solution)/shard_map/all_to_all | solution.py:193
  18.8 0.0 copy-done.3
  18.8 0.6 dynamic_slice.11
  19.4 0.2 reduce_window_sum.23
  19.6 0.8 dynamic_slice.14
  20.4 10.5 %collective-permute-done.1 = bf16[128,3072]{1,0:T(8,128)(2,1)} collective-permute-done((bf16[128,3072]{1,0:T(8,128)(2,1)}, bf16[128,3072]{1,0:T(8,128)(2,1)}, u32[]{:S(2)}, u32[]{:S(2)}) %collective-permute-start.1) | collective-permute-done | bytes 786464 | tf_op jit(solution)/shard_map/ppermute | solution.py:143
  30.9 0.0 collective-permute-start.3
  30.9 3.5 %gather_fusion.1 = s32[512]{0:T(512)S(1)} fusion(s32[512]{0:T(512)S(1)} %dynamic_slice.14, s32[1024]{0:T(1024)S(1)} %pad_clamp_fusion), kind=kCustom, calls=%fused_computation.1 | custom fusion | bytes 6144 | tf_op jit(solution)/shard_map/jit(_take)/gather | solution.py:250
  34.5 0.6 pad_add_fusion
  35.1 0.0 copy-start.2
  35.1 0.5 multiply_cosine_fusion.1
  35.7 0.0 collective-permute-done.2
  35.7 0.0 collective-permute-done.3
  35.7 2.8 %fusion.14 = f32[512,128]{1,0:T(8,128)S(1)} fusion(bf16[3072,128]{1,0:T(8,128)(2,1)} %param.12, bf16[128,3072]{1,0:T(8,128)(2,1)S(1)} %collective-permute-done.3, bf16[128,3072]{1,0:T(8,128)(2,1)} %collective-permute-done.2, bf16[128,3072]{1,0:T(8,128)(2,1)} %collective-permute-done.1, bf16[128,3072]{1,0:T(8,128)(2,1)} %fusion.13), kind=kOutput, calls=%fused_computation.17 | convolution fusion | flops 415236096 | bytes 4194304 | tf_op jit(solution)/shard_map/dot_general | solution.py:229
  38.5 1.2 %fusion.27 = (bf16[512,1,64]{2,0,1:T(8,128)(2,1)S(1)}, bf16[512,1,64]{2,0,1:T(8,128)(2,1)S(1)}) fusion(f32[512,1,128]{2,0,1:T(8,128)S(1)} %bitcast.30, f32[64]{0:T(128)S(1)} %multiply_exponential_fusion, f32[512]{0:T(512)S(1)} %get-tuple-element.39), kind=kLoop, calls=%fused_computation.35 | loop fusion | flops 294912 | bytes 395520 | tf_op jit(solution)/shard_map/sub | solution.py:156
  39.7 0.1 fusion.30
  39.8 0.6 collective-permute-start.4
  40.4 0.0 copy-done
  40.4 3.0 %fusion.15 = f32[512,384]{0,1:T(8,128)S(1)} fusion(bf16[3072,384]{1,0:T(8,128)(2,1)S(1)} %copy-done, bf16[128,3072]{1,0:T(8,128)(2,1)S(1)} %collective-permute-done.3, bf16[128,3072]{1,0:T(8,128)(2,1)} %collective-permute-done.2, bf16[128,3072]{1,0:T(8,128)(2,1)} %collective-permute-done.1, bf16[128,3072]{1,0:T(8,128)(2,1)} %fusion.13), kind=kOutput, calls=%fused_computation.18 | convolution fusion | flops 1220542464 | bytes 6291456 | tf_op jit(solution)/shard_map/dot_general | solution.py:228
  43.4 0.1 subtract_convert_fusion
  43.6 0.0 collective-permute-done.4
  43.7 0.7 broadcast_select_fusion
  44.4 23.2 %all-to-all-done = bf16[64,128,128]{2,1,0:T(8,128)(2,1)} async-done(((bf16[64,128,128]{2,1,0:T(8,128)(2,1)}), bf16[64,128,128]{2,1,0:T(8,128)(2,1)}, u32[]{:S(2)}, u32[]{:S(2)}) %all-to-all-start) | async-done | bytes 2097184 | tf_op jit(solution)/shard_map/all_to_all | solution.py:193
  67.6 0.0 collective-permute-start.5
  67.6 0.2 fusion.33
  67.8 0.2 select_reduce_fusion
  68.0 0.7 fusion.34
  68.8 0.0 copy-done.2
  68.8 0.9 copy.21.refs_7_
  69.6 0.7 add_select_fusion.refs_6_
  70.3 0.9 copy.20.refs_1_
  71.2 0.8 collective-permute-done.5
  72.1 30.8 %paged_prefill_attention.1 = bf16[512,384]{1,0:T(8,128)(2,1)} custom-call(s32[1]{0:T(128)} %bitcast.refs_0_, bf16[512,384]{1,0:T(8,128)(2,1)} %copy.20.refs_1_, bf16[8192,128]{1,0:T(8,128)(2,1)} %bitcast.7.refs_2_, bf16[8192,128]{1,0:T(8,128)(2,1)} %bitcast.8.refs_3_, bf16[512,128]{1,0:T(8,128)(2,1)} %get-tuple-element.17.refs_4_, ...), custom_call_target="tpu_custom_call" | custom-call | flops 6845104128 | bytes 5277696 | tf_op jit(solution)/shard_map/paged_prefill_attention/pallas_call | solution.py:128
  102.8 0.0 collective-permute-done
  102.9 0.2 collective-permute-start.10
  103.1 1.1 fusion.54
  104.1 1.6 %collective-permute-start.8 = (bf16[128,384]{1,0:T(8,128)(2,1)S(1)}, bf16[128,384]{1,0:T(8,128)(2,1)S(1)}, u32[]{:S(2)}, u32[]{:S(2)}) collective-permute-start(bf16[128,384]{1,0:T(8,128)(2,1)S(1)} %get-tuple-element.27), channel_id=1, source_target_pairs={{0,3},{1,2},{2,1},{3,0},{4,7},{5,6},{6,5},{7,4},{8,11},{9,10},{10,... | collective-permute-start | bytes 294920 | tf_op jit(solution)/shard_map/ppermute | solution.py:143
  105.7 0.2 collective-permute-start.7
  105.9 0.5 collective-permute-start.6
  106.4 0.0 collective-permute-done.9
  106.4 2.5 %collective-permute-done.8 = bf16[128,384]{1,0:T(8,128)(2,1)S(1)} collective-permute-done((bf16[128,384]{1,0:T(8,128)(2,1)S(1)}, bf16[128,384]{1,0:T(8,128)(2,1)S(1)}, u32[]{:S(2)}, u32[]{:S(2)}) %collective-permute-start.8) | collective-permute-done | bytes 98336 | tf_op jit(solution)/shard_map/ppermute | solution.py:143
  108.8 0.0 collective-permute-done.7
  108.9 2.6 %collective-permute-done.6 = bf16[128,384]{1,0:T(8,128)(2,1)S(1)} collective-permute-done((bf16[128,384]{1,0:T(8,128)(2,1)S(1)}, bf16[128,384]{1,0:T(8,128)(2,1)S(1)}, u32[]{:S(2)}, u32[]{:S(2)}) %collective-permute-start.6) | collective-permute-done | bytes 98336 | tf_op jit(solution)/shard_map/ppermute | solution.py:143
  111.4 0.0 collective-permute-done.10
  111.4 4.6 %fusion.8 = bf16[128,3072]{1,0:T(8,128)(2,1)} fusion(bf16[384,3072]{1,0:T(8,128)(2,1)S(1)} %collective-permute-done.10, bf16[384,3072]{1,0:T(8,128)(2,1)} %collective-permute-done.9, bf16[384,3072]{1,0:T(8,128)(2,1)} %collective-permute-done, bf16[384,3072]{1,0:T(8,128)(2,1)} %param.13, bf16[128,384]{1,0:T(8,128)(2,1)S(1)} %collective-permute-done.8, ...), kind=kOutput, calls=%fused_computation.10 | convolution fusion | flops 1247674368 | bytes 10616832 | tf_op jit(solution)/shard_map/dot_general | solution.py:278
  (18 shorter events, 0.2 us)
Async XLA Ops:
  0.0 40.4 %copy-start = (bf16[3072,384]{1,0:T(8,128)(2,1)S(1)}, bf16[3072,384]{1,0:T(8,128)(2,1)}, u32[]{:S(2)}) copy-start(bf16[3072,384]{1,0:T(8,128)(2,1)} %param.11) | copy-start | bytes 7077892
  0.0 7.8 %copy-start.1 = (bf16[128,3072]{1,0:T(8,128)(2,1)S(1)}, bf16[128,3072]{1,0:T(8,128)(2,1)}, u32[]{:S(2)}) copy-start(bf16[128,3072]{1,0:T(8,128)(2,1)} %param.9) | copy-start | bytes 2359300
  7.8 10.9 %copy-start.3 = (s32[8]{0:T(128)S(1)}, s32[8]{0:T(128)}, u32[]{:S(2)}) copy-start(s32[8]{0:T(128)} %param.15) | copy-start | bytes 100
  9.3 21.6 %collective-permute-start.1 = (bf16[128,3072]{1,0:T(8,128)(2,1)}, bf16[128,3072]{1,0:T(8,128)(2,1)}, u32[]{:S(2)}, u32[]{:S(2)}) collective-permute-start(bf16[128,3072]{1,0:T(8,128)(2,1)} %fusion.13), channel_id=1, source_target_pairs={{0,2},{1,3},{2,0},{3,1},{4,6},{5,7},{6,4},{7,5},{8,10},{9,11},{10,... | collective-permute-start | bytes 2359304 | tf_op jit(solution)/shard_map/ppermute | solution.py:143
  12.2 23.4 %collective-permute-start.2 = (bf16[128,3072]{1,0:T(8,128)(2,1)}, bf16[128,3072]{1,0:T(8,128)(2,1)}, u32[]{:S(2)}, u32[]{:S(2)}) collective-permute-start(bf16[128,3072]{1,0:T(8,128)(2,1)} %fusion.13), channel_id=1, source_target_pairs={{0,1},{1,0},{2,3},{3,2},{4,5},{5,4},{6,7},{7,6},{8,9},{9,8},{10,11... | collective-permute-start | bytes 2359304 | tf_op jit(solution)/shard_map/ppermute | solution.py:143
  12.2 90.6 %collective-permute-start = (bf16[384,3072]{1,0:T(8,128)(2,1)}, bf16[384,3072]{1,0:T(8,128)(2,1)}, u32[]{:S(2)}, u32[]{:S(2)}) collective-permute-start(bf16[384,3072]{1,0:T(8,128)(2,1)} %param.13), channel_id=1, source_target_pairs={{0,2},{1,3},{2,0},{3,1},{4,6},{5,7},{6,4},{7,5},{8,10},{9,11},{10,... | collective-permute-start | bytes 7077896 | tf_op jit(solution)/shard_map/ppermute | solution.py:143
  12.3 94.1 %collective-permute-start.9 = (bf16[384,3072]{1,0:T(8,128)(2,1)}, bf16[384,3072]{1,0:T(8,128)(2,1)}, u32[]{:S(2)}, u32[]{:S(2)}) collective-permute-start(bf16[384,3072]{1,0:T(8,128)(2,1)} %param.13), channel_id=1, source_target_pairs={{0,1},{1,0},{2,3},{3,2},{4,5},{5,4},{6,7},{7,6},{8,9},{9,8},{10,11... | collective-permute-start | bytes 7077896 | tf_op jit(solution)/shard_map/ppermute | solution.py:143
  12.7 54.8 %all-to-all-start = ((bf16[64,128,128]{2,1,0:T(8,128)(2,1)}), bf16[64,128,128]{2,1,0:T(8,128)(2,1)}, u32[]{:S(2)}, u32[]{:S(2)}) async-start(bf16[64,128,128]{2,1,0:T(8,128)(2,1)} %gather_fusion), calls=%async_computation | async-start | bytes 4194304 | tf_op jit(solution)/shard_map/all_to_all | solution.py:193
  30.9 4.8 %collective-permute-start.3 = (bf16[128,3072]{1,0:T(8,128)(2,1)}, bf16[128,3072]{1,0:T(8,128)(2,1)S(1)}, u32[]{:S(2)}, u32[]{:S(2)}) collective-permute-start(bf16[128,3072]{1,0:T(8,128)(2,1)} %collective-permute-done.1), channel_id=1, source_target_pairs={{0,1},{1,0},{2,3},{3,2},{4,5},{5,4},{6,7},{7,6},{8,9},{9,8},{10,11... | collective-permute-start | bytes 2359304 | tf_op jit(solution)/shard_map/ppermute | solution.py:143
  35.1 33.7 %copy-start.2 = (s32[512]{0:T(512)}, s32[512]{0:T(512)S(1)}, u32[]{:S(2)}) copy-start(s32[512]{0:T(512)S(1)} %get-tuple-element.38) | copy-start | bytes 6148
  39.8 3.8 %collective-permute-start.4 = (bf16[512,128]{1,0:T(8,128)(2,1)S(1)}, bf16[512,128]{1,0:T(8,128)(2,1)S(1)}, u32[]{:S(2)}, u32[]{:S(2)}) collective-permute-start(bf16[512,128]{1,0:T(8,128)(2,1)S(1)} %fusion.30), channel_id=1, source_target_pairs={{0,1},{1,0},{2,3},{3,2},{4,5},{5,4},{6,7},{7,6},{8,9},{9,8},{10,11... | collective-permute-start | bytes 393224 | tf_op jit(solution)/shard_map/ppermute | solution.py:22
  67.6 4.5 %collective-permute-start.5 = (bf16[64,128,128]{2,1,0:T(8,128)(2,1)}, bf16[64,128,128]{2,1,0:T(8,128)(2,1)}, u32[]{:S(2)}, u32[]{:S(2)}) collective-permute-start(bf16[64,128,128]{2,1,0:T(8,128)(2,1)} %all-to-all-done), channel_id=1, source_target_pairs={{0,1},{1,0},{2,3},{3,2},{4,5},{5,4},{6,7},{7,6},{8,9},{9,8},{10,11... | collective-permute-start | bytes 6291464 | tf_op jit(solution)/shard_map/ppermute | solution.py:143
  102.9 8.6 %collective-permute-start.10 = (bf16[384,3072]{1,0:T(8,128)(2,1)}, bf16[384,3072]{1,0:T(8,128)(2,1)S(1)}, u32[]{:S(2)}, u32[]{:S(2)}) collective-permute-start(bf16[384,3072]{1,0:T(8,128)(2,1)} %collective-permute-done), channel_id=1, source_target_pairs={{0,1},{1,0},{2,3},{3,2},{4,5},{5,4},{6,7},{7,6},{8,9},{9,8},{10,11... | collective-permute-start | bytes 7077896 | tf_op jit(solution)/shard_map/ppermute | solution.py:143
  104.1 4.7 %collective-permute-start.8 = (bf16[128,384]{1,0:T(8,128)(2,1)S(1)}, bf16[128,384]{1,0:T(8,128)(2,1)S(1)}, u32[]{:S(2)}, u32[]{:S(2)}) collective-permute-start(bf16[128,384]{1,0:T(8,128)(2,1)S(1)} %get-tuple-element.27), channel_id=1, source_target_pairs={{0,3},{1,2},{2,1},{3,0},{4,7},{5,6},{6,5},{7,4},{8,11},{9,10},{10,... | collective-permute-start | bytes 294920 | tf_op jit(solution)/shard_map/ppermute | solution.py:143
  105.7 3.1 %collective-permute-start.7 = (bf16[128,384]{1,0:T(8,128)(2,1)S(1)}, bf16[128,384]{1,0:T(8,128)(2,1)S(1)}, u32[]{:S(2)}, u32[]{:S(2)}) collective-permute-start(bf16[128,384]{1,0:T(8,128)(2,1)S(1)} %get-tuple-element.28), channel_id=1, source_target_pairs={{0,1},{1,0},{2,3},{3,2},{4,5},{5,4},{6,7},{7,6},{8,9},{9,8},{10,11... | collective-permute-start | bytes 294920 | tf_op jit(solution)/shard_map/ppermute | solution.py:143
  105.9 5.6 %collective-permute-start.6 = (bf16[128,384]{1,0:T(8,128)(2,1)S(1)}, bf16[128,384]{1,0:T(8,128)(2,1)S(1)}, u32[]{:S(2)}, u32[]{:S(2)}) collective-permute-start(bf16[128,384]{1,0:T(8,128)(2,1)S(1)} %get-tuple-element.29), channel_id=1, source_target_pairs={{0,2},{1,3},{2,0},{3,1},{4,6},{5,7},{6,4},{7,5},{8,10},{9,11},{10,... | collective-permute-start | bytes 294920 | tf_op jit(solution)/shard_map/ppermute | solution.py:143

commit v11 on v10

--- a/solution.py
+++ b/solution.py
@@ -238,6 +238,7 @@
     holds_keys = current_head % 2 == 0
     turned = rotate(own_part[:, None, :], positions)[:, 0]
     own_ready = jnp.where(holds_keys, turned, own_part).astype(jnp.bfloat16)
+    received, own_ready = lax.optimization_barrier((received, own_ready))
     partner_ready = from_partner(own_ready, "head", 0)
     partner_blocks = [row_masks.index(m ^ 1) for m in row_masks]
     partner_ready = jnp.concatenate(
@@ -250,9 +251,6 @@
     key_ok = jnp.concatenate([cache_ok, jnp.take(mask_rows, true_row) == 1])
     bias = jnp.where(key_ok, 0.0, -jnp.inf).astype(jnp.float32)
     queries = queries[0:NEWTOK].reshape(NEWTOK, group_heads * head_dim)
-    received, queries, new_keys, new_values = lax.optimization_barrier(
-        (received, queries, new_keys, new_values)
-    )
     other_half = exchange(received, "head", 1)
     pieces = attend(
         queries,

time: 116 us -> 115 us (level)
    all_to_all x1, waiting for transfers between devices: 23.2 us -> 19.4 us  [body(): lax.all_to_all(outgoing, 'dp', split_axis=0, concat_axis=0, tiled=True)]
    ppermute x10, waiting for transfers between devices: 16.4 us -> 19.2 us  [exchange(): return lax.ppermute(value, axis, pairs)]
    all_to_all x1, starting transfers between devices: 6.03 us -> 7.38 us  [body(): lax.all_to_all(outgoing, 'dp', split_axis=0, concat_axis=0, tiled=True)]
    ppermute x10, starting transfers between devices: 5.91 us -> 4.56 us  [exchange(): return lax.ppermute(value, axis, pairs)]
  transfers between devices with their start and end apart: 12 -> 12, of which waited for: 5 -> 5; matrix products, arithmetic and copies ran while one was open for 16% -> 18% of each run, Pallas kernels for 27% -> 27%
where the time goes in v11:
time: 115 us
  waiting for transfers between devices  38.7 us (34%)
  Pallas kernels  30.8 us (27%)
  local copies, waits for them, and re-layouts  12.9 us (11%)
  starting transfers between devices  12.5 us (11%)
  matrix products  10.4 us (9%)
  other arithmetic  8.91 us (8%)
    pallas_call x1, Pallas kernels, attend(): pl.pallas_call(lambda *refs: attend_kernel(n_cache, tk, scale, *refs), ou...  30.8 us
    all_to_all x1, waiting for transfers between devices, body(): lax.all_to_all(outgoing, 'dp', split_axis=0, concat_axis=0, tiled=True)  19.4 us
    ppermute x10, waiting for transfers between devices, exchange(): return lax.ppermute(value, axis, pairs)  19.2 us
    all_to_all x1, starting transfers between devices, body(): lax.all_to_all(outgoing, 'dp', split_axis=0, concat_axis=0, tiled=True)  7.38 us
    gather x1, local copies, waits for them, and re-layouts, body(): outgoing = kv_pool[local_page.reshape(-1), key_value_head, part]  5.06 us
    dot_general x1, matrix products, body(): out = jnp.dot(ordered, held_w, preferred_element_type=jnp.float32)  4.6 us
    ppermute x10, starting transfers between devices, exchange(): return lax.ppermute(value, axis, pairs)  4.56 us
    gather x1, local copies, waits for them, and re-layouts, body(): key_ok = jnp.concatenate([cache_ok, jnp.take(mask_rows, true_row) == 1])  3.48 us
  transfers between devices with their start and end apart: 12, of which 5 were waited for; matrix products, arithmetic and copies ran while one was open for 18% of the time, Pallas kernels for 27%

profile of v11, /device:TPU:0, one launch (start us, length us, event | category | flops | bytes accessed | tf_op | source)
XLA Modules:
  0.0 114.5 jit_solution(8473438137848617835)
XLA Ops:
  0.0 0.0 copy-start
  0.0 0.9 broadcast_compare_fusion.1
  0.9 0.2 reduce_window_sum.22
  1.1 0.7 add_select_fusion.1
  1.8 0.2 select_reduce_fusion.1
  2.0 0.1 reshape.528
  2.1 5.1 %gather_fusion = bf16[64,128,128]{2,1,0:T(8,128)(2,1)} fusion(bf16[48,2,2,128,128]{4,3,2,1,0:T(8,128)(2,1)} %param.14, s32[64]{0:T(128)S(1)} %fusion.45), kind=kCustom, calls=%fused_computation | custom fusion | bytes 4195072 | tf_op jit(solution)/shard_map/gather | solution.py:191
  7.1 0.0 copy-start.3
  7.1 0.0 copy-start.1
  7.1 7.4 %all-to-all-start = ((bf16[64,128,128]{2,1,0:T(8,128)(2,1)}), bf16[64,128,128]{2,1,0:T(8,128)(2,1)}, u32[]{:S(2)}, u32[]{:S(2)}) async-start(bf16[64,128,128]{2,1,0:T(8,128)(2,1)} %gather_fusion), calls=%async_computation | async-start | bytes 4194304 | tf_op jit(solution)/shard_map/all_to_all | solution.py:193
  14.5 0.0 copy-done.3
  14.5 0.0 copy-start.4
  14.6 0.0 copy-done.1
  14.6 0.2 fusion.11
  14.8 1.2 %fusion.13 = bf16[128,3072]{1,0:T(8,128)(2,1)} fusion(bf16[128,3072]{1,0:T(8,128)(2,1)S(1)} %copy-done.1, f32[3072]{0:T(1024)S(1)} %convert_element_type.49, f32[128]{0:T(128)S(1)} %add_rsqrt_fusion), kind=kLoop, calls=%fused_computation.16 | loop fusion | flops 1572864 | bytes 1585664 | tf_op jit(solution)/shard_map/convert_element_type | solution.py:208
  16.0 0.0 collective-permute-start.2
  16.0 1.5 %collective-permute-start.1 = (bf16[128,3072]{1,0:T(8,128)(2,1)}, bf16[128,3072]{1,0:T(8,128)(2,1)}, u32[]{:S(2)}, u32[]{:S(2)}) collective-permute-start(bf16[128,3072]{1,0:T(8,128)(2,1)} %fusion.13), channel_id=1, source_target_pairs={{0,2},{1,3},{2,0},{3,1},{4,6},{5,7},{6,4},{7,5},{8,10},{9,11},{10,... | collective-permute-start | bytes 2359304 | tf_op jit(solution)/shard_map/ppermute | solution.py:143
  17.5 0.5 collective-permute-start
  18.0 0.0 collective-permute-start.9
  18.1 0.2 reduce_window_sum.23
  18.3 0.8 dynamic_slice.14
  19.1 3.5 %gather_fusion.1 = s32[512]{0:T(512)S(1)} fusion(s32[512]{0:T(512)S(1)} %dynamic_slice.14, s32[1024]{0:T(1024)S(1)} %pad_clamp_fusion), kind=kCustom, calls=%fused_computation.1 | custom fusion | bytes 6144 | tf_op jit(solution)/shard_map/jit(_take)/gather | solution.py:251
  22.6 14.0 %collective-permute-done.1 = bf16[128,3072]{1,0:T(8,128)(2,1)} collective-permute-done((bf16[128,3072]{1,0:T(8,128)(2,1)}, bf16[128,3072]{1,0:T(8,128)(2,1)}, u32[]{:S(2)}, u32[]{:S(2)}) %collective-permute-start.1) | collective-permute-done | bytes 786464 | tf_op jit(solution)/shard_map/ppermute | solution.py:143
  36.6 0.0 collective-permute-start.3
  36.6 0.2 fusion.33
  36.9 0.0 copy-done.4
  36.9 0.6 dynamic_slice.11
  37.5 0.2 select_reduce_fusion
  37.7 0.7 fusion.34
  38.5 0.6 pad_add_fusion
  39.1 0.0 copy-start.2
  39.1 0.0 collective-permute-done.2
  39.1 0.1 collective-permute-done.3
  39.3 2.8 %fusion.14 = f32[512,128]{1,0:T(8,128)S(1)} fusion(bf16[3072,128]{1,0:T(8,128)(2,1)} %param.12, bf16[128,3072]{1,0:T(8,128)(2,1)} %collective-permute-done.3, bf16[128,3072]{1,0:T(8,128)(2,1)S(1)} %collective-permute-done.2, bf16[128,3072]{1,0:T(8,128)(2,1)} %collective-permute-done.1, bf16[128,3072]{1,0:T(8,128)(2,1)} %fusion.13), kind=kOutput, calls=%fused_computation.17 | convolution fusion | flops 415236096 | bytes 4194304 | tf_op jit(solution)/shard_map/dot_general | solution.py:229
  42.1 1.2 %fusion.27 = (bf16[512,1,64]{2,0,1:T(8,128)(2,1)S(1)}, bf16[512,1,64]{2,0,1:T(8,128)(2,1)S(1)}) fusion(f32[512,1,128]{2,0,1:T(8,128)S(1)} %bitcast.30, f32[64]{0:T(128)S(1)} %multiply_exponential_fusion, f32[512]{0:T(512)S(1)} %get-tuple-element.35), kind=kLoop, calls=%fused_computation.35 | loop fusion | flops 294912 | bytes 395520 | tf_op jit(solution)/shard_map/sub | solution.py:156
  43.3 0.1 fusion.30
  43.4 19.4 %all-to-all-done = bf16[64,128,128]{2,1,0:T(8,128)(2,1)} async-done(((bf16[64,128,128]{2,1,0:T(8,128)(2,1)}), bf16[64,128,128]{2,1,0:T(8,128)(2,1)}, u32[]{:S(2)}, u32[]{:S(2)}) %all-to-all-start) | async-done | bytes 2097184 | tf_op jit(solution)/shard_map/all_to_all | solution.py:193
  62.9 0.0 collective-permute-start.4
  62.9 0.7 add_select_fusion.refs_6_
  63.5 0.0 copy-done.2
  63.5 0.9 copy.21.refs_7_
  64.4 0.5 multiply_cosine_fusion.1
  65.0 0.0 copy-done
  65.0 3.0 %fusion.15 = f32[512,384]{0,1:T(8,128)S(1)} fusion(bf16[3072,384]{1,0:T(8,128)(2,1)S(1)} %copy-done, bf16[128,3072]{1,0:T(8,128)(2,1)} %collective-permute-done.3, bf16[128,3072]{1,0:T(8,128)(2,1)S(1)} %collective-permute-done.2, bf16[128,3072]{1,0:T(8,128)(2,1)} %collective-permute-done.1, bf16[128,3072]{1,0:T(8,128)(2,1)} %fusion.13), kind=kOutput, calls=%fused_computation.18 | convolution fusion | flops 1220542464 | bytes 6291456 | tf_op jit(solution)/shard_map/dot_general | solution.py:228
  68.0 0.6 collective-permute-start.5
  68.6 0.1 subtract_convert_fusion
  68.8 0.9 copy.20.refs_1_
  69.7 0.0 collective-permute-done.5
  69.7 0.7 broadcast_select_fusion
  70.4 0.0 collective-permute-done.4
  70.4 30.8 %paged_prefill_attention.1 = bf16[512,384]{1,0:T(8,128)(2,1)} custom-call(s32[1]{0:T(128)} %bitcast.refs_0_, bf16[512,384]{1,0:T(8,128)(2,1)} %copy.20.refs_1_, bf16[8192,128]{1,0:T(8,128)(2,1)} %bitcast.7.refs_2_, bf16[8192,128]{1,0:T(8,128)(2,1)} %bitcast.8.refs_3_, bf16[512,128]{1,0:T(8,128)(2,1)} %get-tuple-element.29.refs_4_, ...), custom_call_target="tpu_custom_call" | custom-call | flops 6845104128 | bytes 5277696 | tf_op jit(solution)/shard_map/paged_prefill_attention/pallas_call | solution.py:128
  101.2 0.0 collective-permute-done
  101.2 0.3 collective-permute-start.10
  101.6 1.1 fusion.54
  102.6 1.4 %collective-permute-start.8 = (bf16[128,384]{1,0:T(8,128)(2,1)S(1)}, bf16[128,384]{1,0:T(8,128)(2,1)S(1)}, u32[]{:S(2)}, u32[]{:S(2)}) collective-permute-start(bf16[128,384]{1,0:T(8,128)(2,1)S(1)} %get-tuple-element.23), channel_id=1, source_target_pairs={{0,3},{1,2},{2,1},{3,0},{4,7},{5,6},{6,5},{7,4},{8,11},{9,10},{10,... | collective-permute-start | bytes 294920 | tf_op jit(solution)/shard_map/ppermute | solution.py:143
  104.1 0.2 collective-permute-start.7
  104.3 0.5 collective-permute-start.6
  104.8 0.0 collective-permute-done.9
  104.8 2.6 %collective-permute-done.8 = bf16[128,384]{1,0:T(8,128)(2,1)S(1)} collective-permute-done((bf16[128,384]{1,0:T(8,128)(2,1)S(1)}, bf16[128,384]{1,0:T(8,128)(2,1)S(1)}, u32[]{:S(2)}, u32[]{:S(2)}) %collective-permute-start.8) | collective-permute-done | bytes 98336 | tf_op jit(solution)/shard_map/ppermute | solution.py:143
  107.4 0.0 collective-permute-done.7
  107.4 2.5 %collective-permute-done.6 = bf16[128,384]{1,0:T(8,128)(2,1)S(1)} collective-permute-done((bf16[128,384]{1,0:T(8,128)(2,1)S(1)}, bf16[128,384]{1,0:T(8,128)(2,1)S(1)}, u32[]{:S(2)}, u32[]{:S(2)}) %collective-permute-start.6) | collective-permute-done | bytes 98336 | tf_op jit(solution)/shard_map/ppermute | solution.py:143
  109.9 0.0 collective-permute-done.10
  109.9 4.6 %fusion.8 = bf16[128,3072]{1,0:T(8,128)(2,1)} fusion(bf16[384,3072]{1,0:T(8,128)(2,1)S(1)} %collective-permute-done.10, bf16[384,3072]{1,0:T(8,128)(2,1)} %collective-permute-done.9, bf16[384,3072]{1,0:T(8,128)(2,1)} %collective-permute-done, bf16[384,3072]{1,0:T(8,128)(2,1)} %param.13, bf16[128,384]{1,0:T(8,128)(2,1)S(1)} %collective-permute-done.8, ...), kind=kOutput, calls=%fused_computation.10 | convolution fusion | flops 1247674368 | bytes 10616832 | tf_op jit(solution)/shard_map/dot_general | solution.py:276
  (19 shorter events, 0.2 us)
Async XLA Ops:
  0.0 65.0 %copy-start = (bf16[3072,384]{1,0:T(8,128)(2,1)S(1)}, bf16[3072,384]{1,0:T(8,128)(2,1)}, u32[]{:S(2)}) copy-start(bf16[3072,384]{1,0:T(8,128)(2,1)} %param.11) | copy-start | bytes 7077892
  7.1 7.4 %copy-start.3 = (bf16[3072]{0:T(1024)(128)(2,1)S(1)}, bf16[3072]{0:T(1024)(128)(2,1)}, u32[]{:S(2)}) copy-start(bf16[3072]{0:T(1024)(128)(2,1)} %param.10) | copy-start | bytes 18436
  7.1 7.4 %copy-start.1 = (bf16[128,3072]{1,0:T(8,128)(2,1)S(1)}, bf16[128,3072]{1,0:T(8,128)(2,1)}, u32[]{:S(2)}) copy-start(bf16[128,3072]{1,0:T(8,128)(2,1)} %param.9) | copy-start | bytes 2359300
  7.1 55.7 %all-to-all-start = ((bf16[64,128,128]{2,1,0:T(8,128)(2,1)}), bf16[64,128,128]{2,1,0:T(8,128)(2,1)}, u32[]{:S(2)}, u32[]{:S(2)}) async-start(bf16[64,128,128]{2,1,0:T(8,128)(2,1)} %gather_fusion), calls=%async_computation | async-start | bytes 4194304 | tf_op jit(solution)/shard_map/all_to_all | solution.py:193
  14.5 22.3 %copy-start.4 = (s32[8]{0:T(128)S(1)}, s32[8]{0:T(128)}, u32[]{:S(2)}) copy-start(s32[8]{0:T(128)} %param.15) | copy-start | bytes 100
  16.0 23.1 %collective-permute-start.2 = (bf16[128,3072]{1,0:T(8,128)(2,1)}, bf16[128,3072]{1,0:T(8,128)(2,1)S(1)}, u32[]{:S(2)}, u32[]{:S(2)}) collective-permute-start(bf16[128,3072]{1,0:T(8,128)(2,1)} %fusion.13), channel_id=1, source_target_pairs={{0,1},{1,0},{2,3},{3,2},{4,5},{5,4},{6,7},{7,6},{8,9},{9,8},{10,11... | collective-permute-start | bytes 2359304 | tf_op jit(solution)/shard_map/ppermute | solution.py:143
  16.0 20.7 %collective-permute-start.1 = (bf16[128,3072]{1,0:T(8,128)(2,1)}, bf16[128,3072]{1,0:T(8,128)(2,1)}, u32[]{:S(2)}, u32[]{:S(2)}) collective-permute-start(bf16[128,3072]{1,0:T(8,128)(2,1)} %fusion.13), channel_id=1, source_target_pairs={{0,2},{1,3},{2,0},{3,1},{4,6},{5,7},{6,4},{7,5},{8,10},{9,11},{10,... | collective-permute-start | bytes 2359304 | tf_op jit(solution)/shard_map/ppermute | solution.py:143
  17.5 83.7 %collective-permute-start = (bf16[384,3072]{1,0:T(8,128)(2,1)}, bf16[384,3072]{1,0:T(8,128)(2,1)}, u32[]{:S(2)}, u32[]{:S(2)}) collective-permute-start(bf16[384,3072]{1,0:T(8,128)(2,1)} %param.13), channel_id=1, source_target_pairs={{0,2},{1,3},{2,0},{3,1},{4,6},{5,7},{6,4},{7,5},{8,10},{9,11},{10,... | collective-permute-start | bytes 7077896 | tf_op jit(solution)/shard_map/ppermute | solution.py:143
  18.0 86.8 %collective-permute-start.9 = (bf16[384,3072]{1,0:T(8,128)(2,1)}, bf16[384,3072]{1,0:T(8,128)(2,1)}, u32[]{:S(2)}, u32[]{:S(2)}) collective-permute-start(bf16[384,3072]{1,0:T(8,128)(2,1)} %param.13), channel_id=1, source_target_pairs={{0,1},{1,0},{2,3},{3,2},{4,5},{5,4},{6,7},{7,6},{8,9},{9,8},{10,11... | collective-permute-start | bytes 7077896 | tf_op jit(solution)/shard_map/ppermute | solution.py:143
  36.6 2.6 %collective-permute-start.3 = (bf16[128,3072]{1,0:T(8,128)(2,1)}, bf16[128,3072]{1,0:T(8,128)(2,1)}, u32[]{:S(2)}, u32[]{:S(2)}) collective-permute-start(bf16[128,3072]{1,0:T(8,128)(2,1)} %collective-permute-done.1), channel_id=1, source_target_pairs={{0,1},{1,0},{2,3},{3,2},{4,5},{5,4},{6,7},{7,6},{8,9},{9,8},{10,11... | collective-permute-start | bytes 2359304 | tf_op jit(solution)/shard_map/ppermute | solution.py:143
  39.1 24.4 %copy-start.2 = (s32[512]{0:T(512)}, s32[512]{0:T(512)S(1)}, u32[]{:S(2)}) copy-start(s32[512]{0:T(512)S(1)} %get-tuple-element.34) | copy-start | bytes 6148
  62.9 7.6 %collective-permute-start.4 = (bf16[64,128,128]{2,1,0:T(8,128)(2,1)}, bf16[64,128,128]{2,1,0:T(8,128)(2,1)}, u32[]{:S(2)}, u32[]{:S(2)}) collective-permute-start(bf16[64,128,128]{2,1,0:T(8,128)(2,1)} %all-to-all-done), channel_id=1, source_target_pairs={{0,1},{1,0},{2,3},{3,2},{4,5},{5,4},{6,7},{7,6},{8,9},{9,8},{10,11... | collective-permute-start | bytes 6291464 | tf_op jit(solution)/shard_map/ppermute | solution.py:143
  68.0 1.7 %collective-permute-start.5 = (bf16[512,128]{1,0:T(8,128)(2,1)S(1)}, bf16[512,128]{1,0:T(8,128)(2,1)S(1)}, u32[]{:S(2)}, u32[]{:S(2)}) collective-permute-start(bf16[512,128]{1,0:T(8,128)(2,1)S(1)} %fusion.30), channel_id=1, source_target_pairs={{0,1},{1,0},{2,3},{3,2},{4,5},{5,4},{6,7},{7,6},{8,9},{9,8},{10,11... | collective-permute-start | bytes 393224 | tf_op jit(solution)/shard_map/ppermute | solution.py:22
  101.2 8.7 %collective-permute-start.10 = (bf16[384,3072]{1,0:T(8,128)(2,1)}, bf16[384,3072]{1,0:T(8,128)(2,1)S(1)}, u32[]{:S(2)}, u32[]{:S(2)}) collective-permute-start(bf16[384,3072]{1,0:T(8,128)(2,1)} %collective-permute-done), channel_id=1, source_target_pairs={{0,1},{1,0},{2,3},{3,2},{4,5},{5,4},{6,7},{7,6},{8,9},{9,8},{10,11... | collective-permute-start | bytes 7077896 | tf_op jit(solution)/shard_map/ppermute | solution.py:143
  102.6 4.8 %collective-permute-start.8 = (bf16[128,384]{1,0:T(8,128)(2,1)S(1)}, bf16[128,384]{1,0:T(8,128)(2,1)S(1)}, u32[]{:S(2)}, u32[]{:S(2)}) collective-permute-start(bf16[128,384]{1,0:T(8,128)(2,1)S(1)} %get-tuple-element.23), channel_id=1, source_target_pairs={{0,3},{1,2},{2,1},{3,0},{4,7},{5,6},{6,5},{7,4},{8,11},{9,10},{10,... | collective-permute-start | bytes 294920 | tf_op jit(solution)/shard_map/ppermute | solution.py:143
  104.1 3.4 %collective-permute-start.7 = (bf16[128,384]{1,0:T(8,128)(2,1)S(1)}, bf16[128,384]{1,0:T(8,128)(2,1)S(1)}, u32[]{:S(2)}, u32[]{:S(2)}) collective-permute-start(bf16[128,384]{1,0:T(8,128)(2,1)S(1)} %get-tuple-element.24), channel_id=1, source_target_pairs={{0,1},{1,0},{2,3},{3,2},{4,5},{5,4},{6,7},{7,6},{8,9},{9,8},{10,11... | collective-permute-start | bytes 294920 | tf_op jit(solution)/shard_map/ppermute | solution.py:143
  104.3 5.6 %collective-permute-start.6 = (bf16[128,384]{1,0:T(8,128)(2,1)S(1)}, bf16[128,384]{1,0:T(8,128)(2,1)S(1)}, u32[]{:S(2)}, u32[]{:S(2)}) collective-permute-start(bf16[128,384]{1,0:T(8,128)(2,1)S(1)} %get-tuple-element.25), channel_id=1, source_target_pairs={{0,2},{1,3},{2,0},{3,1},{4,6},{5,7},{6,4},{7,5},{8,10},{9,11},{10,... | collective-permute-start | bytes 294920 | tf_op jit(solution)/shard_map/ppermute | solution.py:143

commit v12 on v11

--- a/solution.py
+++ b/solution.py
@@ -24,8 +24,9 @@
 
 def attend_kernel(
     n_cache, tk, scale, part_ref, q_ref, mine_hbm, other_hbm, nk_hbm, nv_hbm, bias_ref,
-    row_ref, key_ref, o_ref, k_scr, v_scr, s_scr, sems,
+    row_ref, key_ref, *rest,
 ):
+    *o_refs, k_scr, v_scr, s_scr, sems = rest
     bq, head_dim = q_ref.shape
     total = k_scr.shape[0]
     groups = tk // 128
@@ -88,10 +89,12 @@
         return acc + jnp.dot(w, v_scr[pl.ds(start, tk), :], preferred_element_type=jnp.float32)
 
     acc = lax.fori_loop(0, total // tk, weigh, jnp.zeros((bq, head_dim), jnp.float32), unroll=8)
-    o_ref[...] = acc.astype(o_ref.dtype)
-
-
-def attend(queries, mine, other, new_keys, new_values, part, bias, true_row):
+    part_rows = bq // len(o_refs)
+    for k, o_ref in enumerate(o_refs):
+        o_ref[...] = acc[k * part_rows:(k + 1) * part_rows].astype(o_ref.dtype)
+
+
+def attend(queries, mine, other, new_keys, new_values, part, bias, true_row, splits):
     rows, width = queries.shape
     n_cache, head_dim = mine.shape
     total = n_cache + new_keys.shape[0]
@@ -117,7 +120,7 @@
             pl.BlockSpec((rows, 1), lambda h, p: (0, 0)),
             pl.BlockSpec((1, rows), lambda h, p: (0, 0)),
         ],
-        out_specs=pl.BlockSpec((rows, head_dim), lambda h, p: (0, h)),
+        out_specs=[pl.BlockSpec((rows // splits, head_dim), lambda h, p: (0, h))] * splits,
         scratch_shapes=[
             pltpu.VMEM((total, head_dim), jnp.bfloat16),
             pltpu.VMEM((total, head_dim), jnp.bfloat16),
@@ -127,7 +130,7 @@
     )
     return pl.pallas_call(
         lambda *refs: attend_kernel(n_cache, tk, scale, *refs),
-        out_shape=jax.ShapeDtypeStruct((rows, width), jnp.bfloat16),
+        out_shape=[jax.ShapeDtypeStruct((rows // splits, width), jnp.bfloat16)] * splits,
         grid_spec=grid_spec,
         compiler_params=pltpu.CompilerParams(dimension_semantics=("arbitrary",)),
         cost_estimate=cost,
@@ -261,19 +264,18 @@
         part,
         bias.reshape(1, -1),
         true_row,
+        head_number,
     )
     late_w, pieces = lax.optimization_barrier((held_w[1:], pieces))
     held_w = held_w[:1] + list(late_w)
     held_w = held_w + [exchange(piece, "head", 1) for piece in held_w]
     masks = masks + [m ^ 1 for m in masks]
-    held_w = jnp.concatenate(held_w, 0)
-    columns = []
-    for m in masks:
-        k = row_masks.index(m)
-        block = pieces[k * local_rows:(k + 1) * local_rows]
-        columns.append(block if m == 0 else exchange(block, "head", m))
-    ordered = jnp.concatenate(columns, 1)
-    out = jnp.dot(ordered, held_w, preferred_element_type=jnp.float32)
+    out = None
+    for m, w_rows in zip(masks, held_w):
+        block = pieces[row_masks.index(m)]
+        block = block if m == 0 else exchange(block, "head", m)
+        term = jnp.dot(block, w_rows, preferred_element_type=jnp.float32)
+        out = term if out is None else out + term
     return out.astype(jnp.bfloat16)
 
 

time: 115 us -> 116 us (level)
  matrix products: 10.4 us -> 14.1 us
  waiting for transfers between devices: 38.7 us -> 37.1 us
    dot_general x1 -> x4, matrix products: 4.6 us -> 8.27 us  [body(): term = jnp.dot(block, w_rows, preferred_element_type=jnp.float32)]
    ppermute x10, waiting for transfers between devices: 19.2 us -> 17.6 us  [exchange(): return lax.ppermute(value, axis, pairs)]
  transfers between devices with their start and end apart: 12 -> 12, of which waited for: 5 -> 4; matrix products, arithmetic and copies ran while one was open for 18% -> 21% of each run, Pallas kernels for 27% -> 27%
where the time goes in v12:
time: 116 us
  waiting for transfers between devices  37.1 us (32%)
  Pallas kernels  30.8 us (27%)
  matrix products  14.1 us (12%)
  starting transfers between devices  12.4 us (11%)
  local copies, waits for them, and re-layouts  12.2 us (11%)
  other arithmetic  8.94 us (8%)
    pallas_call x1, Pallas kernels, attend(): pl.pallas_call(lambda *refs: attend_kernel(n_cache, tk, scale, *refs), ou...  30.8 us
    all_to_all x1, waiting for transfers between devices, body(): lax.all_to_all(outgoing, 'dp', split_axis=0, concat_axis=0, tiled=True)  19.4 us
    ppermute x10, waiting for transfers between devices, exchange(): return lax.ppermute(value, axis, pairs)  17.6 us
    dot_general x4, matrix products, body(): term = jnp.dot(block, w_rows, preferred_element_type=jnp.float32)  8.27 us
    all_to_all x1, starting transfers between devices, body(): lax.all_to_all(outgoing, 'dp', split_axis=0, concat_axis=0, tiled=True)  7.38 us
    gather x1, local copies, waits for them, and re-layouts, body(): outgoing = kv_pool[local_page.reshape(-1), key_value_head, part]  5.07 us
    ppermute x10, starting transfers between devices, exchange(): return lax.ppermute(value, axis, pairs)  4.49 us
    gather x1, local copies, waits for them, and re-layouts, body(): key_ok = jnp.concatenate([cache_ok, jnp.take(mask_rows, true_row) == 1])  3.48 us
  transfers between devices with their start and end apart: 12, of which 4 were waited for; matrix products, arithmetic and copies ran while one was open for 21% of the time, Pallas kernels for 27%

profile of v12, /device:TPU:0, one launch (start us, length us, event | category | flops | bytes accessed | tf_op | source)
XLA Modules:
  0.0 115.8 jit_solution(8356515125204529779)
XLA Ops:
  0.0 0.0 copy-start
  0.0 0.9 broadcast_compare_fusion.1
  0.9 0.2 reduce_window_sum.22
  1.1 0.7 add_select_fusion.1
  1.8 0.2 select_reduce_fusion.1
  2.0 0.1 reshape.528
  2.1 5.1 %gather_fusion = bf16[64,128,128]{2,1,0:T(8,128)(2,1)} fusion(bf16[48,2,2,128,128]{4,3,2,1,0:T(8,128)(2,1)} %param.14, s32[64]{0:T(128)S(1)} %fusion.30), kind=kCustom, calls=%fused_computation | custom fusion | bytes 4195072 | tf_op jit(solution)/shard_map/gather | solution.py:194
  7.2 7.4 %all-to-all-start = ((bf16[64,128,128]{2,1,0:T(8,128)(2,1)}), bf16[64,128,128]{2,1,0:T(8,128)(2,1)}, u32[]{:S(2)}, u32[]{:S(2)}) async-start(bf16[64,128,128]{2,1,0:T(8,128)(2,1)} %gather_fusion), calls=%async_computation | async-start | bytes 4194304 | tf_op jit(solution)/shard_map/all_to_all | solution.py:196
  14.5 0.0 copy-done.4
  14.5 0.0 copy-start.5
  14.6 0.0 copy-done.1
  14.6 0.2 fusion.3
  14.8 1.2 fusion.5
  16.0 0.0 collective-permute-start.2
  16.0 1.5 %collective-permute-start.1 = (bf16[128,3072]{1,0:T(8,128)(2,1)}, bf16[128,3072]{1,0:T(8,128)(2,1)}, u32[]{:S(2)}, u32[]{:S(2)}) collective-permute-start(bf16[128,3072]{1,0:T(8,128)(2,1)} %fusion.5), channel_id=1, source_target_pairs={{0,2},{1,3},{2,0},{3,1},{4,6},{5,7},{6,4},{7,5},{8,10},{9,11},{10,... | collective-permute-start | bytes 2359304 | tf_op jit(solution)/shard_map/ppermute | solution.py:146
  17.5 0.5 collective-permute-start
  18.0 0.0 collective-permute-start.8
  18.1 0.2 reduce_window_sum.23
  18.3 0.8 dynamic_slice.14
  19.1 3.5 %gather_fusion.1 = s32[512]{0:T(512)S(1)} fusion(s32[512]{0:T(512)S(1)} %dynamic_slice.14, s32[1024]{0:T(1024)S(1)} %pad_clamp_fusion), kind=kCustom, calls=%fused_computation.1 | custom fusion | bytes 6144 | tf_op jit(solution)/shard_map/jit(_take)/gather | solution.py:254
  22.6 14.0 %collective-permute-done.1 = bf16[128,3072]{1,0:T(8,128)(2,1)} collective-permute-done((bf16[128,3072]{1,0:T(8,128)(2,1)}, bf16[128,3072]{1,0:T(8,128)(2,1)}, u32[]{:S(2)}, u32[]{:S(2)}) %collective-permute-start.1) | collective-permute-done | bytes 786464 | tf_op jit(solution)/shard_map/ppermute | solution.py:146
  36.6 0.0 collective-permute-start.3
  36.6 0.2 fusion.18
  36.9 0.0 copy-done.5
  36.9 0.6 dynamic_slice.11
  37.5 0.2 select_reduce_fusion
  37.7 0.7 fusion.19
  38.5 0.6 pad_add_fusion
  39.1 0.0 copy-start.3
  39.2 0.0 collective-permute-done.2
  39.2 0.1 collective-permute-done.3
  39.3 2.8 %fusion.6 = f32[512,128]{1,0:T(8,128)S(1)} fusion(bf16[3072,128]{1,0:T(8,128)(2,1)} %param.12, bf16[128,3072]{1,0:T(8,128)(2,1)} %collective-permute-done.3, bf16[128,3072]{1,0:T(8,128)(2,1)S(1)} %collective-permute-done.2, bf16[128,3072]{1,0:T(8,128)(2,1)} %collective-permute-done.1, bf16[128,3072]{1,0:T(8,128)(2,1)} %fusion.5), kind=kOutput, calls=%fused_computation.12 | convolution fusion | flops 415236096 | bytes 4194304 | tf_op jit(solution)/shard_map/dot_general | solution.py:232
  42.1 1.2 %fusion.12 = (bf16[512,1,64]{2,0,1:T(8,128)(2,1)S(1)}, bf16[512,1,64]{2,0,1:T(8,128)(2,1)S(1)}) fusion(f32[512,1,128]{2,0,1:T(8,128)S(1)} %bitcast.38, f32[64]{0:T(128)S(1)} %multiply_exponential_fusion, f32[512]{0:T(512)S(1)} %get-tuple-element.45), kind=kLoop, calls=%fused_computation.23 | loop fusion | flops 294912 | bytes 395520 | tf_op jit(solution)/shard_map/sub | solution.py:159
  43.3 0.1 fusion.15
  43.4 19.4 %all-to-all-done = bf16[64,128,128]{2,1,0:T(8,128)(2,1)} async-done(((bf16[64,128,128]{2,1,0:T(8,128)(2,1)}), bf16[64,128,128]{2,1,0:T(8,128)(2,1)}, u32[]{:S(2)}, u32[]{:S(2)}) %all-to-all-start) | async-done | bytes 2097184 | tf_op jit(solution)/shard_map/all_to_all | solution.py:196
  62.9 0.0 collective-permute-start.4
  62.9 0.7 add_select_fusion.refs_6_
  63.6 0.0 copy-done.3
  63.6 0.9 copy.21.refs_7_
  64.4 0.5 multiply_cosine_fusion.1
  65.0 0.0 copy-done
  65.0 3.0 %fusion.7 = f32[512,384]{0,1:T(8,128)S(1)} fusion(bf16[3072,384]{1,0:T(8,128)(2,1)S(1)} %copy-done, bf16[128,3072]{1,0:T(8,128)(2,1)} %collective-permute-done.3, bf16[128,3072]{1,0:T(8,128)(2,1)S(1)} %collective-permute-done.2, bf16[128,3072]{1,0:T(8,128)(2,1)} %collective-permute-done.1, bf16[128,3072]{1,0:T(8,128)(2,1)} %fusion.5), kind=kOutput, calls=%fused_computation.13 | convolution fusion | flops 1220542464 | bytes 6291456 | tf_op jit(solution)/shard_map/dot_general | solution.py:231
  68.0 0.6 collective-permute-start.5
  68.6 0.1 subtract_convert_fusion
  68.8 0.9 copy.20.refs_1_
  69.7 0.0 collective-permute-done.5
  69.7 0.8 broadcast_select_fusion
  70.5 0.0 collective-permute-done.4
  70.5 30.8 %paged_prefill_attention.1 = (bf16[128,384]{1,0:T(8,128)(2,1)}, bf16[128,384]{1,0:T(8,128)(2,1)}, bf16[128,384]{1,0:T(8,128)(2,1)}, bf16[128,384]{1,0:T(8,128)(2,1)}) custom-call(s32[1]{0:T(128)} %bitcast.refs_0_, bf16[512,384]{1,0:T(8,128)(2,1)} %copy.20.refs_1_, bf16[8192,128]{1,0:T(8,128)(2,1)} %bitcast.7.refs_2_, bf16[8192,128]{1,0:T(8,128)(2,1)} %bitcast.8.refs_3_, ...), custom_call_target="tpu_custom_call" | custom-call | flops 6845104128 | bytes 5277696 | tf_op jit(solution)/shard_map/paged_prefill_attention/pallas_call | solution.py:131
  101.2 0.0 collective-permute-done
  101.3 0.3 collective-permute-start.10
  101.6 1.5 %collective-permute-start.6 = (bf16[128,384]{1,0:T(8,128)(2,1)}, bf16[128,384]{1,0:T(8,128)(2,1)S(1)}, u32[]{:S(2)}, u32[]{:S(2)}) collective-permute-start(bf16[128,384]{1,0:T(8,128)(2,1)} %get-tuple-element.27), channel_id=1, source_target_pairs={{0,2},{1,3},{2,0},{3,1},{4,6},{5,7},{6,4},{7,5},{8,10},{9,11},{10,... | collective-permute-start | bytes 294920 | tf_op jit(solution)/shard_map/ppermute | solution.py:146
  103.1 0.0 collective-permute-start.7
  103.1 0.6 collective-permute-start.9
  103.7 3.5 %collective-permute-done.6 = bf16[128,384]{1,0:T(8,128)(2,1)S(1)} collective-permute-done((bf16[128,384]{1,0:T(8,128)(2,1)}, bf16[128,384]{1,0:T(8,128)(2,1)S(1)}, u32[]{:S(2)}, u32[]{:S(2)}) %collective-permute-start.6) | collective-permute-done | bytes 98336 | tf_op jit(solution)/shard_map/ppermute | solution.py:146
  107.2 2.2 %fusion.39 = f32[128,3072]{1,0:T(8,128)S(1)} fusion(bf16[128,384]{1,0:T(8,128)(2,1)S(1)} %collective-permute-done.6, bf16[384,3072]{1,0:T(8,128)(2,1)} %collective-permute-done), kind=kOutput, calls=%fused_computation.88 | convolution fusion | flops 301989888 | bytes 4030464 | tf_op jit(solution)/shard_map/dot_general | solution.py:277
  109.4 0.0 collective-permute-done.8
  109.5 0.0 collective-permute-done.7
  109.5 2.2 %fusion.40 = f32[128,3072]{1,0:T(8,128)S(1)} fusion(bf16[128,384]{1,0:T(8,128)(2,1)S(1)} %collective-permute-done.7, bf16[384,3072]{1,0:T(8,128)(2,1)} %collective-permute-done.8), kind=kOutput, calls=%fused_computation.89 | convolution fusion | flops 301989888 | bytes 4030464 | tf_op jit(solution)/shard_map/dot_general | solution.py:277
  111.7 0.0 collective-permute-done.9
  111.7 0.0 collective-permute-done.10
  111.7 0.6 fusion.41
  112.3 0.3 copy-done.2
  112.6 3.2 %fusion.2 = bf16[128,3072]{1,0:T(8,128)(2,1)} fusion(f32[128,3072]{1,0:T(8,128)S(1)} %fusion.41, f32[128,3072]{1,0:T(8,128)S(1)} %fusion.40, f32[128,3072]{1,0:T(8,128)S(1)} %fusion.39, bf16[128,384]{1,0:T(8,128)(2,1)S(1)} %copy-done.2, bf16[384,3072]{1,0:T(8,128)(2,1)} %param.13), kind=kOutput, calls=%fused_computation.5 | convolution fusion | flops 303562752 | bytes 7962624 | tf_op jit(solution)/shard_map/dot_general | solution.py:277
  (22 shorter events, 0.2 us)
Async XLA Ops:
  0.0 65.0 %copy-start = (bf16[3072,384]{1,0:T(8,128)(2,1)S(1)}, bf16[3072,384]{1,0:T(8,128)(2,1)}, u32[]{:S(2)}) copy-start(bf16[3072,384]{1,0:T(8,128)(2,1)} %param.11) | copy-start | bytes 7077892
  7.2 7.4 %copy-start.4 = (bf16[3072]{0:T(1024)(128)(2,1)S(1)}, bf16[3072]{0:T(1024)(128)(2,1)}, u32[]{:S(2)}) copy-start(bf16[3072]{0:T(1024)(128)(2,1)} %param.10) | copy-start | bytes 18436
  7.2 7.4 %copy-start.1 = (bf16[128,3072]{1,0:T(8,128)(2,1)S(1)}, bf16[128,3072]{1,0:T(8,128)(2,1)}, u32[]{:S(2)}) copy-start(bf16[128,3072]{1,0:T(8,128)(2,1)} %param.9) | copy-start | bytes 2359300
  7.2 55.7 %all-to-all-start = ((bf16[64,128,128]{2,1,0:T(8,128)(2,1)}), bf16[64,128,128]{2,1,0:T(8,128)(2,1)}, u32[]{:S(2)}, u32[]{:S(2)}) async-start(bf16[64,128,128]{2,1,0:T(8,128)(2,1)} %gather_fusion), calls=%async_computation | async-start | bytes 4194304 | tf_op jit(solution)/shard_map/all_to_all | solution.py:196
  14.5 22.3 %copy-start.5 = (s32[8]{0:T(128)S(1)}, s32[8]{0:T(128)}, u32[]{:S(2)}) copy-start(s32[8]{0:T(128)} %param.15) | copy-start | bytes 100
  16.0 23.2 %collective-permute-start.2 = (bf16[128,3072]{1,0:T(8,128)(2,1)}, bf16[128,3072]{1,0:T(8,128)(2,1)S(1)}, u32[]{:S(2)}, u32[]{:S(2)}) collective-permute-start(bf16[128,3072]{1,0:T(8,128)(2,1)} %fusion.5), channel_id=1, source_target_pairs={{0,1},{1,0},{2,3},{3,2},{4,5},{5,4},{6,7},{7,6},{8,9},{9,8},{10,11... | collective-permute-start | bytes 2359304 | tf_op jit(solution)/shard_map/ppermute | solution.py:146
  16.0 20.7 %collective-permute-start.1 = (bf16[128,3072]{1,0:T(8,128)(2,1)}, bf16[128,3072]{1,0:T(8,128)(2,1)}, u32[]{:S(2)}, u32[]{:S(2)}) collective-permute-start(bf16[128,3072]{1,0:T(8,128)(2,1)} %fusion.5), channel_id=1, source_target_pairs={{0,2},{1,3},{2,0},{3,1},{4,6},{5,7},{6,4},{7,5},{8,10},{9,11},{10,... | collective-permute-start | bytes 2359304 | tf_op jit(solution)/shard_map/ppermute | solution.py:146
  17.5 83.7 %collective-permute-start = (bf16[384,3072]{1,0:T(8,128)(2,1)}, bf16[384,3072]{1,0:T(8,128)(2,1)}, u32[]{:S(2)}, u32[]{:S(2)}) collective-permute-start(bf16[384,3072]{1,0:T(8,128)(2,1)} %param.13), channel_id=1, source_target_pairs={{0,2},{1,3},{2,0},{3,1},{4,6},{5,7},{6,4},{7,5},{8,10},{9,11},{10,... | collective-permute-start | bytes 7077896 | tf_op jit(solution)/shard_map/ppermute | solution.py:146
  18.0 91.4 %collective-permute-start.8 = (bf16[384,3072]{1,0:T(8,128)(2,1)}, bf16[384,3072]{1,0:T(8,128)(2,1)}, u32[]{:S(2)}, u32[]{:S(2)}) collective-permute-start(bf16[384,3072]{1,0:T(8,128)(2,1)} %param.13), channel_id=1, source_target_pairs={{0,1},{1,0},{2,3},{3,2},{4,5},{5,4},{6,7},{7,6},{8,9},{9,8},{10,11... | collective-permute-start | bytes 7077896 | tf_op jit(solution)/shard_map/ppermute | solution.py:146
  36.6 2.6 %collective-permute-start.3 = (bf16[128,3072]{1,0:T(8,128)(2,1)}, bf16[128,3072]{1,0:T(8,128)(2,1)}, u32[]{:S(2)}, u32[]{:S(2)}) collective-permute-start(bf16[128,3072]{1,0:T(8,128)(2,1)} %collective-permute-done.1), channel_id=1, source_target_pairs={{0,1},{1,0},{2,3},{3,2},{4,5},{5,4},{6,7},{7,6},{8,9},{9,8},{10,11... | collective-permute-start | bytes 2359304 | tf_op jit(solution)/shard_map/ppermute | solution.py:146
  39.1 24.4 %copy-start.3 = (s32[512]{0:T(512)}, s32[512]{0:T(512)S(1)}, u32[]{:S(2)}) copy-start(s32[512]{0:T(512)S(1)} %get-tuple-element.44) | copy-start | bytes 6148
  62.9 7.6 %collective-permute-start.4 = (bf16[64,128,128]{2,1,0:T(8,128)(2,1)}, bf16[64,128,128]{2,1,0:T(8,128)(2,1)}, u32[]{:S(2)}, u32[]{:S(2)}) collective-permute-start(bf16[64,128,128]{2,1,0:T(8,128)(2,1)} %all-to-all-done), channel_id=1, source_target_pairs={{0,1},{1,0},{2,3},{3,2},{4,5},{5,4},{6,7},{7,6},{8,9},{9,8},{10,11... | collective-permute-start | bytes 6291464 | tf_op jit(solution)/shard_map/ppermute | solution.py:146
  68.0 1.7 %collective-permute-start.5 = (bf16[512,128]{1,0:T(8,128)(2,1)S(1)}, bf16[512,128]{1,0:T(8,128)(2,1)S(1)}, u32[]{:S(2)}, u32[]{:S(2)}) collective-permute-start(bf16[512,128]{1,0:T(8,128)(2,1)S(1)} %fusion.15), channel_id=1, source_target_pairs={{0,1},{1,0},{2,3},{3,2},{4,5},{5,4},{6,7},{7,6},{8,9},{9,8},{10,11... | collective-permute-start | bytes 393224 | tf_op jit(solution)/shard_map/ppermute | solution.py:22
  101.3 10.5 %collective-permute-start.10 = (bf16[384,3072]{1,0:T(8,128)(2,1)}, bf16[384,3072]{1,0:T(8,128)(2,1)S(1)}, u32[]{:S(2)}, u32[]{:S(2)}) collective-permute-start(bf16[384,3072]{1,0:T(8,128)(2,1)} %collective-permute-done), channel_id=1, source_target_pairs={{0,1},{1,0},{2,3},{3,2},{4,5},{5,4},{6,7},{7,6},{8,9},{9,8},{10,11... | collective-permute-start | bytes 7077896 | tf_op jit(solution)/shard_map/ppermute | solution.py:146
  101.6 5.6 %collective-permute-start.6 = (bf16[128,384]{1,0:T(8,128)(2,1)}, bf16[128,384]{1,0:T(8,128)(2,1)S(1)}, u32[]{:S(2)}, u32[]{:S(2)}) collective-permute-start(bf16[128,384]{1,0:T(8,128)(2,1)} %get-tuple-element.27), channel_id=1, source_target_pairs={{0,2},{1,3},{2,0},{3,1},{4,6},{5,7},{6,4},{7,5},{8,10},{9,11},{10,... | collective-permute-start | bytes 294920 | tf_op jit(solution)/shard_map/ppermute | solution.py:146
  103.1 6.4 %collective-permute-start.7 = (bf16[128,384]{1,0:T(8,128)(2,1)}, bf16[128,384]{1,0:T(8,128)(2,1)S(1)}, u32[]{:S(2)}, u32[]{:S(2)}) collective-permute-start(bf16[128,384]{1,0:T(8,128)(2,1)} %get-tuple-element.29), channel_id=1, source_target_pairs={{0,1},{1,0},{2,3},{3,2},{4,5},{5,4},{6,7},{7,6},{8,9},{9,8},{10,11... | collective-permute-start | bytes 294920 | tf_op jit(solution)/shard_map/ppermute | solution.py:146
  103.1 8.6 %collective-permute-start.9 = (bf16[128,384]{1,0:T(8,128)(2,1)}, bf16[128,384]{1,0:T(8,128)(2,1)S(1)}, u32[]{:S(2)}, u32[]{:S(2)}) collective-permute-start(bf16[128,384]{1,0:T(8,128)(2,1)} %get-tuple-element.30), channel_id=1, source_target_pairs={{0,3},{1,2},{2,1},{3,0},{4,7},{5,6},{6,5},{7,4},{8,11},{9,10},{10,... | collective-permute-start | bytes 294920 | tf_op jit(solution)/shard_map/ppermute | solution.py:146
  111.7 0.9 copy-start.2

commit v13 on v11

--- a/solution.py
+++ b/solution.py
@@ -24,8 +24,9 @@
 
 def attend_kernel(
     n_cache, tk, scale, part_ref, q_ref, mine_hbm, other_hbm, nk_hbm, nv_hbm, bias_ref,
-    row_ref, key_ref, o_ref, k_scr, v_scr, s_scr, sems,
+    *rest,
 ):
+    *o_refs, k_scr, v_scr, s_scr, sems = rest
     bq, head_dim = q_ref.shape
     total = k_scr.shape[0]
     groups = tk // 128
@@ -53,6 +54,15 @@
             load(other_hbm, mine_hbm)
 
     q = q_ref[...]
+    part_rows = bq // len(o_refs)
+
+    def true_index(offset, axis):
+        place = offset + lax.broadcasted_iota(jnp.int32, (bq, tk), axis)
+        block = place // part_rows
+        base = jnp.zeros_like(place)
+        for k in range(len(o_refs)):
+            base = jnp.where(block == k, part_ref[1 + k], base)
+        return base + place % part_rows
 
     def scores(c, top, causal):
         start = pl.multiple_of(c * tk, tk)
@@ -60,7 +70,7 @@
         s = lax.dot_general(q, keys, (((1,), (1,)), ((), ())), preferred_element_type=jnp.float32)
         s = s * scale + bias_ref[:, pl.ds(start, tk)]
         if causal:
-            s = jnp.where(key_ref[:, pl.ds(start - n_cache, tk)] <= row_ref[...], s, -jnp.inf)
+            s = jnp.where(true_index(start - n_cache, 1) <= true_index(0, 0), s, -jnp.inf)
         s_scr[:, pl.ds(start, tk)] = s
         for g in range(groups):
             top = jnp.maximum(top, s[:, g * 128:(g + 1) * 128])
@@ -88,11 +98,13 @@
         return acc + jnp.dot(w, v_scr[pl.ds(start, tk), :], preferred_element_type=jnp.float32)
 
     acc = lax.fori_loop(0, total // tk, weigh, jnp.zeros((bq, head_dim), jnp.float32), unroll=8)
-    o_ref[...] = acc.astype(o_ref.dtype)
-
-
-def attend(queries, mine, other, new_keys, new_values, part, bias, true_row):
+    for k, o_ref in enumerate(o_refs):
+        o_ref[...] = acc[k * part_rows:(k + 1) * part_rows].astype(o_ref.dtype)
+
+
+def attend(queries, mine, other, new_keys, new_values, part, bias, block_base):
     rows, width = queries.shape
+    splits = block_base.shape[0]
     n_cache, head_dim = mine.shape
     total = n_cache + new_keys.shape[0]
     heads = width // head_dim
@@ -114,10 +126,8 @@
             any_spec,
             any_spec,
             pl.BlockSpec((1, total), lambda h, p: (0, 0)),
-            pl.BlockSpec((rows, 1), lambda h, p: (0, 0)),
-            pl.BlockSpec((1, rows), lambda h, p: (0, 0)),
         ],
-        out_specs=pl.BlockSpec((rows, head_dim), lambda h, p: (0, h)),
+        out_specs=[pl.BlockSpec((rows // splits, head_dim), lambda h, p: (0, h))] * splits,
         scratch_shapes=[
             pltpu.VMEM((total, head_dim), jnp.bfloat16),
             pltpu.VMEM((total, head_dim), jnp.bfloat16),
@@ -127,14 +137,14 @@
     )
     return pl.pallas_call(
         lambda *refs: attend_kernel(n_cache, tk, scale, *refs),
-        out_shape=jax.ShapeDtypeStruct((rows, width), jnp.bfloat16),
+        out_shape=[jax.ShapeDtypeStruct((rows // splits, width), jnp.bfloat16)] * splits,
         grid_spec=grid_spec,
         compiler_params=pltpu.CompilerParams(dimension_semantics=("arbitrary",)),
         cost_estimate=cost,
         name="paged_prefill_attention",
     )(
-        part.reshape(1).astype(jnp.int32), queries, mine, other, new_keys, new_values, bias,
-        true_row.reshape(rows, 1), true_row.reshape(1, rows),
+        jnp.concatenate([part.reshape(1), block_base]).astype(jnp.int32),
+        queries, mine, other, new_keys, new_values, bias,
     )
 
 
@@ -260,7 +270,7 @@
         new_values,
         part,
         bias.reshape(1, -1),
-        true_row,
+        jnp.stack([(current_head ^ m) * local_rows for m in row_masks]),
     )
     late_w, pieces = lax.optimization_barrier((held_w[1:], pieces))
     held_w = held_w[:1] + list(late_w)
@@ -269,8 +279,7 @@
     held_w = jnp.concatenate(held_w, 0)
     columns = []
     for m in masks:
-        k = row_masks.index(m)
-        block = pieces[k * local_rows:(k + 1) * local_rows]
+        block = pieces[row_masks.index(m)]
         columns.append(block if m == 0 else exchange(block, "head", m))
     ordered = jnp.concatenate(columns, 1)
     out = jnp.dot(ordered, held_w, preferred_element_type=jnp.float32)

time: 115 us -> 114 us (level)
  local copies, waits for them, and re-layouts: 12.9 us -> 11.7 us
  transfers between devices with their start and end apart: 12 -> 12, of which waited for: 5 -> 4; matrix products, arithmetic and copies ran while one was open for 18% -> 17% of each run, Pallas kernels for 27% -> 28%
where the time goes in v13:
time: 114 us; the launch traced here: 113 us
  waiting for transfers between devices  38.1 us (33%)
  Pallas kernels  31.4 us (28%)
  starting transfers between devices  12.4 us (11%)
  local copies, waits for them, and re-layouts  11.7 us (10%)
  matrix products  10.5 us (9%)
  other arithmetic  9.02 us (8%)
    pallas_call x1, Pallas kernels, attend(): pl.pallas_call(lambda *refs: attend_kernel(n_cache, tk, scale, *refs), ou...  31.4 us
    all_to_all x1, waiting for transfers between devices, body(): lax.all_to_all(outgoing, 'dp', split_axis=0, concat_axis=0, tiled=True)  19.4 us
    ppermute x10, waiting for transfers between devices, exchange(): return lax.ppermute(value, axis, pairs)  18.7 us
    all_to_all x1, starting transfers between devices, body(): lax.all_to_all(outgoing, 'dp', split_axis=0, concat_axis=0, tiled=True)  7.38 us
    gather x1, local copies, waits for them, and re-layouts, body(): outgoing = kv_pool[local_page.reshape(-1), key_value_head, part]  5.07 us
    dot_general x1, matrix products, body(): out = jnp.dot(ordered, held_w, preferred_element_type=jnp.float32)  4.63 us
    ppermute x10, starting transfers between devices, exchange(): return lax.ppermute(value, axis, pairs)  4.49 us
    gather x1, local copies, waits for them, and re-layouts, body(): key_ok = jnp.concatenate([cache_ok, jnp.take(mask_rows, true_row) == 1])  3.48 us
  transfers between devices with their start and end apart: 12, of which 4 were waited for; matrix products, arithmetic and copies ran while one was open for 17% of the time, Pallas kernels for 28%

profile of v13, /device:TPU:0, one launch (start us, length us, event | category | flops | bytes accessed | tf_op | source)
XLA Modules:
  0.0 113.5 jit_solution(2196172472238889712)
XLA Ops:
  0.0 0.0 copy-start
  0.0 0.9 broadcast_compare_fusion.1
  0.9 0.2 reduce_window_sum.22
  1.1 0.7 add_select_fusion.1
  1.8 0.2 select_reduce_fusion.1
  2.0 0.1 reshape.522
  2.1 5.1 %gather_fusion = bf16[64,128,128]{2,1,0:T(8,128)(2,1)} fusion(bf16[48,2,2,128,128]{4,3,2,1,0:T(8,128)(2,1)} %param.14, s32[64]{0:T(128)S(1)} %fusion.45), kind=kCustom, calls=%fused_computation | custom fusion | bytes 4195072 | tf_op jit(solution)/shard_map/gather | solution.py:201
  7.2 0.0 copy-start.2
  7.2 0.0 copy-start.1
  7.2 7.4 %all-to-all-start = ((bf16[64,128,128]{2,1,0:T(8,128)(2,1)}), bf16[64,128,128]{2,1,0:T(8,128)(2,1)}, u32[]{:S(2)}, u32[]{:S(2)}) async-start(bf16[64,128,128]{2,1,0:T(8,128)(2,1)} %gather_fusion), calls=%async_computation | async-start | bytes 4194304 | tf_op jit(solution)/shard_map/all_to_all | solution.py:203
  14.5 0.0 copy-done.2
  14.5 0.0 copy-start.3
  14.6 0.0 copy-done.1
  14.6 0.2 fusion.11
  14.8 1.2 %fusion.13 = bf16[128,3072]{1,0:T(8,128)(2,1)} fusion(bf16[128,3072]{1,0:T(8,128)(2,1)S(1)} %copy-done.1, f32[3072]{0:T(1024)S(1)} %convert_element_type.49, f32[128]{0:T(128)S(1)} %add_rsqrt_fusion), kind=kLoop, calls=%fused_computation.16 | loop fusion | flops 1572864 | bytes 1585664 | tf_op jit(solution)/shard_map/convert_element_type | solution.py:218
  16.0 0.0 collective-permute-start.2
  16.0 1.5 %collective-permute-start.1 = (bf16[128,3072]{1,0:T(8,128)(2,1)}, bf16[128,3072]{1,0:T(8,128)(2,1)}, u32[]{:S(2)}, u32[]{:S(2)}) collective-permute-start(bf16[128,3072]{1,0:T(8,128)(2,1)} %fusion.13), channel_id=1, source_target_pairs={{0,2},{1,3},{2,0},{3,1},{4,6},{5,7},{6,4},{7,5},{8,10},{9,11},{10,... | collective-permute-start | bytes 2359304 | tf_op jit(solution)/shard_map/ppermute | solution.py:153
  17.5 0.5 collective-permute-start
  18.0 0.0 collective-permute-start.9
  18.1 0.2 reduce_window_sum.23
  18.3 0.8 dynamic_slice.14
  19.1 3.5 %gather_fusion.1 = s32[512]{0:T(512)S(1)} fusion(s32[512]{0:T(512)S(1)} %dynamic_slice.14, s32[1024]{0:T(1024)S(1)} %pad_clamp_fusion), kind=kCustom, calls=%fused_computation.1 | custom fusion | bytes 6144 | tf_op jit(solution)/shard_map/jit(_take)/gather | solution.py:261
  22.6 14.0 %collective-permute-done.1 = bf16[128,3072]{1,0:T(8,128)(2,1)} collective-permute-done((bf16[128,3072]{1,0:T(8,128)(2,1)}, bf16[128,3072]{1,0:T(8,128)(2,1)}, u32[]{:S(2)}, u32[]{:S(2)}) %collective-permute-start.1) | collective-permute-done | bytes 786464 | tf_op jit(solution)/shard_map/ppermute | solution.py:153
  36.6 0.0 collective-permute-start.3
  36.6 0.2 fusion.33
  36.9 0.0 copy-done.3
  36.9 0.7 dynamic_slice.11
  37.5 0.2 select_reduce_fusion
  37.8 0.8 fusion.34
  38.6 0.7 fusion.40
  39.3 0.0 collective-permute-done.2
  39.3 0.0 collective-permute-done.3
  39.3 2.8 %fusion.14 = f32[512,128]{1,0:T(8,128)S(1)} fusion(bf16[3072,128]{1,0:T(8,128)(2,1)} %param.12, bf16[128,3072]{1,0:T(8,128)(2,1)} %collective-permute-done.3, bf16[128,3072]{1,0:T(8,128)(2,1)S(1)} %collective-permute-done.2, bf16[128,3072]{1,0:T(8,128)(2,1)} %collective-permute-done.1, bf16[128,3072]{1,0:T(8,128)(2,1)} %fusion.13), kind=kOutput, calls=%fused_computation.17 | convolution fusion | flops 415236096 | bytes 4194304 | tf_op jit(solution)/shard_map/dot_general | solution.py:239
  42.1 1.2 %fusion.27 = (bf16[512,1,64]{2,0,1:T(8,128)(2,1)S(1)}, bf16[512,1,64]{2,0,1:T(8,128)(2,1)S(1)}) fusion(f32[512,1,128]{2,0,1:T(8,128)S(1)} %bitcast.32, f32[64]{0:T(128)S(1)} %multiply_exponential_fusion, f32[512]{0:T(512)S(1)} %fusion.40), kind=kLoop, calls=%fused_computation.35 | loop fusion | flops 294912 | bytes 395520 | tf_op jit(solution)/shard_map/sub | solution.py:166
  43.4 0.1 fusion.30
  43.5 19.4 %all-to-all-done = bf16[64,128,128]{2,1,0:T(8,128)(2,1)} async-done(((bf16[64,128,128]{2,1,0:T(8,128)(2,1)}), bf16[64,128,128]{2,1,0:T(8,128)(2,1)}, u32[]{:S(2)}, u32[]{:S(2)}) %all-to-all-start) | async-done | bytes 2097184 | tf_op jit(solution)/shard_map/all_to_all | solution.py:203
  62.9 0.0 collective-permute-start.4
  62.9 0.7 add_select_fusion.refs_6_
  63.5 0.7 concatenate.90.refs_0_
  64.2 0.5 multiply_cosine_fusion.1
  64.7 0.0 copy-done
  64.8 3.0 %fusion.15 = f32[512,384]{0,1:T(8,128)S(1)} fusion(bf16[3072,384]{1,0:T(8,128)(2,1)S(1)} %copy-done, bf16[128,3072]{1,0:T(8,128)(2,1)} %collective-permute-done.3, bf16[128,3072]{1,0:T(8,128)(2,1)S(1)} %collective-permute-done.2, bf16[128,3072]{1,0:T(8,128)(2,1)} %collective-permute-done.1, bf16[128,3072]{1,0:T(8,128)(2,1)} %fusion.13), kind=kOutput, calls=%fused_computation.18 | convolution fusion | flops 1220542464 | bytes 6291456 | tf_op jit(solution)/shard_map/dot_general | solution.py:238
  67.8 0.6 collective-permute-start.5
  68.4 0.1 subtract_convert_fusion
  68.6 0.9 copy.19.refs_1_
  69.5 0.0 collective-permute-done.5
  69.5 0.8 broadcast_select_fusion
  70.3 0.0 collective-permute-done.4
  70.3 31.4 %paged_prefill_attention.1 = (bf16[128,384]{1,0:T(8,128)(2,1)}, bf16[128,384]{1,0:T(8,128)(2,1)}, bf16[128,384]{1,0:T(8,128)(2,1)}, bf16[128,384]{1,0:T(8,128)(2,1)}) custom-call(s32[5]{0:T(128)} %concatenate.90.refs_0_, bf16[512,384]{1,0:T(8,128)(2,1)} %copy.19.refs_1_, bf16[8192,128]{1,0:T(8,128)(2,1)} %bitcast.11.refs_2_, ...), custom_call_target="tpu_custom_call" | custom-call | flops 6845104128 | bytes 5277696 | tf_op jit(solution)/shard_map/paged_prefill_attention/pallas_call | solution.py:138
  101.7 0.0 collective-permute-done
  101.7 0.3 collective-permute-start.10
  102.0 1.5 %collective-permute-start.6 = (bf16[128,384]{1,0:T(8,128)(2,1)}, bf16[128,384]{1,0:T(8,128)(2,1)S(1)}, u32[]{:S(2)}, u32[]{:S(2)}) collective-permute-start(bf16[128,384]{1,0:T(8,128)(2,1)} %get-tuple-element.27), channel_id=1, source_target_pairs={{0,2},{1,3},{2,0},{3,1},{4,6},{5,7},{6,4},{7,5},{8,10},{9,11},{10,... | collective-permute-start | bytes 294920 | tf_op jit(solution)/shard_map/ppermute | solution.py:153
  103.6 0.0 collective-permute-start.7
  103.6 0.6 collective-permute-start.8
  104.2 0.0 collective-permute-done.9
  104.2 3.5 %collective-permute-done.6 = bf16[128,384]{1,0:T(8,128)(2,1)S(1)} collective-permute-done((bf16[128,384]{1,0:T(8,128)(2,1)}, bf16[128,384]{1,0:T(8,128)(2,1)S(1)}, u32[]{:S(2)}, u32[]{:S(2)}) %collective-permute-start.6) | collective-permute-done | bytes 98336 | tf_op jit(solution)/shard_map/ppermute | solution.py:153
  107.7 0.0 collective-permute-done.7
  107.7 1.2 %collective-permute-done.8 = bf16[128,384]{1,0:T(8,128)(2,1)S(1)} collective-permute-done((bf16[128,384]{1,0:T(8,128)(2,1)}, bf16[128,384]{1,0:T(8,128)(2,1)S(1)}, u32[]{:S(2)}, u32[]{:S(2)}) %collective-permute-start.8) | collective-permute-done | bytes 98336 | tf_op jit(solution)/shard_map/ppermute | solution.py:153
  108.9 0.0 collective-permute-done.10
  108.9 4.6 %fusion.8 = bf16[128,3072]{1,0:T(8,128)(2,1)} fusion(bf16[384,3072]{1,0:T(8,128)(2,1)S(1)} %collective-permute-done.10, bf16[384,3072]{1,0:T(8,128)(2,1)} %collective-permute-done.9, bf16[384,3072]{1,0:T(8,128)(2,1)} %collective-permute-done, bf16[384,3072]{1,0:T(8,128)(2,1)} %param.13, bf16[128,384]{1,0:T(8,128)(2,1)S(1)} %collective-permute-done.8, ...), kind=kOutput, calls=%fused_computation.10 | convolution fusion | flops 1247674368 | bytes 10616832 | tf_op jit(solution)/shard_map/dot_general | solution.py:285
  (19 shorter events, 0.2 us)
Async XLA Ops:
  0.0 64.8 %copy-start = (bf16[3072,384]{1,0:T(8,128)(2,1)S(1)}, bf16[3072,384]{1,0:T(8,128)(2,1)}, u32[]{:S(2)}) copy-start(bf16[3072,384]{1,0:T(8,128)(2,1)} %param.11) | copy-start | bytes 7077892
  7.2 7.4 %copy-start.2 = (bf16[3072]{0:T(1024)(128)(2,1)S(1)}, bf16[3072]{0:T(1024)(128)(2,1)}, u32[]{:S(2)}) copy-start(bf16[3072]{0:T(1024)(128)(2,1)} %param.10) | copy-start | bytes 18436
  7.2 7.4 %copy-start.1 = (bf16[128,3072]{1,0:T(8,128)(2,1)S(1)}, bf16[128,3072]{1,0:T(8,128)(2,1)}, u32[]{:S(2)}) copy-start(bf16[128,3072]{1,0:T(8,128)(2,1)} %param.9) | copy-start | bytes 2359300
  7.2 55.7 %all-to-all-start = ((bf16[64,128,128]{2,1,0:T(8,128)(2,1)}), bf16[64,128,128]{2,1,0:T(8,128)(2,1)}, u32[]{:S(2)}, u32[]{:S(2)}) async-start(bf16[64,128,128]{2,1,0:T(8,128)(2,1)} %gather_fusion), calls=%async_computation | async-start | bytes 4194304 | tf_op jit(solution)/shard_map/all_to_all | solution.py:203
  14.5 22.3 %copy-start.3 = (s32[8]{0:T(128)S(1)}, s32[8]{0:T(128)}, u32[]{:S(2)}) copy-start(s32[8]{0:T(128)} %param.15) | copy-start | bytes 100
  16.0 23.3 %collective-permute-start.2 = (bf16[128,3072]{1,0:T(8,128)(2,1)}, bf16[128,3072]{1,0:T(8,128)(2,1)S(1)}, u32[]{:S(2)}, u32[]{:S(2)}) collective-permute-start(bf16[128,3072]{1,0:T(8,128)(2,1)} %fusion.13), channel_id=1, source_target_pairs={{0,1},{1,0},{2,3},{3,2},{4,5},{5,4},{6,7},{7,6},{8,9},{9,8},{10,11... | collective-permute-start | bytes 2359304 | tf_op jit(solution)/shard_map/ppermute | solution.py:153
  16.0 20.7 %collective-permute-start.1 = (bf16[128,3072]{1,0:T(8,128)(2,1)}, bf16[128,3072]{1,0:T(8,128)(2,1)}, u32[]{:S(2)}, u32[]{:S(2)}) collective-permute-start(bf16[128,3072]{1,0:T(8,128)(2,1)} %fusion.13), channel_id=1, source_target_pairs={{0,2},{1,3},{2,0},{3,1},{4,6},{5,7},{6,4},{7,5},{8,10},{9,11},{10,... | collective-permute-start | bytes 2359304 | tf_op jit(solution)/shard_map/ppermute | solution.py:153
  17.5 84.2 %collective-permute-start = (bf16[384,3072]{1,0:T(8,128)(2,1)}, bf16[384,3072]{1,0:T(8,128)(2,1)}, u32[]{:S(2)}, u32[]{:S(2)}) collective-permute-start(bf16[384,3072]{1,0:T(8,128)(2,1)} %param.13), channel_id=1, source_target_pairs={{0,2},{1,3},{2,0},{3,1},{4,6},{5,7},{6,4},{7,5},{8,10},{9,11},{10,... | collective-permute-start | bytes 7077896 | tf_op jit(solution)/shard_map/ppermute | solution.py:153
  18.0 86.2 %collective-permute-start.9 = (bf16[384,3072]{1,0:T(8,128)(2,1)}, bf16[384,3072]{1,0:T(8,128)(2,1)}, u32[]{:S(2)}, u32[]{:S(2)}) collective-permute-start(bf16[384,3072]{1,0:T(8,128)(2,1)} %param.13), channel_id=1, source_target_pairs={{0,1},{1,0},{2,3},{3,2},{4,5},{5,4},{6,7},{7,6},{8,9},{9,8},{10,11... | collective-permute-start | bytes 7077896 | tf_op jit(solution)/shard_map/ppermute | solution.py:153
  36.6 2.6 %collective-permute-start.3 = (bf16[128,3072]{1,0:T(8,128)(2,1)}, bf16[128,3072]{1,0:T(8,128)(2,1)}, u32[]{:S(2)}, u32[]{:S(2)}) collective-permute-start(bf16[128,3072]{1,0:T(8,128)(2,1)} %collective-permute-done.1), channel_id=1, source_target_pairs={{0,1},{1,0},{2,3},{3,2},{4,5},{5,4},{6,7},{7,6},{8,9},{9,8},{10,11... | collective-permute-start | bytes 2359304 | tf_op jit(solution)/shard_map/ppermute | solution.py:153
  62.9 7.4 %collective-permute-start.4 = (bf16[64,128,128]{2,1,0:T(8,128)(2,1)}, bf16[64,128,128]{2,1,0:T(8,128)(2,1)}, u32[]{:S(2)}, u32[]{:S(2)}) collective-permute-start(bf16[64,128,128]{2,1,0:T(8,128)(2,1)} %all-to-all-done), channel_id=1, source_target_pairs={{0,1},{1,0},{2,3},{3,2},{4,5},{5,4},{6,7},{7,6},{8,9},{9,8},{10,11... | collective-permute-start | bytes 6291464 | tf_op jit(solution)/shard_map/ppermute | solution.py:153
  67.8 1.7 %collective-permute-start.5 = (bf16[512,128]{1,0:T(8,128)(2,1)S(1)}, bf16[512,128]{1,0:T(8,128)(2,1)S(1)}, u32[]{:S(2)}, u32[]{:S(2)}) collective-permute-start(bf16[512,128]{1,0:T(8,128)(2,1)S(1)} %fusion.30), channel_id=1, source_target_pairs={{0,1},{1,0},{2,3},{3,2},{4,5},{5,4},{6,7},{7,6},{8,9},{9,8},{10,11... | collective-permute-start | bytes 393224 | tf_op jit(solution)/shard_map/ppermute | solution.py:22
  101.7 7.1 %collective-permute-start.10 = (bf16[384,3072]{1,0:T(8,128)(2,1)}, bf16[384,3072]{1,0:T(8,128)(2,1)S(1)}, u32[]{:S(2)}, u32[]{:S(2)}) collective-permute-start(bf16[384,3072]{1,0:T(8,128)(2,1)} %collective-permute-done), channel_id=1, source_target_pairs={{0,1},{1,0},{2,3},{3,2},{4,5},{5,4},{6,7},{7,6},{8,9},{9,8},{10,11... | collective-permute-start | bytes 7077896 | tf_op jit(solution)/shard_map/ppermute | solution.py:153
  102.0 5.6 %collective-permute-start.6 = (bf16[128,384]{1,0:T(8,128)(2,1)}, bf16[128,384]{1,0:T(8,128)(2,1)S(1)}, u32[]{:S(2)}, u32[]{:S(2)}) collective-permute-start(bf16[128,384]{1,0:T(8,128)(2,1)} %get-tuple-element.27), channel_id=1, source_target_pairs={{0,2},{1,3},{2,0},{3,1},{4,6},{5,7},{6,4},{7,5},{8,10},{9,11},{10,... | collective-permute-start | bytes 294920 | tf_op jit(solution)/shard_map/ppermute | solution.py:153
  103.6 4.1 %collective-permute-start.7 = (bf16[128,384]{1,0:T(8,128)(2,1)}, bf16[128,384]{1,0:T(8,128)(2,1)S(1)}, u32[]{:S(2)}, u32[]{:S(2)}) collective-permute-start(bf16[128,384]{1,0:T(8,128)(2,1)} %get-tuple-element.28), channel_id=1, source_target_pairs={{0,1},{1,0},{2,3},{3,2},{4,5},{5,4},{6,7},{7,6},{8,9},{9,8},{10,11... | collective-permute-start | bytes 294920 | tf_op jit(solution)/shard_map/ppermute | solution.py:153
  103.6 5.3 %collective-permute-start.8 = (bf16[128,384]{1,0:T(8,128)(2,1)}, bf16[128,384]{1,0:T(8,128)(2,1)S(1)}, u32[]{:S(2)}, u32[]{:S(2)}) collective-permute-start(bf16[128,384]{1,0:T(8,128)(2,1)} %get-tuple-element.29), channel_id=1, source_target_pairs={{0,3},{1,2},{2,1},{3,0},{4,7},{5,6},{6,5},{7,4},{8,11},{9,10},{10,... | collective-permute-start | bytes 294920 | tf_op jit(solution)/shard_map/ppermute | solution.py:153

commit v14 on v13

--- a/solution.py
+++ b/solution.py
@@ -31,27 +31,31 @@
     total = k_scr.shape[0]
     groups = tk // 128
 
-    @pl.when(pl.program_id(0) == 0)
+    first = pl.program_id(0) == 0
+
+    def loads(src_k, src_v, which=(0, 1, 2, 3)):
+        plan = [
+            (src_k, k_scr.at[pl.ds(0, n_cache)]),
+            (nk_hbm, k_scr.at[pl.ds(n_cache, total - n_cache)]),
+            (src_v, v_scr.at[pl.ds(0, n_cache)]),
+            (nv_hbm, v_scr.at[pl.ds(n_cache, total - n_cache)]),
+        ]
+        return [pltpu.make_async_copy(*plan[i], sems.at[i]) for i in which]
+
+    @pl.when(first & (part_ref[0] == 0))
     def _():
-        def load(src_k, src_v):
-            copies = [
-                pltpu.make_async_copy(src_k, k_scr.at[pl.ds(0, n_cache)], sems.at[0]),
-                pltpu.make_async_copy(src_v, v_scr.at[pl.ds(0, n_cache)], sems.at[1]),
-                pltpu.make_async_copy(nk_hbm, k_scr.at[pl.ds(n_cache, total - n_cache)], sems.at[2]),
-                pltpu.make_async_copy(nv_hbm, v_scr.at[pl.ds(n_cache, total - n_cache)], sems.at[3]),
-            ]
-            for copy in copies:
-                copy.start()
-            for copy in copies:
-                copy.wait()
-
-        @pl.when(part_ref[0] == 0)
-        def _():
-            load(mine_hbm, other_hbm)
-
-        @pl.when(part_ref[0] != 0)
-        def _():
-            load(other_hbm, mine_hbm)
+        for copy in loads(mine_hbm, other_hbm):
+            copy.start()
+
+    @pl.when(first & (part_ref[0] != 0))
+    def _():
+        for copy in loads(other_hbm, mine_hbm):
+            copy.start()
+
+    @pl.when(first)
+    def _():
+        for copy in loads(mine_hbm, other_hbm, (0, 1)):
+            copy.wait()
 
     q = q_ref[...]
     part_rows = bq // len(o_refs)
@@ -96,6 +100,11 @@
         start = pl.multiple_of(c * tk, tk)
         w = (s_scr[:, pl.ds(start, tk)] * inverse).astype(jnp.bfloat16)
         return acc + jnp.dot(w, v_scr[pl.ds(start, tk), :], preferred_element_type=jnp.float32)
+
+    @pl.when(first)
+    def _():
+        for copy in loads(mine_hbm, other_hbm, (2, 3)):
+            copy.wait()
 
     acc = lax.fori_loop(0, total // tk, weigh, jnp.zeros((bq, head_dim), jnp.float32), unroll=8)
     for k, o_ref in enumerate(o_refs):
@@ -248,7 +257,8 @@
     holds_keys = current_head % 2 == 0
     turned = rotate(own_part[:, None, :], positions)[:, 0]
     own_ready = jnp.where(holds_keys, turned, own_part).astype(jnp.bfloat16)
-    received, own_ready = lax.optimization_barrier((received, own_ready))
+    queries = queries[0:NEWTOK].reshape(NEWTOK, group_heads * head_dim)
+    received, own_ready, queries = lax.optimization_barrier((received, own_ready, queries))
     partner_ready = from_partner(own_ready, "head", 0)
     partner_blocks = [row_masks.index(m ^ 1) for m in row_masks]
     partner_ready = jnp.concatenate(
@@ -260,7 +270,6 @@
     cache_ok = (has_page[:, 0, :, None] & (key_pos[:, 0] < my_lengths[0])).reshape(-1)
     key_ok = jnp.concatenate([cache_ok, jnp.take(mask_rows, true_row) == 1])
     bias = jnp.where(key_ok, 0.0, -jnp.inf).astype(jnp.float32)
-    queries = queries[0:NEWTOK].reshape(NEWTOK, group_heads * head_dim)
     other_half = exchange(received, "head", 1)
     pieces = attend(
         queries,

time: 114 us -> 116 us (1.018)
  waiting for transfers between devices: 38.1 us -> 40.5 us
    all_to_all x1, waiting for transfers between devices: 19.4 us -> 26.9 us  [body(): lax.all_to_all(outgoing, 'dp', split_axis=0, concat_axis=0, tiled=True)]
    ppermute x10, waiting for transfers between devices: 18.7 us -> 13.2 us  [exchange(): return lax.ppermute(value, axis, pairs)]
    all_to_all x1, starting transfers between devices: 7.38 us -> 6.05 us  [body(): lax.all_to_all(outgoing, 'dp', split_axis=0, concat_axis=0, tiled=True)]
  transfers between devices with their start and end apart: 12 -> 12, of which waited for: 4 -> 6; matrix products, arithmetic and copies ran while one was open for 17% -> 15% of each run, Pallas kernels for 28% -> 27%
where the time goes in v14:
time: 116 us; the launch traced here: 115 us
  waiting for transfers between devices  40.5 us (35%)
  Pallas kernels  30.9 us (27%)
  starting transfers between devices  12.2 us (11%)
  local copies, waits for them, and re-layouts  11.6 us (10%)
  matrix products  10.3 us (9%)
  other arithmetic  9.64 us (8%)
    pallas_call x1, Pallas kernels, attend(): pl.pallas_call(lambda *refs: attend_kernel(n_cache, tk, scale, *refs), ou...  30.9 us
    all_to_all x1, waiting for transfers between devices, body(): lax.all_to_all(outgoing, 'dp', split_axis=0, concat_axis=0, tiled=True)  26.9 us
    ppermute x10, waiting for transfers between devices, exchange(): return lax.ppermute(value, axis, pairs)  13.2 us
    all_to_all x1, starting transfers between devices, body(): lax.all_to_all(outgoing, 'dp', split_axis=0, concat_axis=0, tiled=True)  6.05 us
    ppermute x10, starting transfers between devices, exchange(): return lax.ppermute(value, axis, pairs)  5.61 us
    gather x1, local copies, waits for them, and re-layouts, body(): outgoing = kv_pool[local_page.reshape(-1), key_value_head, part]  5.06 us
    dot_general x1, matrix products, body(): out = jnp.dot(ordered, held_w, preferred_element_type=jnp.float32)  4.63 us
    gather x1, local copies, waits for them, and re-layouts, body(): key_ok = jnp.concatenate([cache_ok, jnp.take(mask_rows, true_row) == 1])  3.49 us
  transfers between devices with their start and end apart: 12, of which 6 were waited for; matrix products, arithmetic and copies ran while one was open for 15% of the time, Pallas kernels for 27%

profile of v14, /device:TPU:0, one launch (start us, length us, event | category | flops | bytes accessed | tf_op | source)
XLA Modules:
  0.0 115.4 jit_solution(5118075764751295400)
XLA Ops:
  0.0 0.0 copy-start
  0.0 0.0 copy-start.1
  0.0 0.9 broadcast_compare_fusion.1
  0.9 0.2 reduce_window_sum.22
  1.1 0.7 add_select_fusion.1
  1.8 0.2 select_reduce_fusion.1
  2.0 0.1 reshape.522
  2.1 0.7 convert_element_type.49
  2.8 5.1 %gather_fusion = bf16[64,128,128]{2,1,0:T(8,128)(2,1)} fusion(bf16[48,2,2,128,128]{4,3,2,1,0:T(8,128)(2,1)} %param.14, s32[64]{0:T(128)S(1)} %fusion.45), kind=kCustom, calls=%fused_computation | custom fusion | bytes 4195072 | tf_op jit(solution)/shard_map/gather | solution.py:210
  7.8 0.0 copy-done.1
  7.9 0.0 copy-start.3
  7.9 0.2 fusion.11
  8.1 1.2 fusion.13
  9.3 0.5 collective-permute-start.2
  9.7 2.5 %collective-permute-start.1 = (bf16[128,3072]{1,0:T(8,128)(2,1)}, bf16[128,3072]{1,0:T(8,128)(2,1)}, u32[]{:S(2)}, u32[]{:S(2)}) collective-permute-start(bf16[128,3072]{1,0:T(8,128)(2,1)} %fusion.13), channel_id=1, source_target_pairs={{0,2},{1,3},{2,0},{3,1},{4,6},{5,7},{6,4},{7,5},{8,10},{9,11},{10,... | collective-permute-start | bytes 2359304 | tf_op jit(solution)/shard_map/ppermute | solution.py:162
  12.2 0.0 collective-permute-start
  12.3 0.2 collective-permute-start.9
  12.5 6.1 %all-to-all-start = ((bf16[64,128,128]{2,1,0:T(8,128)(2,1)}), bf16[64,128,128]{2,1,0:T(8,128)(2,1)}, u32[]{:S(2)}, u32[]{:S(2)}) async-start(bf16[64,128,128]{2,1,0:T(8,128)(2,1)} %gather_fusion), calls=%async_computation | async-start | bytes 4194304 | tf_op jit(solution)/shard_map/all_to_all | solution.py:212
  18.6 0.0 copy-done.3
  18.6 0.6 dynamic_slice.11
  19.2 0.2 reduce_window_sum.23
  19.4 0.8 dynamic_slice.14
  20.2 3.5 %gather_fusion.1 = s32[512]{0:T(512)S(1)} fusion(s32[512]{0:T(512)S(1)} %dynamic_slice.14, s32[1024]{0:T(1024)S(1)} %pad_clamp_fusion), kind=kCustom, calls=%fused_computation.1 | custom fusion | bytes 6144 | tf_op jit(solution)/shard_map/jit(_take)/gather | solution.py:271
  23.7 0.7 fusion.40
  24.4 6.5 %collective-permute-done.1 = bf16[128,3072]{1,0:T(8,128)(2,1)} collective-permute-done((bf16[128,3072]{1,0:T(8,128)(2,1)}, bf16[128,3072]{1,0:T(8,128)(2,1)}, u32[]{:S(2)}, u32[]{:S(2)}) %collective-permute-start.1) | collective-permute-done | bytes 786464 | tf_op jit(solution)/shard_map/ppermute | solution.py:162
  30.9 0.0 collective-permute-start.3
  31.0 0.5 multiply_cosine_fusion.1
  31.5 0.0 copy-start.2
  31.5 0.0 collective-permute-done.2
  31.5 1.9 %collective-permute-done.3 = bf16[128,3072]{1,0:T(8,128)(2,1)S(1)} collective-permute-done((bf16[128,3072]{1,0:T(8,128)(2,1)}, bf16[128,3072]{1,0:T(8,128)(2,1)S(1)}, u32[]{:S(2)}, u32[]{:S(2)}) %collective-permute-start.3) | collective-permute-done | bytes 786464 | tf_op jit(solution)/shard_map/ppermute | solution.py:162
  33.4 0.0 copy-done
  33.4 3.0 %fusion.14 = f32[512,384]{0,1:T(8,128)S(1)} fusion(bf16[3072,384]{1,0:T(8,128)(2,1)S(1)} %copy-done, bf16[128,3072]{1,0:T(8,128)(2,1)S(1)} %collective-permute-done.3, bf16[128,3072]{1,0:T(8,128)(2,1)} %collective-permute-done.2, bf16[128,3072]{1,0:T(8,128)(2,1)} %collective-permute-done.1, bf16[128,3072]{1,0:T(8,128)(2,1)} %fusion.13), kind=kOutput, calls=%fused_computation.17 | convolution fusion | flops 1220542464 | bytes 6291456 | tf_op jit(solution)/shard_map/dot_general | solution.py:247
  36.5 0.1 subtract_convert_fusion
  36.7 0.0 copy-done.2
  36.7 2.6 %fusion.15 = f32[512,128]{1,0:T(8,128)S(1)} fusion(bf16[3072,128]{1,0:T(8,128)(2,1)S(1)} %copy-done.2, bf16[128,3072]{1,0:T(8,128)(2,1)S(1)} %collective-permute-done.3, bf16[128,3072]{1,0:T(8,128)(2,1)} %collective-permute-done.2, bf16[128,3072]{1,0:T(8,128)(2,1)} %collective-permute-done.1, bf16[128,3072]{1,0:T(8,128)(2,1)} %fusion.13), kind=kOutput, calls=%fused_computation.18 | convolution fusion | flops 415236096 | bytes 4194304 | tf_op jit(solution)/shard_map/dot_general | solution.py:248
  39.3 1.2 %fusion.27 = (bf16[512,1,64]{2,0,1:T(8,128)(2,1)S(1)}, bf16[512,1,64]{2,0,1:T(8,128)(2,1)S(1)}) fusion(f32[512,1,128]{2,0,1:T(8,128)S(1)} %bitcast.32, f32[64]{0:T(128)S(1)} %multiply_exponential_fusion, f32[512]{0:T(512)S(1)} %fusion.40), kind=kLoop, calls=%fused_computation.35 | loop fusion | flops 294912 | bytes 395520 | tf_op jit(solution)/shard_map/sub | solution.py:175
  40.5 0.1 fusion.30
  40.6 26.9 %all-to-all-done = bf16[64,128,128]{2,1,0:T(8,128)(2,1)} async-done(((bf16[64,128,128]{2,1,0:T(8,128)(2,1)}), bf16[64,128,128]{2,1,0:T(8,128)(2,1)}, u32[]{:S(2)}, u32[]{:S(2)}) %all-to-all-start) | async-done | bytes 2097184 | tf_op jit(solution)/shard_map/all_to_all | solution.py:212
  67.6 0.0 collective-permute-start.4
  67.6 0.2 select_reduce_fusion
  67.8 0.2 fusion.33
  68.0 0.7 fusion.34
  68.8 0.6 collective-permute-start.5
  69.3 0.7 add_select_fusion.refs_6_
  70.0 0.6 concatenate.90.refs_0_
  70.6 0.9 copy.19.refs_1_
  71.5 0.4 collective-permute-done.5
  71.9 0.8 broadcast_select_fusion
  72.7 0.0 collective-permute-done.4
  72.7 30.9 %paged_prefill_attention.1 = (bf16[128,384]{1,0:T(8,128)(2,1)}, bf16[128,384]{1,0:T(8,128)(2,1)}, bf16[128,384]{1,0:T(8,128)(2,1)}, bf16[128,384]{1,0:T(8,128)(2,1)}) custom-call(s32[5]{0:T(128)} %concatenate.90.refs_0_, bf16[512,384]{1,0:T(8,128)(2,1)} %copy.19.refs_1_, bf16[8192,128]{1,0:T(8,128)(2,1)} %bitcast.11.refs_2_, ...), custom_call_target="tpu_custom_call" | custom-call | flops 6845104128 | bytes 5277696 | tf_op jit(solution)/shard_map/paged_prefill_attention/pallas_call | solution.py:147
  103.6 0.0 collective-permute-done
  103.6 0.2 collective-permute-start.10
  103.8 1.5 %collective-permute-start.6 = (bf16[128,384]{1,0:T(8,128)(2,1)}, bf16[128,384]{1,0:T(8,128)(2,1)S(1)}, u32[]{:S(2)}, u32[]{:S(2)}) collective-permute-start(bf16[128,384]{1,0:T(8,128)(2,1)} %get-tuple-element.29), channel_id=1, source_target_pairs={{0,2},{1,3},{2,0},{3,1},{4,6},{5,7},{6,4},{7,5},{8,10},{9,11},{10,... | collective-permute-start | bytes 294920 | tf_op jit(solution)/shard_map/ppermute | solution.py:162
  105.3 0.1 collective-permute-start.7
  105.4 0.6 collective-permute-start.8
  106.0 0.0 collective-permute-done.9
  106.0 3.6 %collective-permute-done.6 = bf16[128,384]{1,0:T(8,128)(2,1)S(1)} collective-permute-done((bf16[128,384]{1,0:T(8,128)(2,1)}, bf16[128,384]{1,0:T(8,128)(2,1)S(1)}, u32[]{:S(2)}, u32[]{:S(2)}) %collective-permute-start.6) | collective-permute-done | bytes 98336 | tf_op jit(solution)/shard_map/ppermute | solution.py:162
  109.6 0.0 collective-permute-done.7
  109.6 1.2 %collective-permute-done.8 = bf16[128,384]{1,0:T(8,128)(2,1)S(1)} collective-permute-done((bf16[128,384]{1,0:T(8,128)(2,1)}, bf16[128,384]{1,0:T(8,128)(2,1)S(1)}, u32[]{:S(2)}, u32[]{:S(2)}) %collective-permute-start.8) | collective-permute-done | bytes 98336 | tf_op jit(solution)/shard_map/ppermute | solution.py:162
  110.7 0.0 collective-permute-done.10
  110.7 4.6 %fusion.8 = bf16[128,3072]{1,0:T(8,128)(2,1)} fusion(bf16[384,3072]{1,0:T(8,128)(2,1)S(1)} %collective-permute-done.10, bf16[384,3072]{1,0:T(8,128)(2,1)} %collective-permute-done.9, bf16[384,3072]{1,0:T(8,128)(2,1)} %collective-permute-done, bf16[384,3072]{1,0:T(8,128)(2,1)} %param.13, bf16[128,384]{1,0:T(8,128)(2,1)S(1)} %collective-permute-done.8, ...), kind=kOutput, calls=%fused_computation.10 | convolution fusion | flops 1247674368 | bytes 10616832 | tf_op jit(solution)/shard_map/dot_general | solution.py:294
  (18 shorter events, 0.2 us)
Async XLA Ops:
  0.0 33.4 %copy-start = (bf16[3072,384]{1,0:T(8,128)(2,1)S(1)}, bf16[3072,384]{1,0:T(8,128)(2,1)}, u32[]{:S(2)}) copy-start(bf16[3072,384]{1,0:T(8,128)(2,1)} %param.11) | copy-start | bytes 7077892
  0.0 7.8 %copy-start.1 = (bf16[128,3072]{1,0:T(8,128)(2,1)S(1)}, bf16[128,3072]{1,0:T(8,128)(2,1)}, u32[]{:S(2)}) copy-start(bf16[128,3072]{1,0:T(8,128)(2,1)} %param.9) | copy-start | bytes 2359300
  7.9 10.7 %copy-start.3 = (s32[8]{0:T(128)S(1)}, s32[8]{0:T(128)}, u32[]{:S(2)}) copy-start(s32[8]{0:T(128)} %param.15) | copy-start | bytes 100
  9.3 22.3 %collective-permute-start.2 = (bf16[128,3072]{1,0:T(8,128)(2,1)}, bf16[128,3072]{1,0:T(8,128)(2,1)}, u32[]{:S(2)}, u32[]{:S(2)}) collective-permute-start(bf16[128,3072]{1,0:T(8,128)(2,1)} %fusion.13), channel_id=1, source_target_pairs={{0,1},{1,0},{2,3},{3,2},{4,5},{5,4},{6,7},{7,6},{8,9},{9,8},{10,11... | collective-permute-start | bytes 2359304 | tf_op jit(solution)/shard_map/ppermute | solution.py:162
  9.7 21.2 %collective-permute-start.1 = (bf16[128,3072]{1,0:T(8,128)(2,1)}, bf16[128,3072]{1,0:T(8,128)(2,1)}, u32[]{:S(2)}, u32[]{:S(2)}) collective-permute-start(bf16[128,3072]{1,0:T(8,128)(2,1)} %fusion.13), channel_id=1, source_target_pairs={{0,2},{1,3},{2,0},{3,1},{4,6},{5,7},{6,4},{7,5},{8,10},{9,11},{10,... | collective-permute-start | bytes 2359304 | tf_op jit(solution)/shard_map/ppermute | solution.py:162
  12.2 91.4 %collective-permute-start = (bf16[384,3072]{1,0:T(8,128)(2,1)}, bf16[384,3072]{1,0:T(8,128)(2,1)}, u32[]{:S(2)}, u32[]{:S(2)}) collective-permute-start(bf16[384,3072]{1,0:T(8,128)(2,1)} %param.13), channel_id=1, source_target_pairs={{0,2},{1,3},{2,0},{3,1},{4,6},{5,7},{6,4},{7,5},{8,10},{9,11},{10,... | collective-permute-start | bytes 7077896 | tf_op jit(solution)/shard_map/ppermute | solution.py:162
  12.3 93.7 %collective-permute-start.9 = (bf16[384,3072]{1,0:T(8,128)(2,1)}, bf16[384,3072]{1,0:T(8,128)(2,1)}, u32[]{:S(2)}, u32[]{:S(2)}) collective-permute-start(bf16[384,3072]{1,0:T(8,128)(2,1)} %param.13), channel_id=1, source_target_pairs={{0,1},{1,0},{2,3},{3,2},{4,5},{5,4},{6,7},{7,6},{8,9},{9,8},{10,11... | collective-permute-start | bytes 7077896 | tf_op jit(solution)/shard_map/ppermute | solution.py:162
  12.5 55.1 %all-to-all-start = ((bf16[64,128,128]{2,1,0:T(8,128)(2,1)}), bf16[64,128,128]{2,1,0:T(8,128)(2,1)}, u32[]{:S(2)}, u32[]{:S(2)}) async-start(bf16[64,128,128]{2,1,0:T(8,128)(2,1)} %gather_fusion), calls=%async_computation | async-start | bytes 4194304 | tf_op jit(solution)/shard_map/all_to_all | solution.py:212
  30.9 2.5 %collective-permute-start.3 = (bf16[128,3072]{1,0:T(8,128)(2,1)}, bf16[128,3072]{1,0:T(8,128)(2,1)S(1)}, u32[]{:S(2)}, u32[]{:S(2)}) collective-permute-start(bf16[128,3072]{1,0:T(8,128)(2,1)} %collective-permute-done.1), channel_id=1, source_target_pairs={{0,1},{1,0},{2,3},{3,2},{4,5},{5,4},{6,7},{7,6},{8,9},{9,8},{10,11... | collective-permute-start | bytes 2359304 | tf_op jit(solution)/shard_map/ppermute | solution.py:162
  31.5 5.1 %copy-start.2 = (bf16[3072,128]{1,0:T(8,128)(2,1)S(1)}, bf16[3072,128]{1,0:T(8,128)(2,1)}, u32[]{:S(2)}) copy-start(bf16[3072,128]{1,0:T(8,128)(2,1)} %param.12) | copy-start | bytes 2359300
  67.6 5.1 %collective-permute-start.4 = (bf16[64,128,128]{2,1,0:T(8,128)(2,1)}, bf16[64,128,128]{2,1,0:T(8,128)(2,1)}, u32[]{:S(2)}, u32[]{:S(2)}) collective-permute-start(bf16[64,128,128]{2,1,0:T(8,128)(2,1)} %all-to-all-done), channel_id=1, source_target_pairs={{0,1},{1,0},{2,3},{3,2},{4,5},{5,4},{6,7},{7,6},{8,9},{9,8},{10,11... | collective-permute-start | bytes 6291464 | tf_op jit(solution)/shard_map/ppermute | solution.py:162
  68.8 3.1 %collective-permute-start.5 = (bf16[512,128]{1,0:T(8,128)(2,1)S(1)}, bf16[512,128]{1,0:T(8,128)(2,1)S(1)}, u32[]{:S(2)}, u32[]{:S(2)}) collective-permute-start(bf16[512,128]{1,0:T(8,128)(2,1)S(1)} %fusion.30), channel_id=1, source_target_pairs={{0,1},{1,0},{2,3},{3,2},{4,5},{5,4},{6,7},{7,6},{8,9},{9,8},{10,11... | collective-permute-start | bytes 393224 | tf_op jit(solution)/shard_map/ppermute | solution.py:22
  103.6 7.1 %collective-permute-start.10 = (bf16[384,3072]{1,0:T(8,128)(2,1)}, bf16[384,3072]{1,0:T(8,128)(2,1)S(1)}, u32[]{:S(2)}, u32[]{:S(2)}) collective-permute-start(bf16[384,3072]{1,0:T(8,128)(2,1)} %collective-permute-done), channel_id=1, source_target_pairs={{0,1},{1,0},{2,3},{3,2},{4,5},{5,4},{6,7},{7,6},{8,9},{9,8},{10,11... | collective-permute-start | bytes 7077896 | tf_op jit(solution)/shard_map/ppermute | solution.py:162
  103.8 5.8 %collective-permute-start.6 = (bf16[128,384]{1,0:T(8,128)(2,1)}, bf16[128,384]{1,0:T(8,128)(2,1)S(1)}, u32[]{:S(2)}, u32[]{:S(2)}) collective-permute-start(bf16[128,384]{1,0:T(8,128)(2,1)} %get-tuple-element.29), channel_id=1, source_target_pairs={{0,2},{1,3},{2,0},{3,1},{4,6},{5,7},{6,4},{7,5},{8,10},{9,11},{10,... | collective-permute-start | bytes 294920 | tf_op jit(solution)/shard_map/ppermute | solution.py:162
  105.3 4.2 %collective-permute-start.7 = (bf16[128,384]{1,0:T(8,128)(2,1)}, bf16[128,384]{1,0:T(8,128)(2,1)S(1)}, u32[]{:S(2)}, u32[]{:S(2)}) collective-permute-start(bf16[128,384]{1,0:T(8,128)(2,1)} %get-tuple-element.30), channel_id=1, source_target_pairs={{0,1},{1,0},{2,3},{3,2},{4,5},{5,4},{6,7},{7,6},{8,9},{9,8},{10,11... | collective-permute-start | bytes 294920 | tf_op jit(solution)/shard_map/ppermute | solution.py:162
  105.4 5.3 %collective-permute-start.8 = (bf16[128,384]{1,0:T(8,128)(2,1)}, bf16[128,384]{1,0:T(8,128)(2,1)S(1)}, u32[]{:S(2)}, u32[]{:S(2)}) collective-permute-start(bf16[128,384]{1,0:T(8,128)(2,1)} %get-tuple-element.31), channel_id=1, source_target_pairs={{0,3},{1,2},{2,1},{3,0},{4,7},{5,6},{6,5},{7,4},{8,11},{9,10},{10,... | collective-permute-start | bytes 294920 | tf_op jit(solution)/shard_map/ppermute | solution.py:162

commit v15 on v14

--- a/solution.py
+++ b/solution.py
@@ -257,8 +257,7 @@
     holds_keys = current_head % 2 == 0
     turned = rotate(own_part[:, None, :], positions)[:, 0]
     own_ready = jnp.where(holds_keys, turned, own_part).astype(jnp.bfloat16)
-    queries = queries[0:NEWTOK].reshape(NEWTOK, group_heads * head_dim)
-    received, own_ready, queries = lax.optimization_barrier((received, own_ready, queries))
+    received, own_ready = lax.optimization_barrier((received, own_ready))
     partner_ready = from_partner(own_ready, "head", 0)
     partner_blocks = [row_masks.index(m ^ 1) for m in row_masks]
     partner_ready = jnp.concatenate(
@@ -270,6 +269,7 @@
     cache_ok = (has_page[:, 0, :, None] & (key_pos[:, 0] < my_lengths[0])).reshape(-1)
     key_ok = jnp.concatenate([cache_ok, jnp.take(mask_rows, true_row) == 1])
     bias = jnp.where(key_ok, 0.0, -jnp.inf).astype(jnp.float32)
+    queries = queries[0:NEWTOK].reshape(NEWTOK, group_heads * head_dim)
     other_half = exchange(received, "head", 1)
     pieces = attend(
         queries,

time: 116 us -> 113 us (0.974)
  waiting for transfers between devices: 40.5 us -> 38.1 us
    all_to_all x1, waiting for transfers between devices: 26.9 us -> 19.4 us  [body(): lax.all_to_all(outgoing, 'dp', split_axis=0, concat_axis=0, tiled=True)]
    ppermute x10, waiting for transfers between devices: 13.2 us -> 18.7 us  [exchange(): return lax.ppermute(value, axis, pairs)]
    all_to_all x1, starting transfers between devices: 6.05 us -> 7.38 us  [body(): lax.all_to_all(outgoing, 'dp', split_axis=0, concat_axis=0, tiled=True)]
  transfers between devices with their start and end apart: 12 -> 12, of which waited for: 6 -> 4; matrix products, arithmetic and copies ran while one was open for 15% -> 17% of each run, Pallas kernels for 27% -> 27%
where the time goes in v15:
time: 113 us
  waiting for transfers between devices  38.1 us (34%)
  Pallas kernels  30.9 us (27%)
  starting transfers between devices  12.4 us (11%)
  local copies, waits for them, and re-layouts  11.7 us (10%)
  matrix products  10.5 us (9%)
  other arithmetic  9.02 us (8%)
    pallas_call x1, Pallas kernels, attend(): pl.pallas_call(lambda *refs: attend_kernel(n_cache, tk, scale, *refs), ou...  30.9 us
    all_to_all x1, waiting for transfers between devices, body(): lax.all_to_all(outgoing, 'dp', split_axis=0, concat_axis=0, tiled=True)  19.4 us
    ppermute x10, waiting for transfers between devices, exchange(): return lax.ppermute(value, axis, pairs)  18.7 us
    all_to_all x1, starting transfers between devices, body(): lax.all_to_all(outgoing, 'dp', split_axis=0, concat_axis=0, tiled=True)  7.38 us
    gather x1, local copies, waits for them, and re-layouts, body(): outgoing = kv_pool[local_page.reshape(-1), key_value_head, part]  5.07 us
    dot_general x1, matrix products, body(): out = jnp.dot(ordered, held_w, preferred_element_type=jnp.float32)  4.63 us
    ppermute x10, starting transfers between devices, exchange(): return lax.ppermute(value, axis, pairs)  4.49 us
    gather x1, local copies, waits for them, and re-layouts, body(): key_ok = jnp.concatenate([cache_ok, jnp.take(mask_rows, true_row) == 1])  3.48 us
  transfers between devices with their start and end apart: 12, of which 4 were waited for; matrix products, arithmetic and copies ran while one was open for 17% of the time, Pallas kernels for 27%

profile of v15, /device:TPU:0, one launch (start us, length us, event | category | flops | bytes accessed | tf_op | source)
XLA Modules:
  0.0 112.9 jit_solution(16983997942441537358)
XLA Ops:
  0.0 0.0 copy-start
  0.0 0.9 broadcast_compare_fusion.1
  0.9 0.2 reduce_window_sum.22
  1.1 0.7 add_select_fusion.1
  1.8 0.2 select_reduce_fusion.1
  2.0 0.1 reshape.522
  2.1 5.1 %gather_fusion = bf16[64,128,128]{2,1,0:T(8,128)(2,1)} fusion(bf16[48,2,2,128,128]{4,3,2,1,0:T(8,128)(2,1)} %param.14, s32[64]{0:T(128)S(1)} %fusion.45), kind=kCustom, calls=%fused_computation | custom fusion | bytes 4195072 | tf_op jit(solution)/shard_map/gather | solution.py:210
  7.2 0.0 copy-start.2
  7.2 0.0 copy-start.1
  7.2 7.4 %all-to-all-start = ((bf16[64,128,128]{2,1,0:T(8,128)(2,1)}), bf16[64,128,128]{2,1,0:T(8,128)(2,1)}, u32[]{:S(2)}, u32[]{:S(2)}) async-start(bf16[64,128,128]{2,1,0:T(8,128)(2,1)} %gather_fusion), calls=%async_computation | async-start | bytes 4194304 | tf_op jit(solution)/shard_map/all_to_all | solution.py:212
  14.5 0.0 copy-done.2
  14.5 0.0 copy-start.3
  14.6 0.0 copy-done.1
  14.6 0.2 fusion.11
  14.8 1.2 %fusion.13 = bf16[128,3072]{1,0:T(8,128)(2,1)} fusion(bf16[128,3072]{1,0:T(8,128)(2,1)S(1)} %copy-done.1, f32[3072]{0:T(1024)S(1)} %convert_element_type.49, f32[128]{0:T(128)S(1)} %add_rsqrt_fusion), kind=kLoop, calls=%fused_computation.16 | loop fusion | flops 1572864 | bytes 1585664 | tf_op jit(solution)/shard_map/convert_element_type | solution.py:227
  16.0 0.0 collective-permute-start.2
  16.0 1.5 %collective-permute-start.1 = (bf16[128,3072]{1,0:T(8,128)(2,1)}, bf16[128,3072]{1,0:T(8,128)(2,1)}, u32[]{:S(2)}, u32[]{:S(2)}) collective-permute-start(bf16[128,3072]{1,0:T(8,128)(2,1)} %fusion.13), channel_id=1, source_target_pairs={{0,2},{1,3},{2,0},{3,1},{4,6},{5,7},{6,4},{7,5},{8,10},{9,11},{10,... | collective-permute-start | bytes 2359304 | tf_op jit(solution)/shard_map/ppermute | solution.py:162
  17.5 0.5 collective-permute-start
  18.0 0.0 collective-permute-start.9
  18.1 0.2 reduce_window_sum.23
  18.3 0.8 dynamic_slice.14
  19.1 3.5 %gather_fusion.1 = s32[512]{0:T(512)S(1)} fusion(s32[512]{0:T(512)S(1)} %dynamic_slice.14, s32[1024]{0:T(1024)S(1)} %pad_clamp_fusion), kind=kCustom, calls=%fused_computation.1 | custom fusion | bytes 6144 | tf_op jit(solution)/shard_map/jit(_take)/gather | solution.py:270
  22.6 14.0 %collective-permute-done.1 = bf16[128,3072]{1,0:T(8,128)(2,1)} collective-permute-done((bf16[128,3072]{1,0:T(8,128)(2,1)}, bf16[128,3072]{1,0:T(8,128)(2,1)}, u32[]{:S(2)}, u32[]{:S(2)}) %collective-permute-start.1) | collective-permute-done | bytes 786464 | tf_op jit(solution)/shard_map/ppermute | solution.py:162
  36.6 0.0 collective-permute-start.3
  36.6 0.2 fusion.33
  36.9 0.0 copy-done.3
  36.9 0.7 dynamic_slice.11
  37.5 0.2 select_reduce_fusion
  37.8 0.8 fusion.34
  38.6 0.7 fusion.40
  39.3 0.0 collective-permute-done.2
  39.3 0.0 collective-permute-done.3
  39.3 2.8 %fusion.14 = f32[512,128]{1,0:T(8,128)S(1)} fusion(bf16[3072,128]{1,0:T(8,128)(2,1)} %param.12, bf16[128,3072]{1,0:T(8,128)(2,1)} %collective-permute-done.3, bf16[128,3072]{1,0:T(8,128)(2,1)S(1)} %collective-permute-done.2, bf16[128,3072]{1,0:T(8,128)(2,1)} %collective-permute-done.1, bf16[128,3072]{1,0:T(8,128)(2,1)} %fusion.13), kind=kOutput, calls=%fused_computation.17 | convolution fusion | flops 415236096 | bytes 4194304 | tf_op jit(solution)/shard_map/dot_general | solution.py:248
  42.1 1.2 %fusion.27 = (bf16[512,1,64]{2,0,1:T(8,128)(2,1)S(1)}, bf16[512,1,64]{2,0,1:T(8,128)(2,1)S(1)}) fusion(f32[512,1,128]{2,0,1:T(8,128)S(1)} %bitcast.32, f32[64]{0:T(128)S(1)} %multiply_exponential_fusion, f32[512]{0:T(512)S(1)} %fusion.40), kind=kLoop, calls=%fused_computation.35 | loop fusion | flops 294912 | bytes 395520 | tf_op jit(solution)/shard_map/sub | solution.py:175
  43.4 0.1 fusion.30
  43.5 19.4 %all-to-all-done = bf16[64,128,128]{2,1,0:T(8,128)(2,1)} async-done(((bf16[64,128,128]{2,1,0:T(8,128)(2,1)}), bf16[64,128,128]{2,1,0:T(8,128)(2,1)}, u32[]{:S(2)}, u32[]{:S(2)}) %all-to-all-start) | async-done | bytes 2097184 | tf_op jit(solution)/shard_map/all_to_all | solution.py:212
  62.9 0.0 collective-permute-start.4
  62.9 0.7 add_select_fusion.refs_6_
  63.5 0.7 concatenate.90.refs_0_
  64.2 0.5 multiply_cosine_fusion.1
  64.7 0.0 copy-done
  64.8 3.0 %fusion.15 = f32[512,384]{0,1:T(8,128)S(1)} fusion(bf16[3072,384]{1,0:T(8,128)(2,1)S(1)} %copy-done, bf16[128,3072]{1,0:T(8,128)(2,1)} %collective-permute-done.3, bf16[128,3072]{1,0:T(8,128)(2,1)S(1)} %collective-permute-done.2, bf16[128,3072]{1,0:T(8,128)(2,1)} %collective-permute-done.1, bf16[128,3072]{1,0:T(8,128)(2,1)} %fusion.13), kind=kOutput, calls=%fused_computation.18 | convolution fusion | flops 1220542464 | bytes 6291456 | tf_op jit(solution)/shard_map/dot_general | solution.py:247
  67.8 0.6 collective-permute-start.5
  68.4 0.1 subtract_convert_fusion
  68.6 0.9 copy.19.refs_1_
  69.5 0.0 collective-permute-done.5
  69.5 0.8 broadcast_select_fusion
  70.3 0.0 collective-permute-done.4
  70.3 30.9 %paged_prefill_attention.1 = (bf16[128,384]{1,0:T(8,128)(2,1)}, bf16[128,384]{1,0:T(8,128)(2,1)}, bf16[128,384]{1,0:T(8,128)(2,1)}, bf16[128,384]{1,0:T(8,128)(2,1)}) custom-call(s32[5]{0:T(128)} %concatenate.90.refs_0_, bf16[512,384]{1,0:T(8,128)(2,1)} %copy.19.refs_1_, bf16[8192,128]{1,0:T(8,128)(2,1)} %bitcast.11.refs_2_, ...), custom_call_target="tpu_custom_call" | custom-call | flops 6845104128 | bytes 5277696 | tf_op jit(solution)/shard_map/paged_prefill_attention/pallas_call | solution.py:147
  101.2 0.0 collective-permute-done
  101.2 0.3 collective-permute-start.10
  101.5 1.5 %collective-permute-start.6 = (bf16[128,384]{1,0:T(8,128)(2,1)}, bf16[128,384]{1,0:T(8,128)(2,1)S(1)}, u32[]{:S(2)}, u32[]{:S(2)}) collective-permute-start(bf16[128,384]{1,0:T(8,128)(2,1)} %get-tuple-element.27), channel_id=1, source_target_pairs={{0,2},{1,3},{2,0},{3,1},{4,6},{5,7},{6,4},{7,5},{8,10},{9,11},{10,... | collective-permute-start | bytes 294920 | tf_op jit(solution)/shard_map/ppermute | solution.py:162
  103.0 0.0 collective-permute-start.7
  103.0 0.6 collective-permute-start.8
  103.6 0.0 collective-permute-done.9
  103.6 3.5 %collective-permute-done.6 = bf16[128,384]{1,0:T(8,128)(2,1)S(1)} collective-permute-done((bf16[128,384]{1,0:T(8,128)(2,1)}, bf16[128,384]{1,0:T(8,128)(2,1)S(1)}, u32[]{:S(2)}, u32[]{:S(2)}) %collective-permute-start.6) | collective-permute-done | bytes 98336 | tf_op jit(solution)/shard_map/ppermute | solution.py:162
  107.1 0.0 collective-permute-done.7
  107.1 1.2 %collective-permute-done.8 = bf16[128,384]{1,0:T(8,128)(2,1)S(1)} collective-permute-done((bf16[128,384]{1,0:T(8,128)(2,1)}, bf16[128,384]{1,0:T(8,128)(2,1)S(1)}, u32[]{:S(2)}, u32[]{:S(2)}) %collective-permute-start.8) | collective-permute-done | bytes 98336 | tf_op jit(solution)/shard_map/ppermute | solution.py:162
  108.3 0.0 collective-permute-done.10
  108.3 4.6 %fusion.8 = bf16[128,3072]{1,0:T(8,128)(2,1)} fusion(bf16[384,3072]{1,0:T(8,128)(2,1)S(1)} %collective-permute-done.10, bf16[384,3072]{1,0:T(8,128)(2,1)} %collective-permute-done.9, bf16[384,3072]{1,0:T(8,128)(2,1)} %collective-permute-done, bf16[384,3072]{1,0:T(8,128)(2,1)} %param.13, bf16[128,384]{1,0:T(8,128)(2,1)S(1)} %collective-permute-done.8, ...), kind=kOutput, calls=%fused_computation.10 | convolution fusion | flops 1247674368 | bytes 10616832 | tf_op jit(solution)/shard_map/dot_general | solution.py:294
  (19 shorter events, 0.2 us)
Async XLA Ops:
  0.0 64.8 %copy-start = (bf16[3072,384]{1,0:T(8,128)(2,1)S(1)}, bf16[3072,384]{1,0:T(8,128)(2,1)}, u32[]{:S(2)}) copy-start(bf16[3072,384]{1,0:T(8,128)(2,1)} %param.11) | copy-start | bytes 7077892
  7.2 7.4 %copy-start.2 = (bf16[3072]{0:T(1024)(128)(2,1)S(1)}, bf16[3072]{0:T(1024)(128)(2,1)}, u32[]{:S(2)}) copy-start(bf16[3072]{0:T(1024)(128)(2,1)} %param.10) | copy-start | bytes 18436
  7.2 7.4 %copy-start.1 = (bf16[128,3072]{1,0:T(8,128)(2,1)S(1)}, bf16[128,3072]{1,0:T(8,128)(2,1)}, u32[]{:S(2)}) copy-start(bf16[128,3072]{1,0:T(8,128)(2,1)} %param.9) | copy-start | bytes 2359300
  7.2 55.7 %all-to-all-start = ((bf16[64,128,128]{2,1,0:T(8,128)(2,1)}), bf16[64,128,128]{2,1,0:T(8,128)(2,1)}, u32[]{:S(2)}, u32[]{:S(2)}) async-start(bf16[64,128,128]{2,1,0:T(8,128)(2,1)} %gather_fusion), calls=%async_computation | async-start | bytes 4194304 | tf_op jit(solution)/shard_map/all_to_all | solution.py:212
  14.5 22.3 %copy-start.3 = (s32[8]{0:T(128)S(1)}, s32[8]{0:T(128)}, u32[]{:S(2)}) copy-start(s32[8]{0:T(128)} %param.15) | copy-start | bytes 100
  16.0 23.3 %collective-permute-start.2 = (bf16[128,3072]{1,0:T(8,128)(2,1)}, bf16[128,3072]{1,0:T(8,128)(2,1)S(1)}, u32[]{:S(2)}, u32[]{:S(2)}) collective-permute-start(bf16[128,3072]{1,0:T(8,128)(2,1)} %fusion.13), channel_id=1, source_target_pairs={{0,1},{1,0},{2,3},{3,2},{4,5},{5,4},{6,7},{7,6},{8,9},{9,8},{10,11... | collective-permute-start | bytes 2359304 | tf_op jit(solution)/shard_map/ppermute | solution.py:162
  16.0 20.7 %collective-permute-start.1 = (bf16[128,3072]{1,0:T(8,128)(2,1)}, bf16[128,3072]{1,0:T(8,128)(2,1)}, u32[]{:S(2)}, u32[]{:S(2)}) collective-permute-start(bf16[128,3072]{1,0:T(8,128)(2,1)} %fusion.13), channel_id=1, source_target_pairs={{0,2},{1,3},{2,0},{3,1},{4,6},{5,7},{6,4},{7,5},{8,10},{9,11},{10,... | collective-permute-start | bytes 2359304 | tf_op jit(solution)/shard_map/ppermute | solution.py:162
  17.5 83.7 %collective-permute-start = (bf16[384,3072]{1,0:T(8,128)(2,1)}, bf16[384,3072]{1,0:T(8,128)(2,1)}, u32[]{:S(2)}, u32[]{:S(2)}) collective-permute-start(bf16[384,3072]{1,0:T(8,128)(2,1)} %param.13), channel_id=1, source_target_pairs={{0,2},{1,3},{2,0},{3,1},{4,6},{5,7},{6,4},{7,5},{8,10},{9,11},{10,... | collective-permute-start | bytes 7077896 | tf_op jit(solution)/shard_map/ppermute | solution.py:162
  18.0 85.6 %collective-permute-start.9 = (bf16[384,3072]{1,0:T(8,128)(2,1)}, bf16[384,3072]{1,0:T(8,128)(2,1)}, u32[]{:S(2)}, u32[]{:S(2)}) collective-permute-start(bf16[384,3072]{1,0:T(8,128)(2,1)} %param.13), channel_id=1, source_target_pairs={{0,1},{1,0},{2,3},{3,2},{4,5},{5,4},{6,7},{7,6},{8,9},{9,8},{10,11... | collective-permute-start | bytes 7077896 | tf_op jit(solution)/shard_map/ppermute | solution.py:162
  36.6 2.6 %collective-permute-start.3 = (bf16[128,3072]{1,0:T(8,128)(2,1)}, bf16[128,3072]{1,0:T(8,128)(2,1)}, u32[]{:S(2)}, u32[]{:S(2)}) collective-permute-start(bf16[128,3072]{1,0:T(8,128)(2,1)} %collective-permute-done.1), channel_id=1, source_target_pairs={{0,1},{1,0},{2,3},{3,2},{4,5},{5,4},{6,7},{7,6},{8,9},{9,8},{10,11... | collective-permute-start | bytes 2359304 | tf_op jit(solution)/shard_map/ppermute | solution.py:162
  62.9 7.4 %collective-permute-start.4 = (bf16[64,128,128]{2,1,0:T(8,128)(2,1)}, bf16[64,128,128]{2,1,0:T(8,128)(2,1)}, u32[]{:S(2)}, u32[]{:S(2)}) collective-permute-start(bf16[64,128,128]{2,1,0:T(8,128)(2,1)} %all-to-all-done), channel_id=1, source_target_pairs={{0,1},{1,0},{2,3},{3,2},{4,5},{5,4},{6,7},{7,6},{8,9},{9,8},{10,11... | collective-permute-start | bytes 6291464 | tf_op jit(solution)/shard_map/ppermute | solution.py:162
  67.8 1.7 %collective-permute-start.5 = (bf16[512,128]{1,0:T(8,128)(2,1)S(1)}, bf16[512,128]{1,0:T(8,128)(2,1)S(1)}, u32[]{:S(2)}, u32[]{:S(2)}) collective-permute-start(bf16[512,128]{1,0:T(8,128)(2,1)S(1)} %fusion.30), channel_id=1, source_target_pairs={{0,1},{1,0},{2,3},{3,2},{4,5},{5,4},{6,7},{7,6},{8,9},{9,8},{10,11... | collective-permute-start | bytes 393224 | tf_op jit(solution)/shard_map/ppermute | solution.py:22
  101.2 7.1 %collective-permute-start.10 = (bf16[384,3072]{1,0:T(8,128)(2,1)}, bf16[384,3072]{1,0:T(8,128)(2,1)S(1)}, u32[]{:S(2)}, u32[]{:S(2)}) collective-permute-start(bf16[384,3072]{1,0:T(8,128)(2,1)} %collective-permute-done), channel_id=1, source_target_pairs={{0,1},{1,0},{2,3},{3,2},{4,5},{5,4},{6,7},{7,6},{8,9},{9,8},{10,11... | collective-permute-start | bytes 7077896 | tf_op jit(solution)/shard_map/ppermute | solution.py:162
  101.5 5.6 %collective-permute-start.6 = (bf16[128,384]{1,0:T(8,128)(2,1)}, bf16[128,384]{1,0:T(8,128)(2,1)S(1)}, u32[]{:S(2)}, u32[]{:S(2)}) collective-permute-start(bf16[128,384]{1,0:T(8,128)(2,1)} %get-tuple-element.27), channel_id=1, source_target_pairs={{0,2},{1,3},{2,0},{3,1},{4,6},{5,7},{6,4},{7,5},{8,10},{9,11},{10,... | collective-permute-start | bytes 294920 | tf_op jit(solution)/shard_map/ppermute | solution.py:162
  103.0 4.1 %collective-permute-start.7 = (bf16[128,384]{1,0:T(8,128)(2,1)}, bf16[128,384]{1,0:T(8,128)(2,1)S(1)}, u32[]{:S(2)}, u32[]{:S(2)}) collective-permute-start(bf16[128,384]{1,0:T(8,128)(2,1)} %get-tuple-element.28), channel_id=1, source_target_pairs={{0,1},{1,0},{2,3},{3,2},{4,5},{5,4},{6,7},{7,6},{8,9},{9,8},{10,11... | collective-permute-start | bytes 294920 | tf_op jit(solution)/shard_map/ppermute | solution.py:162
  103.0 5.3 %collective-permute-start.8 = (bf16[128,384]{1,0:T(8,128)(2,1)}, bf16[128,384]{1,0:T(8,128)(2,1)S(1)}, u32[]{:S(2)}, u32[]{:S(2)}) collective-permute-start(bf16[128,384]{1,0:T(8,128)(2,1)} %get-tuple-element.29), channel_id=1, source_target_pairs={{0,3},{1,2},{2,1},{3,0},{4,7},{5,6},{6,5},{7,4},{8,11},{9,10},{10,... | collective-permute-start | bytes 294920 | tf_op jit(solution)/shard_map/ppermute | solution.py:162

commit v16 on v13

--- a/solution.py
+++ b/solution.py
@@ -23,8 +23,8 @@
 
 
 def attend_kernel(
-    n_cache, tk, scale, part_ref, q_ref, mine_hbm, other_hbm, nk_hbm, nv_hbm, bias_ref,
-    *rest,
+    n_cache, tk, scale, blocks, part_ref, q_ref, mine_hbm, other_hbm, own_hbm, partner_hbm,
+    bias_ref, *rest,
 ):
     *o_refs, k_scr, v_scr, s_scr, sems = rest
     bq, head_dim = q_ref.shape
@@ -33,12 +33,19 @@
 
     @pl.when(pl.program_id(0) == 0)
     def _():
-        def load(src_k, src_v):
+        def load(src_k, src_v, own_dst, partner_dst):
+            span = (total - n_cache) // len(blocks)
             copies = [
                 pltpu.make_async_copy(src_k, k_scr.at[pl.ds(0, n_cache)], sems.at[0]),
                 pltpu.make_async_copy(src_v, v_scr.at[pl.ds(0, n_cache)], sems.at[1]),
-                pltpu.make_async_copy(nk_hbm, k_scr.at[pl.ds(n_cache, total - n_cache)], sems.at[2]),
-                pltpu.make_async_copy(nv_hbm, v_scr.at[pl.ds(n_cache, total - n_cache)], sems.at[3]),
+                pltpu.make_async_copy(own_hbm, own_dst.at[pl.ds(n_cache, total - n_cache)], sems.at[2]),
+            ] + [
+                pltpu.make_async_copy(
+                    partner_hbm.at[pl.ds(j * span, span)],
+                    partner_dst.at[pl.ds(n_cache + k * span, span)],
+                    sems.at[3 + k],
+                )
+                for k, j in enumerate(blocks)
             ]
             for copy in copies:
                 copy.start()
@@ -47,11 +54,11 @@
 
         @pl.when(part_ref[0] == 0)
         def _():
-            load(mine_hbm, other_hbm)
+            load(mine_hbm, other_hbm, k_scr, v_scr)
 
         @pl.when(part_ref[0] != 0)
         def _():
-            load(other_hbm, mine_hbm)
+            load(other_hbm, mine_hbm, v_scr, k_scr)
 
     q = q_ref[...]
     part_rows = bq // len(o_refs)
@@ -102,11 +109,11 @@
         o_ref[...] = acc[k * part_rows:(k + 1) * part_rows].astype(o_ref.dtype)
 
 
-def attend(queries, mine, other, new_keys, new_values, part, bias, block_base):
+def attend(queries, mine, other, own_new, partner_new, blocks, part, bias, block_base):
     rows, width = queries.shape
     splits = block_base.shape[0]
     n_cache, head_dim = mine.shape
-    total = n_cache + new_keys.shape[0]
+    total = n_cache + own_new.shape[0]
     heads = width // head_dim
     tk = next(t for t in (512, 256, 128) if total % t == 0 and n_cache % t == 0)
     scale = 1.0 / math.sqrt(head_dim)
@@ -132,11 +139,11 @@
             pltpu.VMEM((total, head_dim), jnp.bfloat16),
             pltpu.VMEM((total, head_dim), jnp.bfloat16),
             pltpu.VMEM((rows, total), jnp.float32),
-            pltpu.SemaphoreType.DMA((4,)),
+            pltpu.SemaphoreType.DMA((3 + len(blocks),)),
         ],
     )
     return pl.pallas_call(
-        lambda *refs: attend_kernel(n_cache, tk, scale, *refs),
+        lambda *refs: attend_kernel(n_cache, tk, scale, blocks, *refs),
         out_shape=[jax.ShapeDtypeStruct((rows // splits, width), jnp.bfloat16)] * splits,
         grid_spec=grid_spec,
         compiler_params=pltpu.CompilerParams(dimension_semantics=("arbitrary",)),
@@ -144,7 +151,7 @@
         name="paged_prefill_attention",
     )(
         jnp.concatenate([part.reshape(1), block_base]).astype(jnp.int32),
-        queries, mine, other, new_keys, new_values, bias,
+        queries, mine, other, own_new, partner_new, bias,
     )
 
 
@@ -251,11 +258,6 @@
     received, own_ready = lax.optimization_barrier((received, own_ready))
     partner_ready = from_partner(own_ready, "head", 0)
     partner_blocks = [row_masks.index(m ^ 1) for m in row_masks]
-    partner_ready = jnp.concatenate(
-        [partner_ready[j * local_rows:(j + 1) * local_rows] for j in partner_blocks], 0
-    )
-    new_keys = jnp.where(holds_keys, own_ready, partner_ready)
-    new_values = jnp.where(holds_keys, partner_ready, own_ready)
     mask_rows = lax.dynamic_slice_in_dim(token_mask, me_dp * block_rows, block_rows, 0)
     cache_ok = (has_page[:, 0, :, None] & (key_pos[:, 0] < my_lengths[0])).reshape(-1)
     key_ok = jnp.concatenate([cache_ok, jnp.take(mask_rows, true_row) == 1])
@@ -266,8 +268,9 @@
         queries,
         received.reshape(-1, head_dim),
         other_half.reshape(-1, head_dim),
-        new_keys,
-        new_values,
+        own_ready,
+        partner_ready,
+        partner_blocks,
         part,
         bias.reshape(1, -1),
         jnp.stack([(current_head ^ m) * local_rows for m in row_masks]),

time: 114 us -> 113 us (level)
  transfers between devices with their start and end apart: 12 -> 12, of which waited for: 4 -> 4; matrix products, arithmetic and copies ran while one was open for 17% -> 16% of each run, Pallas kernels for 28% -> 28%
where the time goes in v16:
time: 113 us
  waiting for transfers between devices  37.7 us (33%)
  Pallas kernels  31.5 us (28%)
  starting transfers between devices  12.4 us (11%)
  local copies, waits for them, and re-layouts  12.2 us (11%)
  matrix products  10.5 us (9%)
  other arithmetic  8.18 us (7%)
    pallas_call x1, Pallas kernels, attend(): pl.pallas_call(lambda *refs: attend_kernel(n_cache, tk, scale, blocks, *r...  31.5 us
    all_to_all x1, waiting for transfers between devices, body(): lax.all_to_all(outgoing, 'dp', split_axis=0, concat_axis=0, tiled=True)  19.2 us
    ppermute x10, waiting for transfers between devices, exchange(): return lax.ppermute(value, axis, pairs)  18.5 us
    all_to_all x1, starting transfers between devices, body(): lax.all_to_all(outgoing, 'dp', split_axis=0, concat_axis=0, tiled=True)  7.38 us
    gather x1, local copies, waits for them, and re-layouts, body(): outgoing = kv_pool[local_page.reshape(-1), key_value_head, part]  5.07 us
    dot_general x1, matrix products, body(): out = jnp.dot(ordered, held_w, preferred_element_type=jnp.float32)  4.63 us
    ppermute x10, starting transfers between devices, exchange(): return lax.ppermute(value, axis, pairs)  4.48 us
    gather x1, local copies, waits for them, and re-layouts, body(): key_ok = jnp.concatenate([cache_ok, jnp.take(mask_rows, true_row) == 1])  3.48 us
  transfers between devices with their start and end apart: 12, of which 4 were waited for; matrix products, arithmetic and copies ran while one was open for 16% of the time, Pallas kernels for 28%

profile of v16, /device:TPU:0, one launch (start us, length us, event | category | flops | bytes accessed | tf_op | source)
XLA Modules:
  0.0 112.8 jit_solution(7738682730829227878)
XLA Ops:
  0.0 0.0 copy-start
  0.0 0.9 broadcast_compare_fusion.1
  0.9 0.2 reduce_window_sum.22
  1.1 0.7 add_select_fusion.1
  1.8 0.2 select_reduce_fusion.1
  2.0 0.1 reshape.522
  2.1 5.1 %gather_fusion = bf16[64,128,128]{2,1,0:T(8,128)(2,1)} fusion(bf16[48,2,2,128,128]{4,3,2,1,0:T(8,128)(2,1)} %param.14, s32[64]{0:T(128)S(1)} %fusion.45), kind=kCustom, calls=%fused_computation | custom fusion | bytes 4195072 | tf_op jit(solution)/shard_map/gather | solution.py:208
  7.2 0.0 copy-start.3
  7.2 0.0 copy-start.1
  7.2 7.4 %all-to-all-start = ((bf16[64,128,128]{2,1,0:T(8,128)(2,1)}), bf16[64,128,128]{2,1,0:T(8,128)(2,1)}, u32[]{:S(2)}, u32[]{:S(2)}) async-start(bf16[64,128,128]{2,1,0:T(8,128)(2,1)} %gather_fusion), calls=%async_computation | async-start | bytes 4194304 | tf_op jit(solution)/shard_map/all_to_all | solution.py:210
  14.5 0.0 copy-done.3
  14.5 0.0 copy-start.5
  14.6 0.0 copy-done.1
  14.6 0.2 fusion.11
  14.8 1.2 %fusion.13 = bf16[128,3072]{1,0:T(8,128)(2,1)} fusion(bf16[128,3072]{1,0:T(8,128)(2,1)S(1)} %copy-done.1, f32[3072]{0:T(1024)S(1)} %convert_element_type.49, f32[128]{0:T(128)S(1)} %add_rsqrt_fusion), kind=kLoop, calls=%fused_computation.16 | loop fusion | flops 1572864 | bytes 1585664 | tf_op jit(solution)/shard_map/convert_element_type | solution.py:225
  16.0 0.0 collective-permute-start.2
  16.0 1.5 %collective-permute-start.1 = (bf16[128,3072]{1,0:T(8,128)(2,1)}, bf16[128,3072]{1,0:T(8,128)(2,1)}, u32[]{:S(2)}, u32[]{:S(2)}) collective-permute-start(bf16[128,3072]{1,0:T(8,128)(2,1)} %fusion.13), channel_id=1, source_target_pairs={{0,2},{1,3},{2,0},{3,1},{4,6},{5,7},{6,4},{7,5},{8,10},{9,11},{10,... | collective-permute-start | bytes 2359304 | tf_op jit(solution)/shard_map/ppermute | solution.py:160
  17.5 0.5 collective-permute-start
  18.0 0.0 collective-permute-start.9
  18.1 0.2 reduce_window_sum.23
  18.3 0.8 dynamic_slice.14
  19.1 3.5 %gather_fusion.1 = s32[512]{0:T(512)S(1)} fusion(s32[512]{0:T(512)S(1)} %dynamic_slice.14, s32[1024]{0:T(1024)S(1)} %pad_clamp_fusion), kind=kCustom, calls=%fused_computation.1 | custom fusion | bytes 6144 | tf_op jit(solution)/shard_map/jit(_take)/gather | solution.py:263
  22.6 0.2 fusion.33
  22.8 13.8 %collective-permute-done.1 = bf16[128,3072]{1,0:T(8,128)(2,1)} collective-permute-done((bf16[128,3072]{1,0:T(8,128)(2,1)}, bf16[128,3072]{1,0:T(8,128)(2,1)}, u32[]{:S(2)}, u32[]{:S(2)}) %collective-permute-start.1) | collective-permute-done | bytes 786464 | tf_op jit(solution)/shard_map/ppermute | solution.py:160
  36.6 0.0 collective-permute-start.3
  36.6 0.0 copy-done.5
  36.6 0.6 dynamic_slice.11
  37.3 0.2 select_reduce_fusion
  37.5 0.7 fusion.34
  38.2 0.6 concatenate.86.refs_0_
  38.9 0.7 fusion.40
  39.5 0.0 collective-permute-done.2
  39.5 0.0 collective-permute-done.3
  39.5 2.8 %fusion.14 = f32[512,128]{1,0:T(8,128)S(1)} fusion(bf16[3072,128]{1,0:T(8,128)(2,1)} %param.12, bf16[128,3072]{1,0:T(8,128)(2,1)} %collective-permute-done.3, bf16[128,3072]{1,0:T(8,128)(2,1)S(1)} %collective-permute-done.2, bf16[128,3072]{1,0:T(8,128)(2,1)} %collective-permute-done.1, bf16[128,3072]{1,0:T(8,128)(2,1)} %fusion.13), kind=kOutput, calls=%fused_computation.17 | convolution fusion | flops 415236096 | bytes 4194304 | tf_op jit(solution)/shard_map/dot_general | solution.py:246
  42.4 1.2 %fusion.27 = (bf16[512,1,64]{2,0,1:T(8,128)(2,1)S(1)}, bf16[512,1,64]{2,0,1:T(8,128)(2,1)S(1)}) fusion(f32[512,1,128]{2,0,1:T(8,128)S(1)} %bitcast.32, f32[64]{0:T(128)S(1)} %multiply_exponential_fusion, f32[512]{0:T(512)S(1)} %fusion.40), kind=kLoop, calls=%fused_computation.35 | loop fusion | flops 294912 | bytes 395520 | tf_op jit(solution)/shard_map/sub | solution.py:173
  43.6 0.1 fusion.30.refs_4_
  43.7 0.0 copy-start.2
  43.7 19.2 %all-to-all-done = bf16[64,128,128]{2,1,0:T(8,128)(2,1)} async-done(((bf16[64,128,128]{2,1,0:T(8,128)(2,1)}), bf16[64,128,128]{2,1,0:T(8,128)(2,1)}, u32[]{:S(2)}, u32[]{:S(2)}) %all-to-all-start) | async-done | bytes 2097184 | tf_op jit(solution)/shard_map/all_to_all | solution.py:210
  62.9 0.0 collective-permute-start.4
  62.9 0.5 multiply_cosine_fusion.1
  63.4 0.7 add_select_fusion.refs_6_
  64.1 0.0 copy-done
  64.1 3.0 %fusion.15 = f32[512,384]{0,1:T(8,128)S(1)} fusion(bf16[3072,384]{1,0:T(8,128)(2,1)S(1)} %copy-done, bf16[128,3072]{1,0:T(8,128)(2,1)} %collective-permute-done.3, bf16[128,3072]{1,0:T(8,128)(2,1)S(1)} %collective-permute-done.2, bf16[128,3072]{1,0:T(8,128)(2,1)} %collective-permute-done.1, bf16[128,3072]{1,0:T(8,128)(2,1)} %fusion.13), kind=kOutput, calls=%fused_computation.18 | convolution fusion | flops 1220542464 | bytes 6291456 | tf_op jit(solution)/shard_map/dot_general | solution.py:245
  67.1 0.0 copy-done.2
  67.2 0.6 collective-permute-start.5
  67.7 0.1 subtract_convert_fusion
  67.9 0.9 copy.19.refs_1_
  68.8 0.0 collective-permute-done.5.refs_5_
  68.8 0.0 copy-start.4
  68.8 0.0 collective-permute-done.4
  68.8 0.6 copy-done.4
  69.5 31.5 %paged_prefill_attention.1 = (bf16[128,384]{1,0:T(8,128)(2,1)}, bf16[128,384]{1,0:T(8,128)(2,1)}, bf16[128,384]{1,0:T(8,128)(2,1)}, bf16[128,384]{1,0:T(8,128)(2,1)}) custom-call(s32[5]{0:T(128)} %concatenate.86.refs_0_, bf16[512,384]{1,0:T(8,128)(2,1)} %copy.19.refs_1_, bf16[8192,128]{1,0:T(8,128)(2,1)} %bitcast.11.refs_2_, ...), custom_call_target="tpu_custom_call" | custom-call | flops 6845104128 | bytes 5277696 | tf_op jit(solution)/shard_map/paged_prefill_attention/pallas_call | solution.py:145
  101.0 0.0 collective-permute-done
  101.0 0.3 collective-permute-start.10
  101.3 1.5 %collective-permute-start.6 = (bf16[128,384]{1,0:T(8,128)(2,1)}, bf16[128,384]{1,0:T(8,128)(2,1)S(1)}, u32[]{:S(2)}, u32[]{:S(2)}) collective-permute-start(bf16[128,384]{1,0:T(8,128)(2,1)} %get-tuple-element.27), channel_id=1, source_target_pairs={{0,2},{1,3},{2,0},{3,1},{4,6},{5,7},{6,4},{7,5},{8,10},{9,11},{10,... | collective-permute-start | bytes 294920 | tf_op jit(solution)/shard_map/ppermute | solution.py:160
  102.8 0.0 collective-permute-start.7
  102.9 0.6 collective-permute-start.8
  103.5 0.0 collective-permute-done.9
  103.5 3.5 %collective-permute-done.6 = bf16[128,384]{1,0:T(8,128)(2,1)S(1)} collective-permute-done((bf16[128,384]{1,0:T(8,128)(2,1)}, bf16[128,384]{1,0:T(8,128)(2,1)S(1)}, u32[]{:S(2)}, u32[]{:S(2)}) %collective-permute-start.6) | collective-permute-done | bytes 98336 | tf_op jit(solution)/shard_map/ppermute | solution.py:160
  107.0 0.0 collective-permute-done.7
  107.0 1.2 %collective-permute-done.8 = bf16[128,384]{1,0:T(8,128)(2,1)S(1)} collective-permute-done((bf16[128,384]{1,0:T(8,128)(2,1)}, bf16[128,384]{1,0:T(8,128)(2,1)S(1)}, u32[]{:S(2)}, u32[]{:S(2)}) %collective-permute-start.8) | collective-permute-done | bytes 98336 | tf_op jit(solution)/shard_map/ppermute | solution.py:160
  108.1 0.0 collective-permute-done.10
  108.1 4.6 %fusion.8 = bf16[128,3072]{1,0:T(8,128)(2,1)} fusion(bf16[384,3072]{1,0:T(8,128)(2,1)S(1)} %collective-permute-done.10, bf16[384,3072]{1,0:T(8,128)(2,1)} %collective-permute-done.9, bf16[384,3072]{1,0:T(8,128)(2,1)} %collective-permute-done, bf16[384,3072]{1,0:T(8,128)(2,1)} %param.13, bf16[128,384]{1,0:T(8,128)(2,1)S(1)} %collective-permute-done.8, ...), kind=kOutput, calls=%fused_computation.10 | convolution fusion | flops 1247674368 | bytes 10616832 | tf_op jit(solution)/shard_map/dot_general | solution.py:288
  (18 shorter events, 0.2 us)
Async XLA Ops:
  0.0 64.1 %copy-start = (bf16[3072,384]{1,0:T(8,128)(2,1)S(1)}, bf16[3072,384]{1,0:T(8,128)(2,1)}, u32[]{:S(2)}) copy-start(bf16[3072,384]{1,0:T(8,128)(2,1)} %param.11) | copy-start | bytes 7077892
  7.2 7.4 %copy-start.3 = (bf16[3072]{0:T(1024)(128)(2,1)S(1)}, bf16[3072]{0:T(1024)(128)(2,1)}, u32[]{:S(2)}) copy-start(bf16[3072]{0:T(1024)(128)(2,1)} %param.10) | copy-start | bytes 18436
  7.2 7.4 %copy-start.1 = (bf16[128,3072]{1,0:T(8,128)(2,1)S(1)}, bf16[128,3072]{1,0:T(8,128)(2,1)}, u32[]{:S(2)}) copy-start(bf16[128,3072]{1,0:T(8,128)(2,1)} %param.9) | copy-start | bytes 2359300
  7.2 55.7 %all-to-all-start = ((bf16[64,128,128]{2,1,0:T(8,128)(2,1)}), bf16[64,128,128]{2,1,0:T(8,128)(2,1)}, u32[]{:S(2)}, u32[]{:S(2)}) async-start(bf16[64,128,128]{2,1,0:T(8,128)(2,1)} %gather_fusion), calls=%async_computation | async-start | bytes 4194304 | tf_op jit(solution)/shard_map/all_to_all | solution.py:210
  14.5 22.1 %copy-start.5 = (s32[8]{0:T(128)S(1)}, s32[8]{0:T(128)}, u32[]{:S(2)}) copy-start(s32[8]{0:T(128)} %param.15) | copy-start | bytes 100
  16.0 23.5 %collective-permute-start.2 = (bf16[128,3072]{1,0:T(8,128)(2,1)}, bf16[128,3072]{1,0:T(8,128)(2,1)S(1)}, u32[]{:S(2)}, u32[]{:S(2)}) collective-permute-start(bf16[128,3072]{1,0:T(8,128)(2,1)} %fusion.13), channel_id=1, source_target_pairs={{0,1},{1,0},{2,3},{3,2},{4,5},{5,4},{6,7},{7,6},{8,9},{9,8},{10,11... | collective-permute-start | bytes 2359304 | tf_op jit(solution)/shard_map/ppermute | solution.py:160
  16.0 20.7 %collective-permute-start.1 = (bf16[128,3072]{1,0:T(8,128)(2,1)}, bf16[128,3072]{1,0:T(8,128)(2,1)}, u32[]{:S(2)}, u32[]{:S(2)}) collective-permute-start(bf16[128,3072]{1,0:T(8,128)(2,1)} %fusion.13), channel_id=1, source_target_pairs={{0,2},{1,3},{2,0},{3,1},{4,6},{5,7},{6,4},{7,5},{8,10},{9,11},{10,... | collective-permute-start | bytes 2359304 | tf_op jit(solution)/shard_map/ppermute | solution.py:160
  17.5 83.5 %collective-permute-start = (bf16[384,3072]{1,0:T(8,128)(2,1)}, bf16[384,3072]{1,0:T(8,128)(2,1)}, u32[]{:S(2)}, u32[]{:S(2)}) collective-permute-start(bf16[384,3072]{1,0:T(8,128)(2,1)} %param.13), channel_id=1, source_target_pairs={{0,2},{1,3},{2,0},{3,1},{4,6},{5,7},{6,4},{7,5},{8,10},{9,11},{10,... | collective-permute-start | bytes 7077896 | tf_op jit(solution)/shard_map/ppermute | solution.py:160
  18.0 85.5 %collective-permute-start.9 = (bf16[384,3072]{1,0:T(8,128)(2,1)}, bf16[384,3072]{1,0:T(8,128)(2,1)}, u32[]{:S(2)}, u32[]{:S(2)}) collective-permute-start(bf16[384,3072]{1,0:T(8,128)(2,1)} %param.13), channel_id=1, source_target_pairs={{0,1},{1,0},{2,3},{3,2},{4,5},{5,4},{6,7},{7,6},{8,9},{9,8},{10,11... | collective-permute-start | bytes 7077896 | tf_op jit(solution)/shard_map/ppermute | solution.py:160
  36.6 2.9 %collective-permute-start.3 = (bf16[128,3072]{1,0:T(8,128)(2,1)}, bf16[128,3072]{1,0:T(8,128)(2,1)}, u32[]{:S(2)}, u32[]{:S(2)}) collective-permute-start(bf16[128,3072]{1,0:T(8,128)(2,1)} %collective-permute-done.1), channel_id=1, source_target_pairs={{0,1},{1,0},{2,3},{3,2},{4,5},{5,4},{6,7},{7,6},{8,9},{9,8},{10,11... | collective-permute-start | bytes 2359304 | tf_op jit(solution)/shard_map/ppermute | solution.py:160
  43.7 23.4 %copy-start.2 = (bf16[512,128]{1,0:T(8,128)(2,1)}, bf16[512,128]{1,0:T(8,128)(2,1)S(1)}, u32[]{:S(2)}) copy-start(bf16[512,128]{1,0:T(8,128)(2,1)S(1)} %fusion.30.refs_4_) | copy-start | bytes 393220
  62.9 5.9 %collective-permute-start.4 = (bf16[64,128,128]{2,1,0:T(8,128)(2,1)}, bf16[64,128,128]{2,1,0:T(8,128)(2,1)}, u32[]{:S(2)}, u32[]{:S(2)}) collective-permute-start(bf16[64,128,128]{2,1,0:T(8,128)(2,1)} %all-to-all-done), channel_id=1, source_target_pairs={{0,1},{1,0},{2,3},{3,2},{4,5},{5,4},{6,7},{7,6},{8,9},{9,8},{10,11... | collective-permute-start | bytes 6291464 | tf_op jit(solution)/shard_map/ppermute | solution.py:160
  67.2 1.7 %collective-permute-start.5 = (bf16[512,128]{1,0:T(8,128)(2,1)S(1)}, bf16[512,128]{1,0:T(8,128)(2,1)S(1)}, u32[]{:S(2)}, u32[]{:S(2)}) collective-permute-start(bf16[512,128]{1,0:T(8,128)(2,1)S(1)} %fusion.30.refs_4_), channel_id=1, source_target_pairs={{0,1},{1,0},{2,3},{3,2},{4,5},{5,4},{6,7},{7,6},{8,9},{9,8},{10,11... | collective-permute-start | bytes 393224 | tf_op jit(solution)/shard_map/ppermute | solution.py:22
  68.8 0.7 copy-start.4
  101.0 7.1 %collective-permute-start.10 = (bf16[384,3072]{1,0:T(8,128)(2,1)}, bf16[384,3072]{1,0:T(8,128)(2,1)S(1)}, u32[]{:S(2)}, u32[]{:S(2)}) collective-permute-start(bf16[384,3072]{1,0:T(8,128)(2,1)} %collective-permute-done), channel_id=1, source_target_pairs={{0,1},{1,0},{2,3},{3,2},{4,5},{5,4},{6,7},{7,6},{8,9},{9,8},{10,11... | collective-permute-start | bytes 7077896 | tf_op jit(solution)/shard_map/ppermute | solution.py:160
  101.3 5.6 %collective-permute-start.6 = (bf16[128,384]{1,0:T(8,128)(2,1)}, bf16[128,384]{1,0:T(8,128)(2,1)S(1)}, u32[]{:S(2)}, u32[]{:S(2)}) collective-permute-start(bf16[128,384]{1,0:T(8,128)(2,1)} %get-tuple-element.27), channel_id=1, source_target_pairs={{0,2},{1,3},{2,0},{3,1},{4,6},{5,7},{6,4},{7,5},{8,10},{9,11},{10,... | collective-permute-start | bytes 294920 | tf_op jit(solution)/shard_map/ppermute | solution.py:160
  102.8 4.1 %collective-permute-start.7 = (bf16[128,384]{1,0:T(8,128)(2,1)}, bf16[128,384]{1,0:T(8,128)(2,1)S(1)}, u32[]{:S(2)}, u32[]{:S(2)}) collective-permute-start(bf16[128,384]{1,0:T(8,128)(2,1)} %get-tuple-element.28), channel_id=1, source_target_pairs={{0,1},{1,0},{2,3},{3,2},{4,5},{5,4},{6,7},{7,6},{8,9},{9,8},{10,11... | collective-permute-start | bytes 294920 | tf_op jit(solution)/shard_map/ppermute | solution.py:160
  102.9 5.3 %collective-permute-start.8 = (bf16[128,384]{1,0:T(8,128)(2,1)}, bf16[128,384]{1,0:T(8,128)(2,1)S(1)}, u32[]{:S(2)}, u32[]{:S(2)}) collective-permute-start(bf16[128,384]{1,0:T(8,128)(2,1)} %get-tuple-element.29), channel_id=1, source_target_pairs={{0,3},{1,2},{2,1},{3,0},{4,7},{5,6},{6,5},{7,4},{8,11},{9,10},{10,... | collective-permute-start | bytes 294920 | tf_op jit(solution)/shard_map/ppermute | solution.py:160

commit v17 on v13

--- a/solution.py
+++ b/solution.py
@@ -89,7 +89,8 @@
             part = part + e[:, g * 128:(g + 1) * 128]
         return part
 
-    part = lax.fori_loop(0, total // tk, expo, jnp.zeros((bq, 128), jnp.float32), unroll=8)
+    part = lax.fori_loop(0, n_cache // tk, expo, jnp.zeros((bq, 128), jnp.float32), unroll=8)
+    part = lax.fori_loop(n_cache // tk, total // tk, expo, part)
     inverse = 1.0 / jnp.sum(part, -1, keepdims=True)
 
     def weigh(c, acc):
@@ -97,7 +98,8 @@
         w = (s_scr[:, pl.ds(start, tk)] * inverse).astype(jnp.bfloat16)
         return acc + jnp.dot(w, v_scr[pl.ds(start, tk), :], preferred_element_type=jnp.float32)
 
-    acc = lax.fori_loop(0, total // tk, weigh, jnp.zeros((bq, head_dim), jnp.float32), unroll=8)
+    acc = lax.fori_loop(0, n_cache // tk, weigh, jnp.zeros((bq, head_dim), jnp.float32), unroll=8)
+    acc = lax.fori_loop(n_cache // tk, total // tk, weigh, acc)
     for k, o_ref in enumerate(o_refs):
         o_ref[...] = acc[k * part_rows:(k + 1) * part_rows].astype(o_ref.dtype)
 

time: 114 us -> 114 us (level)
  no operation moved by 1% of the time
where the time goes in v17:
time: 114 us; the launch traced here: 113 us
  waiting for transfers between devices  38.1 us (33%)
  Pallas kernels  31.4 us (28%)
  starting transfers between devices  12.4 us (11%)
  local copies, waits for them, and re-layouts  11.7 us (10%)
  matrix products  10.5 us (9%)
  other arithmetic  9.02 us (8%)
    pallas_call x1, Pallas kernels, attend(): pl.pallas_call(lambda *refs: attend_kernel(n_cache, tk, scale, *refs), ou...  31.4 us
    all_to_all x1, waiting for transfers between devices, body(): lax.all_to_all(outgoing, 'dp', split_axis=0, concat_axis=0, tiled=True)  19.4 us
    ppermute x10, waiting for transfers between devices, exchange(): return lax.ppermute(value, axis, pairs)  18.7 us
    all_to_all x1, starting transfers between devices, body(): lax.all_to_all(outgoing, 'dp', split_axis=0, concat_axis=0, tiled=True)  7.38 us
    gather x1, local copies, waits for them, and re-layouts, body(): outgoing = kv_pool[local_page.reshape(-1), key_value_head, part]  5.07 us
    dot_general x1, matrix products, body(): out = jnp.dot(ordered, held_w, preferred_element_type=jnp.float32)  4.63 us
    ppermute x10, starting transfers between devices, exchange(): return lax.ppermute(value, axis, pairs)  4.49 us
    gather x1, local copies, waits for them, and re-layouts, body(): key_ok = jnp.concatenate([cache_ok, jnp.take(mask_rows, true_row) == 1])  3.48 us
  transfers between devices with their start and end apart: 12, of which 4 were waited for; matrix products, arithmetic and copies ran while one was open for 17% of the time, Pallas kernels for 28%

profile of v17, /device:TPU:0, one launch (start us, length us, event | category | flops | bytes accessed | tf_op | source)
XLA Modules:
  0.0 113.5 jit_solution(2196172472238889712)
XLA Ops:
  0.0 0.0 copy-start
  0.0 0.9 broadcast_compare_fusion.1
  0.9 0.2 reduce_window_sum.22
  1.1 0.7 add_select_fusion.1
  1.8 0.2 select_reduce_fusion.1
  2.0 0.1 reshape.522
  2.1 5.1 %gather_fusion = bf16[64,128,128]{2,1,0:T(8,128)(2,1)} fusion(bf16[48,2,2,128,128]{4,3,2,1,0:T(8,128)(2,1)} %param.14, s32[64]{0:T(128)S(1)} %fusion.45), kind=kCustom, calls=%fused_computation | custom fusion | bytes 4195072 | tf_op jit(solution)/shard_map/gather | solution.py:203
  7.2 0.0 copy-start.2
  7.2 0.0 copy-start.1
  7.2 7.4 %all-to-all-start = ((bf16[64,128,128]{2,1,0:T(8,128)(2,1)}), bf16[64,128,128]{2,1,0:T(8,128)(2,1)}, u32[]{:S(2)}, u32[]{:S(2)}) async-start(bf16[64,128,128]{2,1,0:T(8,128)(2,1)} %gather_fusion), calls=%async_computation | async-start | bytes 4194304 | tf_op jit(solution)/shard_map/all_to_all | solution.py:205
  14.5 0.0 copy-done.2
  14.5 0.0 copy-start.3
  14.6 0.0 copy-done.1
  14.6 0.2 fusion.11
  14.8 1.2 %fusion.13 = bf16[128,3072]{1,0:T(8,128)(2,1)} fusion(bf16[128,3072]{1,0:T(8,128)(2,1)S(1)} %copy-done.1, f32[3072]{0:T(1024)S(1)} %convert_element_type.49, f32[128]{0:T(128)S(1)} %add_rsqrt_fusion), kind=kLoop, calls=%fused_computation.16 | loop fusion | flops 1572864 | bytes 1585664 | tf_op jit(solution)/shard_map/convert_element_type | solution.py:220
  16.0 0.0 collective-permute-start.2
  16.0 1.5 %collective-permute-start.1 = (bf16[128,3072]{1,0:T(8,128)(2,1)}, bf16[128,3072]{1,0:T(8,128)(2,1)}, u32[]{:S(2)}, u32[]{:S(2)}) collective-permute-start(bf16[128,3072]{1,0:T(8,128)(2,1)} %fusion.13), channel_id=1, source_target_pairs={{0,2},{1,3},{2,0},{3,1},{4,6},{5,7},{6,4},{7,5},{8,10},{9,11},{10,... | collective-permute-start | bytes 2359304 | tf_op jit(solution)/shard_map/ppermute | solution.py:155
  17.5 0.5 collective-permute-start
  18.0 0.0 collective-permute-start.9
  18.1 0.2 reduce_window_sum.23
  18.3 0.8 dynamic_slice.14
  19.1 3.5 %gather_fusion.1 = s32[512]{0:T(512)S(1)} fusion(s32[512]{0:T(512)S(1)} %dynamic_slice.14, s32[1024]{0:T(1024)S(1)} %pad_clamp_fusion), kind=kCustom, calls=%fused_computation.1 | custom fusion | bytes 6144 | tf_op jit(solution)/shard_map/jit(_take)/gather | solution.py:263
  22.6 14.0 %collective-permute-done.1 = bf16[128,3072]{1,0:T(8,128)(2,1)} collective-permute-done((bf16[128,3072]{1,0:T(8,128)(2,1)}, bf16[128,3072]{1,0:T(8,128)(2,1)}, u32[]{:S(2)}, u32[]{:S(2)}) %collective-permute-start.1) | collective-permute-done | bytes 786464 | tf_op jit(solution)/shard_map/ppermute | solution.py:155
  36.6 0.0 collective-permute-start.3
  36.6 0.2 fusion.33
  36.9 0.0 copy-done.3
  36.9 0.7 dynamic_slice.11
  37.5 0.2 select_reduce_fusion
  37.8 0.8 fusion.34
  38.6 0.7 fusion.40
  39.3 0.0 collective-permute-done.2
  39.3 0.0 collective-permute-done.3
  39.3 2.8 %fusion.14 = f32[512,128]{1,0:T(8,128)S(1)} fusion(bf16[3072,128]{1,0:T(8,128)(2,1)} %param.12, bf16[128,3072]{1,0:T(8,128)(2,1)} %collective-permute-done.3, bf16[128,3072]{1,0:T(8,128)(2,1)S(1)} %collective-permute-done.2, bf16[128,3072]{1,0:T(8,128)(2,1)} %collective-permute-done.1, bf16[128,3072]{1,0:T(8,128)(2,1)} %fusion.13), kind=kOutput, calls=%fused_computation.17 | convolution fusion | flops 415236096 | bytes 4194304 | tf_op jit(solution)/shard_map/dot_general | solution.py:241
  42.1 1.2 %fusion.27 = (bf16[512,1,64]{2,0,1:T(8,128)(2,1)S(1)}, bf16[512,1,64]{2,0,1:T(8,128)(2,1)S(1)}) fusion(f32[512,1,128]{2,0,1:T(8,128)S(1)} %bitcast.32, f32[64]{0:T(128)S(1)} %multiply_exponential_fusion, f32[512]{0:T(512)S(1)} %fusion.40), kind=kLoop, calls=%fused_computation.35 | loop fusion | flops 294912 | bytes 395520 | tf_op jit(solution)/shard_map/sub | solution.py:168
  43.4 0.1 fusion.30
  43.5 19.4 %all-to-all-done = bf16[64,128,128]{2,1,0:T(8,128)(2,1)} async-done(((bf16[64,128,128]{2,1,0:T(8,128)(2,1)}), bf16[64,128,128]{2,1,0:T(8,128)(2,1)}, u32[]{:S(2)}, u32[]{:S(2)}) %all-to-all-start) | async-done | bytes 2097184 | tf_op jit(solution)/shard_map/all_to_all | solution.py:205
  62.9 0.0 collective-permute-start.4
  62.9 0.7 add_select_fusion.refs_6_
  63.5 0.7 concatenate.90.refs_0_
  64.2 0.5 multiply_cosine_fusion.1
  64.7 0.0 copy-done
  64.8 3.0 %fusion.15 = f32[512,384]{0,1:T(8,128)S(1)} fusion(bf16[3072,384]{1,0:T(8,128)(2,1)S(1)} %copy-done, bf16[128,3072]{1,0:T(8,128)(2,1)} %collective-permute-done.3, bf16[128,3072]{1,0:T(8,128)(2,1)S(1)} %collective-permute-done.2, bf16[128,3072]{1,0:T(8,128)(2,1)} %collective-permute-done.1, bf16[128,3072]{1,0:T(8,128)(2,1)} %fusion.13), kind=kOutput, calls=%fused_computation.18 | convolution fusion | flops 1220542464 | bytes 6291456 | tf_op jit(solution)/shard_map/dot_general | solution.py:240
  67.8 0.6 collective-permute-start.5
  68.4 0.1 subtract_convert_fusion
  68.6 0.9 copy.19.refs_1_
  69.5 0.0 collective-permute-done.5
  69.5 0.8 broadcast_select_fusion
  70.3 0.0 collective-permute-done.4
  70.3 31.4 %paged_prefill_attention.1 = (bf16[128,384]{1,0:T(8,128)(2,1)}, bf16[128,384]{1,0:T(8,128)(2,1)}, bf16[128,384]{1,0:T(8,128)(2,1)}, bf16[128,384]{1,0:T(8,128)(2,1)}) custom-call(s32[5]{0:T(128)} %concatenate.90.refs_0_, bf16[512,384]{1,0:T(8,128)(2,1)} %copy.19.refs_1_, bf16[8192,128]{1,0:T(8,128)(2,1)} %bitcast.11.refs_2_, ...), custom_call_target="tpu_custom_call" | custom-call | flops 6845104128 | bytes 5277696 | tf_op jit(solution)/shard_map/paged_prefill_attention/pallas_call | solution.py:140
  101.7 0.0 collective-permute-done
  101.7 0.3 collective-permute-start.10
  102.0 1.5 %collective-permute-start.6 = (bf16[128,384]{1,0:T(8,128)(2,1)}, bf16[128,384]{1,0:T(8,128)(2,1)S(1)}, u32[]{:S(2)}, u32[]{:S(2)}) collective-permute-start(bf16[128,384]{1,0:T(8,128)(2,1)} %get-tuple-element.27), channel_id=1, source_target_pairs={{0,2},{1,3},{2,0},{3,1},{4,6},{5,7},{6,4},{7,5},{8,10},{9,11},{10,... | collective-permute-start | bytes 294920 | tf_op jit(solution)/shard_map/ppermute | solution.py:155
  103.6 0.0 collective-permute-start.7
  103.6 0.6 collective-permute-start.8
  104.2 0.0 collective-permute-done.9
  104.2 3.5 %collective-permute-done.6 = bf16[128,384]{1,0:T(8,128)(2,1)S(1)} collective-permute-done((bf16[128,384]{1,0:T(8,128)(2,1)}, bf16[128,384]{1,0:T(8,128)(2,1)S(1)}, u32[]{:S(2)}, u32[]{:S(2)}) %collective-permute-start.6) | collective-permute-done | bytes 98336 | tf_op jit(solution)/shard_map/ppermute | solution.py:155
  107.7 0.0 collective-permute-done.7
  107.7 1.2 %collective-permute-done.8 = bf16[128,384]{1,0:T(8,128)(2,1)S(1)} collective-permute-done((bf16[128,384]{1,0:T(8,128)(2,1)}, bf16[128,384]{1,0:T(8,128)(2,1)S(1)}, u32[]{:S(2)}, u32[]{:S(2)}) %collective-permute-start.8) | collective-permute-done | bytes 98336 | tf_op jit(solution)/shard_map/ppermute | solution.py:155
  108.9 0.0 collective-permute-done.10
  108.9 4.6 %fusion.8 = bf16[128,3072]{1,0:T(8,128)(2,1)} fusion(bf16[384,3072]{1,0:T(8,128)(2,1)S(1)} %collective-permute-done.10, bf16[384,3072]{1,0:T(8,128)(2,1)} %collective-permute-done.9, bf16[384,3072]{1,0:T(8,128)(2,1)} %collective-permute-done, bf16[384,3072]{1,0:T(8,128)(2,1)} %param.13, bf16[128,384]{1,0:T(8,128)(2,1)S(1)} %collective-permute-done.8, ...), kind=kOutput, calls=%fused_computation.10 | convolution fusion | flops 1247674368 | bytes 10616832 | tf_op jit(solution)/shard_map/dot_general | solution.py:287
  (19 shorter events, 0.2 us)
Async XLA Ops:
  0.0 64.8 %copy-start = (bf16[3072,384]{1,0:T(8,128)(2,1)S(1)}, bf16[3072,384]{1,0:T(8,128)(2,1)}, u32[]{:S(2)}) copy-start(bf16[3072,384]{1,0:T(8,128)(2,1)} %param.11) | copy-start | bytes 7077892
  7.2 7.4 %copy-start.2 = (bf16[3072]{0:T(1024)(128)(2,1)S(1)}, bf16[3072]{0:T(1024)(128)(2,1)}, u32[]{:S(2)}) copy-start(bf16[3072]{0:T(1024)(128)(2,1)} %param.10) | copy-start | bytes 18436
  7.2 7.4 %copy-start.1 = (bf16[128,3072]{1,0:T(8,128)(2,1)S(1)}, bf16[128,3072]{1,0:T(8,128)(2,1)}, u32[]{:S(2)}) copy-start(bf16[128,3072]{1,0:T(8,128)(2,1)} %param.9) | copy-start | bytes 2359300
  7.2 55.7 %all-to-all-start = ((bf16[64,128,128]{2,1,0:T(8,128)(2,1)}), bf16[64,128,128]{2,1,0:T(8,128)(2,1)}, u32[]{:S(2)}, u32[]{:S(2)}) async-start(bf16[64,128,128]{2,1,0:T(8,128)(2,1)} %gather_fusion), calls=%async_computation | async-start | bytes 4194304 | tf_op jit(solution)/shard_map/all_to_all | solution.py:205
  14.5 22.3 %copy-start.3 = (s32[8]{0:T(128)S(1)}, s32[8]{0:T(128)}, u32[]{:S(2)}) copy-start(s32[8]{0:T(128)} %param.15) | copy-start | bytes 100
  16.0 23.3 %collective-permute-start.2 = (bf16[128,3072]{1,0:T(8,128)(2,1)}, bf16[128,3072]{1,0:T(8,128)(2,1)S(1)}, u32[]{:S(2)}, u32[]{:S(2)}) collective-permute-start(bf16[128,3072]{1,0:T(8,128)(2,1)} %fusion.13), channel_id=1, source_target_pairs={{0,1},{1,0},{2,3},{3,2},{4,5},{5,4},{6,7},{7,6},{8,9},{9,8},{10,11... | collective-permute-start | bytes 2359304 | tf_op jit(solution)/shard_map/ppermute | solution.py:155
  16.0 20.7 %collective-permute-start.1 = (bf16[128,3072]{1,0:T(8,128)(2,1)}, bf16[128,3072]{1,0:T(8,128)(2,1)}, u32[]{:S(2)}, u32[]{:S(2)}) collective-permute-start(bf16[128,3072]{1,0:T(8,128)(2,1)} %fusion.13), channel_id=1, source_target_pairs={{0,2},{1,3},{2,0},{3,1},{4,6},{5,7},{6,4},{7,5},{8,10},{9,11},{10,... | collective-permute-start | bytes 2359304 | tf_op jit(solution)/shard_map/ppermute | solution.py:155
  17.5 84.2 %collective-permute-start = (bf16[384,3072]{1,0:T(8,128)(2,1)}, bf16[384,3072]{1,0:T(8,128)(2,1)}, u32[]{:S(2)}, u32[]{:S(2)}) collective-permute-start(bf16[384,3072]{1,0:T(8,128)(2,1)} %param.13), channel_id=1, source_target_pairs={{0,2},{1,3},{2,0},{3,1},{4,6},{5,7},{6,4},{7,5},{8,10},{9,11},{10,... | collective-permute-start | bytes 7077896 | tf_op jit(solution)/shard_map/ppermute | solution.py:155
  18.0 86.2 %collective-permute-start.9 = (bf16[384,3072]{1,0:T(8,128)(2,1)}, bf16[384,3072]{1,0:T(8,128)(2,1)}, u32[]{:S(2)}, u32[]{:S(2)}) collective-permute-start(bf16[384,3072]{1,0:T(8,128)(2,1)} %param.13), channel_id=1, source_target_pairs={{0,1},{1,0},{2,3},{3,2},{4,5},{5,4},{6,7},{7,6},{8,9},{9,8},{10,11... | collective-permute-start | bytes 7077896 | tf_op jit(solution)/shard_map/ppermute | solution.py:155
  36.6 2.6 %collective-permute-start.3 = (bf16[128,3072]{1,0:T(8,128)(2,1)}, bf16[128,3072]{1,0:T(8,128)(2,1)}, u32[]{:S(2)}, u32[]{:S(2)}) collective-permute-start(bf16[128,3072]{1,0:T(8,128)(2,1)} %collective-permute-done.1), channel_id=1, source_target_pairs={{0,1},{1,0},{2,3},{3,2},{4,5},{5,4},{6,7},{7,6},{8,9},{9,8},{10,11... | collective-permute-start | bytes 2359304 | tf_op jit(solution)/shard_map/ppermute | solution.py:155
  62.9 7.4 %collective-permute-start.4 = (bf16[64,128,128]{2,1,0:T(8,128)(2,1)}, bf16[64,128,128]{2,1,0:T(8,128)(2,1)}, u32[]{:S(2)}, u32[]{:S(2)}) collective-permute-start(bf16[64,128,128]{2,1,0:T(8,128)(2,1)} %all-to-all-done), channel_id=1, source_target_pairs={{0,1},{1,0},{2,3},{3,2},{4,5},{5,4},{6,7},{7,6},{8,9},{9,8},{10,11... | collective-permute-start | bytes 6291464 | tf_op jit(solution)/shard_map/ppermute | solution.py:155
  67.8 1.7 %collective-permute-start.5 = (bf16[512,128]{1,0:T(8,128)(2,1)S(1)}, bf16[512,128]{1,0:T(8,128)(2,1)S(1)}, u32[]{:S(2)}, u32[]{:S(2)}) collective-permute-start(bf16[512,128]{1,0:T(8,128)(2,1)S(1)} %fusion.30), channel_id=1, source_target_pairs={{0,1},{1,0},{2,3},{3,2},{4,5},{5,4},{6,7},{7,6},{8,9},{9,8},{10,11... | collective-permute-start | bytes 393224 | tf_op jit(solution)/shard_map/ppermute | solution.py:22
  101.7 7.1 %collective-permute-start.10 = (bf16[384,3072]{1,0:T(8,128)(2,1)}, bf16[384,3072]{1,0:T(8,128)(2,1)S(1)}, u32[]{:S(2)}, u32[]{:S(2)}) collective-permute-start(bf16[384,3072]{1,0:T(8,128)(2,1)} %collective-permute-done), channel_id=1, source_target_pairs={{0,1},{1,0},{2,3},{3,2},{4,5},{5,4},{6,7},{7,6},{8,9},{9,8},{10,11... | collective-permute-start | bytes 7077896 | tf_op jit(solution)/shard_map/ppermute | solution.py:155
  102.0 5.6 %collective-permute-start.6 = (bf16[128,384]{1,0:T(8,128)(2,1)}, bf16[128,384]{1,0:T(8,128)(2,1)S(1)}, u32[]{:S(2)}, u32[]{:S(2)}) collective-permute-start(bf16[128,384]{1,0:T(8,128)(2,1)} %get-tuple-element.27), channel_id=1, source_target_pairs={{0,2},{1,3},{2,0},{3,1},{4,6},{5,7},{6,4},{7,5},{8,10},{9,11},{10,... | collective-permute-start | bytes 294920 | tf_op jit(solution)/shard_map/ppermute | solution.py:155
  103.6 4.1 %collective-permute-start.7 = (bf16[128,384]{1,0:T(8,128)(2,1)}, bf16[128,384]{1,0:T(8,128)(2,1)S(1)}, u32[]{:S(2)}, u32[]{:S(2)}) collective-permute-start(bf16[128,384]{1,0:T(8,128)(2,1)} %get-tuple-element.28), channel_id=1, source_target_pairs={{0,1},{1,0},{2,3},{3,2},{4,5},{5,4},{6,7},{7,6},{8,9},{9,8},{10,11... | collective-permute-start | bytes 294920 | tf_op jit(solution)/shard_map/ppermute | solution.py:155
  103.6 5.3 %collective-permute-start.8 = (bf16[128,384]{1,0:T(8,128)(2,1)}, bf16[128,384]{1,0:T(8,128)(2,1)S(1)}, u32[]{:S(2)}, u32[]{:S(2)}) collective-permute-start(bf16[128,384]{1,0:T(8,128)(2,1)} %get-tuple-element.29), channel_id=1, source_target_pairs={{0,3},{1,2},{2,1},{3,0},{4,7},{5,6},{6,5},{7,4},{8,11},{9,10},{10,... | collective-permute-start | bytes 294920 | tf_op jit(solution)/shard_map/ppermute | solution.py:155
